TPU v7x, 256 devices: a whole 4x4x8 slice. The times are simulated.
256 devices in a mesh: seq: 256 (over y, x, z, core).
Axes of the slice: x: 4, y: 4, z: 8, core: 2. Of those that a mesh axis runs over, the one named last changes fastest.
Arguments:
- tokens: int32 [32768], P('seq'), may hold values from 0 to 4
- mask_flags: int32 [32768], P('seq'), may hold values from 0 to 1, as said below
- hidden_in: bfloat16 [32768, 1280], P('seq'), may hold values from -24 to 24
- grad_above: bfloat16 [32768, 1280], P('seq'), may hold values from -1.25 to 1.25
- w_in: bfloat16 [1280, 640], replicated, may hold values from -0.15625 to 0.15625
- conv_weight: bfloat16 [5, 640, 640], replicated, may hold values from -0.109375 to 0.109375
- w_out: bfloat16 [1280, 640], replicated, may hold values from -0.25 to 0.25
- head_weight: bfloat16 [1280, 6], replicated, may hold values from -0.15625 to 0.15625
Outputs:
- mean_loss: float32 [], replicated
- grad_up: bfloat16 [1280, 640], P('seq')
- grad_down: bfloat16 [1280, 640], P('seq')
Inputs may be any that keep to these rules, and one draw needn't show every extreme that they name: `mask_flags`: each flag is 0 or 1; the last position of the context is always masked.
All inputs are finite; a program needn't handle non-finite values.
Results may differ from a plain program's by a relative error of at most 0.009.
Values may be sent and summed in bfloat16 or wider, within the bound.
No kernel may reach another device: no remote copies, remote signals or barrier semaphores. Data moves between devices by JAX's collectives and lax.ppermute only.
A program may use at most 64 MiB of HBM per device.

v0:
```python
import jax
import jax.numpy as jnp
from jax import lax
from jax.sharding import PartitionSpec as P


def from_behind(block, axis, distance):
    devices = range(lax.axis_size(axis))
    route = [(i - distance, i) for i in devices if i - distance in devices]
    return lax.ppermute(block, axis, route)


def norm_gelu(values):
    centered = values - jnp.mean(values, -1, keepdims=True)
    variance = jnp.mean(centered * centered, -1, keepdims=True)
    return jax.nn.gelu(centered * lax.rsqrt(variance + 1e-05))


def spread(source_field, shard_reach):
    near_pieces = {}
    far_pieces = {}
    for direction in (1, -1):
        near_pieces[direction] = from_behind(source_field, "seq", direction * shard_reach)
    for direction in (1, -1):
        far_pieces[direction] = from_behind(source_field, "seq", 2 * direction * shard_reach)
    return [far_pieces[1], near_pieces[1], source_field, near_pieces[-1], far_pieces[-1]]


def shards(tokens, mask_flags, hidden_in, grad_above, w_in, conv_weight, w_out, head_weight):
    local_rows = tokens.shape[0]
    vocab_size = head_weight.shape[1]
    seq_devices = lax.axis_size("seq")
    shard_reach = 4
    context_rows = float(local_rows * seq_devices)
    masked = mask_flags.astype(jnp.float32)
    local_count = jnp.sum(masked)
    alphabet = jnp.arange(vocab_size, dtype=jnp.int32)
    first_act = norm_gelu(hidden_in.astype(jnp.float32)).astype(jnp.bfloat16)
    first_pre = jnp.dot(first_act, w_in, preferred_element_type=jnp.float32)
    narrow_activation = norm_gelu(first_pre).astype(jnp.bfloat16)
    kernel_tap_pile = jnp.stack(spread(narrow_activation, shard_reach))
    conv_pre = jnp.einsum(
        "krc,kcb->rb", kernel_tap_pile, conv_weight, preferred_element_type=jnp.float32
    )
    conv_act = norm_gelu(conv_pre).astype(jnp.bfloat16)
    projected = lax.dot_general(
        conv_act, w_out, (((1,), (1,)), ((), ())), preferred_element_type=jnp.float32
    )
    block_out = (hidden_in.astype(jnp.float32) + projected).astype(jnp.bfloat16)
    logits_t = lax.dot_general(
        head_weight, block_out, (((0,), (1,)), ((), ())), preferred_element_type=jnp.float32
    )
    log_total = jnp.log(jnp.sum(jnp.exp(logits_t), 0))
    target_hot = (alphabet[:, None] == tokens[None, :]).astype(jnp.float32)
    cross_ent = log_total - jnp.sum(target_hot * logits_t, 0)
    local_loss = jnp.sum(masked * cross_ent)
    loss_total, mask_total = lax.psum((local_loss, local_count), "seq")
    probability = jnp.exp(logits_t - log_total[None, :])
    grad_logits = (
        masked[None, :] * (probability - target_hot) * (context_rows / mask_total)
    ).astype(jnp.bfloat16)
    head_part = lax.dot_general(
        grad_logits, head_weight, (((0,), (1,)), ((), ())), preferred_element_type=jnp.float32
    )
    grad_block = (head_part + grad_above.astype(jnp.float32)).astype(jnp.bfloat16)
    columns = grad_block
    grad_down = lax.psum_scatter(
        lax.dot_general(
            columns, conv_act, (((0,), (0,)), ((), ())), preferred_element_type=jnp.float32
        ),
        "seq",
        scatter_dimension=0,
        tiled=True,
    ).astype(jnp.bfloat16)
    grad_conv_act = jnp.dot(grad_block, w_out, preferred_element_type=jnp.float32)
    gradient_before_activation = jax.vjp(norm_gelu, conv_pre)[1](grad_conv_act)[0].astype(
        jnp.bfloat16
    )
    back_pieces = spread(gradient_before_activation, shard_reach)
    backward_tap_pile = jnp.stack(back_pieces[::-1])
    grad_neck = jnp.einsum(
        "krc,kbc->rb", backward_tap_pile, conv_weight, preferred_element_type=jnp.float32
    )
    grad_first = jax.vjp(norm_gelu, first_pre)[1](grad_neck)[0].astype(jnp.bfloat16)
    columns = first_act
    grad_up = lax.psum_scatter(
        lax.dot_general(
            columns, grad_first, (((0,), (0,)), ((), ())), preferred_element_type=jnp.float32
        ),
        "seq",
        scatter_dimension=0,
        tiled=True,
    ).astype(jnp.bfloat16)
    return (loss_total / mask_total, grad_up, grad_down)


def solution(mesh):
    placed = (P("seq"), P("seq"), P("seq", None), P("seq", None), P(), P(), P(), P())
    return jax.shard_map(
        shards,
        mesh=mesh,
        in_specs=placed,
        out_specs=(P(), P("seq", None), P("seq", None)),
        check_vma=False,
    )
```

profile of v0, /device:TPU:32, one launch (start us, length us, event | category | flops | bytes accessed | tf_op | source)
XLA Modules:
  0.0 302.5 jit_solution(3535265371084264928)
XLA Ops:
  0.6 0.0 copy-start
  0.6 1.2 convert_reduce_fusion
  1.9 1.2 fusion.14
  3.1 2.2 fusion.42
  5.3 0.2 multiply_reduce_fusion.3
  5.5 0.2 multiply_convert_fusion.1
  5.7 8.2 %collective-permute-start = (bf16[128,640]{1,0:T(8,128)(2,1)S(1)}, bf16[128,640]{1,0:T(8,128)(2,1)S(1)}, u32[]{:S(2)}, u32[]{:S(2)}) collective-permute-start(bf16[128,640]{1,0:T(8,128)(2,1)S(1)} %multiply_convert_fusion.1), channel_id=1, source_target_pairs={{0,8},{1,9},{2,10},{3,11},{4,12},{5,13},{6,14},{7,15},{8,16},{9,17... | collective-permute-start | bytes 491528 | tf_op jit(solution)/shard_map/ppermute | solution.py:10
  14.0 3.4 %collective-permute-start.1 = (bf16[128,640]{1,0:T(8,128)(2,1)S(1)}, bf16[128,640]{1,0:T(8,128)(2,1)S(1)}, u32[]{:S(2)}, u32[]{:S(2)}) collective-permute-start(bf16[128,640]{1,0:T(8,128)(2,1)S(1)} %multiply_convert_fusion.1), channel_id=1, source_target_pairs={{0,4},{1,5},{2,6},{3,7},{4,8},{5,9},{6,10},{7,11},{8,12},{9,13},{1... | collective-permute-start | bytes 491528 | tf_op jit(solution)/shard_map/ppermute | solution.py:10
  17.4 1.3 collective-permute-start.2
  18.7 1.3 collective-permute-start.3
  20.0 0.0 collective-permute-done
  20.0 8.4 %collective-permute-done.1 = bf16[128,640]{1,0:T(8,128)(2,1)S(1)} collective-permute-done((bf16[128,640]{1,0:T(8,128)(2,1)S(1)}, bf16[128,640]{1,0:T(8,128)(2,1)S(1)}, u32[]{:S(2)}, u32[]{:S(2)}) %collective-permute-start.1) | collective-permute-done | bytes 163872 | tf_op jit(solution)/shard_map/ppermute | solution.py:10
  28.5 0.2 bitcast_dynamic-update-slice_fusion.7
  28.7 0.0 collective-permute-done.2
  28.8 9.4 %collective-permute-done.3 = bf16[128,640]{1,0:T(8,128)(2,1)S(1)} collective-permute-done((bf16[128,640]{1,0:T(8,128)(2,1)S(1)}, bf16[128,640]{1,0:T(8,128)(2,1)S(1)}, u32[]{:S(2)}, u32[]{:S(2)}) %collective-permute-start.3) | collective-permute-done | bytes 163872 | tf_op jit(solution)/shard_map/ppermute | solution.py:10
  38.1 0.0 copy-start.2
  38.2 0.0 copy-start.4
  38.2 0.0 copy-start.6
  38.2 3.1 %fusion.43 = (f32[128]{0:T(128)S(1)}, f32[128,640]{1,0:T(8,128)S(1)}) fusion(bf16[5,128,640]{2,1,0:T(8,128)(2,1)S(1)} %bitcast_dynamic-update-slice_fusion.5, bf16[5,640,640]{2,1,0:T(8,128)(2,1)} %param.13), kind=kOutput, calls=%fused_computation.90 | convolution fusion | flops 524369792 | bytes 5243392 | tf_op jit(solution)/shard_map/krc,kcb->rb/dot_general | solution.py:42
  41.3 0.0 copy-start.3
  41.3 0.2 multiply_reduce_fusion.2
  41.5 0.0 copy-done
  41.5 0.0 copy-done.2
  41.6 0.0 copy-done.4
  41.6 0.0 copy-done.6
  41.6 0.9 exponential_reduce_fusion
  42.5 0.6 convert_reduce_fusion.1
  43.1 78.2 %psum.15 = f32[]{:T(128)} all-reduce(f32[]{:T(128)} %get-tuple-element.5), channel_id=1, replica_groups=mesh['seq'=256] {'seq'}, use_global_device_ids=true, to_apply=%region_11.0 | all-reduce | flops 1 | bytes 8 | tf_op jit(solution)/shard_map/psum | solution.py:57
  122.0 0.3 fusion
  122.3 0.7 multiply_reduce_fusion.1
  123.0 0.5 fusion.41
  123.5 0.1 add_convert_fusion.1
  123.6 1.3 collective-permute-start.4
  124.9 1.3 collective-permute-start.5
  126.2 5.5 %collective-permute-start.6 = (bf16[128,640]{1,0:T(8,128)(2,1)S(1)}, bf16[128,640]{1,0:T(8,128)(2,1)S(1)}, u32[]{:S(2)}, u32[]{:S(2)}) collective-permute-start(bf16[128,640]{1,0:T(8,128)(2,1)S(1)} %add_convert_fusion.1), channel_id=1, source_target_pairs={{0,4},{1,5},{2,6},{3,7},{4,8},{5,9},{6,10},{7,11},{8,12},{9,13},{1... | collective-permute-start | bytes 491528 | tf_op jit(solution)/shard_map/ppermute | solution.py:10
  131.7 8.5 %collective-permute-start.7 = (bf16[128,640]{1,0:T(8,128)(2,1)S(1)}, bf16[128,640]{1,0:T(8,128)(2,1)S(1)}, u32[]{:S(2)}, u32[]{:S(2)}) collective-permute-start(bf16[128,640]{1,0:T(8,128)(2,1)S(1)} %add_convert_fusion.1), channel_id=1, source_target_pairs={{0,8},{1,9},{2,10},{3,11},{4,12},{5,13},{6,14},{7,15},{8,16},{9,17... | collective-permute-start | bytes 491528 | tf_op jit(solution)/shard_map/ppermute | solution.py:10
  140.1 0.0 copy-start.1
  140.2 2.4 fusion.36
  142.6 0.0 collective-permute-done.4
  142.6 0.0 collective-permute-done.5
  142.6 0.1 bitcast_dynamic-update-slice_fusion.2
  142.8 0.0 collective-permute-done.6
  142.8 3.7 %collective-permute-done.7 = bf16[128,640]{1,0:T(8,128)(2,1)S(1)} collective-permute-done((bf16[128,640]{1,0:T(8,128)(2,1)S(1)}, bf16[128,640]{1,0:T(8,128)(2,1)S(1)}, u32[]{:S(2)}, u32[]{:S(2)}) %collective-permute-start.7) | collective-permute-done | bytes 163872 | tf_op jit(solution)/shard_map/ppermute | solution.py:10
  146.5 1.5 multiply_reduce_fusion
  148.1 0.2 fusion.40
  148.3 2.5 fusion.28
  150.8 147.9 %all-reduce.4 = (f32[]{:T(128)}, bf16[1280,640]{1,0:T(8,128)(2,1)S(1)}, bf16[1280,640]{1,0:T(8,128)(2,1)}) all-reduce(f32[]{:T(128)} %get-tuple-element.6, f32[1280,640]{1,0:T(8,128)} %fusion.28, f32[1280,640]{1,0:T(8,128)} %fusion.36), channel_id=1, replica_groups=mesh['seq'=256] {'seq'}, use_global_device_ids=true, to_apply=%region_9.0 | all-reduce | flops 1638401 | bytes 9830408 | tf_op jit(solution)/shard_map/psum | solution.py:57
  300.0 1.4 dynamic-slice_convert_fusion
  (23 shorter events, 0.2 us)
Async XLA Ops:
  0.6 40.9 %copy-start = (bf16[1280,640]{1,0:T(8,128)(2,1)S(1)}, bf16[1280,640]{1,0:T(8,128)(2,1)}, u32[]{:S(2)}) copy-start(bf16[1280,640]{1,0:T(8,128)(2,1)} %param.14) | copy-start | bytes 4915204
  3.1 16.9 %copy-start.5 = (s32[128]{0:T(128)S(1)}, s32[128]{0:T(128)}, u32[]{:S(2)}) copy-start(s32[128]{0:T(128)} %param.9) | copy-start | bytes 1540
  5.7 14.2 %collective-permute-start = (bf16[128,640]{1,0:T(8,128)(2,1)S(1)}, bf16[128,640]{1,0:T(8,128)(2,1)S(1)}, u32[]{:S(2)}, u32[]{:S(2)}) collective-permute-start(bf16[128,640]{1,0:T(8,128)(2,1)S(1)} %multiply_convert_fusion.1), channel_id=1, source_target_pairs={{0,8},{1,9},{2,10},{3,11},{4,12},{5,13},{6,14},{7,15},{8,16},{9,17... | collective-permute-start | bytes 491528 | tf_op jit(solution)/shard_map/ppermute | solution.py:10
  14.0 14.5 %collective-permute-start.1 = (bf16[128,640]{1,0:T(8,128)(2,1)S(1)}, bf16[128,640]{1,0:T(8,128)(2,1)S(1)}, u32[]{:S(2)}, u32[]{:S(2)}) collective-permute-start(bf16[128,640]{1,0:T(8,128)(2,1)S(1)} %multiply_convert_fusion.1), channel_id=1, source_target_pairs={{0,4},{1,5},{2,6},{3,7},{4,8},{5,9},{6,10},{7,11},{8,12},{9,13},{1... | collective-permute-start | bytes 491528 | tf_op jit(solution)/shard_map/ppermute | solution.py:10
  17.4 11.4 %collective-permute-start.2 = (bf16[128,640]{1,0:T(8,128)(2,1)S(1)}, bf16[128,640]{1,0:T(8,128)(2,1)S(1)}, u32[]{:S(2)}, u32[]{:S(2)}) collective-permute-start(bf16[128,640]{1,0:T(8,128)(2,1)S(1)} %multiply_convert_fusion.1), channel_id=1, source_target_pairs={{4,0},{5,1},{6,2},{7,3},{8,4},{9,5},{10,6},{11,7},{12,8},{13,9},{1... | collective-permute-start | bytes 491528 | tf_op jit(solution)/shard_map/ppermute | solution.py:10
  18.7 19.5 %collective-permute-start.3 = (bf16[128,640]{1,0:T(8,128)(2,1)S(1)}, bf16[128,640]{1,0:T(8,128)(2,1)S(1)}, u32[]{:S(2)}, u32[]{:S(2)}) collective-permute-start(bf16[128,640]{1,0:T(8,128)(2,1)S(1)} %multiply_convert_fusion.1), channel_id=1, source_target_pairs={{8,0},{9,1},{10,2},{11,3},{12,4},{13,5},{14,6},{15,7},{16,8},{17,9... | collective-permute-start | bytes 491528 | tf_op jit(solution)/shard_map/ppermute | solution.py:10
  38.1 3.4 %copy-start.2 = (bf16[128,1280]{1,0:T(8,128)(2,1)S(1)}, bf16[128,1280]{1,0:T(8,128)(2,1)}, u32[]{:S(2)}) copy-start(bf16[128,1280]{1,0:T(8,128)(2,1)} %param.10) | copy-start | bytes 983044
  38.2 3.4 %copy-start.4 = (bf16[1280,6]{0,1:T(8,128)(2,1)S(1)}, bf16[1280,6]{0,1:T(8,128)(2,1)}, u32[]{:S(2)}) copy-start(bf16[1280,6]{0,1:T(8,128)(2,1)} %param.15) | copy-start | bytes 46084
  38.2 3.4 %copy-start.6 = (s32[128]{0:T(128)S(1)}, s32[128]{0:T(128)}, u32[]{:S(2)}) copy-start(s32[128]{0:T(128)} %param.8) | copy-start | bytes 1540
  41.3 80.7 %copy-start.3 = (bf16[128,1280]{1,0:T(8,128)(2,1)S(1)}, bf16[128,1280]{1,0:T(8,128)(2,1)}, u32[]{:S(2)}) copy-start(bf16[128,1280]{1,0:T(8,128)(2,1)} %param.11) | copy-start | bytes 983044
  123.6 19.0 %collective-permute-start.4 = (bf16[128,640]{1,0:T(8,128)(2,1)S(1)}, bf16[128,640]{1,0:T(8,128)(2,1)S(1)}, u32[]{:S(2)}, u32[]{:S(2)}) collective-permute-start(bf16[128,640]{1,0:T(8,128)(2,1)S(1)} %add_convert_fusion.1), channel_id=1, source_target_pairs={{8,0},{9,1},{10,2},{11,3},{12,4},{13,5},{14,6},{15,7},{16,8},{17,9... | collective-permute-start | bytes 491528 | tf_op jit(solution)/shard_map/ppermute | solution.py:10
  124.9 17.7 %collective-permute-start.5 = (bf16[128,640]{1,0:T(8,128)(2,1)S(1)}, bf16[128,640]{1,0:T(8,128)(2,1)S(1)}, u32[]{:S(2)}, u32[]{:S(2)}) collective-permute-start(bf16[128,640]{1,0:T(8,128)(2,1)S(1)} %add_convert_fusion.1), channel_id=1, source_target_pairs={{4,0},{5,1},{6,2},{7,3},{8,4},{9,5},{10,6},{11,7},{12,8},{13,9},{1... | collective-permute-start | bytes 491528 | tf_op jit(solution)/shard_map/ppermute | solution.py:10
  126.2 16.5 %collective-permute-start.6 = (bf16[128,640]{1,0:T(8,128)(2,1)S(1)}, bf16[128,640]{1,0:T(8,128)(2,1)S(1)}, u32[]{:S(2)}, u32[]{:S(2)}) collective-permute-start(bf16[128,640]{1,0:T(8,128)(2,1)S(1)} %add_convert_fusion.1), channel_id=1, source_target_pairs={{0,4},{1,5},{2,6},{3,7},{4,8},{5,9},{6,10},{7,11},{8,12},{9,13},{1... | collective-permute-start | bytes 491528 | tf_op jit(solution)/shard_map/ppermute | solution.py:10
  131.7 14.8 %collective-permute-start.7 = (bf16[128,640]{1,0:T(8,128)(2,1)S(1)}, bf16[128,640]{1,0:T(8,128)(2,1)S(1)}, u32[]{:S(2)}, u32[]{:S(2)}) collective-permute-start(bf16[128,640]{1,0:T(8,128)(2,1)S(1)} %add_convert_fusion.1), channel_id=1, source_target_pairs={{0,8},{1,9},{2,10},{3,11},{4,12},{5,13},{6,14},{7,15},{8,16},{9,17... | collective-permute-start | bytes 491528 | tf_op jit(solution)/shard_map/ppermute | solution.py:10
  140.1 6.3 %copy-start.1 = (bf16[5,640,640]{2,1,0:T(8,128)(2,1)S(1)}, bf16[5,640,640]{2,1,0:T(8,128)(2,1)}, u32[]{:S(2)}) copy-start(bf16[5,640,640]{2,1,0:T(8,128)(2,1)} %param.13) | copy-start | bytes 12288004
where the time goes:
time: 303 us
  blocking collectives  226 us (75%)
  starting transfers between devices  30.7 us (10%)
  waiting for transfers between devices  21.5 us (7%)
  matrix products  13.7 us (5%)
  other arithmetic  4.85 us (2%)
  between operations  4.17 us (1%)
    psum x2, blocking collectives, shards(): loss_total, mask_total = lax.psum((local_loss, local_count), 'seq')  226 us
    ppermute x8, starting transfers between devices, from_behind(): return lax.ppermute(block, axis, route)  30.7 us
    ppermute x8, waiting for transfers between devices, from_behind(): return lax.ppermute(block, axis, route)  21.5 us
  transfers between devices with their start and end apart: 8, of which 3 were waited for; matrix products, arithmetic and copies ran while one was open for 1% of the time, Pallas kernels for 0%

commit v1 on v0

--- a/solution.py
+++ b/solution.py
@@ -26,6 +26,12 @@
     return [far_pieces[1], near_pieces[1], source_field, near_pieces[-1], far_pieces[-1]]
 
 
+def own_rows(summed, axis):
+    devices = lax.axis_size(axis)
+    share = summed.shape[0] // devices
+    return lax.dynamic_slice_in_dim(summed, lax.axis_index(axis) * share, share, 0)
+
+
 def shards(tokens, mask_flags, hidden_in, grad_above, w_in, conv_weight, w_out, head_weight):
     local_rows = tokens.shape[0]
     vocab_size = head_weight.shape[1]
@@ -34,11 +40,15 @@
     context_rows = float(local_rows * seq_devices)
     masked = mask_flags.astype(jnp.float32)
     local_count = jnp.sum(masked)
+    count_tile = jnp.broadcast_to(local_count, (256, 128))
+    count_summed = lax.psum(count_tile, "seq")
     alphabet = jnp.arange(vocab_size, dtype=jnp.int32)
     first_act = norm_gelu(hidden_in.astype(jnp.float32)).astype(jnp.bfloat16)
     first_pre = jnp.dot(first_act, w_in, preferred_element_type=jnp.float32)
     narrow_activation = norm_gelu(first_pre).astype(jnp.bfloat16)
     kernel_tap_pile = jnp.stack(spread(narrow_activation, shard_reach))
+    count_summed, kernel_tap_pile = lax.optimization_barrier((count_summed, kernel_tap_pile))
+    mask_total = count_summed[0, 0]
     conv_pre = jnp.einsum(
         "krc,kcb->rb", kernel_tap_pile, conv_weight, preferred_element_type=jnp.float32
     )
@@ -54,7 +64,6 @@
     target_hot = (alphabet[:, None] == tokens[None, :]).astype(jnp.float32)
     cross_ent = log_total - jnp.sum(target_hot * logits_t, 0)
     local_loss = jnp.sum(masked * cross_ent)
-    loss_total, mask_total = lax.psum((local_loss, local_count), "seq")
     probability = jnp.exp(logits_t - log_total[None, :])
     grad_logits = (
         masked[None, :] * (probability - target_hot) * (context_rows / mask_total)
@@ -64,14 +73,10 @@
     )
     grad_block = (head_part + grad_above.astype(jnp.float32)).astype(jnp.bfloat16)
     columns = grad_block
-    grad_down = lax.psum_scatter(
-        lax.dot_general(
-            columns, conv_act, (((0,), (0,)), ((), ())), preferred_element_type=jnp.float32
-        ),
-        "seq",
-        scatter_dimension=0,
-        tiled=True,
-    ).astype(jnp.bfloat16)
+    down_partial = lax.dot_general(
+        columns, conv_act, (((0,), (0,)), ((), ())), preferred_element_type=jnp.float32
+    )
+    loss_rows = jnp.broadcast_to(local_loss, (8, down_partial.shape[1]))
     grad_conv_act = jnp.dot(grad_block, w_out, preferred_element_type=jnp.float32)
     gradient_before_activation = jax.vjp(norm_gelu, conv_pre)[1](grad_conv_act)[0].astype(
         jnp.bfloat16
@@ -83,14 +88,14 @@
     )
     grad_first = jax.vjp(norm_gelu, first_pre)[1](grad_neck)[0].astype(jnp.bfloat16)
     columns = first_act
-    grad_up = lax.psum_scatter(
-        lax.dot_general(
-            columns, grad_first, (((0,), (0,)), ((), ())), preferred_element_type=jnp.float32
-        ),
-        "seq",
-        scatter_dimension=0,
-        tiled=True,
-    ).astype(jnp.bfloat16)
+    up_partial = lax.dot_general(
+        columns, grad_first, (((0,), (0,)), ((), ())), preferred_element_type=jnp.float32
+    )
+    width = down_partial.shape[0]
+    summed = lax.psum(jnp.concatenate([down_partial, up_partial, loss_rows], 0), "seq")
+    loss_total = summed[-1, 0]
+    grad_down = own_rows(summed[:width], "seq").astype(jnp.bfloat16)
+    grad_up = own_rows(summed[width : 2 * width], "seq").astype(jnp.bfloat16)
     return (loss_total / mask_total, grad_up, grad_down)
 
 

time: 303 us -> 617 us (2.04)
  waiting for transfers between devices: 21.5 us -> 537 us
  blocking collectives: 226 us -> 0 us
  between operations: 4.17 us -> 17.6 us
  local copies, waits for them, and re-layouts: 1.56 us -> 8.45 us
    psum x0 -> x2, waiting for transfers between devices: none -> 519 us  [the longest x1 284 us: shards(): lax.psum(jnp.concatenate([down_partial, up_partial, loss_rows], 0), 'seq')]
    psum x2 -> x0, blocking collectives: 226 us -> none  [shards(): loss_total, mask_total = lax.psum((local_loss, local_count), 'seq')]
  transfers between devices with their start and end apart: 8 -> 10, of which waited for: 3 -> 5; matrix products, arithmetic and copies ran while one was open for 1% -> 1% of each run, Pallas kernels for 0% -> 0%
where the time goes in v1:
time: 617 us; the launch traced here: 615 us
  waiting for transfers between devices  537 us (87%)
  starting transfers between devices  31 us (5%)
  between operations  17.6 us (3%)
  matrix products  10.3 us (2%)
  other arithmetic  9.96 us (2%)
  local copies, waits for them, and re-layouts  8.45 us (1%)
    psum x1, waiting for transfers between devices, shards(): lax.psum(jnp.concatenate([down_partial, up_partial, loss_rows], 0), 'seq')  284 us
    psum x1, waiting for transfers between devices, shards(): count_summed = lax.psum(count_tile, 'seq')  235 us
    ppermute x8, starting transfers between devices, from_behind(): return lax.ppermute(block, axis, route)  30.9 us
    ppermute x8, waiting for transfers between devices, from_behind(): return lax.ppermute(block, axis, route)  18.4 us
  transfers between devices with their start and end apart: 10, of which 5 were waited for; matrix products, arithmetic and copies ran while one was open for 1% of the time, Pallas kernels for 0%

profile of v1, /device:TPU:32, one launch (start us, length us, event | category | flops | bytes accessed | tf_op | source)
XLA Modules:
  0.0 614.7 jit_solution(16605529733078837877)
XLA Ops:
  7.2 0.0 copy-start
  7.2 0.0 all-reduce.3.cloned.1.call-start
  7.2 1.2 convert_reduce_fusion
  8.5 1.2 fusion.14
  9.7 2.2 fusion.43
  11.9 0.2 multiply_reduce_fusion.3
  12.1 0.9 multiply_convert_fusion.1
  13.0 8.2 %collective-permute-start = (bf16[128,640]{1,0:T(8,128)(2,1)}, bf16[128,640]{1,0:T(8,128)(2,1)S(1)}, u32[]{:S(2)}, u32[]{:S(2)}) collective-permute-start(bf16[128,640]{1,0:T(8,128)(2,1)} %multiply_convert_fusion.1), channel_id=1, source_target_pairs={{0,8},{1,9},{2,10},{3,11},{4,12},{5,13},{6,14},{7,15},{8,16},{9,17... | collective-permute-start | bytes 491528 | tf_op jit(solution)/shard_map/ppermute | solution.py:10
  21.2 3.4 collective-permute-start.1
  24.6 1.3 collective-permute-start.2
  25.9 1.3 collective-permute-start.3
  27.2 0.6 convert_reduce_fusion.1
  27.8 1.3 broadcast_in_dim.12
  29.1 0.0 all-reduce.3.cloned.1.call-update
  29.1 0.0 all-reduce.5.cloned.1.call-start
  29.2 6.8 %collective-permute-done.1 = bf16[128,640]{1,0:T(8,128)(2,1)S(1)} collective-permute-done((bf16[128,640]{1,0:T(8,128)(2,1)}, bf16[128,640]{1,0:T(8,128)(2,1)S(1)}, u32[]{:S(2)}, u32[]{:S(2)}) %collective-permute-start.1) | collective-permute-done | bytes 163872 | tf_op jit(solution)/shard_map/ppermute | solution.py:10
  36.0 0.2 bitcast_dynamic-update-slice_fusion.7
  36.3 9.3 %collective-permute-done.3 = bf16[128,640]{1,0:T(8,128)(2,1)S(1)} collective-permute-done((bf16[128,640]{1,0:T(8,128)(2,1)}, bf16[128,640]{1,0:T(8,128)(2,1)S(1)}, u32[]{:S(2)}, u32[]{:S(2)}) %collective-permute-start.3) | collective-permute-done | bytes 163872 | tf_op jit(solution)/shard_map/ppermute | solution.py:10
  45.6 0.0 copy-start.4
  45.6 0.0 copy-start.6
  45.6 235.0 %all-reduce.3.cloned.1.call-done = f32[256,128]{1,0:T(8,128)} async-done(((f32[256,128]{1,0:T(8,128)}), f32[256,128]{1,0:T(8,128)}) %all-reduce.3.cloned.1.call-update) | async-done | bytes 131088 | tf_op jit(solution)/shard_map/psum | solution.py:44
  280.6 3.1 fusion.44
  283.7 0.0 copy-start.3
  283.7 0.2 multiply_reduce_fusion.2
  283.9 1.2 slice.12
  285.1 0.9 select_reduce_fusion
  286.0 0.6 multiply_reduce_fusion.4
  287.3 0.3 fusion
  287.7 0.7 multiply_reduce_fusion.1
  288.3 0.5 fusion.41
  288.8 0.1 add_convert_fusion.1
  288.9 1.6 collective-permute-start.4
  290.5 1.3 collective-permute-start.5
  291.8 5.5 collective-permute-start.6
  297.3 8.5 %collective-permute-start.7 = (bf16[128,640]{1,0:T(8,128)(2,1)S(1)}, bf16[128,640]{1,0:T(8,128)(2,1)S(1)}, u32[]{:S(2)}, u32[]{:S(2)}) collective-permute-start(bf16[128,640]{1,0:T(8,128)(2,1)S(1)} %add_convert_fusion.1), channel_id=1, source_target_pairs={{0,8},{1,9},{2,10},{3,11},{4,12},{5,13},{6,14},{7,15},{8,16},{9,17... | collective-permute-start | bytes 491528 | tf_op jit(solution)/shard_map/ppermute | solution.py:10
  305.7 0.6 broadcast_in_dim.17
  306.4 0.7 fusion.36
  307.2 0.1 bitcast_dynamic-update-slice_fusion.2
  307.3 2.3 collective-permute-done.6
  309.7 1.6 multiply_reduce_fusion
  311.3 0.2 fusion.40
  311.5 0.8 fusion.28
  312.3 3.9 maximum_maximum_fusion
  316.2 0.0 all-reduce.5.cloned.1.call-update
  316.3 284.1 %all-reduce.5.cloned.1.call-done = f32[2568,640]{1,0:T(8,128)} async-done(((f32[2568,640]{1,0:T(8,128)}), f32[2568,640]{1,0:T(8,128)}) %all-reduce.5.cloned.1.call-update) | async-done | bytes 6574096 | tf_op jit(solution)/shard_map/psum | solution.py:95
  600.3 1.2 slice.16
  602.9 3.3 fusion.42
  606.1 0.6 dynamic-slice_convert_fusion
  (35 shorter events, 0.3 us)
Async XLA Ops:
  7.2 277.9 %copy-start = (bf16[1280,640]{1,0:T(8,128)(2,1)S(1)}, bf16[1280,640]{1,0:T(8,128)(2,1)}, u32[]{:S(2)}) copy-start(bf16[1280,640]{1,0:T(8,128)(2,1)} %param.14) | copy-start | bytes 4915204
  7.2 20.0 %copy-start.5 = (s32[128]{0:T(128)S(1)}, s32[128]{0:T(128)}, u32[]{:S(2)}) copy-start(s32[128]{0:T(128)} %param.9) | copy-start | bytes 1540
  7.2 273.4 %all-reduce.3.cloned.1.call-start = ((), (), s32[]{:S(2)}) async-start(), calls=%async_computation | async-start | bytes 262144 | tf_op jit(solution)/shard_map/psum | solution.py:44
  13.0 16.2 %collective-permute-start = (bf16[128,640]{1,0:T(8,128)(2,1)}, bf16[128,640]{1,0:T(8,128)(2,1)S(1)}, u32[]{:S(2)}, u32[]{:S(2)}) collective-permute-start(bf16[128,640]{1,0:T(8,128)(2,1)} %multiply_convert_fusion.1), channel_id=1, source_target_pairs={{0,8},{1,9},{2,10},{3,11},{4,12},{5,13},{6,14},{7,15},{8,16},{9,17... | collective-permute-start | bytes 491528 | tf_op jit(solution)/shard_map/ppermute | solution.py:10
  21.2 14.8 %collective-permute-start.1 = (bf16[128,640]{1,0:T(8,128)(2,1)}, bf16[128,640]{1,0:T(8,128)(2,1)S(1)}, u32[]{:S(2)}, u32[]{:S(2)}) collective-permute-start(bf16[128,640]{1,0:T(8,128)(2,1)} %multiply_convert_fusion.1), channel_id=1, source_target_pairs={{0,4},{1,5},{2,6},{3,7},{4,8},{5,9},{6,10},{7,11},{8,12},{9,13},{1... | collective-permute-start | bytes 491528 | tf_op jit(solution)/shard_map/ppermute | solution.py:10
  24.6 11.7 %collective-permute-start.2 = (bf16[128,640]{1,0:T(8,128)(2,1)}, bf16[128,640]{1,0:T(8,128)(2,1)S(1)}, u32[]{:S(2)}, u32[]{:S(2)}) collective-permute-start(bf16[128,640]{1,0:T(8,128)(2,1)} %multiply_convert_fusion.1), channel_id=1, source_target_pairs={{4,0},{5,1},{6,2},{7,3},{8,4},{9,5},{10,6},{11,7},{12,8},{13,9},{1... | collective-permute-start | bytes 491528 | tf_op jit(solution)/shard_map/ppermute | solution.py:10
  25.9 19.7 %collective-permute-start.3 = (bf16[128,640]{1,0:T(8,128)(2,1)}, bf16[128,640]{1,0:T(8,128)(2,1)S(1)}, u32[]{:S(2)}, u32[]{:S(2)}) collective-permute-start(bf16[128,640]{1,0:T(8,128)(2,1)} %multiply_convert_fusion.1), channel_id=1, source_target_pairs={{8,0},{9,1},{10,2},{11,3},{12,4},{13,5},{14,6},{15,7},{16,8},{17,9... | collective-permute-start | bytes 491528 | tf_op jit(solution)/shard_map/ppermute | solution.py:10
  29.1 571.2 %all-reduce.5.cloned.1.call-start = ((), (), s32[]{:S(2)}) async-start(), calls=%async_computation.1 | async-start | bytes 13148160 | tf_op jit(solution)/shard_map/psum | solution.py:95
  45.6 239.5 %copy-start.2 = (bf16[128,1280]{1,0:T(8,128)(2,1)S(1)}, bf16[128,1280]{1,0:T(8,128)(2,1)}, u32[]{:S(2)}) copy-start(bf16[128,1280]{1,0:T(8,128)(2,1)} %param.10) | copy-start | bytes 983044
  45.6 239.5 %copy-start.4 = (bf16[1280,6]{0,1:T(8,128)(2,1)S(1)}, bf16[1280,6]{0,1:T(8,128)(2,1)}, u32[]{:S(2)}) copy-start(bf16[1280,6]{0,1:T(8,128)(2,1)} %param.15) | copy-start | bytes 46084
  45.6 239.5 %copy-start.6 = (s32[128]{0:T(128)S(1)}, s32[128]{0:T(128)}, u32[]{:S(2)}) copy-start(s32[128]{0:T(128)} %param.8) | copy-start | bytes 1540
  283.7 3.7 copy-start.3
  288.8 20.9 %copy-start.1 = (bf16[5,640,640]{2,1,0:T(8,128)(2,1)S(1)}, bf16[5,640,640]{2,1,0:T(8,128)(2,1)}, u32[]{:S(2)}) copy-start(bf16[5,640,640]{2,1,0:T(8,128)(2,1)} %param.13) | copy-start | bytes 12288004
  288.9 18.2 %collective-permute-start.4 = (bf16[128,640]{1,0:T(8,128)(2,1)S(1)}, bf16[128,640]{1,0:T(8,128)(2,1)S(1)}, u32[]{:S(2)}, u32[]{:S(2)}) collective-permute-start(bf16[128,640]{1,0:T(8,128)(2,1)S(1)} %add_convert_fusion.1), channel_id=1, source_target_pairs={{8,0},{9,1},{10,2},{11,3},{12,4},{13,5},{14,6},{15,7},{16,8},{17,9... | collective-permute-start | bytes 491528 | tf_op jit(solution)/shard_map/ppermute | solution.py:10
  290.5 16.7 %collective-permute-start.5 = (bf16[128,640]{1,0:T(8,128)(2,1)S(1)}, bf16[128,640]{1,0:T(8,128)(2,1)S(1)}, u32[]{:S(2)}, u32[]{:S(2)}) collective-permute-start(bf16[128,640]{1,0:T(8,128)(2,1)S(1)} %add_convert_fusion.1), channel_id=1, source_target_pairs={{4,0},{5,1},{6,2},{7,3},{8,4},{9,5},{10,6},{11,7},{12,8},{13,9},{1... | collective-permute-start | bytes 491528 | tf_op jit(solution)/shard_map/ppermute | solution.py:10
  291.8 17.8 %collective-permute-start.6 = (bf16[128,640]{1,0:T(8,128)(2,1)S(1)}, bf16[128,640]{1,0:T(8,128)(2,1)S(1)}, u32[]{:S(2)}, u32[]{:S(2)}) collective-permute-start(bf16[128,640]{1,0:T(8,128)(2,1)S(1)} %add_convert_fusion.1), channel_id=1, source_target_pairs={{0,4},{1,5},{2,6},{3,7},{4,8},{5,9},{6,10},{7,11},{8,12},{9,13},{1... | collective-permute-start | bytes 491528 | tf_op jit(solution)/shard_map/ppermute | solution.py:10
  297.3 12.4 %collective-permute-start.7 = (bf16[128,640]{1,0:T(8,128)(2,1)S(1)}, bf16[128,640]{1,0:T(8,128)(2,1)S(1)}, u32[]{:S(2)}, u32[]{:S(2)}) collective-permute-start(bf16[128,640]{1,0:T(8,128)(2,1)S(1)} %add_convert_fusion.1), channel_id=1, source_target_pairs={{0,8},{1,9},{2,10},{3,11},{4,12},{5,13},{6,14},{7,15},{8,16},{9,17... | collective-permute-start | bytes 491528 | tf_op jit(solution)/shard_map/ppermute | solution.py:10
Sparse Core Ops, SparseCore 0:
  29.2 251.3 all-reduce.2
  316.4 283.9 all-reduce.4

commit v2 on v0

--- a/solution.py
+++ b/solution.py
@@ -8,6 +8,42 @@
     devices = range(lax.axis_size(axis))
     route = [(i - distance, i) for i in devices if i - distance in devices]
     return lax.ppermute(block, axis, route)
+
+
+def swap_with(block, axis, bit):
+    devices = lax.axis_size(axis)
+    return lax.ppermute(block, axis, [(i, i ^ bit) for i in range(devices)])
+
+
+def link_order(devices):
+    bits = [1 << k for k in range(devices.bit_length() - 1)]
+    near = [1, 2, 16, 64, 4, 32, 128, 8]
+    return [b for b in near if b in bits] + [b for b in bits if b not in near]
+
+
+def tree_sum(values, axis):
+    for bit in link_order(lax.axis_size(axis)):
+        values = values + swap_with(values, axis, bit)
+    return values
+
+
+def tree_scatter(partial, axis):
+    devices = lax.axis_size(axis)
+    depth = devices.bit_length() - 1
+    me = lax.axis_index(axis)
+    rows, cols = partial.shape
+    blocks = partial.reshape((2,) * depth + (rows // devices, cols))
+    dim_bits = [1 << (depth - 1 - d) for d in range(depth)]
+    for bit in link_order(devices):
+        at = dim_bits.index(bit)
+        upper = (me & bit) != 0
+        low = lax.index_in_dim(blocks, 0, at, keepdims=False)
+        high = lax.index_in_dim(blocks, 1, at, keepdims=False)
+        keep = jnp.where(upper, high, low)
+        send = jnp.where(upper, low, high).astype(jnp.bfloat16)
+        blocks = keep + swap_with(send, axis, bit).astype(jnp.float32)
+        dim_bits.pop(at)
+    return blocks
 
 
 def norm_gelu(values):
@@ -34,6 +70,7 @@
     context_rows = float(local_rows * seq_devices)
     masked = mask_flags.astype(jnp.float32)
     local_count = jnp.sum(masked)
+    mask_total = tree_sum(jnp.broadcast_to(local_count, (8, 128)), "seq")[0, 0]
     alphabet = jnp.arange(vocab_size, dtype=jnp.int32)
     first_act = norm_gelu(hidden_in.astype(jnp.float32)).astype(jnp.bfloat16)
     first_pre = jnp.dot(first_act, w_in, preferred_element_type=jnp.float32)
@@ -54,7 +91,6 @@
     target_hot = (alphabet[:, None] == tokens[None, :]).astype(jnp.float32)
     cross_ent = log_total - jnp.sum(target_hot * logits_t, 0)
     local_loss = jnp.sum(masked * cross_ent)
-    loss_total, mask_total = lax.psum((local_loss, local_count), "seq")
     probability = jnp.exp(logits_t - log_total[None, :])
     grad_logits = (
         masked[None, :] * (probability - target_hot) * (context_rows / mask_total)
@@ -64,13 +100,11 @@
     )
     grad_block = (head_part + grad_above.astype(jnp.float32)).astype(jnp.bfloat16)
     columns = grad_block
-    grad_down = lax.psum_scatter(
+    grad_down = tree_scatter(
         lax.dot_general(
             columns, conv_act, (((0,), (0,)), ((), ())), preferred_element_type=jnp.float32
         ),
         "seq",
-        scatter_dimension=0,
-        tiled=True,
     ).astype(jnp.bfloat16)
     grad_conv_act = jnp.dot(grad_block, w_out, preferred_element_type=jnp.float32)
     gradient_before_activation = jax.vjp(norm_gelu, conv_pre)[1](grad_conv_act)[0].astype(
@@ -83,14 +117,13 @@
     )
     grad_first = jax.vjp(norm_gelu, first_pre)[1](grad_neck)[0].astype(jnp.bfloat16)
     columns = first_act
-    grad_up = lax.psum_scatter(
+    grad_up = tree_scatter(
         lax.dot_general(
             columns, grad_first, (((0,), (0,)), ((), ())), preferred_element_type=jnp.float32
         ),
         "seq",
-        scatter_dimension=0,
-        tiled=True,
     ).astype(jnp.bfloat16)
+    loss_total = tree_sum(jnp.broadcast_to(local_loss, (8, 128)), "seq")[0, 0]
     return (loss_total / mask_total, grad_up, grad_down)
 
 

time: 303 us -> 241 us (0.80); the launches traced: 303 us -> 236 us
  blocking collectives: 226 us -> 0 us
  starting transfers between devices: 30.7 us -> 99.8 us
  waiting for transfers between devices: 21.5 us -> 80.3 us
  local copies, waits for them, and re-layouts: 1.56 us -> 22.8 us
  other arithmetic: 4.85 us -> 17 us
    psum x2 -> x0, blocking collectives: 226 us -> none  [shards(): loss_total, mask_total = lax.psum((local_loss, local_count), 'seq')]
    ppermute x0 -> x32, starting transfers between devices: none -> 68.9 us  [swap_with(): return lax.ppermute(block, axis, [(i, i ^ bit) for i in range(devices)])]
    ppermute x0 -> x32, waiting for transfers between devices: none -> 62.4 us  [swap_with(): return lax.ppermute(block, axis, [(i, i ^ bit) for i in range(devices)])]
    reshape x0 -> x2, local copies, waits for them, and re-layouts: none -> 9.75 us  [tree_scatter(): blocks = partial.reshape((2,) * depth + (rows // devices, cols))]
    add x0 -> x30, other arithmetic: none -> 7.26 us  [the longest x14 4.63 us: tree_scatter(): blocks = keep + swap_with(send, axis, bit).astype(jnp.float32)]
    convert_element_type x0 -> x18, other arithmetic: none -> 4.94 us  [the longest x16 3.73 us: tree_scatter(): send = jnp.where(upper, low, high).astype(jnp.bfloat16)]
    unnamed x20 -> x30, local copies, waits for them, and re-layouts: 0.17 us -> 4.36 us
    slice x0 -> x6, local copies, waits for them, and re-layouts: none -> 4.05 us  [the longest x1 2.87 us: tree_scatter(): high = lax.index_in_dim(blocks, 1, at, keepdims=False)]
  transfers between devices with their start and end apart: 8 -> 40, of which waited for: 3 -> 27; matrix products, arithmetic and copies ran while one was open for 1% -> 16% of each run, Pallas kernels for 0% -> 0%
where the time goes in v2:
time: 241 us; the launch traced here: 236 us
  starting transfers between devices  99.8 us (41%)
  waiting for transfers between devices  80.3 us (33%)
  local copies, waits for them, and re-layouts  22.8 us (9%)
  other arithmetic  17 us (7%)
  matrix products  11.7 us (5%)
  between operations  4.85 us (2%)
    ppermute x32, starting transfers between devices, swap_with(): return lax.ppermute(block, axis, [(i, i ^ bit) for i in range(devices)])  68.9 us
    ppermute x32, waiting for transfers between devices, swap_with(): return lax.ppermute(block, axis, [(i, i ^ bit) for i in range(devices)])  62.4 us
    ppermute x8, starting transfers between devices, from_behind(): return lax.ppermute(block, axis, route)  30.9 us
    ppermute x8, waiting for transfers between devices, from_behind(): return lax.ppermute(block, axis, route)  17.8 us
    reshape x2, local copies, waits for them, and re-layouts, tree_scatter(): blocks = partial.reshape((2,) * depth + (rows // devices, cols))  9.75 us
  transfers between devices with their start and end apart: 40, of which 27 were waited for; matrix products, arithmetic and copies ran while one was open for 16% of the time, Pallas kernels for 0%

profile of v2, /device:TPU:32, one launch (start us, length us, event | category | flops | bytes accessed | tf_op | source)
XLA Modules:
  0.0 236.5 jit_solution(4169318938951392626)
XLA Ops:
  3.1 2.3 fusion.69
  5.9 8.2 %collective-permute-start = (bf16[128,640]{1,0:T(8,128)(2,1)S(1)}, bf16[128,640]{1,0:T(8,128)(2,1)S(1)}, u32[]{:S(2)}, u32[]{:S(2)}) collective-permute-start(bf16[128,640]{1,0:T(8,128)(2,1)S(1)} %multiply_convert_fusion.1), channel_id=1, source_target_pairs={{0,8},{1,9},{2,10},{3,11},{4,12},{5,13},{6,14},{7,15},{8,16},{9,17... | collective-permute-start | bytes 491528 | tf_op jit(solution)/shard_map/ppermute | solution.py:10
  14.1 3.4 %collective-permute-start.1 = (bf16[128,640]{1,0:T(8,128)(2,1)S(1)}, bf16[128,640]{1,0:T(8,128)(2,1)S(1)}, u32[]{:S(2)}, u32[]{:S(2)}) collective-permute-start(bf16[128,640]{1,0:T(8,128)(2,1)S(1)} %multiply_convert_fusion.1), channel_id=1, source_target_pairs={{0,4},{1,5},{2,6},{3,7},{4,8},{5,9},{6,10},{7,11},{8,12},{9,13},{1... | collective-permute-start | bytes 491528 | tf_op jit(solution)/shard_map/ppermute | solution.py:10
  20.1 8.5 %collective-permute-done.1 = bf16[128,640]{1,0:T(8,128)(2,1)S(1)} collective-permute-done((bf16[128,640]{1,0:T(8,128)(2,1)S(1)}, bf16[128,640]{1,0:T(8,128)(2,1)S(1)}, u32[]{:S(2)}, u32[]{:S(2)}) %collective-permute-start.1) | collective-permute-done | bytes 163872 | tf_op jit(solution)/shard_map/ppermute | solution.py:10
  28.9 9.4 %collective-permute-done.3 = bf16[128,640]{1,0:T(8,128)(2,1)S(1)} collective-permute-done((bf16[128,640]{1,0:T(8,128)(2,1)S(1)}, bf16[128,640]{1,0:T(8,128)(2,1)S(1)}, u32[]{:S(2)}, u32[]{:S(2)}) %collective-permute-start.3) | collective-permute-done | bytes 163872 | tf_op jit(solution)/shard_map/ppermute | solution.py:10
  43.7 3.6 %collective-permute-done.13 = f32[8,128]{1,0:T(8,128)S(1)} collective-permute-done((f32[8,128]{1,0:T(8,128)S(1)}, f32[8,128]{1,0:T(8,128)S(1)}, u32[]{:S(2)}, u32[]{:S(2)}) %collective-permute-start.13) | collective-permute-done | bytes 4128 | tf_op jit(solution)/shard_map/ppermute | solution.py:15
  48.0 2.4 %collective-permute-start.14 = (f32[8,128]{1,0:T(8,128)S(1)}, f32[8,128]{1,0:T(8,128)S(1)}, u32[]{:S(2)}, u32[]{:S(2)}) collective-permute-start(f32[8,128]{1,0:T(8,128)S(1)} %fusion.82), channel_id=1, source_target_pairs={{0,16},{1,17},{2,18},{3,19},{4,20},{5,21},{6,22},{7,23},{8,24},{9,... | collective-permute-start | bytes 12296 | tf_op jit(solution)/shard_map/ppermute | solution.py:15
  52.0 2.1 collective-permute-start.15
  55.7 4.5 %collective-permute-done.16 = f32[8,128]{1,0:T(8,128)S(1)} collective-permute-done((f32[8,128]{1,0:T(8,128)S(1)}, f32[8,128]{1,0:T(8,128)S(1)}, u32[]{:S(2)}, u32[]{:S(2)}) %collective-permute-start.16) | collective-permute-done | bytes 4128 | tf_op jit(solution)/shard_map/ppermute | solution.py:15
  60.2 3.4 %collective-permute-start.17 = (f32[8,128]{1,0:T(8,128)S(1)}, f32[8,128]{1,0:T(8,128)S(1)}, u32[]{:S(2)}, u32[]{:S(2)}) collective-permute-start(f32[8,128]{1,0:T(8,128)S(1)} %add.182), channel_id=1, source_target_pairs={{0,32},{1,33},{2,34},{3,35},{4,36},{5,37},{6,38},{7,39},{8,40},{9,... | collective-permute-start | bytes 12296 | tf_op jit(solution)/shard_map/ppermute | solution.py:15
  65.3 3.6 %collective-permute-start.18 = (f32[8,128]{1,0:T(8,128)S(1)}, f32[8,128]{1,0:T(8,128)S(1)}, u32[]{:S(2)}, u32[]{:S(2)}) collective-permute-start(f32[8,128]{1,0:T(8,128)S(1)} %add.183), channel_id=1, source_target_pairs={{0,128},{1,129},{2,130},{3,131},{4,132},{5,133},{6,134},{7,135},{8... | collective-permute-start | bytes 12296 | tf_op jit(solution)/shard_map/ppermute | solution.py:15
  70.5 4.9 %collective-permute-start.19 = (f32[8,128]{1,0:T(8,128)S(1)}, f32[8,128]{1,0:T(8,128)S(1)}, u32[]{:S(2)}, u32[]{:S(2)}) collective-permute-start(f32[8,128]{1,0:T(8,128)S(1)} %add.184), channel_id=1, source_target_pairs={{0,8},{1,9},{2,10},{3,11},{4,12},{5,13},{6,14},{7,15},{8,0},{9,1},... | collective-permute-start | bytes 12296 | tf_op jit(solution)/shard_map/ppermute | solution.py:15
  76.2 1.8 collective-permute-done.19
  83.4 5.5 %collective-permute-start.22 = (bf16[128,640]{1,0:T(8,128)(2,1)S(1)}, bf16[128,640]{1,0:T(8,128)(2,1)S(1)}, u32[]{:S(2)}, u32[]{:S(2)}) collective-permute-start(bf16[128,640]{1,0:T(8,128)(2,1)S(1)} %add_convert_fusion.1), channel_id=1, source_target_pairs={{0,4},{1,5},{2,6},{3,7},{4,8},{5,9},{6,10},{7,11},{8,12},{9,13},{1... | collective-permute-start | bytes 491528 | tf_op jit(solution)/shard_map/ppermute | solution.py:10
  88.9 8.6 %collective-permute-start.23 = (bf16[128,640]{1,0:T(8,128)(2,1)S(1)}, bf16[128,640]{1,0:T(8,128)(2,1)S(1)}, u32[]{:S(2)}, u32[]{:S(2)}) collective-permute-start(bf16[128,640]{1,0:T(8,128)(2,1)S(1)} %add_convert_fusion.1), channel_id=1, source_target_pairs={{0,8},{1,9},{2,10},{3,11},{4,12},{5,13},{6,14},{7,15},{8,16},{9,17... | collective-permute-start | bytes 491528 | tf_op jit(solution)/shard_map/ppermute | solution.py:10
  97.5 2.5 %fusion.59 = f32[1280,640]{1,0:T(8,128)} fusion(bf16[128,1280]{1,0:T(8,128)(2,1)S(1)} %fusion, f32[128,640]{1,0:T(8,128)S(1)} %get-tuple-element.23, f32[128]{0:T(128)S(1)} %fusion.58, f32[128]{0:T(128)S(1)} %broadcast_multiply_fusion), kind=kOutput, calls=%fused_computation.143 | convolution fusion | flops 210616320 | bytes 3933184 | tf_op jit(solution)/shard_map/dot_general | solution.py:104
  100.0 4.9 %reshape.161 = f32[2,2,2,2,2,2,2,2,5,640]{9,8,7,6,5,4,3,2,1,0:T(8,128)} reshape(f32[1280,640]{1,0:T(8,128)} %fusion.59) | data formatting | bytes 6553600 | tf_op jit(solution)/shard_map/reshape | solution.py:35
  104.8 2.9 %fusion.65 = (f32[2,2,2,2,2,2,2,1,5,640]{9,8,7,6,5,4,3,2,1,0:T(8,128)S(1)}, f32[2,2,2,2,2,2,2,1,5,640]{9,8,7,6,5,4,3,2,1,0:T(8,128)S(1)}) fusion(f32[2,2,2,2,2,2,2,2,5,640]{9,8,7,6,5,4,3,2,1,0:T(8,128)} %reshape.161), kind=kLoop, calls=%fused_computation.147 | loop fusion | bytes 6553600 | tf_op jit(solution)/shard_map/slice | solution.py:41
  110.4 1.8 copy.75
  116.1 2.6 %fusion.36 = f32[1280,640]{1,0:T(8,128)} fusion(f32[128,640]{1,0:T(8,128)S(1)} %get-tuple-element.8, f32[128]{0:T(128)S(1)} %negate_multiply_fusion, bf16[128,1280]{1,0:T(8,128)(2,1)S(1)} %copy-done.5, f32[128]{0:T(128)S(1)} %add_rsqrt_fusion, f32[128]{0:T(128)S(1)} %broadcast_multiply_fusion.2), kind=kOutput, calls=%fused_computation.75 | convolution fusion | flops 211845120 | bytes 3933696 | tf_op jit(solution)/shard_map/dot_general | solution.py:121
  118.7 4.9 %reshape.160 = f32[2,2,2,2,2,2,2,2,5,640]{9,8,7,6,5,4,3,2,1,0:T(8,128)} reshape(f32[1280,640]{1,0:T(8,128)} %fusion.36) | data formatting | bytes 6553600 | tf_op jit(solution)/shard_map/reshape | solution.py:35
  123.6 2.8 %fusion.2 = bf16[2,2,2,2,2,2,2,5,640]{8,7,6,5,4,3,2,1,0:T(8,128)(2,1)S(1)} fusion(f32[2,2,2,2,2,2,2,2,5,640]{9,8,7,6,5,4,3,2,1,0:T(8,128)} %reshape.160, pred[]{:T(512)S(6)} %ne.39), kind=kLoop, calls=%fused_computation.8 | loop fusion | flops 409600 | bytes 2457601 | tf_op jit(solution)/shard_map/convert_element_type | solution.py:43
  128.3 1.9 collective-permute-start.6
  132.0 5.0 %collective-permute-start.7 = (f32[8,128]{1,0:T(8,128)S(1)}, f32[8,128]{1,0:T(8,128)S(1)}, u32[]{:S(2)}, u32[]{:S(2)}) collective-permute-start(f32[8,128]{1,0:T(8,128)S(1)} %add.172), channel_id=1, source_target_pairs={{0,64},{1,65},{2,66},{3,67},{4,68},{5,69},{6,70},{7,71},{8,72},{9,... | collective-permute-start | bytes 12296 | tf_op jit(solution)/shard_map/ppermute | solution.py:15
  139.2 3.9 %collective-permute-done.8 = f32[8,128]{1,0:T(8,128)S(1)} collective-permute-done((f32[8,128]{1,0:T(8,128)S(1)}, f32[8,128]{1,0:T(8,128)S(1)}, u32[]{:S(2)}, u32[]{:S(2)}) %collective-permute-start.8) | collective-permute-done | bytes 4128 | tf_op jit(solution)/shard_map/ppermute | solution.py:15
  143.2 3.1 %collective-permute-start.9 = (f32[8,128]{1,0:T(8,128)S(1)}, f32[8,128]{1,0:T(8,128)S(1)}, u32[]{:S(2)}, u32[]{:S(2)}) collective-permute-start(f32[8,128]{1,0:T(8,128)S(1)} %add.174), channel_id=1, source_target_pairs={{0,32},{1,33},{2,34},{3,35},{4,36},{5,37},{6,38},{7,39},{8,40},{9,... | collective-permute-start | bytes 12296 | tf_op jit(solution)/shard_map/ppermute | solution.py:15
  146.3 2.0 collective-permute-done.9
  148.3 3.6 %collective-permute-start.10 = (f32[8,128]{1,0:T(8,128)S(1)}, f32[8,128]{1,0:T(8,128)S(1)}, u32[]{:S(2)}, u32[]{:S(2)}) collective-permute-start(f32[8,128]{1,0:T(8,128)S(1)} %add.175), channel_id=1, source_target_pairs={{0,128},{1,129},{2,130},{3,131},{4,132},{5,133},{6,134},{7,135},{8... | collective-permute-start | bytes 12296 | tf_op jit(solution)/shard_map/ppermute | solution.py:15
  153.5 4.8 %collective-permute-start.11 = (f32[8,128]{1,0:T(8,128)S(1)}, f32[8,128]{1,0:T(8,128)S(1)}, u32[]{:S(2)}, u32[]{:S(2)}) collective-permute-start(f32[8,128]{1,0:T(8,128)S(1)} %add.176), channel_id=1, source_target_pairs={{0,8},{1,9},{2,10},{3,11},{4,12},{5,13},{6,14},{7,15},{8,0},{9,1},... | collective-permute-start | bytes 12296 | tf_op jit(solution)/shard_map/ppermute | solution.py:15
  158.3 2.7 %collective-permute-done.11 = f32[8,128]{1,0:T(8,128)S(1)} collective-permute-done((f32[8,128]{1,0:T(8,128)S(1)}, f32[8,128]{1,0:T(8,128)S(1)}, u32[]{:S(2)}, u32[]{:S(2)}) %collective-permute-start.11) | collective-permute-done | bytes 4128 | tf_op jit(solution)/shard_map/ppermute | solution.py:15
  163.2 3.2 %bitcast_add_fusion = f32[2,2,2,2,2,2,2,5,640]{8,7,4,0,2,5,1,3,6:T(8,128)S(1)} fusion(f32[2,2,2,2,2,2,2,1,5,640]{9,8,7,6,5,4,3,2,1,0:T(8,128)} %copy-done.2, f32[2,2,2,2,2,2,2,1,5,640]{9,8,7,6,5,4,3,2,1,0:T(8,128)} %copy-done.1, bf16[2,2,2,2,2,2,2,5,640]{8,6,7,5,4,3,2,1,0:T(2,128)(2,1)} %collective-permute-done.32, pred[]{:T(512)S(6)} %ne.39), kind=kLoop, calls=%fused_computation | loop fusion | flops 1228800 | bytes 5734401 | tf_op jit(solution)/shard_map/add | solution.py:44
  167.1 2.3 collective-permute-start.33
  170.5 6.6 %collective-permute-done.33 = bf16[2,2,2,2,2,2,5,640]{7,5,6,4,3,2,1,0:T(2,128)(2,1)S(1)} collective-permute-done((bf16[2,2,2,2,2,2,5,640]{7,5,6,4,3,2,1,0:T(2,128)(2,1)S(1)}, bf16[2,2,2,2,2,2,5,640]{7,5,6,4,3,2,1,0:T(2,128)(2,1)S(1)}, u32[]{:S(2)}, u32[]{:S(2)}) %collective-permute-start.33) | collective-permute-done | bytes 409632 | tf_op jit(solution)/shard_map/ppermute | solution.py:15
  178.2 3.4 %collective-permute-done.25 = bf16[2,2,2,2,2,2,5,640]{7,5,6,4,3,2,1,0:T(2,128)(2,1)S(1)} collective-permute-done((bf16[2,2,2,2,2,2,5,640]{7,5,6,4,3,2,1,0:T(2,128)(2,1)S(1)}, bf16[2,2,2,2,2,2,5,640]{7,5,6,4,3,2,1,0:T(2,128)(2,1)S(1)}, u32[]{:S(2)}, u32[]{:S(2)}) %collective-permute-start.25) | collective-permute-done | bytes 409632 | tf_op jit(solution)/shard_map/ppermute | solution.py:15
  181.8 3.0 %collective-permute-done.34 = bf16[2,2,2,2,2,5,640]{6,5,3,0,2,4,1:T(8,128)(2,1)S(1)} collective-permute-done((bf16[2,2,2,2,2,5,640]{6,5,3,0,2,4,1:T(8,128)(2,1)S(1)}, bf16[2,2,2,2,2,5,640]{6,5,3,0,2,4,1:T(8,128)(2,1)S(1)}, u32[]{:S(2)}, u32[]{:S(2)}) %collective-permute-start.34) | collective-permute-done | bytes 204832 | tf_op jit(solution)/shard_map/ppermute | solution.py:15
  186.8 3.5 %collective-permute-done.35 = bf16[2,2,2,2,5,640]{5,4,2,0,1,3:T(8,128)(2,1)S(1)} collective-permute-done((bf16[2,2,2,2,5,640]{5,4,2,0,1,3:T(8,128)(2,1)S(1)}, bf16[2,2,2,2,5,640]{5,4,2,0,1,3:T(8,128)(2,1)S(1)}, u32[]{:S(2)}, u32[]{:S(2)}) %collective-permute-start.35) | collective-permute-done | bytes 102432 | tf_op jit(solution)/shard_map/ppermute | solution.py:15
  190.4 4.9 %collective-permute-start.36 = (bf16[2,2,2,5,640]{4,3,2,0,1:T(8,128)(2,1)S(1)}, bf16[2,2,2,5,640]{4,3,2,0,1:T(8,128)(2,1)S(1)}, u32[]{:S(2)}, u32[]{:S(2)}) collective-permute-start(bf16[2,2,2,5,640]{4,3,2,0,1:T(8,128)(2,1)S(1)} %fusion.42), channel_id=1, source_target_pairs={{0,4},{1,5},{2,6},{3,7},{4,0},{5,1},{6,2},{7,3},{8,12},{9,13},{10,... | collective-permute-start | bytes 153608 | tf_op jit(solution)/shard_map/ppermute | solution.py:15
  195.4 2.0 collective-permute-start.26
  198.8 4.0 %collective-permute-start.37 = (bf16[2,2,5,640]{3,2,1,0:T(8,128)(2,1)S(1)}, bf16[2,2,5,640]{3,2,1,0:T(8,128)(2,1)S(1)}, u32[]{:S(2)}, u32[]{:S(2)}) collective-permute-start(bf16[2,2,5,640]{3,2,1,0:T(8,128)(2,1)S(1)} %fusion.46), channel_id=1, source_target_pairs={{0,32},{1,33},{2,34},{3,35},{4,36},{5,37},{6,38},{7,39},{8,40},{9,... | collective-permute-start | bytes 76808 | tf_op jit(solution)/shard_map/ppermute | solution.py:15
  204.6 2.3 collective-permute-done.37
  206.9 3.6 %collective-permute-start.38 = (bf16[2,5,640]{2,1,0:T(8,128)(2,1)S(1)}, bf16[2,5,640]{2,1,0:T(8,128)(2,1)S(1)}, u32[]{:S(2)}, u32[]{:S(2)}) collective-permute-start(bf16[2,5,640]{2,1,0:T(8,128)(2,1)S(1)} %fusion.48), channel_id=1, source_target_pairs={{0,128},{1,129},{2,130},{3,131},{4,132},{5,133},{6,134},{7,135},{8... | collective-permute-start | bytes 38408 | tf_op jit(solution)/shard_map/ppermute | solution.py:15
  212.2 3.8 %collective-permute-done.28 = bf16[2,2,2,5,640]{4,3,2,1,0:T(8,128)(2,1)S(1)} collective-permute-done((bf16[2,2,2,5,640]{4,3,2,1,0:T(8,128)(2,1)S(1)}, bf16[2,2,2,5,640]{4,3,2,1,0:T(8,128)(2,1)S(1)}, u32[]{:S(2)}, u32[]{:S(2)}) %collective-permute-start.28) | collective-permute-done | bytes 51232 | tf_op jit(solution)/shard_map/ppermute | solution.py:15
  216.1 2.0 collective-permute-start.29
  218.1 3.5 %collective-permute-done.29 = bf16[2,2,5,640]{3,2,1,0:T(8,128)(2,1)S(1)} collective-permute-done((bf16[2,2,5,640]{3,2,1,0:T(8,128)(2,1)S(1)}, bf16[2,2,5,640]{3,2,1,0:T(8,128)(2,1)S(1)}, u32[]{:S(2)}, u32[]{:S(2)}) %collective-permute-start.29) | collective-permute-done | bytes 25632 | tf_op jit(solution)/shard_map/ppermute | solution.py:15
  221.7 1.8 collective-permute-start.30
  223.5 2.9 %collective-permute-start.39 = (bf16[5,640]{1,0:T(8,128)(2,1)S(1)}, bf16[5,640]{1,0:T(8,128)(2,1)S(1)}, u32[]{:S(2)}, u32[]{:S(2)}) collective-permute-start(bf16[5,640]{1,0:T(8,128)(2,1)S(1)} %fusion.52), channel_id=1, source_target_pairs={{0,8},{1,9},{2,10},{3,11},{4,12},{5,13},{6,14},{7,15},{8,0},{9,1},... | collective-permute-start | bytes 19208 | tf_op jit(solution)/shard_map/ppermute | solution.py:15
  227.1 3.1 %collective-permute-start.31 = (bf16[5,640]{1,0:T(8,128)(2,1)S(1)}, bf16[5,640]{1,0:T(8,128)(2,1)S(1)}, u32[]{:S(2)}, u32[]{:S(2)}) collective-permute-start(bf16[5,640]{1,0:T(8,128)(2,1)S(1)} %fusion.51), channel_id=1, source_target_pairs={{0,8},{1,9},{2,10},{3,11},{4,12},{5,13},{6,14},{7,15},{8,0},{9,1},... | collective-permute-start | bytes 19208 | tf_op jit(solution)/shard_map/ppermute | solution.py:15
  231.7 3.0 %collective-permute-done.31 = bf16[5,640]{1,0:T(8,128)(2,1)S(1)} collective-permute-done((bf16[5,640]{1,0:T(8,128)(2,1)S(1)}, bf16[5,640]{1,0:T(8,128)(2,1)S(1)}, u32[]{:S(2)}, u32[]{:S(2)}) %collective-permute-start.31) | collective-permute-done | bytes 6432 | tf_op jit(solution)/shard_map/ppermute | solution.py:15
  (157 shorter events, 50.8 us)
Async XLA Ops:
  0.6 38.9 %copy-start = (bf16[1280,640]{1,0:T(8,128)(2,1)S(1)}, bf16[1280,640]{1,0:T(8,128)(2,1)}, u32[]{:S(2)}) copy-start(bf16[1280,640]{1,0:T(8,128)(2,1)} %param.14) | copy-start | bytes 4915204
  3.1 35.2 %copy-start.3 = (bf16[5,640,640]{2,1,0:T(8,128)(2,1)S(1)}, bf16[5,640,640]{2,1,0:T(8,128)(2,1)}, u32[]{:S(2)}) copy-start(bf16[5,640,640]{2,1,0:T(8,128)(2,1)} %param.13) | copy-start | bytes 12288004
  5.9 14.2 %collective-permute-start = (bf16[128,640]{1,0:T(8,128)(2,1)S(1)}, bf16[128,640]{1,0:T(8,128)(2,1)S(1)}, u32[]{:S(2)}, u32[]{:S(2)}) collective-permute-start(bf16[128,640]{1,0:T(8,128)(2,1)S(1)} %multiply_convert_fusion.1), channel_id=1, source_target_pairs={{0,8},{1,9},{2,10},{3,11},{4,12},{5,13},{6,14},{7,15},{8,16},{9,17... | collective-permute-start | bytes 491528 | tf_op jit(solution)/shard_map/ppermute | solution.py:10
  14.1 14.5 %collective-permute-start.1 = (bf16[128,640]{1,0:T(8,128)(2,1)S(1)}, bf16[128,640]{1,0:T(8,128)(2,1)S(1)}, u32[]{:S(2)}, u32[]{:S(2)}) collective-permute-start(bf16[128,640]{1,0:T(8,128)(2,1)S(1)} %multiply_convert_fusion.1), channel_id=1, source_target_pairs={{0,4},{1,5},{2,6},{3,7},{4,8},{5,9},{6,10},{7,11},{8,12},{9,13},{1... | collective-permute-start | bytes 491528 | tf_op jit(solution)/shard_map/ppermute | solution.py:10
  17.5 11.4 %collective-permute-start.2 = (bf16[128,640]{1,0:T(8,128)(2,1)S(1)}, bf16[128,640]{1,0:T(8,128)(2,1)S(1)}, u32[]{:S(2)}, u32[]{:S(2)}) collective-permute-start(bf16[128,640]{1,0:T(8,128)(2,1)S(1)} %multiply_convert_fusion.1), channel_id=1, source_target_pairs={{4,0},{5,1},{6,2},{7,3},{8,4},{9,5},{10,6},{11,7},{12,8},{13,9},{1... | collective-permute-start | bytes 491528 | tf_op jit(solution)/shard_map/ppermute | solution.py:10
  18.8 19.5 %collective-permute-start.3 = (bf16[128,640]{1,0:T(8,128)(2,1)S(1)}, bf16[128,640]{1,0:T(8,128)(2,1)S(1)}, u32[]{:S(2)}, u32[]{:S(2)}) collective-permute-start(bf16[128,640]{1,0:T(8,128)(2,1)S(1)} %multiply_convert_fusion.1), channel_id=1, source_target_pairs={{8,0},{9,1},{10,2},{11,3},{12,4},{13,5},{14,6},{15,7},{16,8},{17,9... | collective-permute-start | bytes 491528 | tf_op jit(solution)/shard_map/ppermute | solution.py:10
  39.3 40.0 %copy-start.6 = (bf16[128,1280]{1,0:T(8,128)(2,1)S(1)}, bf16[128,1280]{1,0:T(8,128)(2,1)}, u32[]{:S(2)}) copy-start(bf16[128,1280]{1,0:T(8,128)(2,1)} %param.11) | copy-start | bytes 983044
  41.7 1.3 collective-permute-start.12
  43.6 3.7 %collective-permute-start.13 = (f32[8,128]{1,0:T(8,128)S(1)}, f32[8,128]{1,0:T(8,128)S(1)}, u32[]{:S(2)}, u32[]{:S(2)}) collective-permute-start(f32[8,128]{1,0:T(8,128)S(1)} %broadcast_add_fusion), channel_id=1, source_target_pairs={{0,2},{1,3},{2,0},{3,1},{4,6},{5,7},{6,4},{7,5},{8,10},{9,11},{10,... | collective-permute-start | bytes 12296 | tf_op jit(solution)/shard_map/ppermute | solution.py:15
  48.0 4.0 %collective-permute-start.14 = (f32[8,128]{1,0:T(8,128)S(1)}, f32[8,128]{1,0:T(8,128)S(1)}, u32[]{:S(2)}, u32[]{:S(2)}) collective-permute-start(f32[8,128]{1,0:T(8,128)S(1)} %fusion.82), channel_id=1, source_target_pairs={{0,16},{1,17},{2,18},{3,19},{4,20},{5,21},{6,22},{7,23},{8,24},{9,... | collective-permute-start | bytes 12296 | tf_op jit(solution)/shard_map/ppermute | solution.py:15
  52.0 3.7 %collective-permute-start.15 = (f32[8,128]{1,0:T(8,128)S(1)}, f32[8,128]{1,0:T(8,128)S(1)}, u32[]{:S(2)}, u32[]{:S(2)}) collective-permute-start(f32[8,128]{1,0:T(8,128)S(1)} %add.180), channel_id=1, source_target_pairs={{0,64},{1,65},{2,66},{3,67},{4,68},{5,69},{6,70},{7,71},{8,72},{9,... | collective-permute-start | bytes 12296 | tf_op jit(solution)/shard_map/ppermute | solution.py:15
  55.6 4.5 %collective-permute-start.16 = (f32[8,128]{1,0:T(8,128)S(1)}, f32[8,128]{1,0:T(8,128)S(1)}, u32[]{:S(2)}, u32[]{:S(2)}) collective-permute-start(f32[8,128]{1,0:T(8,128)S(1)} %add.181), channel_id=1, source_target_pairs={{0,4},{1,5},{2,6},{3,7},{4,0},{5,1},{6,2},{7,3},{8,12},{9,13},{10,... | collective-permute-start | bytes 12296 | tf_op jit(solution)/shard_map/ppermute | solution.py:15
  60.2 5.1 %collective-permute-start.17 = (f32[8,128]{1,0:T(8,128)S(1)}, f32[8,128]{1,0:T(8,128)S(1)}, u32[]{:S(2)}, u32[]{:S(2)}) collective-permute-start(f32[8,128]{1,0:T(8,128)S(1)} %add.182), channel_id=1, source_target_pairs={{0,32},{1,33},{2,34},{3,35},{4,36},{5,37},{6,38},{7,39},{8,40},{9,... | collective-permute-start | bytes 12296 | tf_op jit(solution)/shard_map/ppermute | solution.py:15
  65.3 5.2 %collective-permute-start.18 = (f32[8,128]{1,0:T(8,128)S(1)}, f32[8,128]{1,0:T(8,128)S(1)}, u32[]{:S(2)}, u32[]{:S(2)}) collective-permute-start(f32[8,128]{1,0:T(8,128)S(1)} %add.183), channel_id=1, source_target_pairs={{0,128},{1,129},{2,130},{3,131},{4,132},{5,133},{6,134},{7,135},{8... | collective-permute-start | bytes 12296 | tf_op jit(solution)/shard_map/ppermute | solution.py:15
  69.6 5.9 %collective-permute-start.4 = (f32[8,128]{1,0:T(8,128)S(1)}, f32[8,128]{1,0:T(8,128)S(1)}, u32[]{:S(2)}, u32[]{:S(2)}) collective-permute-start(f32[8,128]{1,0:T(8,128)S(1)} %broadcast_in_dim.12), channel_id=1, source_target_pairs={{0,1},{1,0},{2,3},{3,2},{4,5},{5,4},{6,7},{7,6},{8,9},{9,8},{10,11... | collective-permute-start | bytes 12296 | tf_op jit(solution)/shard_map/ppermute | solution.py:15
  70.5 7.5 %collective-permute-start.19 = (f32[8,128]{1,0:T(8,128)S(1)}, f32[8,128]{1,0:T(8,128)S(1)}, u32[]{:S(2)}, u32[]{:S(2)}) collective-permute-start(f32[8,128]{1,0:T(8,128)S(1)} %add.184), channel_id=1, source_target_pairs={{0,8},{1,9},{2,10},{3,11},{4,12},{5,13},{6,14},{7,15},{8,0},{9,1},... | collective-permute-start | bytes 12296 | tf_op jit(solution)/shard_map/ppermute | solution.py:15
  76.1 51.6 %collective-permute-start.5 = (f32[8,128]{1,0:T(8,128)S(1)}, f32[8,128]{1,0:T(8,128)S(1)}, u32[]{:S(2)}, u32[]{:S(2)}) collective-permute-start(f32[8,128]{1,0:T(8,128)S(1)} %broadcast_add_fusion.1), channel_id=1, source_target_pairs={{0,2},{1,3},{2,0},{3,1},{4,6},{5,7},{6,4},{7,5},{8,10},{9,11},{10,... | collective-permute-start | bytes 12296 | tf_op jit(solution)/shard_map/ppermute | solution.py:15
  80.8 31.4 %collective-permute-start.20 = (bf16[128,640]{1,0:T(8,128)(2,1)S(1)}, bf16[128,640]{1,0:T(8,128)(2,1)}, u32[]{:S(2)}, u32[]{:S(2)}) collective-permute-start(bf16[128,640]{1,0:T(8,128)(2,1)S(1)} %add_convert_fusion.1), channel_id=1, source_target_pairs={{8,0},{9,1},{10,2},{11,3},{12,4},{13,5},{14,6},{15,7},{16,8},{17,9... | collective-permute-start | bytes 491528 | tf_op jit(solution)/shard_map/ppermute | solution.py:10
  82.1 31.1 %collective-permute-start.21 = (bf16[128,640]{1,0:T(8,128)(2,1)S(1)}, bf16[128,640]{1,0:T(8,128)(2,1)}, u32[]{:S(2)}, u32[]{:S(2)}) collective-permute-start(bf16[128,640]{1,0:T(8,128)(2,1)S(1)} %add_convert_fusion.1), channel_id=1, source_target_pairs={{4,0},{5,1},{6,2},{7,3},{8,4},{9,5},{10,6},{11,7},{12,8},{13,9},{1... | collective-permute-start | bytes 491528 | tf_op jit(solution)/shard_map/ppermute | solution.py:10
  83.4 30.8 %collective-permute-start.22 = (bf16[128,640]{1,0:T(8,128)(2,1)S(1)}, bf16[128,640]{1,0:T(8,128)(2,1)S(1)}, u32[]{:S(2)}, u32[]{:S(2)}) collective-permute-start(bf16[128,640]{1,0:T(8,128)(2,1)S(1)} %add_convert_fusion.1), channel_id=1, source_target_pairs={{0,4},{1,5},{2,6},{3,7},{4,8},{5,9},{6,10},{7,11},{8,12},{9,13},{1... | collective-permute-start | bytes 491528 | tf_op jit(solution)/shard_map/ppermute | solution.py:10
  88.9 25.4 %collective-permute-start.23 = (bf16[128,640]{1,0:T(8,128)(2,1)S(1)}, bf16[128,640]{1,0:T(8,128)(2,1)S(1)}, u32[]{:S(2)}, u32[]{:S(2)}) collective-permute-start(bf16[128,640]{1,0:T(8,128)(2,1)S(1)} %add_convert_fusion.1), channel_id=1, source_target_pairs={{0,8},{1,9},{2,10},{3,11},{4,12},{5,13},{6,14},{7,15},{8,16},{9,17... | collective-permute-start | bytes 491528 | tf_op jit(solution)/shard_map/ppermute | solution.py:10
  107.7 1.6 copy-start.1
  107.7 2.7 %copy-start.2 = (f32[2,2,2,2,2,2,2,1,5,640]{9,8,7,6,5,4,3,2,1,0:T(8,128)}, f32[2,2,2,2,2,2,2,1,5,640]{9,8,7,6,5,4,3,2,1,0:T(8,128)S(1)}, u32[]{:S(2)}) copy-start(f32[2,2,2,2,2,2,2,1,5,640]{9,8,7,6,5,4,3,2,1,0:T(8,128)S(1)} %get-tuple-element.12) | copy-start | bytes 4915204
  107.7 6.6 %copy-start.4 = (bf16[5,640,640]{2,1,0:T(8,128)(2,1)S(1)}, bf16[5,640,640]{2,1,0:T(8,128)(2,1)}, u32[]{:S(2)}) copy-start(bf16[5,640,640]{2,1,0:T(8,128)(2,1)} %param.13) | copy-start | bytes 12288004
  112.2 51.0 %collective-permute-start.32 = (bf16[2,2,2,2,2,2,2,5,640]{8,6,7,5,4,3,2,1,0:T(2,128)(2,1)}, bf16[2,2,2,2,2,2,2,5,640]{8,6,7,5,4,3,2,1,0:T(2,128)(2,1)}, u32[]{:S(2)}, u32[]{:S(2)}) collective-permute-start(bf16[2,2,2,2,2,2,2,5,640]{8,6,7,5,4,3,2,1,0:T(2,128)(2,1)} %copy.75), channel_id=1, source_target_pairs={{0,1},{1,0},{2,3},{3,2},{4,5},{5,4},{6,7},{7,6},{8,9},{9,8},{10,11... | collective-permute-start | bytes 2457608 | tf_op jit(solution)/shard_map/ppermute | solution.py:15
  127.1 42.3 %collective-permute-start.24 = (bf16[2,2,2,2,2,2,2,5,640]{8,6,7,5,4,3,2,1,0:T(2,128)(2,1)S(1)}, bf16[2,2,2,2,2,2,2,5,640]{8,6,7,5,4,3,2,1,0:T(2,128)(2,1)S(1)}, u32[]{:S(2)}, u32[]{:S(2)}) collective-permute-start(bf16[2,2,2,2,2,2,2,5,640]{8,6,7,5,4,3,2,1,0:T(2,128)(2,1)S(1)} %copy.48), channel_id=1, source_target_pairs={{0,1},{1,0},{2,3},{3,2},{4,5},{5,4},{6,7},{7,6},{8,9},{9,8},{10,11... | collective-permute-start | bytes 2457608 | tf_op jit(solution)/shard_map/ppermute | solution.py:15
  128.3 3.7 %collective-permute-start.6 = (f32[8,128]{1,0:T(8,128)S(1)}, f32[8,128]{1,0:T(8,128)S(1)}, u32[]{:S(2)}, u32[]{:S(2)}) collective-permute-start(f32[8,128]{1,0:T(8,128)S(1)} %fusion.83), channel_id=1, source_target_pairs={{0,16},{1,17},{2,18},{3,19},{4,20},{5,21},{6,22},{7,23},{8,24},{9,... | collective-permute-start | bytes 12296 | tf_op jit(solution)/shard_map/ppermute | solution.py:15
  132.0 6.6 %collective-permute-start.7 = (f32[8,128]{1,0:T(8,128)S(1)}, f32[8,128]{1,0:T(8,128)S(1)}, u32[]{:S(2)}, u32[]{:S(2)}) collective-permute-start(f32[8,128]{1,0:T(8,128)S(1)} %add.172), channel_id=1, source_target_pairs={{0,64},{1,65},{2,66},{3,67},{4,68},{5,69},{6,70},{7,71},{8,72},{9,... | collective-permute-start | bytes 12296 | tf_op jit(solution)/shard_map/ppermute | solution.py:15
  138.7 4.5 %collective-permute-start.8 = (f32[8,128]{1,0:T(8,128)S(1)}, f32[8,128]{1,0:T(8,128)S(1)}, u32[]{:S(2)}, u32[]{:S(2)}) collective-permute-start(f32[8,128]{1,0:T(8,128)S(1)} %add.173), channel_id=1, source_target_pairs={{0,4},{1,5},{2,6},{3,7},{4,0},{5,1},{6,2},{7,3},{8,12},{9,13},{10,... | collective-permute-start | bytes 12296 | tf_op jit(solution)/shard_map/ppermute | solution.py:15
  143.2 5.1 %collective-permute-start.9 = (f32[8,128]{1,0:T(8,128)S(1)}, f32[8,128]{1,0:T(8,128)S(1)}, u32[]{:S(2)}, u32[]{:S(2)}) collective-permute-start(f32[8,128]{1,0:T(8,128)S(1)} %add.174), channel_id=1, source_target_pairs={{0,32},{1,33},{2,34},{3,35},{4,36},{5,37},{6,38},{7,39},{8,40},{9,... | collective-permute-start | bytes 12296 | tf_op jit(solution)/shard_map/ppermute | solution.py:15
  148.3 5.2 %collective-permute-start.10 = (f32[8,128]{1,0:T(8,128)S(1)}, f32[8,128]{1,0:T(8,128)S(1)}, u32[]{:S(2)}, u32[]{:S(2)}) collective-permute-start(f32[8,128]{1,0:T(8,128)S(1)} %add.175), channel_id=1, source_target_pairs={{0,128},{1,129},{2,130},{3,131},{4,132},{5,133},{6,134},{7,135},{8... | collective-permute-start | bytes 12296 | tf_op jit(solution)/shard_map/ppermute | solution.py:15
  153.5 7.5 %collective-permute-start.11 = (f32[8,128]{1,0:T(8,128)S(1)}, f32[8,128]{1,0:T(8,128)S(1)}, u32[]{:S(2)}, u32[]{:S(2)}) collective-permute-start(f32[8,128]{1,0:T(8,128)S(1)} %add.176), channel_id=1, source_target_pairs={{0,8},{1,9},{2,10},{3,11},{4,12},{5,13},{6,14},{7,15},{8,0},{9,1},... | collective-permute-start | bytes 12296 | tf_op jit(solution)/shard_map/ppermute | solution.py:15
  161.6 7.9 %slice-start = ((s8[5242880]{0:T(1024)(128)(4,1)}), s8[4194304]{0:T(1024)(128)(4,1)S(1)}, s32[]{:S(2)}) async-start(s8[5242880]{0:T(1024)(128)(4,1)} %bitcast.128), calls=%async_computation | async-start | bytes 8388608
  163.2 6.2 %slice-start.1 = ((s8[5242880]{0:T(1024)(128)(4,1)}), s8[1048576]{0:T(1024)(128)(4,1)S(1)}, s32[]{:S(2)}) async-start(s8[5242880]{0:T(1024)(128)(4,1)} %bitcast.128), calls=%async_computation.1 | async-start | bytes 2097152
  167.1 10.0 %collective-permute-start.33 = (bf16[2,2,2,2,2,2,5,640]{7,5,6,4,3,2,1,0:T(2,128)(2,1)S(1)}, bf16[2,2,2,2,2,2,5,640]{7,5,6,4,3,2,1,0:T(2,128)(2,1)S(1)}, u32[]{:S(2)}, u32[]{:S(2)}) collective-permute-start(bf16[2,2,2,2,2,2,5,640]{7,5,6,4,3,2,1,0:T(2,128)(2,1)S(1)} %copy.77), channel_id=1, source_target_pairs={{0,2},{1,3},{2,0},{3,1},{4,6},{5,7},{6,4},{7,5},{8,10},{9,11},{10,... | collective-permute-start | bytes 1228808 | tf_op jit(solution)/shard_map/ppermute | solution.py:15
  170.4 11.1 %collective-permute-start.25 = (bf16[2,2,2,2,2,2,5,640]{7,5,6,4,3,2,1,0:T(2,128)(2,1)S(1)}, bf16[2,2,2,2,2,2,5,640]{7,5,6,4,3,2,1,0:T(2,128)(2,1)S(1)}, u32[]{:S(2)}, u32[]{:S(2)}) collective-permute-start(bf16[2,2,2,2,2,2,5,640]{7,5,6,4,3,2,1,0:T(2,128)(2,1)S(1)} %copy.52), channel_id=1, source_target_pairs={{0,2},{1,3},{2,0},{3,1},{4,6},{5,7},{6,4},{7,5},{8,10},{9,11},{10,... | collective-permute-start | bytes 1228808 | tf_op jit(solution)/shard_map/ppermute | solution.py:15
  177.4 7.3 %collective-permute-start.34 = (bf16[2,2,2,2,2,5,640]{6,5,3,0,2,4,1:T(8,128)(2,1)S(1)}, bf16[2,2,2,2,2,5,640]{6,5,3,0,2,4,1:T(8,128)(2,1)S(1)}, u32[]{:S(2)}, u32[]{:S(2)}) collective-permute-start(bf16[2,2,2,2,2,5,640]{6,5,3,0,2,4,1:T(8,128)(2,1)S(1)} %fusion.34), channel_id=1, source_target_pairs={{0,16},{1,17},{2,18},{3,19},{4,20},{5,21},{6,22},{7,23},{8,24},{9,... | collective-permute-start | bytes 614408 | tf_op jit(solution)/shard_map/ppermute | solution.py:15
  184.9 5.4 %collective-permute-start.35 = (bf16[2,2,2,2,5,640]{5,4,2,0,1,3:T(8,128)(2,1)S(1)}, bf16[2,2,2,2,5,640]{5,4,2,0,1,3:T(8,128)(2,1)S(1)}, u32[]{:S(2)}, u32[]{:S(2)}) collective-permute-start(bf16[2,2,2,2,5,640]{5,4,2,0,1,3:T(8,128)(2,1)S(1)} %fusion.38), channel_id=1, source_target_pairs={{0,64},{1,65},{2,66},{3,67},{4,68},{5,69},{6,70},{7,71},{8,72},{9,... | collective-permute-start | bytes 307208 | tf_op jit(solution)/shard_map/ppermute | solution.py:15
  190.4 8.3 %collective-permute-start.36 = (bf16[2,2,2,5,640]{4,3,2,0,1:T(8,128)(2,1)S(1)}, bf16[2,2,2,5,640]{4,3,2,0,1:T(8,128)(2,1)S(1)}, u32[]{:S(2)}, u32[]{:S(2)}) collective-permute-start(bf16[2,2,2,5,640]{4,3,2,0,1:T(8,128)(2,1)S(1)} %fusion.42), channel_id=1, source_target_pairs={{0,4},{1,5},{2,6},{3,7},{4,0},{5,1},{6,2},{7,3},{8,12},{9,13},{10,... | collective-permute-start | bytes 153608 | tf_op jit(solution)/shard_map/ppermute | solution.py:15
  195.4 7.3 %collective-permute-start.26 = (bf16[2,2,2,2,2,5,640]{6,5,4,3,2,1,0:T(8,128)(2,1)S(1)}, bf16[2,2,2,2,2,5,640]{6,5,4,3,2,1,0:T(8,128)(2,1)S(1)}, u32[]{:S(2)}, u32[]{:S(2)}) collective-permute-start(bf16[2,2,2,2,2,5,640]{6,5,4,3,2,1,0:T(8,128)(2,1)S(1)} %fusion.33), channel_id=1, source_target_pairs={{0,16},{1,17},{2,18},{3,19},{4,20},{5,21},{6,22},{7,23},{8,24},{9,... | collective-permute-start | bytes 614408 | tf_op jit(solution)/shard_map/ppermute | solution.py:15
  198.8 8.1 %collective-permute-start.37 = (bf16[2,2,5,640]{3,2,1,0:T(8,128)(2,1)S(1)}, bf16[2,2,5,640]{3,2,1,0:T(8,128)(2,1)S(1)}, u32[]{:S(2)}, u32[]{:S(2)}) collective-permute-start(bf16[2,2,5,640]{3,2,1,0:T(8,128)(2,1)S(1)} %fusion.46), channel_id=1, source_target_pairs={{0,32},{1,33},{2,34},{3,35},{4,36},{5,37},{6,38},{7,39},{8,40},{9,... | collective-permute-start | bytes 76808 | tf_op jit(solution)/shard_map/ppermute | solution.py:15
  203.0 7.5 %collective-permute-start.27 = (bf16[2,2,2,2,5,640]{5,4,3,2,1,0:T(8,128)(2,1)S(1)}, bf16[2,2,2,2,5,640]{5,4,3,2,1,0:T(8,128)(2,1)S(1)}, u32[]{:S(2)}, u32[]{:S(2)}) collective-permute-start(bf16[2,2,2,2,5,640]{5,4,3,2,1,0:T(8,128)(2,1)S(1)} %fusion.37), channel_id=1, source_target_pairs={{0,64},{1,65},{2,66},{3,67},{4,68},{5,69},{6,70},{7,71},{8,72},{9,... | collective-permute-start | bytes 307208 | tf_op jit(solution)/shard_map/ppermute | solution.py:15
  206.9 11.2 %collective-permute-start.38 = (bf16[2,5,640]{2,1,0:T(8,128)(2,1)S(1)}, bf16[2,5,640]{2,1,0:T(8,128)(2,1)S(1)}, u32[]{:S(2)}, u32[]{:S(2)}) collective-permute-start(bf16[2,5,640]{2,1,0:T(8,128)(2,1)S(1)} %fusion.48), channel_id=1, source_target_pairs={{0,128},{1,129},{2,130},{3,131},{4,132},{5,133},{6,134},{7,135},{8... | collective-permute-start | bytes 38408 | tf_op jit(solution)/shard_map/ppermute | solution.py:15
  210.6 5.4 %collective-permute-start.28 = (bf16[2,2,2,5,640]{4,3,2,1,0:T(8,128)(2,1)S(1)}, bf16[2,2,2,5,640]{4,3,2,1,0:T(8,128)(2,1)S(1)}, u32[]{:S(2)}, u32[]{:S(2)}) collective-permute-start(bf16[2,2,2,5,640]{4,3,2,1,0:T(8,128)(2,1)S(1)} %fusion.41), channel_id=1, source_target_pairs={{0,4},{1,5},{2,6},{3,7},{4,0},{5,1},{6,2},{7,3},{8,12},{9,13},{10,... | collective-permute-start | bytes 153608 | tf_op jit(solution)/shard_map/ppermute | solution.py:15
  216.1 5.6 %collective-permute-start.29 = (bf16[2,2,5,640]{3,2,1,0:T(8,128)(2,1)S(1)}, bf16[2,2,5,640]{3,2,1,0:T(8,128)(2,1)S(1)}, u32[]{:S(2)}, u32[]{:S(2)}) collective-permute-start(bf16[2,2,5,640]{3,2,1,0:T(8,128)(2,1)S(1)} %fusion.45), channel_id=1, source_target_pairs={{0,32},{1,33},{2,34},{3,35},{4,36},{5,37},{6,38},{7,39},{8,40},{9,... | collective-permute-start | bytes 76808 | tf_op jit(solution)/shard_map/ppermute | solution.py:15
  221.7 5.4 %collective-permute-start.30 = (bf16[2,5,640]{2,1,0:T(8,128)(2,1)S(1)}, bf16[2,5,640]{2,1,0:T(8,128)(2,1)S(1)}, u32[]{:S(2)}, u32[]{:S(2)}) collective-permute-start(bf16[2,5,640]{2,1,0:T(8,128)(2,1)S(1)} %fusion.47), channel_id=1, source_target_pairs={{0,128},{1,129},{2,130},{3,131},{4,132},{5,133},{6,134},{7,135},{8... | collective-permute-start | bytes 38408 | tf_op jit(solution)/shard_map/ppermute | solution.py:15
  223.5 7.6 %collective-permute-start.39 = (bf16[5,640]{1,0:T(8,128)(2,1)S(1)}, bf16[5,640]{1,0:T(8,128)(2,1)S(1)}, u32[]{:S(2)}, u32[]{:S(2)}) collective-permute-start(bf16[5,640]{1,0:T(8,128)(2,1)S(1)} %fusion.52), channel_id=1, source_target_pairs={{0,8},{1,9},{2,10},{3,11},{4,12},{5,13},{6,14},{7,15},{8,0},{9,1},... | collective-permute-start | bytes 19208 | tf_op jit(solution)/shard_map/ppermute | solution.py:15
  227.1 7.7 %collective-permute-start.31 = (bf16[5,640]{1,0:T(8,128)(2,1)S(1)}, bf16[5,640]{1,0:T(8,128)(2,1)S(1)}, u32[]{:S(2)}, u32[]{:S(2)}) collective-permute-start(bf16[5,640]{1,0:T(8,128)(2,1)S(1)} %fusion.51), channel_id=1, source_target_pairs={{0,8},{1,9},{2,10},{3,11},{4,12},{5,13},{6,14},{7,15},{8,0},{9,1},... | collective-permute-start | bytes 19208 | tf_op jit(solution)/shard_map/ppermute | solution.py:15
  (4 other events, 4.8 us)

commit v3 on v2

--- a/solution.py
+++ b/solution.py
@@ -27,12 +27,11 @@
     return values
 
 
-def tree_scatter(partial, axis):
+def tree_scatter(partial, extra, axis):
     devices = lax.axis_size(axis)
     depth = devices.bit_length() - 1
     me = lax.axis_index(axis)
-    rows, cols = partial.shape
-    blocks = partial.reshape((2,) * depth + (rows // devices, cols))
+    blocks = partial.reshape((2,) * depth + partial.shape[1:])
     dim_bits = [1 << (depth - 1 - d) for d in range(depth)]
     for bit in link_order(devices):
         at = dim_bits.index(bit)
@@ -41,9 +40,11 @@
         high = lax.index_in_dim(blocks, 1, at, keepdims=False)
         keep = jnp.where(upper, high, low)
         send = jnp.where(upper, low, high).astype(jnp.bfloat16)
-        blocks = keep + swap_with(send, axis, bit).astype(jnp.float32)
+        got, got_extra = swap_with((send, extra), axis, bit)
+        blocks = keep + got.astype(jnp.float32)
+        extra = extra + got_extra
         dim_bits.pop(at)
-    return blocks
+    return blocks, extra
 
 
 def norm_gelu(values):
@@ -100,12 +101,9 @@
     )
     grad_block = (head_part + grad_above.astype(jnp.float32)).astype(jnp.bfloat16)
     columns = grad_block
-    grad_down = tree_scatter(
-        lax.dot_general(
-            columns, conv_act, (((0,), (0,)), ((), ())), preferred_element_type=jnp.float32
-        ),
-        "seq",
-    ).astype(jnp.bfloat16)
+    down_partial = lax.dot_general(
+        columns, conv_act, (((0,), (0,)), ((), ())), preferred_element_type=jnp.float32
+    )
     grad_conv_act = jnp.dot(grad_block, w_out, preferred_element_type=jnp.float32)
     gradient_before_activation = jax.vjp(norm_gelu, conv_pre)[1](grad_conv_act)[0].astype(
         jnp.bfloat16
@@ -117,13 +115,21 @@
     )
     grad_first = jax.vjp(norm_gelu, first_pre)[1](grad_neck)[0].astype(jnp.bfloat16)
     columns = first_act
-    grad_up = tree_scatter(
-        lax.dot_general(
-            columns, grad_first, (((0,), (0,)), ((), ())), preferred_element_type=jnp.float32
-        ),
-        "seq",
-    ).astype(jnp.bfloat16)
-    loss_total = tree_sum(jnp.broadcast_to(local_loss, (8, 128)), "seq")[0, 0]
+    up_partial = lax.dot_general(
+        columns, grad_first, (((0,), (0,)), ((), ())), preferred_element_type=jnp.float32
+    )
+    share = up_partial.shape[0] // seq_devices
+    both = jnp.concatenate(
+        [
+            down_partial.reshape(seq_devices, share, -1),
+            up_partial.reshape(seq_devices, share, -1),
+        ],
+        1,
+    )
+    mine, loss_tile = tree_scatter(both, jnp.broadcast_to(local_loss, (8, 128)), "seq")
+    grad_down = mine[:share].astype(jnp.bfloat16)
+    grad_up = mine[share:].astype(jnp.bfloat16)
+    loss_total = loss_tile[0, 0]
     return (loss_total / mask_total, grad_up, grad_down)
 
 

time: 241 us -> 245 us (1.017); the launches traced: 236 us -> 244 us
  starting transfers between devices: 99.8 us -> 83.7 us
  waiting for transfers between devices: 80.3 us -> 95.5 us
  other arithmetic: 17 us -> 24.9 us
    ppermute x32 -> x24, starting transfers between devices: 68.9 us -> 52.9 us  [swap_with(): return lax.ppermute(block, axis, [(i, i ^ bit) for i in range(devices)])]
    ppermute x32 -> x24, waiting for transfers between devices: 62.4 us -> 77.6 us  [swap_with(): return lax.ppermute(block, axis, [(i, i ^ bit) for i in range(devices)])]
    reshape x2 -> x0, local copies, waits for them, and re-layouts: 9.75 us -> none  [tree_scatter(): blocks = partial.reshape((2,) * depth + (rows // devices, cols))]
    concatenate x0 -> x2, local copies, waits for them, and re-layouts: none -> 9.64 us  [shards(): jnp.concatenate([down_partial.reshape(seq_devices, share, -1), up_partial...]
    add x14 -> x15, other arithmetic: 4.63 us -> 12.6 us  [the longest x7 11.3 us: tree_scatter(): blocks = keep + got.astype(jnp.float32)]
    convert_element_type x16 -> x8, other arithmetic: 3.73 us -> 6.14 us  [tree_scatter(): send = jnp.where(upper, low, high).astype(jnp.bfloat16)]
    unnamed x30 -> x26, local copies, waits for them, and re-layouts: 4.36 us -> 5.71 us
  transfers between devices with their start and end apart: 40 -> 32, of which waited for: 27 -> 21; matrix products, arithmetic and copies ran while one was open for 16% -> 5% of each run, Pallas kernels for 0% -> 0%
where the time goes in v3:
time: 245 us; the launch traced here: 244 us
  waiting for transfers between devices  95.5 us (39%)
  starting transfers between devices  83.7 us (34%)
  other arithmetic  24.9 us (10%)
  local copies, waits for them, and re-layouts  21.7 us (9%)
  matrix products  13.9 us (6%)
  between operations  4.38 us (2%)
    ppermute x24, waiting for transfers between devices, swap_with(): return lax.ppermute(block, axis, [(i, i ^ bit) for i in range(devices)])  77.6 us
    ppermute x24, starting transfers between devices, swap_with(): return lax.ppermute(block, axis, [(i, i ^ bit) for i in range(devices)])  52.9 us
    ppermute x8, starting transfers between devices, from_behind(): return lax.ppermute(block, axis, route)  30.9 us
    ppermute x8, waiting for transfers between devices, from_behind(): return lax.ppermute(block, axis, route)  17.8 us
    add x7, other arithmetic, tree_scatter(): blocks = keep + got.astype(jnp.float32)  11.3 us
    concatenate x2, local copies, waits for them, and re-layouts, shards(): jnp.concatenate([down_partial.reshape(seq_devices, share, -1), up_partial...  9.64 us
    convert_element_type x8, other arithmetic, tree_scatter(): send = jnp.where(upper, low, high).astype(jnp.bfloat16)  6.14 us
    unnamed x26, local copies, waits for them, and re-layouts  5.71 us
  transfers between devices with their start and end apart: 32, of which 21 were waited for; matrix products, arithmetic and copies ran while one was open for 5% of the time, Pallas kernels for 0%

profile of v3, /device:TPU:32, one launch (start us, length us, event | category | flops | bytes accessed | tf_op | source)
XLA Modules:
  0.0 244.1 jit_solution(9979684045937725656)
XLA Ops:
  3.1 2.3 fusion.59
  5.9 8.2 %collective-permute-start = (bf16[128,640]{1,0:T(8,128)(2,1)S(1)}, bf16[128,640]{1,0:T(8,128)(2,1)S(1)}, u32[]{:S(2)}, u32[]{:S(2)}) collective-permute-start(bf16[128,640]{1,0:T(8,128)(2,1)S(1)} %multiply_convert_fusion.1), channel_id=1, source_target_pairs={{0,8},{1,9},{2,10},{3,11},{4,12},{5,13},{6,14},{7,15},{8,16},{9,17... | collective-permute-start | bytes 491528 | tf_op jit(solution)/shard_map/ppermute | solution.py:10
  14.1 3.4 %collective-permute-start.1 = (bf16[128,640]{1,0:T(8,128)(2,1)S(1)}, bf16[128,640]{1,0:T(8,128)(2,1)S(1)}, u32[]{:S(2)}, u32[]{:S(2)}) collective-permute-start(bf16[128,640]{1,0:T(8,128)(2,1)S(1)} %multiply_convert_fusion.1), channel_id=1, source_target_pairs={{0,4},{1,5},{2,6},{3,7},{4,8},{5,9},{6,10},{7,11},{8,12},{9,13},{1... | collective-permute-start | bytes 491528 | tf_op jit(solution)/shard_map/ppermute | solution.py:10
  20.1 8.5 %collective-permute-done.1 = bf16[128,640]{1,0:T(8,128)(2,1)S(1)} collective-permute-done((bf16[128,640]{1,0:T(8,128)(2,1)S(1)}, bf16[128,640]{1,0:T(8,128)(2,1)S(1)}, u32[]{:S(2)}, u32[]{:S(2)}) %collective-permute-start.1) | collective-permute-done | bytes 163872 | tf_op jit(solution)/shard_map/ppermute | solution.py:10
  28.9 9.4 %collective-permute-done.3 = bf16[128,640]{1,0:T(8,128)(2,1)S(1)} collective-permute-done((bf16[128,640]{1,0:T(8,128)(2,1)S(1)}, bf16[128,640]{1,0:T(8,128)(2,1)S(1)}, u32[]{:S(2)}, u32[]{:S(2)}) %collective-permute-start.3) | collective-permute-done | bytes 163872 | tf_op jit(solution)/shard_map/ppermute | solution.py:10
  43.7 3.6 %collective-permute-done.13 = f32[8,128]{1,0:T(8,128)S(1)} collective-permute-done((f32[8,128]{1,0:T(8,128)S(1)}, f32[8,128]{1,0:T(8,128)S(1)}, u32[]{:S(2)}, u32[]{:S(2)}) %collective-permute-start.13) | collective-permute-done | bytes 4128 | tf_op jit(solution)/shard_map/ppermute | solution.py:15
  47.9 2.4 %collective-permute-start.14 = (f32[8,128]{1,0:T(8,128)S(1)}, f32[8,128]{1,0:T(8,128)S(1)}, u32[]{:S(2)}, u32[]{:S(2)}) collective-permute-start(f32[8,128]{1,0:T(8,128)S(1)} %fusion.72), channel_id=1, source_target_pairs={{0,16},{1,17},{2,18},{3,19},{4,20},{5,21},{6,22},{7,23},{8,24},{9,... | collective-permute-start | bytes 12296 | tf_op jit(solution)/shard_map/ppermute | solution.py:15
  50.4 1.6 collective-permute-done.14
  52.0 2.1 collective-permute-start.15
  55.6 4.5 %collective-permute-done.16 = f32[8,128]{1,0:T(8,128)S(1)} collective-permute-done((f32[8,128]{1,0:T(8,128)S(1)}, f32[8,128]{1,0:T(8,128)S(1)}, u32[]{:S(2)}, u32[]{:S(2)}) %collective-permute-start.16) | collective-permute-done | bytes 4128 | tf_op jit(solution)/shard_map/ppermute | solution.py:15
  60.1 3.4 %collective-permute-start.17 = (f32[8,128]{1,0:T(8,128)S(1)}, f32[8,128]{1,0:T(8,128)S(1)}, u32[]{:S(2)}, u32[]{:S(2)}) collective-permute-start(f32[8,128]{1,0:T(8,128)S(1)} %add.158), channel_id=1, source_target_pairs={{0,32},{1,33},{2,34},{3,35},{4,36},{5,37},{6,38},{7,39},{8,40},{9,... | collective-permute-start | bytes 12296 | tf_op jit(solution)/shard_map/ppermute | solution.py:15
  63.5 1.7 collective-permute-done.17
  65.3 3.6 %collective-permute-start.18 = (f32[8,128]{1,0:T(8,128)S(1)}, f32[8,128]{1,0:T(8,128)S(1)}, u32[]{:S(2)}, u32[]{:S(2)}) collective-permute-start(f32[8,128]{1,0:T(8,128)S(1)} %add.159), channel_id=1, source_target_pairs={{0,128},{1,129},{2,130},{3,131},{4,132},{5,133},{6,134},{7,135},{8... | collective-permute-start | bytes 12296 | tf_op jit(solution)/shard_map/ppermute | solution.py:15
  70.5 4.9 %collective-permute-start.19 = (f32[8,128]{1,0:T(8,128)S(1)}, f32[8,128]{1,0:T(8,128)S(1)}, u32[]{:S(2)}, u32[]{:S(2)}) collective-permute-start(f32[8,128]{1,0:T(8,128)S(1)} %add.160), channel_id=1, source_target_pairs={{0,8},{1,9},{2,10},{3,11},{4,12},{5,13},{6,14},{7,15},{8,0},{9,1},... | collective-permute-start | bytes 12296 | tf_op jit(solution)/shard_map/ppermute | solution.py:15
  75.4 2.6 %collective-permute-done.19 = f32[8,128]{1,0:T(8,128)S(1)} collective-permute-done((f32[8,128]{1,0:T(8,128)S(1)}, f32[8,128]{1,0:T(8,128)S(1)}, u32[]{:S(2)}, u32[]{:S(2)}) %collective-permute-start.19) | collective-permute-done | bytes 4128 | tf_op jit(solution)/shard_map/ppermute | solution.py:15
  83.4 5.5 %collective-permute-start.22 = (bf16[128,640]{1,0:T(8,128)(2,1)S(1)}, bf16[128,640]{1,0:T(8,128)(2,1)S(1)}, u32[]{:S(2)}, u32[]{:S(2)}) collective-permute-start(bf16[128,640]{1,0:T(8,128)(2,1)S(1)} %add_convert_fusion.1), channel_id=1, source_target_pairs={{0,4},{1,5},{2,6},{3,7},{4,8},{5,9},{6,10},{7,11},{8,12},{9,13},{1... | collective-permute-start | bytes 491528 | tf_op jit(solution)/shard_map/ppermute | solution.py:10
  88.9 8.6 %collective-permute-start.23 = (bf16[128,640]{1,0:T(8,128)(2,1)S(1)}, bf16[128,640]{1,0:T(8,128)(2,1)S(1)}, u32[]{:S(2)}, u32[]{:S(2)}) collective-permute-start(bf16[128,640]{1,0:T(8,128)(2,1)S(1)} %add_convert_fusion.1), channel_id=1, source_target_pairs={{0,8},{1,9},{2,10},{3,11},{4,12},{5,13},{6,14},{7,15},{8,16},{9,17... | collective-permute-start | bytes 491528 | tf_op jit(solution)/shard_map/ppermute | solution.py:10
  97.5 2.4 fusion.52
  99.9 4.8 %concatenate.8 = f32[2,2,2,2,2,2,2,2,5,640]{9,8,7,6,5,4,3,2,1,0:T(8,128)} reshape(f32[1280,640]{1,0:T(8,128)} %fusion.52) | data formatting | bytes 6553600 | tf_op jit(solution)/shard_map/concatenate | solution.py:122
  106.8 3.7 %multiply_reduce_fusion = (f32[128]{0:T(128)S(1)}, f32[128,640]{1,0:T(8,128)S(1)}) fusion(f32[128,640]{1,0:T(8,128)S(1)} %get-tuple-element.15, f32[128]{0:T(128)S(1)} %broadcast_multiply_fusion.1, f32[128]{0:T(128)S(1)} %fusion.50, bf16[5,128,640]{2,1,0:T(8,128)(2,1)S(1)} %bitcast_dynamic-update-slice_fusion, bf16[5,640,640]{2,1,0:T(8,128)(2,1)} %param.13), kind=kOutput, calls=%fused_computation.64 | convolution fusion | flops 526172032 | bytes 5572096 | tf_op jit(solution)/shard_map/krc,kbc->rb/dot_general | solution.py:113
  110.8 2.7 %fusion.37 = f32[1280,640]{1,0:T(8,128)} fusion(f32[128,640]{1,0:T(8,128)S(1)} %get-tuple-element.8, f32[128]{0:T(128)S(1)} %negate_multiply_fusion, bf16[128,1280]{1,0:T(8,128)(2,1)S(1)} %copy-done.5, f32[128]{0:T(128)S(1)} %add_rsqrt_fusion, f32[128]{0:T(128)S(1)} %broadcast_multiply_fusion.2), kind=kOutput, calls=%fused_computation.71 | convolution fusion | flops 211845120 | bytes 3933696 | tf_op jit(solution)/shard_map/dot_general | solution.py:118
  113.4 4.8 %concatenate.9 = f32[2,2,2,2,2,2,2,2,5,640]{9,8,7,6,5,4,3,2,1,0:T(8,128)} reshape(f32[1280,640]{1,0:T(8,128)} %fusion.37) | data formatting | bytes 6553600 | tf_op jit(solution)/shard_map/concatenate | solution.py:122
  118.3 4.9 %fusion.1 = bf16[2,2,2,2,2,2,2,10,640]{8,7,6,5,4,3,2,1,0:T(8,128)(2,1)S(1)} fusion(pred[]{:T(512)S(6)} %ne.31, f32[2,2,2,2,2,2,2,2,5,640]{9,8,7,6,5,4,3,2,1,0:T(8,128)} %concatenate.9, f32[2,2,2,2,2,2,2,2,5,640]{9,8,7,6,5,4,3,2,1,0:T(8,128)} %concatenate.8), kind=kLoop, calls=%fused_computation.6 | loop fusion | flops 7372800 | bytes 8192001 | tf_op jit(solution)/shard_map/convert_element_type | solution.py:42
  123.2 2.4 copy.37
  125.6 3.7 %collective-permute-done.24 = bf16[2,2,2,2,2,2,2,10,640]{8,6,7,5,4,3,2,1,0:T(2,128)(2,1)S(1)} collective-permute-done((bf16[2,2,2,2,2,2,2,10,640]{8,6,7,5,4,3,2,1,0:T(2,128)(2,1)}, bf16[2,2,2,2,2,2,2,10,640]{8,6,7,5,4,3,2,1,0:T(2,128)(2,1)S(1)}, u32[]{:S(2)}, u32[]{:S(2)}) %collective-permute-start.24) | collective-permute-done | bytes 1638432 | tf_op jit(solution)/shard_map/ppermute | solution.py:15
  129.3 5.0 %bitcast_add_fusion = f32[2,2,2,2,2,2,2,10,640]{8,7,6,5,4,3,2,1,0:T(8,128)S(1)} fusion(bf16[2,2,2,2,2,2,2,10,640]{8,6,7,5,4,3,2,1,0:T(2,128)(2,1)S(1)} %collective-permute-done.24, pred[]{:T(512)S(6)} %ne.31, f32[2,2,2,2,2,2,2,2,5,640]{9,8,7,6,5,4,3,2,1,0:T(8,128)} %concatenate.9, f32[2,2,2,2,2,2,2,2,5,640]{9,8,7,6,5,4,3,2,1,0:T(8,128)} %concatenate.8), kind=kLoop, calls=%fused_computation.4 | loop fusion | flops 4096000 | bytes 11468801 | tf_op jit(solution)/shard_map/add | solution.py:44
  136.6 1.9 collective-permute-start.25
  138.6 18.5 %collective-permute-done.25 = bf16[2,2,2,2,2,2,10,640]{7,5,6,4,3,2,1,0:T(2,128)(2,1)S(1)} collective-permute-done((bf16[2,2,2,2,2,2,10,640]{7,5,6,4,3,2,1,0:T(2,128)(2,1)S(1)}, bf16[2,2,2,2,2,2,10,640]{7,5,6,4,3,2,1,0:T(2,128)(2,1)S(1)}, u32[]{:S(2)}, u32[]{:S(2)}) %collective-permute-start.25) | collective-permute-done | bytes 819232 | tf_op jit(solution)/shard_map/ppermute | solution.py:15
  157.1 3.1 %bitcast_add_fusion.1 = f32[2,2,2,2,2,2,10,640]{7,6,5,4,3,2,1,0:T(8,128)S(1)} fusion(f32[2,2,2,2,2,2,2,10,640]{8,7,6,5,4,3,2,1,0:T(8,128)} %copy-done.1, bf16[2,2,2,2,2,2,10,640]{7,5,6,4,3,2,1,0:T(2,128)(2,1)S(1)} %collective-permute-done.25, pred[]{:T(512)S(6)} %ne.30), kind=kLoop, calls=%fused_computation.7 | loop fusion | flops 1228800 | bytes 5734401 | tf_op jit(solution)/shard_map/add | solution.py:44
  162.2 2.8 %collective-permute-start.26 = (bf16[2,2,2,2,2,10,640]{6,4,5,3,2,1,0:T(2,128)(2,1)S(1)}, bf16[2,2,2,2,2,10,640]{6,4,5,3,2,1,0:T(2,128)(2,1)S(1)}, u32[]{:S(2)}, u32[]{:S(2)}) collective-permute-start(bf16[2,2,2,2,2,10,640]{6,4,5,3,2,1,0:T(2,128)(2,1)S(1)} %copy.41), channel_id=1, source_target_pairs={{0,16},{1,17},{2,18},{3,19},{4,20},{5,21},{6,22},{7,23},{8,24},{9,... | collective-permute-start | bytes 1228808 | tf_op jit(solution)/shard_map/ppermute | solution.py:15
  165.0 8.9 %collective-permute-done.26 = bf16[2,2,2,2,2,10,640]{6,4,5,3,2,1,0:T(2,128)(2,1)S(1)} collective-permute-done((bf16[2,2,2,2,2,10,640]{6,4,5,3,2,1,0:T(2,128)(2,1)S(1)}, bf16[2,2,2,2,2,10,640]{6,4,5,3,2,1,0:T(2,128)(2,1)S(1)}, u32[]{:S(2)}, u32[]{:S(2)}) %collective-permute-start.26) | collective-permute-done | bytes 409632 | tf_op jit(solution)/shard_map/ppermute | solution.py:15
  173.9 1.9 bitcast_add_fusion.2
  176.6 7.4 %collective-permute-start.27 = (bf16[2,2,2,2,10,640]{5,4,3,2,1,0:T(8,128)(2,1)}, bf16[2,2,2,2,10,640]{5,4,3,2,1,0:T(8,128)(2,1)S(1)}, u32[]{:S(2)}, u32[]{:S(2)}) collective-permute-start(bf16[2,2,2,2,10,640]{5,4,3,2,1,0:T(8,128)(2,1)} %fusion.34), channel_id=1, source_target_pairs={{0,64},{1,65},{2,66},{3,67},{4,68},{5,69},{6,70},{7,71},{8,72},{9,... | collective-permute-start | bytes 614408 | tf_op jit(solution)/shard_map/ppermute | solution.py:15
  184.1 6.5 %collective-permute-done.27 = bf16[2,2,2,2,10,640]{5,4,3,2,1,0:T(8,128)(2,1)S(1)} collective-permute-done((bf16[2,2,2,2,10,640]{5,4,3,2,1,0:T(8,128)(2,1)}, bf16[2,2,2,2,10,640]{5,4,3,2,1,0:T(8,128)(2,1)S(1)}, u32[]{:S(2)}, u32[]{:S(2)}) %collective-permute-start.27) | collective-permute-done | bytes 204832 | tf_op jit(solution)/shard_map/ppermute | solution.py:15
  193.7 4.3 %collective-permute-done.28 = bf16[2,2,2,10,640]{4,3,2,1,0:T(8,128)(2,1)S(1)} collective-permute-done((bf16[2,2,2,10,640]{4,3,2,1,0:T(8,128)(2,1)S(1)}, bf16[2,2,2,10,640]{4,3,2,1,0:T(8,128)(2,1)S(1)}, u32[]{:S(2)}, u32[]{:S(2)}) %collective-permute-start.28) | collective-permute-done | bytes 102432 | tf_op jit(solution)/shard_map/ppermute | solution.py:15
  199.1 1.7 collective-permute-start.29
  201.4 1.7 collective-permute-start.5
  203.2 2.0 collective-permute-done.29
  205.2 3.4 %collective-permute-start.30 = (bf16[2,10,640]{2,1,0:T(8,128)(2,1)S(1)}, bf16[2,10,640]{2,1,0:T(8,128)(2,1)S(1)}, u32[]{:S(2)}, u32[]{:S(2)}) collective-permute-start(bf16[2,10,640]{2,1,0:T(8,128)(2,1)S(1)} %fusion.43), channel_id=1, source_target_pairs={{0,128},{1,129},{2,130},{3,131},{4,132},{5,133},{6,134},{7,135},{8... | collective-permute-start | bytes 76808 | tf_op jit(solution)/shard_map/ppermute | solution.py:15
  210.0 3.0 %collective-permute-done.6 = f32[8,128]{1,0:T(8,128)S(1)} collective-permute-done((f32[8,128]{1,0:T(8,128)S(1)}, f32[8,128]{1,0:T(8,128)S(1)}, u32[]{:S(2)}, u32[]{:S(2)}) %collective-permute-start.6) | collective-permute-done | bytes 4128 | tf_op jit(solution)/shard_map/ppermute | solution.py:15
  213.6 3.0 %collective-permute-done.7 = f32[8,128]{1,0:T(8,128)S(1)} collective-permute-done((f32[8,128]{1,0:T(8,128)S(1)}, f32[8,128]{1,0:T(8,128)S(1)}, u32[]{:S(2)}, u32[]{:S(2)}) %collective-permute-start.7) | collective-permute-done | bytes 4128 | tf_op jit(solution)/shard_map/ppermute | solution.py:15
  216.6 3.1 %collective-permute-start.8 = (f32[8,128]{1,0:T(8,128)S(1)}, f32[8,128]{1,0:T(8,128)S(1)}, u32[]{:S(2)}, u32[]{:S(2)}) collective-permute-start(f32[8,128]{1,0:T(8,128)S(1)} %add.149), channel_id=1, source_target_pairs={{0,4},{1,5},{2,6},{3,7},{4,0},{5,1},{6,2},{7,3},{8,12},{9,13},{10,... | collective-permute-start | bytes 12296 | tf_op jit(solution)/shard_map/ppermute | solution.py:15
  219.8 2.9 %collective-permute-start.31 = (bf16[10,640]{1,0:T(8,128)(2,1)S(1)}, bf16[10,640]{1,0:T(8,128)(2,1)S(1)}, u32[]{:S(2)}, u32[]{:S(2)}) collective-permute-start(bf16[10,640]{1,0:T(8,128)(2,1)S(1)} %fusion.45), channel_id=1, source_target_pairs={{0,8},{1,9},{2,10},{3,11},{4,12},{5,13},{6,14},{7,15},{8,0},{9,1},... | collective-permute-start | bytes 38408 | tf_op jit(solution)/shard_map/ppermute | solution.py:15
  222.7 3.5 %collective-permute-start.9 = (f32[8,128]{1,0:T(8,128)S(1)}, f32[8,128]{1,0:T(8,128)S(1)}, u32[]{:S(2)}, u32[]{:S(2)}) collective-permute-start(f32[8,128]{1,0:T(8,128)S(1)} %add.150), channel_id=1, source_target_pairs={{0,32},{1,33},{2,34},{3,35},{4,36},{5,37},{6,38},{7,39},{8,40},{9,... | collective-permute-start | bytes 12296 | tf_op jit(solution)/shard_map/ppermute | solution.py:15
  227.8 1.8 collective-permute-start.10
  229.6 3.3 %collective-permute-done.10 = f32[8,128]{1,0:T(8,128)S(1)} collective-permute-done((f32[8,128]{1,0:T(8,128)S(1)}, f32[8,128]{1,0:T(8,128)S(1)}, u32[]{:S(2)}, u32[]{:S(2)}) %collective-permute-start.10) | collective-permute-done | bytes 4128 | tf_op jit(solution)/shard_map/ppermute | solution.py:15
  233.0 3.1 %collective-permute-start.11 = (f32[8,128]{1,0:T(8,128)S(1)}, f32[8,128]{1,0:T(8,128)S(1)}, u32[]{:S(2)}, u32[]{:S(2)}) collective-permute-start(f32[8,128]{1,0:T(8,128)S(1)} %add.152), channel_id=1, source_target_pairs={{0,8},{1,9},{2,10},{3,11},{4,12},{5,13},{6,14},{7,15},{8,0},{9,1},... | collective-permute-start | bytes 12296 | tf_op jit(solution)/shard_map/ppermute | solution.py:15
  236.0 4.4 %collective-permute-done.11 = f32[8,128]{1,0:T(8,128)S(1)} collective-permute-done((f32[8,128]{1,0:T(8,128)S(1)}, f32[8,128]{1,0:T(8,128)S(1)}, u32[]{:S(2)}, u32[]{:S(2)}) %collective-permute-start.11) | collective-permute-done | bytes 4128 | tf_op jit(solution)/shard_map/ppermute | solution.py:15
  (116 shorter events, 36.5 us)
Async XLA Ops:
  0.6 38.8 %copy-start = (bf16[1280,640]{1,0:T(8,128)(2,1)S(1)}, bf16[1280,640]{1,0:T(8,128)(2,1)}, u32[]{:S(2)}) copy-start(bf16[1280,640]{1,0:T(8,128)(2,1)} %param.14) | copy-start | bytes 4915204
  3.1 35.2 %copy-start.3 = (bf16[5,640,640]{2,1,0:T(8,128)(2,1)S(1)}, bf16[5,640,640]{2,1,0:T(8,128)(2,1)}, u32[]{:S(2)}) copy-start(bf16[5,640,640]{2,1,0:T(8,128)(2,1)} %param.13) | copy-start | bytes 12288004
  5.9 14.2 %collective-permute-start = (bf16[128,640]{1,0:T(8,128)(2,1)S(1)}, bf16[128,640]{1,0:T(8,128)(2,1)S(1)}, u32[]{:S(2)}, u32[]{:S(2)}) collective-permute-start(bf16[128,640]{1,0:T(8,128)(2,1)S(1)} %multiply_convert_fusion.1), channel_id=1, source_target_pairs={{0,8},{1,9},{2,10},{3,11},{4,12},{5,13},{6,14},{7,15},{8,16},{9,17... | collective-permute-start | bytes 491528 | tf_op jit(solution)/shard_map/ppermute | solution.py:10
  14.1 14.5 %collective-permute-start.1 = (bf16[128,640]{1,0:T(8,128)(2,1)S(1)}, bf16[128,640]{1,0:T(8,128)(2,1)S(1)}, u32[]{:S(2)}, u32[]{:S(2)}) collective-permute-start(bf16[128,640]{1,0:T(8,128)(2,1)S(1)} %multiply_convert_fusion.1), channel_id=1, source_target_pairs={{0,4},{1,5},{2,6},{3,7},{4,8},{5,9},{6,10},{7,11},{8,12},{9,13},{1... | collective-permute-start | bytes 491528 | tf_op jit(solution)/shard_map/ppermute | solution.py:10
  17.5 11.4 %collective-permute-start.2 = (bf16[128,640]{1,0:T(8,128)(2,1)S(1)}, bf16[128,640]{1,0:T(8,128)(2,1)S(1)}, u32[]{:S(2)}, u32[]{:S(2)}) collective-permute-start(bf16[128,640]{1,0:T(8,128)(2,1)S(1)} %multiply_convert_fusion.1), channel_id=1, source_target_pairs={{4,0},{5,1},{6,2},{7,3},{8,4},{9,5},{10,6},{11,7},{12,8},{13,9},{1... | collective-permute-start | bytes 491528 | tf_op jit(solution)/shard_map/ppermute | solution.py:10
  18.8 19.5 %collective-permute-start.3 = (bf16[128,640]{1,0:T(8,128)(2,1)S(1)}, bf16[128,640]{1,0:T(8,128)(2,1)S(1)}, u32[]{:S(2)}, u32[]{:S(2)}) collective-permute-start(bf16[128,640]{1,0:T(8,128)(2,1)S(1)} %multiply_convert_fusion.1), channel_id=1, source_target_pairs={{8,0},{9,1},{10,2},{11,3},{12,4},{13,5},{14,6},{15,7},{16,8},{17,9... | collective-permute-start | bytes 491528 | tf_op jit(solution)/shard_map/ppermute | solution.py:10
  38.3 1.2 copy-start.5
  38.3 1.2 copy-start.7
  38.3 1.2 copy-start.9
  39.2 1.2 copy-start.8
  39.3 40.0 %copy-start.6 = (bf16[128,1280]{1,0:T(8,128)(2,1)S(1)}, bf16[128,1280]{1,0:T(8,128)(2,1)}, u32[]{:S(2)}) copy-start(bf16[128,1280]{1,0:T(8,128)(2,1)} %param.11) | copy-start | bytes 983044
  41.7 1.3 collective-permute-start.12
  43.6 3.7 %collective-permute-start.13 = (f32[8,128]{1,0:T(8,128)S(1)}, f32[8,128]{1,0:T(8,128)S(1)}, u32[]{:S(2)}, u32[]{:S(2)}) collective-permute-start(f32[8,128]{1,0:T(8,128)S(1)} %broadcast_add_fusion), channel_id=1, source_target_pairs={{0,2},{1,3},{2,0},{3,1},{4,6},{5,7},{6,4},{7,5},{8,10},{9,11},{10,... | collective-permute-start | bytes 12296 | tf_op jit(solution)/shard_map/ppermute | solution.py:15
  47.9 4.0 %collective-permute-start.14 = (f32[8,128]{1,0:T(8,128)S(1)}, f32[8,128]{1,0:T(8,128)S(1)}, u32[]{:S(2)}, u32[]{:S(2)}) collective-permute-start(f32[8,128]{1,0:T(8,128)S(1)} %fusion.72), channel_id=1, source_target_pairs={{0,16},{1,17},{2,18},{3,19},{4,20},{5,21},{6,22},{7,23},{8,24},{9,... | collective-permute-start | bytes 12296 | tf_op jit(solution)/shard_map/ppermute | solution.py:15
  52.0 3.6 %collective-permute-start.15 = (f32[8,128]{1,0:T(8,128)S(1)}, f32[8,128]{1,0:T(8,128)S(1)}, u32[]{:S(2)}, u32[]{:S(2)}) collective-permute-start(f32[8,128]{1,0:T(8,128)S(1)} %add.156), channel_id=1, source_target_pairs={{0,64},{1,65},{2,66},{3,67},{4,68},{5,69},{6,70},{7,71},{8,72},{9,... | collective-permute-start | bytes 12296 | tf_op jit(solution)/shard_map/ppermute | solution.py:15
  55.6 4.5 %collective-permute-start.16 = (f32[8,128]{1,0:T(8,128)S(1)}, f32[8,128]{1,0:T(8,128)S(1)}, u32[]{:S(2)}, u32[]{:S(2)}) collective-permute-start(f32[8,128]{1,0:T(8,128)S(1)} %add.157), channel_id=1, source_target_pairs={{0,4},{1,5},{2,6},{3,7},{4,0},{5,1},{6,2},{7,3},{8,12},{9,13},{10,... | collective-permute-start | bytes 12296 | tf_op jit(solution)/shard_map/ppermute | solution.py:15
  60.1 5.1 %collective-permute-start.17 = (f32[8,128]{1,0:T(8,128)S(1)}, f32[8,128]{1,0:T(8,128)S(1)}, u32[]{:S(2)}, u32[]{:S(2)}) collective-permute-start(f32[8,128]{1,0:T(8,128)S(1)} %add.158), channel_id=1, source_target_pairs={{0,32},{1,33},{2,34},{3,35},{4,36},{5,37},{6,38},{7,39},{8,40},{9,... | collective-permute-start | bytes 12296 | tf_op jit(solution)/shard_map/ppermute | solution.py:15
  65.3 5.2 %collective-permute-start.18 = (f32[8,128]{1,0:T(8,128)S(1)}, f32[8,128]{1,0:T(8,128)S(1)}, u32[]{:S(2)}, u32[]{:S(2)}) collective-permute-start(f32[8,128]{1,0:T(8,128)S(1)} %add.159), channel_id=1, source_target_pairs={{0,128},{1,129},{2,130},{3,131},{4,132},{5,133},{6,134},{7,135},{8... | collective-permute-start | bytes 12296 | tf_op jit(solution)/shard_map/ppermute | solution.py:15
  70.5 7.5 %collective-permute-start.19 = (f32[8,128]{1,0:T(8,128)S(1)}, f32[8,128]{1,0:T(8,128)S(1)}, u32[]{:S(2)}, u32[]{:S(2)}) collective-permute-start(f32[8,128]{1,0:T(8,128)S(1)} %add.160), channel_id=1, source_target_pairs={{0,8},{1,9},{2,10},{3,11},{4,12},{5,13},{6,14},{7,15},{8,0},{9,1},... | collective-permute-start | bytes 12296 | tf_op jit(solution)/shard_map/ppermute | solution.py:15
  80.8 24.0 %collective-permute-start.20 = (bf16[128,640]{1,0:T(8,128)(2,1)S(1)}, bf16[128,640]{1,0:T(8,128)(2,1)}, u32[]{:S(2)}, u32[]{:S(2)}) collective-permute-start(bf16[128,640]{1,0:T(8,128)(2,1)S(1)} %add_convert_fusion.1), channel_id=1, source_target_pairs={{8,0},{9,1},{10,2},{11,3},{12,4},{13,5},{14,6},{15,7},{16,8},{17,9... | collective-permute-start | bytes 491528 | tf_op jit(solution)/shard_map/ppermute | solution.py:10
  82.1 23.6 %collective-permute-start.21 = (bf16[128,640]{1,0:T(8,128)(2,1)S(1)}, bf16[128,640]{1,0:T(8,128)(2,1)}, u32[]{:S(2)}, u32[]{:S(2)}) collective-permute-start(bf16[128,640]{1,0:T(8,128)(2,1)S(1)} %add_convert_fusion.1), channel_id=1, source_target_pairs={{4,0},{5,1},{6,2},{7,3},{8,4},{9,5},{10,6},{11,7},{12,8},{13,9},{1... | collective-permute-start | bytes 491528 | tf_op jit(solution)/shard_map/ppermute | solution.py:10
  83.4 23.3 %collective-permute-start.22 = (bf16[128,640]{1,0:T(8,128)(2,1)S(1)}, bf16[128,640]{1,0:T(8,128)(2,1)S(1)}, u32[]{:S(2)}, u32[]{:S(2)}) collective-permute-start(bf16[128,640]{1,0:T(8,128)(2,1)S(1)} %add_convert_fusion.1), channel_id=1, source_target_pairs={{0,4},{1,5},{2,6},{3,7},{4,8},{5,9},{6,10},{7,11},{8,12},{9,13},{1... | collective-permute-start | bytes 491528 | tf_op jit(solution)/shard_map/ppermute | solution.py:10
  88.9 17.9 %collective-permute-start.23 = (bf16[128,640]{1,0:T(8,128)(2,1)S(1)}, bf16[128,640]{1,0:T(8,128)(2,1)S(1)}, u32[]{:S(2)}, u32[]{:S(2)}) collective-permute-start(bf16[128,640]{1,0:T(8,128)(2,1)S(1)} %add_convert_fusion.1), channel_id=1, source_target_pairs={{0,8},{1,9},{2,10},{3,11},{4,12},{5,13},{6,14},{7,15},{8,16},{9,17... | collective-permute-start | bytes 491528 | tf_op jit(solution)/shard_map/ppermute | solution.py:10
  125.6 3.7 %collective-permute-start.24 = (bf16[2,2,2,2,2,2,2,10,640]{8,6,7,5,4,3,2,1,0:T(2,128)(2,1)}, bf16[2,2,2,2,2,2,2,10,640]{8,6,7,5,4,3,2,1,0:T(2,128)(2,1)S(1)}, u32[]{:S(2)}, u32[]{:S(2)}) collective-permute-start(bf16[2,2,2,2,2,2,2,10,640]{8,6,7,5,4,3,2,1,0:T(2,128)(2,1)} %copy.37), channel_id=1, source_target_pairs={{0,1},{1,0},{2,3},{3,2},{4,5},{5,4},{6,7},{7,6},{8,9},{9,8},{10,11... | collective-permute-start | bytes 4915208 | tf_op jit(solution)/shard_map/ppermute | solution.py:15
  134.3 2.3 copy-start.1
  136.6 20.5 %collective-permute-start.25 = (bf16[2,2,2,2,2,2,10,640]{7,5,6,4,3,2,1,0:T(2,128)(2,1)S(1)}, bf16[2,2,2,2,2,2,10,640]{7,5,6,4,3,2,1,0:T(2,128)(2,1)S(1)}, u32[]{:S(2)}, u32[]{:S(2)}) collective-permute-start(bf16[2,2,2,2,2,2,10,640]{7,5,6,4,3,2,1,0:T(2,128)(2,1)S(1)} %copy.39), channel_id=1, source_target_pairs={{0,2},{1,3},{2,0},{3,1},{4,6},{5,7},{6,4},{7,5},{8,10},{9,11},{10,... | collective-permute-start | bytes 2457608 | tf_op jit(solution)/shard_map/ppermute | solution.py:15
  160.3 1.5 copy-start.2
  162.2 11.7 %collective-permute-start.26 = (bf16[2,2,2,2,2,10,640]{6,4,5,3,2,1,0:T(2,128)(2,1)S(1)}, bf16[2,2,2,2,2,10,640]{6,4,5,3,2,1,0:T(2,128)(2,1)S(1)}, u32[]{:S(2)}, u32[]{:S(2)}) collective-permute-start(bf16[2,2,2,2,2,10,640]{6,4,5,3,2,1,0:T(2,128)(2,1)S(1)} %copy.41), channel_id=1, source_target_pairs={{0,16},{1,17},{2,18},{3,19},{4,20},{5,21},{6,22},{7,23},{8,24},{9,... | collective-permute-start | bytes 1228808 | tf_op jit(solution)/shard_map/ppermute | solution.py:15
  176.6 13.9 %collective-permute-start.27 = (bf16[2,2,2,2,10,640]{5,4,3,2,1,0:T(8,128)(2,1)}, bf16[2,2,2,2,10,640]{5,4,3,2,1,0:T(8,128)(2,1)S(1)}, u32[]{:S(2)}, u32[]{:S(2)}) collective-permute-start(bf16[2,2,2,2,10,640]{5,4,3,2,1,0:T(8,128)(2,1)} %fusion.34), channel_id=1, source_target_pairs={{0,64},{1,65},{2,66},{3,67},{4,68},{5,69},{6,70},{7,71},{8,72},{9,... | collective-permute-start | bytes 614408 | tf_op jit(solution)/shard_map/ppermute | solution.py:15
  190.7 0.8 copy-start.4
  191.5 6.4 %collective-permute-start.28 = (bf16[2,2,2,10,640]{4,3,2,1,0:T(8,128)(2,1)S(1)}, bf16[2,2,2,10,640]{4,3,2,1,0:T(8,128)(2,1)S(1)}, u32[]{:S(2)}, u32[]{:S(2)}) collective-permute-start(bf16[2,2,2,10,640]{4,3,2,1,0:T(8,128)(2,1)S(1)} %fusion.38), channel_id=1, source_target_pairs={{0,4},{1,5},{2,6},{3,7},{4,0},{5,1},{6,2},{7,3},{8,12},{9,13},{10,... | collective-permute-start | bytes 307208 | tf_op jit(solution)/shard_map/ppermute | solution.py:15
  193.4 7.4 %collective-permute-start.4 = (f32[8,128]{1,0:T(8,128)S(1)}, f32[8,128]{1,0:T(8,128)S(1)}, u32[]{:S(2)}, u32[]{:S(2)}) collective-permute-start(f32[8,128]{1,0:T(8,128)S(1)} %broadcast_in_dim.12), channel_id=1, source_target_pairs={{0,1},{1,0},{2,3},{3,2},{4,5},{5,4},{6,7},{7,6},{8,9},{9,8},{10,11... | collective-permute-start | bytes 12296 | tf_op jit(solution)/shard_map/ppermute | solution.py:15
  199.1 6.0 %collective-permute-start.29 = (bf16[2,2,10,640]{3,2,1,0:T(8,128)(2,1)S(1)}, bf16[2,2,10,640]{3,2,1,0:T(8,128)(2,1)S(1)}, u32[]{:S(2)}, u32[]{:S(2)}) collective-permute-start(bf16[2,2,10,640]{3,2,1,0:T(8,128)(2,1)S(1)} %fusion.42), channel_id=1, source_target_pairs={{0,32},{1,33},{2,34},{3,35},{4,36},{5,37},{6,38},{7,39},{8,40},{9,... | collective-permute-start | bytes 153608 | tf_op jit(solution)/shard_map/ppermute | solution.py:15
  201.4 7.2 %collective-permute-start.5 = (f32[8,128]{1,0:T(8,128)S(1)}, f32[8,128]{1,0:T(8,128)S(1)}, u32[]{:S(2)}, u32[]{:S(2)}) collective-permute-start(f32[8,128]{1,0:T(8,128)S(1)} %broadcast_add_fusion.1), channel_id=1, source_target_pairs={{0,2},{1,3},{2,0},{3,1},{4,6},{5,7},{6,4},{7,5},{8,10},{9,11},{10,... | collective-permute-start | bytes 12296 | tf_op jit(solution)/shard_map/ppermute | solution.py:15
  205.2 14.5 %collective-permute-start.30 = (bf16[2,10,640]{2,1,0:T(8,128)(2,1)S(1)}, bf16[2,10,640]{2,1,0:T(8,128)(2,1)S(1)}, u32[]{:S(2)}, u32[]{:S(2)}) collective-permute-start(bf16[2,10,640]{2,1,0:T(8,128)(2,1)S(1)} %fusion.43), channel_id=1, source_target_pairs={{0,128},{1,129},{2,130},{3,131},{4,132},{5,133},{6,134},{7,135},{8... | collective-permute-start | bytes 76808 | tf_op jit(solution)/shard_map/ppermute | solution.py:15
  209.3 3.7 %collective-permute-start.6 = (f32[8,128]{1,0:T(8,128)S(1)}, f32[8,128]{1,0:T(8,128)S(1)}, u32[]{:S(2)}, u32[]{:S(2)}) collective-permute-start(f32[8,128]{1,0:T(8,128)S(1)} %fusion.73), channel_id=1, source_target_pairs={{0,16},{1,17},{2,18},{3,19},{4,20},{5,21},{6,22},{7,23},{8,24},{9,... | collective-permute-start | bytes 12296 | tf_op jit(solution)/shard_map/ppermute | solution.py:15
  213.0 3.6 %collective-permute-start.7 = (f32[8,128]{1,0:T(8,128)S(1)}, f32[8,128]{1,0:T(8,128)S(1)}, u32[]{:S(2)}, u32[]{:S(2)}) collective-permute-start(f32[8,128]{1,0:T(8,128)S(1)} %add.148), channel_id=1, source_target_pairs={{0,64},{1,65},{2,66},{3,67},{4,68},{5,69},{6,70},{7,71},{8,72},{9,... | collective-permute-start | bytes 12296 | tf_op jit(solution)/shard_map/ppermute | solution.py:15
  216.6 6.1 %collective-permute-start.8 = (f32[8,128]{1,0:T(8,128)S(1)}, f32[8,128]{1,0:T(8,128)S(1)}, u32[]{:S(2)}, u32[]{:S(2)}) collective-permute-start(f32[8,128]{1,0:T(8,128)S(1)} %add.149), channel_id=1, source_target_pairs={{0,4},{1,5},{2,6},{3,7},{4,0},{5,1},{6,2},{7,3},{8,12},{9,13},{10,... | collective-permute-start | bytes 12296 | tf_op jit(solution)/shard_map/ppermute | solution.py:15
  219.8 22.6 %collective-permute-start.31 = (bf16[10,640]{1,0:T(8,128)(2,1)S(1)}, bf16[10,640]{1,0:T(8,128)(2,1)S(1)}, u32[]{:S(2)}, u32[]{:S(2)}) collective-permute-start(bf16[10,640]{1,0:T(8,128)(2,1)S(1)} %fusion.45), channel_id=1, source_target_pairs={{0,8},{1,9},{2,10},{3,11},{4,12},{5,13},{6,14},{7,15},{8,0},{9,1},... | collective-permute-start | bytes 38408 | tf_op jit(solution)/shard_map/ppermute | solution.py:15
  222.7 5.1 %collective-permute-start.9 = (f32[8,128]{1,0:T(8,128)S(1)}, f32[8,128]{1,0:T(8,128)S(1)}, u32[]{:S(2)}, u32[]{:S(2)}) collective-permute-start(f32[8,128]{1,0:T(8,128)S(1)} %add.150), channel_id=1, source_target_pairs={{0,32},{1,33},{2,34},{3,35},{4,36},{5,37},{6,38},{7,39},{8,40},{9,... | collective-permute-start | bytes 12296 | tf_op jit(solution)/shard_map/ppermute | solution.py:15
  227.8 5.1 %collective-permute-start.10 = (f32[8,128]{1,0:T(8,128)S(1)}, f32[8,128]{1,0:T(8,128)S(1)}, u32[]{:S(2)}, u32[]{:S(2)}) collective-permute-start(f32[8,128]{1,0:T(8,128)S(1)} %add.151), channel_id=1, source_target_pairs={{0,128},{1,129},{2,130},{3,131},{4,132},{5,133},{6,134},{7,135},{8... | collective-permute-start | bytes 12296 | tf_op jit(solution)/shard_map/ppermute | solution.py:15
  233.0 7.5 %collective-permute-start.11 = (f32[8,128]{1,0:T(8,128)S(1)}, f32[8,128]{1,0:T(8,128)S(1)}, u32[]{:S(2)}, u32[]{:S(2)}) collective-permute-start(f32[8,128]{1,0:T(8,128)S(1)} %add.152), channel_id=1, source_target_pairs={{0,8},{1,9},{2,10},{3,11},{4,12},{5,13},{6,14},{7,15},{8,0},{9,1},... | collective-permute-start | bytes 12296 | tf_op jit(solution)/shard_map/ppermute | solution.py:15

commit v4 on v3

--- a/solution.py
+++ b/solution.py
@@ -27,24 +27,43 @@
     return values
 
 
-def tree_scatter(partial, extra, axis):
+def count_sum(counts, axis):
+    order = link_order(lax.axis_size(axis))
+    for first, second in zip(order[0::2], order[1::2]):
+        counts = (
+            counts
+            + swap_with(counts, axis, first)
+            + swap_with(counts, axis, second)
+            + swap_with(counts, axis, first ^ second)
+        )
+    return counts
+
+
+def tree_layout(columns, axis):
     devices = lax.axis_size(axis)
     depth = devices.bit_length() - 1
+    rows, width = columns.shape
+    split = columns.reshape((rows,) + (2,) * depth + (width // devices,))
+    axes = [1 + depth - 1 - (bit.bit_length() - 1) for bit in link_order(devices)]
+    return split.transpose([0] + axes + [depth + 1]).reshape(rows, width)
+
+
+def tree_scatter(partials, extra, axis):
+    devices = lax.axis_size(axis)
     me = lax.axis_index(axis)
-    blocks = partial.reshape((2,) * depth + partial.shape[1:])
-    dim_bits = [1 << (depth - 1 - d) for d in range(depth)]
+    blocks = [p.reshape(devices, p.shape[0] // devices, -1) for p in partials]
     for bit in link_order(devices):
-        at = dim_bits.index(bit)
-        upper = (me & bit) != 0
-        low = lax.index_in_dim(blocks, 0, at, keepdims=False)
-        high = lax.index_in_dim(blocks, 1, at, keepdims=False)
-        keep = jnp.where(upper, high, low)
-        send = jnp.where(upper, low, high).astype(jnp.bfloat16)
+        half = blocks[0].shape[0] // 2
+        upper = (me // bit) % 2
+        keep = [lax.dynamic_slice_in_dim(b, upper * half, half, 0) for b in blocks]
+        send = [
+            lax.dynamic_slice_in_dim(b, (1 - upper) * half, half, 0).astype(jnp.bfloat16)
+            for b in blocks
+        ]
         got, got_extra = swap_with((send, extra), axis, bit)
-        blocks = keep + got.astype(jnp.float32)
+        blocks = [k + g.astype(jnp.float32) for k, g in zip(keep, got)]
         extra = extra + got_extra
-        dim_bits.pop(at)
-    return blocks, extra
+    return [b[0] for b in blocks], extra
 
 
 def norm_gelu(values):
@@ -71,7 +90,7 @@
     context_rows = float(local_rows * seq_devices)
     masked = mask_flags.astype(jnp.float32)
     local_count = jnp.sum(masked)
-    mask_total = tree_sum(jnp.broadcast_to(local_count, (8, 128)), "seq")[0, 0]
+    mask_total = count_sum(jnp.broadcast_to(local_count, (8, 128)), "seq")[0, 0]
     alphabet = jnp.arange(vocab_size, dtype=jnp.int32)
     first_act = norm_gelu(hidden_in.astype(jnp.float32)).astype(jnp.bfloat16)
     first_pre = jnp.dot(first_act, w_in, preferred_element_type=jnp.float32)
@@ -100,7 +119,7 @@
         grad_logits, head_weight, (((0,), (1,)), ((), ())), preferred_element_type=jnp.float32
     )
     grad_block = (head_part + grad_above.astype(jnp.float32)).astype(jnp.bfloat16)
-    columns = grad_block
+    columns = tree_layout(grad_block, "seq")
     down_partial = lax.dot_general(
         columns, conv_act, (((0,), (0,)), ((), ())), preferred_element_type=jnp.float32
     )
@@ -114,21 +133,15 @@
         "krc,kbc->rb", backward_tap_pile, conv_weight, preferred_element_type=jnp.float32
     )
     grad_first = jax.vjp(norm_gelu, first_pre)[1](grad_neck)[0].astype(jnp.bfloat16)
-    columns = first_act
+    columns = tree_layout(first_act, "seq")
     up_partial = lax.dot_general(
         columns, grad_first, (((0,), (0,)), ((), ())), preferred_element_type=jnp.float32
     )
-    share = up_partial.shape[0] // seq_devices
-    both = jnp.concatenate(
-        [
-            down_partial.reshape(seq_devices, share, -1),
-            up_partial.reshape(seq_devices, share, -1),
-        ],
-        1,
+    (grad_down, grad_up), loss_tile = tree_scatter(
+        (down_partial, up_partial), jnp.broadcast_to(local_loss, (8, 128)), "seq"
     )
-    mine, loss_tile = tree_scatter(both, jnp.broadcast_to(local_loss, (8, 128)), "seq")
-    grad_down = mine[:share].astype(jnp.bfloat16)
-    grad_up = mine[share:].astype(jnp.bfloat16)
+    grad_down = grad_down.astype(jnp.bfloat16)
+    grad_up = grad_up.astype(jnp.bfloat16)
     loss_total = loss_tile[0, 0]
     return (loss_total / mask_total, grad_up, grad_down)
 

time: 245 us -> 217 us (0.89)
  waiting for transfers between devices: 95.5 us -> 80.5 us
  other arithmetic: 24.9 us -> 14.6 us
  starting transfers between devices: 83.7 us -> 89.5 us
  matrix products: 13.9 us -> 8.74 us
  local copies, waits for them, and re-layouts: 21.7 us -> 17.8 us
    ppermute x24 -> x36, waiting for transfers between devices: 77.6 us -> 62.6 us  [swap_with(): return lax.ppermute(block, axis, [(i, i ^ bit) for i in range(devices)])]
    concatenate x2 -> x0, local copies, waits for them, and re-layouts: 9.64 us -> none  [shards(): jnp.concatenate([down_partial.reshape(seq_devices, share, -1), up_partial...]
    add x15 -> x18, other arithmetic: 12.6 us -> 6.38 us  [the longest x14 5.72 us: tree_scatter(): blocks = [k + g.astype(jnp.float32) for k, g in zip(keep, got)]]
    ppermute x24 -> x36, starting transfers between devices: 52.9 us -> 58 us  [swap_with(): return lax.ppermute(block, axis, [(i, i ^ bit) for i in range(devices)])]
    convert_element_type x8 -> x3, other arithmetic: 6.14 us -> 1.44 us  [the longest x1 1.39 us: shards(): first_act = norm_gelu(hidden_in.astype(jnp.float32)).astype(jnp.bfloat16)]
    unnamed x26 -> x32, local copies, waits for them, and re-layouts: 5.71 us -> 8.4 us
  transfers between devices with their start and end apart: 32 -> 44, of which waited for: 21 -> 28; matrix products, arithmetic and copies ran while one was open for 5% -> 10% of each run, Pallas kernels for 0% -> 0%
where the time goes in v4:
time: 217 us; the launch traced here: 216 us
  starting transfers between devices  89.5 us (41%)
  waiting for transfers between devices  80.5 us (37%)
  local copies, waits for them, and re-layouts  17.8 us (8%)
  other arithmetic  14.6 us (7%)
  matrix products  8.74 us (4%)
  between operations  4.54 us (2%)
    ppermute x36, waiting for transfers between devices, swap_with(): return lax.ppermute(block, axis, [(i, i ^ bit) for i in range(devices)])  62.6 us
    ppermute x36, starting transfers between devices, swap_with(): return lax.ppermute(block, axis, [(i, i ^ bit) for i in range(devices)])  58 us
    ppermute x8, starting transfers between devices, from_behind(): return lax.ppermute(block, axis, route)  31.5 us
    ppermute x8, waiting for transfers between devices, from_behind(): return lax.ppermute(block, axis, route)  17.9 us
    unnamed x32, local copies, waits for them, and re-layouts  8.4 us
    add x14, other arithmetic, tree_scatter(): blocks = [k + g.astype(jnp.float32) for k, g in zip(keep, got)]  5.72 us
  transfers between devices with their start and end apart: 44, of which 28 were waited for; matrix products, arithmetic and copies ran while one was open for 10% of the time, Pallas kernels for 0%

profile of v4, /device:TPU:32, one launch (start us, length us, event | category | flops | bytes accessed | tf_op | source)
XLA Modules:
  0.0 215.7 jit_solution(8327115290457185338)
XLA Ops:
  3.1 1.4 fusion.9
  4.5 2.1 fusion.44
  7.0 8.2 %collective-permute-start = (bf16[128,640]{1,0:T(8,128)(2,1)S(1)}, bf16[128,640]{1,0:T(8,128)(2,1)S(1)}, u32[]{:S(2)}, u32[]{:S(2)}) collective-permute-start(bf16[128,640]{1,0:T(8,128)(2,1)S(1)} %multiply_convert_fusion.1), channel_id=1, source_target_pairs={{0,8},{1,9},{2,10},{3,11},{4,12},{5,13},{6,14},{7,15},{8,16},{9,17... | collective-permute-start | bytes 491528 | tf_op jit(solution)/shard_map/ppermute | solution.py:10
  15.2 3.4 %collective-permute-start.1 = (bf16[128,640]{1,0:T(8,128)(2,1)S(1)}, bf16[128,640]{1,0:T(8,128)(2,1)S(1)}, u32[]{:S(2)}, u32[]{:S(2)}) collective-permute-start(bf16[128,640]{1,0:T(8,128)(2,1)S(1)} %multiply_convert_fusion.1), channel_id=1, source_target_pairs={{0,4},{1,5},{2,6},{3,7},{4,8},{5,9},{6,10},{7,11},{8,12},{9,13},{1... | collective-permute-start | bytes 491528 | tf_op jit(solution)/shard_map/ppermute | solution.py:10
  18.6 1.3 collective-permute-start.2
  21.3 8.5 %collective-permute-done.1 = bf16[128,640]{1,0:T(8,128)(2,1)S(1)} collective-permute-done((bf16[128,640]{1,0:T(8,128)(2,1)S(1)}, bf16[128,640]{1,0:T(8,128)(2,1)S(1)}, u32[]{:S(2)}, u32[]{:S(2)}) %collective-permute-start.1) | collective-permute-done | bytes 163872 | tf_op jit(solution)/shard_map/ppermute | solution.py:10
  30.0 9.4 %collective-permute-done.3 = bf16[128,640]{1,0:T(8,128)(2,1)S(1)} collective-permute-done((bf16[128,640]{1,0:T(8,128)(2,1)S(1)}, bf16[128,640]{1,0:T(8,128)(2,1)S(1)}, u32[]{:S(2)}, u32[]{:S(2)}) %collective-permute-start.3) | collective-permute-done | bytes 163872 | tf_op jit(solution)/shard_map/ppermute | solution.py:10
  42.9 1.5 collective-permute-start.13
  47.3 5.0 %collective-permute-start.17 = (f32[8,128]{1,0:T(8,128)S(1)}, f32[8,128]{1,0:T(8,128)S(1)}, u32[]{:S(2)}, u32[]{:S(2)}) collective-permute-start(f32[8,128]{1,0:T(8,128)S(1)} %add_add_fusion.5), channel_id=1, source_target_pairs={{0,80},{1,81},{2,82},{3,83},{4,84},{5,85},{6,86},{7,87},{8,88},{9,... | collective-permute-start | bytes 12296 | tf_op jit(solution)/shard_map/ppermute | solution.py:15
  53.9 2.0 collective-permute-done.16
  56.4 2.7 %collective-permute-start.19 = (f32[8,128]{1,0:T(8,128)S(1)}, f32[8,128]{1,0:T(8,128)S(1)}, u32[]{:S(2)}, u32[]{:S(2)}) collective-permute-start(f32[8,128]{1,0:T(8,128)S(1)} %add_add_fusion.4), channel_id=1, source_target_pairs={{0,32},{1,33},{2,34},{3,35},{4,36},{5,37},{6,38},{7,39},{8,40},{9,... | collective-permute-start | bytes 12296 | tf_op jit(solution)/shard_map/ppermute | solution.py:15
  59.1 3.2 %collective-permute-start.18 = (f32[8,128]{1,0:T(8,128)S(1)}, f32[8,128]{1,0:T(8,128)S(1)}, u32[]{:S(2)}, u32[]{:S(2)}) collective-permute-start(f32[8,128]{1,0:T(8,128)S(1)} %add_add_fusion.4), channel_id=1, source_target_pairs={{0,4},{1,5},{2,6},{3,7},{4,0},{5,1},{6,2},{7,3},{8,12},{9,13},{10,... | collective-permute-start | bytes 12296 | tf_op jit(solution)/shard_map/ppermute | solution.py:15
  63.8 7.0 %collective-permute-start.23 = (f32[8,128]{1,0:T(8,128)S(1)}, f32[8,128]{1,0:T(8,128)S(1)}, u32[]{:S(2)}, u32[]{:S(2)}) collective-permute-start(f32[8,128]{1,0:T(8,128)S(1)} %add_add_fusion.3), channel_id=1, source_target_pairs={{0,136},{1,137},{2,138},{3,139},{4,140},{5,141},{6,142},{7,143},{8... | collective-permute-start | bytes 12296 | tf_op jit(solution)/shard_map/ppermute | solution.py:15
  70.8 1.6 collective-permute-start.22
  74.3 4.0 %collective-permute-done.22 = f32[8,128]{1,0:T(8,128)S(1)} collective-permute-done((f32[8,128]{1,0:T(8,128)S(1)}, f32[8,128]{1,0:T(8,128)S(1)}, u32[]{:S(2)}, u32[]{:S(2)}) %collective-permute-start.22) | collective-permute-done | bytes 4128 | tf_op jit(solution)/shard_map/ppermute | solution.py:15
  85.4 6.3 %collective-permute-start.26 = (bf16[128,640]{1,0:T(8,128)(2,1)}, bf16[128,640]{1,0:T(8,128)(2,1)}, u32[]{:S(2)}, u32[]{:S(2)}) collective-permute-start(bf16[128,640]{1,0:T(8,128)(2,1)} %add_convert_fusion.1), channel_id=1, source_target_pairs={{0,4},{1,5},{2,6},{3,7},{4,8},{5,9},{6,10},{7,11},{8,12},{9,13},{1... | collective-permute-start | bytes 491528 | tf_op jit(solution)/shard_map/ppermute | solution.py:10
  91.7 8.5 %collective-permute-start.27 = (bf16[128,640]{1,0:T(8,128)(2,1)}, bf16[128,640]{1,0:T(8,128)(2,1)}, u32[]{:S(2)}, u32[]{:S(2)}) collective-permute-start(bf16[128,640]{1,0:T(8,128)(2,1)} %add_convert_fusion.1), channel_id=1, source_target_pairs={{0,8},{1,9},{2,10},{3,11},{4,12},{5,13},{6,14},{7,15},{8,16},{9,17... | collective-permute-start | bytes 491528 | tf_op jit(solution)/shard_map/ppermute | solution.py:10
  103.5 1.7 copy-done.3
  109.3 1.5 multiply_reduce_fusion
  111.7 1.7 copy-done.4
  115.0 2.0 convert_add_fusion
  117.0 2.1 collective-permute-start.37
  119.9 1.4 convert_add_fusion.1
  122.1 2.0 collective-permute-start.29
  124.1 5.4 %collective-permute-done.37 = bf16[64,5,640]{2,0,1:T(8,128)(2,1)S(1)} collective-permute-done((bf16[64,5,640]{2,0,1:T(8,128)(2,1)S(1)}, bf16[64,5,640]{2,0,1:T(8,128)(2,1)S(1)}, u32[]{:S(2)}, u32[]{:S(2)}) %collective-permute-start.37) | collective-permute-done | bytes 409632 | tf_op jit(solution)/shard_map/ppermute | solution.py:15
  131.1 6.2 %collective-permute-start.38 = (bf16[32,5,640]{2,0,1:T(8,128)(2,1)}, bf16[32,5,640]{2,0,1:T(8,128)(2,1)S(1)}, u32[]{:S(2)}, u32[]{:S(2)}) collective-permute-start(bf16[32,5,640]{2,0,1:T(8,128)(2,1)} %dynamic-slice_convert_fusion.4), channel_id=1, source_target_pairs={{0,16},{1,17},{2,18},{3,19},{4,20},{5,21},{6,22},{7,23},{8,24},{9,... | collective-permute-start | bytes 614408 | tf_op jit(solution)/shard_map/ppermute | solution.py:15
  138.1 3.6 %collective-permute-done.6 = f32[8,128]{1,0:T(8,128)S(1)} collective-permute-done((f32[8,128]{1,0:T(8,128)S(1)}, f32[8,128]{1,0:T(8,128)S(1)}, u32[]{:S(2)}, u32[]{:S(2)}) %collective-permute-start.6) | collective-permute-done | bytes 4128 | tf_op jit(solution)/shard_map/ppermute | solution.py:15
  141.7 4.6 %collective-permute-start.7 = (f32[8,128]{1,0:T(8,128)S(1)}, f32[8,128]{1,0:T(8,128)S(1)}, u32[]{:S(2)}, u32[]{:S(2)}) collective-permute-start(f32[8,128]{1,0:T(8,128)S(1)} %add.282), channel_id=1, source_target_pairs={{0,64},{1,65},{2,66},{3,67},{4,68},{5,69},{6,70},{7,71},{8,72},{9,... | collective-permute-start | bytes 12296 | tf_op jit(solution)/shard_map/ppermute | solution.py:15
  146.3 1.6 collective-permute-done.7
  147.9 4.5 %collective-permute-done.8 = f32[8,128]{1,0:T(8,128)S(1)} collective-permute-done((f32[8,128]{1,0:T(8,128)S(1)}, f32[8,128]{1,0:T(8,128)S(1)}, u32[]{:S(2)}, u32[]{:S(2)}) %collective-permute-start.8) | collective-permute-done | bytes 4128 | tf_op jit(solution)/shard_map/ppermute | solution.py:15
  152.4 5.1 %collective-permute-done.9 = f32[8,128]{1,0:T(8,128)S(1)} collective-permute-done((f32[8,128]{1,0:T(8,128)S(1)}, f32[8,128]{1,0:T(8,128)S(1)}, u32[]{:S(2)}, u32[]{:S(2)}) %collective-permute-start.9) | collective-permute-done | bytes 4128 | tf_op jit(solution)/shard_map/ppermute | solution.py:15
  157.5 1.7 collective-permute-start.10
  159.2 3.4 %collective-permute-done.10 = f32[8,128]{1,0:T(8,128)S(1)} collective-permute-done((f32[8,128]{1,0:T(8,128)S(1)}, f32[8,128]{1,0:T(8,128)S(1)}, u32[]{:S(2)}, u32[]{:S(2)}) %collective-permute-start.10) | collective-permute-done | bytes 4128 | tf_op jit(solution)/shard_map/ppermute | solution.py:15
  162.6 7.5 %collective-permute-done.11 = f32[8,128]{1,0:T(8,128)S(1)} collective-permute-done((f32[8,128]{1,0:T(8,128)S(1)}, f32[8,128]{1,0:T(8,128)S(1)}, u32[]{:S(2)}, u32[]{:S(2)}) %collective-permute-start.11) | collective-permute-done | bytes 4128 | tf_op jit(solution)/shard_map/ppermute | solution.py:15
  173.1 2.3 %collective-permute-start.39 = (bf16[16,5,640]{2,0,1:T(8,128)(2,1)S(1)}, bf16[16,5,640]{2,0,1:T(8,128)(2,1)S(1)}, u32[]{:S(2)}, u32[]{:S(2)}) collective-permute-start(bf16[16,5,640]{2,0,1:T(8,128)(2,1)S(1)} %dynamic-slice_convert_fusion.6), channel_id=1, source_target_pairs={{0,64},{1,65},{2,66},{3,67},{4,68},{5,69},{6,70},{7,71},{8,72},{9,... | collective-permute-start | bytes 307208 | tf_op jit(solution)/shard_map/ppermute | solution.py:15
  176.5 2.4 %collective-permute-done.39 = bf16[16,5,640]{2,0,1:T(8,128)(2,1)S(1)} collective-permute-done((bf16[16,5,640]{2,0,1:T(8,128)(2,1)S(1)}, bf16[16,5,640]{2,0,1:T(8,128)(2,1)S(1)}, u32[]{:S(2)}, u32[]{:S(2)}) %collective-permute-start.39) | collective-permute-done | bytes 102432 | tf_op jit(solution)/shard_map/ppermute | solution.py:15
  179.6 4.4 %collective-permute-done.40 = bf16[8,5,640]{2,0,1:T(8,128)(2,1)S(1)} collective-permute-done((bf16[8,5,640]{2,0,1:T(8,128)(2,1)S(1)}, bf16[8,5,640]{2,0,1:T(8,128)(2,1)S(1)}, u32[]{:S(2)}, u32[]{:S(2)}) %collective-permute-start.40) | collective-permute-done | bytes 51232 | tf_op jit(solution)/shard_map/ppermute | solution.py:15
  185.0 2.6 %collective-permute-start.31 = (bf16[16,5,640]{2,0,1:T(8,128)(2,1)S(1)}, bf16[16,5,640]{2,0,1:T(8,128)(2,1)S(1)}, u32[]{:S(2)}, u32[]{:S(2)}) collective-permute-start(bf16[16,5,640]{2,0,1:T(8,128)(2,1)S(1)} %dynamic-slice_convert_fusion.7), channel_id=1, source_target_pairs={{0,64},{1,65},{2,66},{3,67},{4,68},{5,69},{6,70},{7,71},{8,72},{9,... | collective-permute-start | bytes 307208 | tf_op jit(solution)/shard_map/ppermute | solution.py:15
  187.6 1.9 collective-permute-done.41
  190.3 3.0 %collective-permute-start.32 = (bf16[8,5,640]{2,0,1:T(8,128)(2,1)S(1)}, bf16[8,5,640]{2,0,1:T(8,128)(2,1)S(1)}, u32[]{:S(2)}, u32[]{:S(2)}) collective-permute-start(bf16[8,5,640]{2,0,1:T(8,128)(2,1)S(1)} %dynamic-slice_convert_fusion.9), channel_id=1, source_target_pairs={{0,4},{1,5},{2,6},{3,7},{4,0},{5,1},{6,2},{7,3},{8,12},{9,13},{10,... | collective-permute-start | bytes 153608 | tf_op jit(solution)/shard_map/ppermute | solution.py:15
  193.3 1.8 collective-permute-start.42
  195.4 2.8 %collective-permute-start.33 = (bf16[4,5,640]{2,0,1:T(4,128)(2,1)S(1)}, bf16[4,5,640]{2,0,1:T(4,128)(2,1)S(1)}, u32[]{:S(2)}, u32[]{:S(2)}) collective-permute-start(bf16[4,5,640]{2,0,1:T(4,128)(2,1)S(1)} %dynamic-slice_convert_fusion.11), channel_id=1, source_target_pairs={{0,32},{1,33},{2,34},{3,35},{4,36},{5,37},{6,38},{7,39},{8,40},{9,... | collective-permute-start | bytes 76808 | tf_op jit(solution)/shard_map/ppermute | solution.py:15
  198.6 2.3 %collective-permute-done.33 = bf16[4,5,640]{2,0,1:T(4,128)(2,1)S(1)} collective-permute-done((bf16[4,5,640]{2,0,1:T(4,128)(2,1)S(1)}, bf16[4,5,640]{2,0,1:T(4,128)(2,1)S(1)}, u32[]{:S(2)}, u32[]{:S(2)}) %collective-permute-start.33) | collective-permute-done | bytes 25632 | tf_op jit(solution)/shard_map/ppermute | solution.py:15
  200.9 1.8 collective-permute-start.34
  203.1 3.1 %collective-permute-done.34 = bf16[2,5,640]{2,0,1:T(2,128)(2,1)S(1)} collective-permute-done((bf16[2,5,640]{2,0,1:T(2,128)(2,1)S(1)}, bf16[2,5,640]{2,0,1:T(2,128)(2,1)S(1)}, u32[]{:S(2)}, u32[]{:S(2)}) %collective-permute-start.34) | collective-permute-done | bytes 12832 | tf_op jit(solution)/shard_map/ppermute | solution.py:15
  206.2 2.6 %collective-permute-start.35 = (bf16[1,5,640]{2,0,1:T(2,128)(2,1)S(1)}, bf16[1,5,640]{2,0,1:T(2,128)(2,1)S(1)}, u32[]{:S(2)}, u32[]{:S(2)}) collective-permute-start(bf16[1,5,640]{2,0,1:T(2,128)(2,1)S(1)} %dynamic-slice_convert_fusion.15), channel_id=1, source_target_pairs={{0,8},{1,9},{2,10},{3,11},{4,12},{5,13},{6,14},{7,15},{8,0},{9,1},... | collective-permute-start | bytes 19208 | tf_op jit(solution)/shard_map/ppermute | solution.py:15
  208.9 1.5 collective-permute-done.43
  211.0 2.9 %collective-permute-done.35 = bf16[1,5,640]{2,0,1:T(2,128)(2,1)S(1)} collective-permute-done((bf16[1,5,640]{2,0,1:T(2,128)(2,1)S(1)}, bf16[1,5,640]{2,0,1:T(2,128)(2,1)S(1)}, u32[]{:S(2)}, u32[]{:S(2)}) %collective-permute-start.35) | collective-permute-done | bytes 6432 | tf_op jit(solution)/shard_map/ppermute | solution.py:15
  (163 shorter events, 43.9 us)
Async XLA Ops:
  0.6 40.0 %copy-start = (bf16[1280,640]{1,0:T(8,128)(2,1)S(1)}, bf16[1280,640]{1,0:T(8,128)(2,1)}, u32[]{:S(2)}) copy-start(bf16[1280,640]{1,0:T(8,128)(2,1)} %param.14) | copy-start | bytes 4915204
  4.5 34.9 %copy-start.1 = (bf16[5,640,640]{2,1,0:T(8,128)(2,1)S(1)}, bf16[5,640,640]{2,1,0:T(8,128)(2,1)}, u32[]{:S(2)}) copy-start(bf16[5,640,640]{2,1,0:T(8,128)(2,1)} %param.13) | copy-start | bytes 12288004
  7.0 14.2 %collective-permute-start = (bf16[128,640]{1,0:T(8,128)(2,1)S(1)}, bf16[128,640]{1,0:T(8,128)(2,1)S(1)}, u32[]{:S(2)}, u32[]{:S(2)}) collective-permute-start(bf16[128,640]{1,0:T(8,128)(2,1)S(1)} %multiply_convert_fusion.1), channel_id=1, source_target_pairs={{0,8},{1,9},{2,10},{3,11},{4,12},{5,13},{6,14},{7,15},{8,16},{9,17... | collective-permute-start | bytes 491528 | tf_op jit(solution)/shard_map/ppermute | solution.py:10
  15.2 14.5 %collective-permute-start.1 = (bf16[128,640]{1,0:T(8,128)(2,1)S(1)}, bf16[128,640]{1,0:T(8,128)(2,1)S(1)}, u32[]{:S(2)}, u32[]{:S(2)}) collective-permute-start(bf16[128,640]{1,0:T(8,128)(2,1)S(1)} %multiply_convert_fusion.1), channel_id=1, source_target_pairs={{0,4},{1,5},{2,6},{3,7},{4,8},{5,9},{6,10},{7,11},{8,12},{9,13},{1... | collective-permute-start | bytes 491528 | tf_op jit(solution)/shard_map/ppermute | solution.py:10
  18.6 11.4 %collective-permute-start.2 = (bf16[128,640]{1,0:T(8,128)(2,1)S(1)}, bf16[128,640]{1,0:T(8,128)(2,1)S(1)}, u32[]{:S(2)}, u32[]{:S(2)}) collective-permute-start(bf16[128,640]{1,0:T(8,128)(2,1)S(1)} %multiply_convert_fusion.1), channel_id=1, source_target_pairs={{4,0},{5,1},{6,2},{7,3},{8,4},{9,5},{10,6},{11,7},{12,8},{13,9},{1... | collective-permute-start | bytes 491528 | tf_op jit(solution)/shard_map/ppermute | solution.py:10
  19.9 19.5 %collective-permute-start.3 = (bf16[128,640]{1,0:T(8,128)(2,1)S(1)}, bf16[128,640]{1,0:T(8,128)(2,1)S(1)}, u32[]{:S(2)}, u32[]{:S(2)}) collective-permute-start(bf16[128,640]{1,0:T(8,128)(2,1)S(1)} %multiply_convert_fusion.1), channel_id=1, source_target_pairs={{8,0},{9,1},{10,2},{11,3},{12,4},{13,5},{14,6},{15,7},{16,8},{17,9... | collective-permute-start | bytes 491528 | tf_op jit(solution)/shard_map/ppermute | solution.py:10
  42.8 3.1 %collective-permute-start.14 = (f32[8,128]{1,0:T(8,128)S(1)}, f32[8,128]{1,0:T(8,128)S(1)}, u32[]{:S(2)}, u32[]{:S(2)}) collective-permute-start(f32[8,128]{1,0:T(8,128)S(1)} %broadcast_in_dim.13), channel_id=1, source_target_pairs={{0,3},{1,2},{2,1},{3,0},{4,7},{5,6},{6,5},{7,4},{8,11},{9,10},{10,... | collective-permute-start | bytes 12296 | tf_op jit(solution)/shard_map/ppermute | solution.py:15
  42.9 3.7 %collective-permute-start.13 = (f32[8,128]{1,0:T(8,128)S(1)}, f32[8,128]{1,0:T(8,128)S(1)}, u32[]{:S(2)}, u32[]{:S(2)}) collective-permute-start(f32[8,128]{1,0:T(8,128)S(1)} %broadcast_in_dim.13), channel_id=1, source_target_pairs={{0,2},{1,3},{2,0},{3,1},{4,6},{5,7},{6,4},{7,5},{8,10},{9,11},{10,... | collective-permute-start | bytes 12296 | tf_op jit(solution)/shard_map/ppermute | solution.py:15
  44.4 2.2 %collective-permute-start.12 = (f32[8,128]{1,0:T(8,128)S(1)}, f32[8,128]{1,0:T(8,128)S(1)}, u32[]{:S(2)}, u32[]{:S(2)}) collective-permute-start(f32[8,128]{1,0:T(8,128)S(1)} %broadcast_in_dim.13), channel_id=1, source_target_pairs={{0,1},{1,0},{2,3},{3,2},{4,5},{5,4},{6,7},{7,6},{8,9},{9,8},{10,11... | collective-permute-start | bytes 12296 | tf_op jit(solution)/shard_map/ppermute | solution.py:15
  47.3 6.6 %collective-permute-start.17 = (f32[8,128]{1,0:T(8,128)S(1)}, f32[8,128]{1,0:T(8,128)S(1)}, u32[]{:S(2)}, u32[]{:S(2)}) collective-permute-start(f32[8,128]{1,0:T(8,128)S(1)} %add_add_fusion.5), channel_id=1, source_target_pairs={{0,80},{1,81},{2,82},{3,83},{4,84},{5,85},{6,86},{7,87},{8,88},{9,... | collective-permute-start | bytes 12296 | tf_op jit(solution)/shard_map/ppermute | solution.py:15
  52.3 3.6 %collective-permute-start.16 = (f32[8,128]{1,0:T(8,128)S(1)}, f32[8,128]{1,0:T(8,128)S(1)}, u32[]{:S(2)}, u32[]{:S(2)}) collective-permute-start(f32[8,128]{1,0:T(8,128)S(1)} %add_add_fusion.5), channel_id=1, source_target_pairs={{0,64},{1,65},{2,66},{3,67},{4,68},{5,69},{6,70},{7,71},{8,72},{9,... | collective-permute-start | bytes 12296 | tf_op jit(solution)/shard_map/ppermute | solution.py:15
  52.7 3.6 %collective-permute-start.15 = (f32[8,128]{1,0:T(8,128)S(1)}, f32[8,128]{1,0:T(8,128)S(1)}, u32[]{:S(2)}, u32[]{:S(2)}) collective-permute-start(f32[8,128]{1,0:T(8,128)S(1)} %add_add_fusion.5), channel_id=1, source_target_pairs={{0,16},{1,17},{2,18},{3,19},{4,20},{5,21},{6,22},{7,23},{8,24},{9,... | collective-permute-start | bytes 12296 | tf_op jit(solution)/shard_map/ppermute | solution.py:15
  56.4 6.9 %collective-permute-start.20 = (f32[8,128]{1,0:T(8,128)S(1)}, f32[8,128]{1,0:T(8,128)S(1)}, u32[]{:S(2)}, u32[]{:S(2)}) collective-permute-start(f32[8,128]{1,0:T(8,128)S(1)} %add_add_fusion.4), channel_id=1, source_target_pairs={{0,36},{1,37},{2,38},{3,39},{4,32},{5,33},{6,34},{7,35},{8,44},{9,... | collective-permute-start | bytes 12296 | tf_op jit(solution)/shard_map/ppermute | solution.py:15
  56.4 6.9 %collective-permute-start.19 = (f32[8,128]{1,0:T(8,128)S(1)}, f32[8,128]{1,0:T(8,128)S(1)}, u32[]{:S(2)}, u32[]{:S(2)}) collective-permute-start(f32[8,128]{1,0:T(8,128)S(1)} %add_add_fusion.4), channel_id=1, source_target_pairs={{0,32},{1,33},{2,34},{3,35},{4,36},{5,37},{6,38},{7,39},{8,40},{9,... | collective-permute-start | bytes 12296 | tf_op jit(solution)/shard_map/ppermute | solution.py:15
  59.1 4.8 %collective-permute-start.18 = (f32[8,128]{1,0:T(8,128)S(1)}, f32[8,128]{1,0:T(8,128)S(1)}, u32[]{:S(2)}, u32[]{:S(2)}) collective-permute-start(f32[8,128]{1,0:T(8,128)S(1)} %add_add_fusion.4), channel_id=1, source_target_pairs={{0,4},{1,5},{2,6},{3,7},{4,0},{5,1},{6,2},{7,3},{8,12},{9,13},{10,... | collective-permute-start | bytes 12296 | tf_op jit(solution)/shard_map/ppermute | solution.py:15
  63.8 10.5 %collective-permute-start.23 = (f32[8,128]{1,0:T(8,128)S(1)}, f32[8,128]{1,0:T(8,128)S(1)}, u32[]{:S(2)}, u32[]{:S(2)}) collective-permute-start(f32[8,128]{1,0:T(8,128)S(1)} %add_add_fusion.3), channel_id=1, source_target_pairs={{0,136},{1,137},{2,138},{3,139},{4,140},{5,141},{6,142},{7,143},{8... | collective-permute-start | bytes 12296 | tf_op jit(solution)/shard_map/ppermute | solution.py:15
  70.8 7.5 %collective-permute-start.22 = (f32[8,128]{1,0:T(8,128)S(1)}, f32[8,128]{1,0:T(8,128)S(1)}, u32[]{:S(2)}, u32[]{:S(2)}) collective-permute-start(f32[8,128]{1,0:T(8,128)S(1)} %add_add_fusion.3), channel_id=1, source_target_pairs={{0,8},{1,9},{2,10},{3,11},{4,12},{5,13},{6,14},{7,15},{8,0},{9,1},... | collective-permute-start | bytes 12296 | tf_op jit(solution)/shard_map/ppermute | solution.py:15
  72.4 6.0 %collective-permute-start.21 = (f32[8,128]{1,0:T(8,128)S(1)}, f32[8,128]{1,0:T(8,128)S(1)}, u32[]{:S(2)}, u32[]{:S(2)}) collective-permute-start(f32[8,128]{1,0:T(8,128)S(1)} %add_add_fusion.3), channel_id=1, source_target_pairs={{0,128},{1,129},{2,130},{3,131},{4,132},{5,133},{6,134},{7,135},{8... | collective-permute-start | bytes 12296 | tf_op jit(solution)/shard_map/ppermute | solution.py:15
  82.8 22.6 %collective-permute-start.24 = (bf16[128,640]{1,0:T(8,128)(2,1)}, bf16[128,640]{1,0:T(8,128)(2,1)}, u32[]{:S(2)}, u32[]{:S(2)}) collective-permute-start(bf16[128,640]{1,0:T(8,128)(2,1)} %add_convert_fusion.1), channel_id=1, source_target_pairs={{8,0},{9,1},{10,2},{11,3},{12,4},{13,5},{14,6},{15,7},{16,8},{17,9... | collective-permute-start | bytes 491528 | tf_op jit(solution)/shard_map/ppermute | solution.py:10
  84.1 22.3 %collective-permute-start.25 = (bf16[128,640]{1,0:T(8,128)(2,1)}, bf16[128,640]{1,0:T(8,128)(2,1)}, u32[]{:S(2)}, u32[]{:S(2)}) collective-permute-start(bf16[128,640]{1,0:T(8,128)(2,1)} %add_convert_fusion.1), channel_id=1, source_target_pairs={{4,0},{5,1},{6,2},{7,3},{8,4},{9,5},{10,6},{11,7},{12,8},{13,9},{1... | collective-permute-start | bytes 491528 | tf_op jit(solution)/shard_map/ppermute | solution.py:10
  85.4 22.0 %collective-permute-start.26 = (bf16[128,640]{1,0:T(8,128)(2,1)}, bf16[128,640]{1,0:T(8,128)(2,1)}, u32[]{:S(2)}, u32[]{:S(2)}) collective-permute-start(bf16[128,640]{1,0:T(8,128)(2,1)} %add_convert_fusion.1), channel_id=1, source_target_pairs={{0,4},{1,5},{2,6},{3,7},{4,8},{5,9},{6,10},{7,11},{8,12},{9,13},{1... | collective-permute-start | bytes 491528 | tf_op jit(solution)/shard_map/ppermute | solution.py:10
  91.7 16.7 %collective-permute-start.27 = (bf16[128,640]{1,0:T(8,128)(2,1)}, bf16[128,640]{1,0:T(8,128)(2,1)}, u32[]{:S(2)}, u32[]{:S(2)}) collective-permute-start(bf16[128,640]{1,0:T(8,128)(2,1)} %add_convert_fusion.1), channel_id=1, source_target_pairs={{0,8},{1,9},{2,10},{3,11},{4,12},{5,13},{6,14},{7,15},{8,16},{9,17... | collective-permute-start | bytes 491528 | tf_op jit(solution)/shard_map/ppermute | solution.py:10
  102.8 6.5 %copy-start.2 = (bf16[5,640,640]{2,1,0:T(8,128)(2,1)S(1)}, bf16[5,640,640]{2,1,0:T(8,128)(2,1)}, u32[]{:S(2)}) copy-start(bf16[5,640,640]{2,1,0:T(8,128)(2,1)} %param.13) | copy-start | bytes 12288004
  105.3 9.7 %collective-permute-start.36 = (bf16[128,5,640]{2,0,1:T(8,128)(2,1)S(1)}, bf16[128,5,640]{2,0,1:T(8,128)(2,1)}, u32[]{:S(2)}, u32[]{:S(2)}) collective-permute-start(bf16[128,5,640]{2,0,1:T(8,128)(2,1)S(1)} %dynamic-slice_convert_fusion), channel_id=1, source_target_pairs={{0,1},{1,0},{2,3},{3,2},{4,5},{5,4},{6,7},{7,6},{8,9},{9,8},{10,11... | collective-permute-start | bytes 2457608 | tf_op jit(solution)/shard_map/ppermute | solution.py:15
  113.5 6.4 %collective-permute-start.28 = (bf16[128,5,640]{2,0,1:T(8,128)(2,1)S(1)}, bf16[128,5,640]{2,0,1:T(8,128)(2,1)}, u32[]{:S(2)}, u32[]{:S(2)}) collective-permute-start(bf16[128,5,640]{2,0,1:T(8,128)(2,1)S(1)} %dynamic-slice_convert_fusion.1), channel_id=1, source_target_pairs={{0,1},{1,0},{2,3},{3,2},{4,5},{5,4},{6,7},{7,6},{8,9},{9,8},{10,11... | collective-permute-start | bytes 2457608 | tf_op jit(solution)/shard_map/ppermute | solution.py:15
  114.8 5.1 %copy-start.5 = (f32[256,5,640]{2,0,1:T(8,128)S(1)}, f32[256,5,640]{2,0,1:T(8,128)}, u32[]{:S(2)}) copy-start(f32[256,5,640]{2,0,1:T(8,128)} %copy-done.4) | copy-start | bytes 9830404
  114.8 4.3 %collective-permute-start.4 = (f32[8,128]{1,0:T(8,128)S(1)}, f32[8,128]{1,0:T(8,128)S(1)}, u32[]{:S(2)}, u32[]{:S(2)}) collective-permute-start(f32[8,128]{1,0:T(8,128)S(1)} %broadcast_in_dim.12), channel_id=1, source_target_pairs={{0,1},{1,0},{2,3},{3,2},{4,5},{5,4},{6,7},{7,6},{8,9},{9,8},{10,11... | collective-permute-start | bytes 12296 | tf_op jit(solution)/shard_map/ppermute | solution.py:15
  117.0 12.4 %collective-permute-start.37 = (bf16[64,5,640]{2,0,1:T(8,128)(2,1)S(1)}, bf16[64,5,640]{2,0,1:T(8,128)(2,1)S(1)}, u32[]{:S(2)}, u32[]{:S(2)}) collective-permute-start(bf16[64,5,640]{2,0,1:T(8,128)(2,1)S(1)} %dynamic-slice_convert_fusion.2), channel_id=1, source_target_pairs={{0,2},{1,3},{2,0},{3,1},{4,6},{5,7},{6,4},{7,5},{8,10},{9,11},{10,... | collective-permute-start | bytes 1228808 | tf_op jit(solution)/shard_map/ppermute | solution.py:15
  119.8 17.6 %collective-permute-start.5 = (f32[8,128]{1,0:T(8,128)S(1)}, f32[8,128]{1,0:T(8,128)S(1)}, u32[]{:S(2)}, u32[]{:S(2)}) collective-permute-start(f32[8,128]{1,0:T(8,128)S(1)} %broadcast_add_fusion), channel_id=1, source_target_pairs={{0,2},{1,3},{2,0},{3,1},{4,6},{5,7},{6,4},{7,5},{8,10},{9,11},{10,... | collective-permute-start | bytes 12296 | tf_op jit(solution)/shard_map/ppermute | solution.py:15
  122.1 53.3 %collective-permute-start.29 = (bf16[64,5,640]{2,0,1:T(8,128)(2,1)}, bf16[64,5,640]{2,0,1:T(8,128)(2,1)}, u32[]{:S(2)}, u32[]{:S(2)}) collective-permute-start(bf16[64,5,640]{2,0,1:T(8,128)(2,1)} %dynamic-slice_convert_fusion.3), channel_id=1, source_target_pairs={{0,2},{1,3},{2,0},{3,1},{4,6},{5,7},{6,4},{7,5},{8,10},{9,11},{10,... | collective-permute-start | bytes 1228808 | tf_op jit(solution)/shard_map/ppermute | solution.py:15
  131.1 40.8 %collective-permute-start.38 = (bf16[32,5,640]{2,0,1:T(8,128)(2,1)}, bf16[32,5,640]{2,0,1:T(8,128)(2,1)S(1)}, u32[]{:S(2)}, u32[]{:S(2)}) collective-permute-start(bf16[32,5,640]{2,0,1:T(8,128)(2,1)} %dynamic-slice_convert_fusion.4), channel_id=1, source_target_pairs={{0,16},{1,17},{2,18},{3,19},{4,20},{5,21},{6,22},{7,23},{8,24},{9,... | collective-permute-start | bytes 614408 | tf_op jit(solution)/shard_map/ppermute | solution.py:15
  138.0 3.7 %collective-permute-start.6 = (f32[8,128]{1,0:T(8,128)S(1)}, f32[8,128]{1,0:T(8,128)S(1)}, u32[]{:S(2)}, u32[]{:S(2)}) collective-permute-start(f32[8,128]{1,0:T(8,128)S(1)} %fusion.57), channel_id=1, source_target_pairs={{0,16},{1,17},{2,18},{3,19},{4,20},{5,21},{6,22},{7,23},{8,24},{9,... | collective-permute-start | bytes 12296 | tf_op jit(solution)/shard_map/ppermute | solution.py:15
  141.7 6.1 %collective-permute-start.7 = (f32[8,128]{1,0:T(8,128)S(1)}, f32[8,128]{1,0:T(8,128)S(1)}, u32[]{:S(2)}, u32[]{:S(2)}) collective-permute-start(f32[8,128]{1,0:T(8,128)S(1)} %add.282), channel_id=1, source_target_pairs={{0,64},{1,65},{2,66},{3,67},{4,68},{5,69},{6,70},{7,71},{8,72},{9,... | collective-permute-start | bytes 12296 | tf_op jit(solution)/shard_map/ppermute | solution.py:15
  147.9 4.5 %collective-permute-start.8 = (f32[8,128]{1,0:T(8,128)S(1)}, f32[8,128]{1,0:T(8,128)S(1)}, u32[]{:S(2)}, u32[]{:S(2)}) collective-permute-start(f32[8,128]{1,0:T(8,128)S(1)} %add.283), channel_id=1, source_target_pairs={{0,4},{1,5},{2,6},{3,7},{4,0},{5,1},{6,2},{7,3},{8,12},{9,13},{10,... | collective-permute-start | bytes 12296 | tf_op jit(solution)/shard_map/ppermute | solution.py:15
  152.4 5.1 %collective-permute-start.9 = (f32[8,128]{1,0:T(8,128)S(1)}, f32[8,128]{1,0:T(8,128)S(1)}, u32[]{:S(2)}, u32[]{:S(2)}) collective-permute-start(f32[8,128]{1,0:T(8,128)S(1)} %add.284), channel_id=1, source_target_pairs={{0,32},{1,33},{2,34},{3,35},{4,36},{5,37},{6,38},{7,39},{8,40},{9,... | collective-permute-start | bytes 12296 | tf_op jit(solution)/shard_map/ppermute | solution.py:15
  157.5 5.1 %collective-permute-start.10 = (f32[8,128]{1,0:T(8,128)S(1)}, f32[8,128]{1,0:T(8,128)S(1)}, u32[]{:S(2)}, u32[]{:S(2)}) collective-permute-start(f32[8,128]{1,0:T(8,128)S(1)} %add.285), channel_id=1, source_target_pairs={{0,128},{1,129},{2,130},{3,131},{4,132},{5,133},{6,134},{7,135},{8... | collective-permute-start | bytes 12296 | tf_op jit(solution)/shard_map/ppermute | solution.py:15
  162.6 7.5 %collective-permute-start.11 = (f32[8,128]{1,0:T(8,128)S(1)}, f32[8,128]{1,0:T(8,128)S(1)}, u32[]{:S(2)}, u32[]{:S(2)}) collective-permute-start(f32[8,128]{1,0:T(8,128)S(1)} %add.286), channel_id=1, source_target_pairs={{0,8},{1,9},{2,10},{3,11},{4,12},{5,13},{6,14},{7,15},{8,0},{9,1},... | collective-permute-start | bytes 12296 | tf_op jit(solution)/shard_map/ppermute | solution.py:15
  173.1 5.8 %collective-permute-start.39 = (bf16[16,5,640]{2,0,1:T(8,128)(2,1)S(1)}, bf16[16,5,640]{2,0,1:T(8,128)(2,1)S(1)}, u32[]{:S(2)}, u32[]{:S(2)}) collective-permute-start(bf16[16,5,640]{2,0,1:T(8,128)(2,1)S(1)} %dynamic-slice_convert_fusion.6), channel_id=1, source_target_pairs={{0,64},{1,65},{2,66},{3,67},{4,68},{5,69},{6,70},{7,71},{8,72},{9,... | collective-permute-start | bytes 307208 | tf_op jit(solution)/shard_map/ppermute | solution.py:15
  178.9 5.1 %collective-permute-start.40 = (bf16[8,5,640]{2,0,1:T(8,128)(2,1)S(1)}, bf16[8,5,640]{2,0,1:T(8,128)(2,1)S(1)}, u32[]{:S(2)}, u32[]{:S(2)}) collective-permute-start(bf16[8,5,640]{2,0,1:T(8,128)(2,1)S(1)} %dynamic-slice_convert_fusion.8), channel_id=1, source_target_pairs={{0,4},{1,5},{2,6},{3,7},{4,0},{5,1},{6,2},{7,3},{8,12},{9,13},{10,... | collective-permute-start | bytes 153608 | tf_op jit(solution)/shard_map/ppermute | solution.py:15
  179.1 5.8 %collective-permute-start.30 = (bf16[32,5,640]{2,0,1:T(8,128)(2,1)S(1)}, bf16[32,5,640]{2,0,1:T(8,128)(2,1)S(1)}, u32[]{:S(2)}, u32[]{:S(2)}) collective-permute-start(bf16[32,5,640]{2,0,1:T(8,128)(2,1)S(1)} %dynamic-slice_convert_fusion.5), channel_id=1, source_target_pairs={{0,16},{1,17},{2,18},{3,19},{4,20},{5,21},{6,22},{7,23},{8,24},{9,... | collective-permute-start | bytes 614408 | tf_op jit(solution)/shard_map/ppermute | solution.py:15
  184.1 5.4 %collective-permute-start.41 = (bf16[4,5,640]{2,0,1:T(4,128)(2,1)S(1)}, bf16[4,5,640]{2,0,1:T(4,128)(2,1)S(1)}, u32[]{:S(2)}, u32[]{:S(2)}) collective-permute-start(bf16[4,5,640]{2,0,1:T(4,128)(2,1)S(1)} %dynamic-slice_convert_fusion.10), channel_id=1, source_target_pairs={{0,32},{1,33},{2,34},{3,35},{4,36},{5,37},{6,38},{7,39},{8,40},{9,... | collective-permute-start | bytes 76808 | tf_op jit(solution)/shard_map/ppermute | solution.py:15
  185.0 5.2 %collective-permute-start.31 = (bf16[16,5,640]{2,0,1:T(8,128)(2,1)S(1)}, bf16[16,5,640]{2,0,1:T(8,128)(2,1)S(1)}, u32[]{:S(2)}, u32[]{:S(2)}) collective-permute-start(bf16[16,5,640]{2,0,1:T(8,128)(2,1)S(1)} %dynamic-slice_convert_fusion.7), channel_id=1, source_target_pairs={{0,64},{1,65},{2,66},{3,67},{4,68},{5,69},{6,70},{7,71},{8,72},{9,... | collective-permute-start | bytes 307208 | tf_op jit(solution)/shard_map/ppermute | solution.py:15
  190.3 5.1 %collective-permute-start.32 = (bf16[8,5,640]{2,0,1:T(8,128)(2,1)S(1)}, bf16[8,5,640]{2,0,1:T(8,128)(2,1)S(1)}, u32[]{:S(2)}, u32[]{:S(2)}) collective-permute-start(bf16[8,5,640]{2,0,1:T(8,128)(2,1)S(1)} %dynamic-slice_convert_fusion.9), channel_id=1, source_target_pairs={{0,4},{1,5},{2,6},{3,7},{4,0},{5,1},{6,2},{7,3},{8,12},{9,13},{10,... | collective-permute-start | bytes 153608 | tf_op jit(solution)/shard_map/ppermute | solution.py:15
  193.3 5.3 %collective-permute-start.42 = (bf16[2,5,640]{2,0,1:T(2,128)(2,1)S(1)}, bf16[2,5,640]{2,0,1:T(2,128)(2,1)S(1)}, u32[]{:S(2)}, u32[]{:S(2)}) collective-permute-start(bf16[2,5,640]{2,0,1:T(2,128)(2,1)S(1)} %dynamic-slice_convert_fusion.12), channel_id=1, source_target_pairs={{0,128},{1,129},{2,130},{3,131},{4,132},{5,133},{6,134},{7,135},{8... | collective-permute-start | bytes 38408 | tf_op jit(solution)/shard_map/ppermute | solution.py:15
  195.4 5.4 %collective-permute-start.33 = (bf16[4,5,640]{2,0,1:T(4,128)(2,1)S(1)}, bf16[4,5,640]{2,0,1:T(4,128)(2,1)S(1)}, u32[]{:S(2)}, u32[]{:S(2)}) collective-permute-start(bf16[4,5,640]{2,0,1:T(4,128)(2,1)S(1)} %dynamic-slice_convert_fusion.11), channel_id=1, source_target_pairs={{0,32},{1,33},{2,34},{3,35},{4,36},{5,37},{6,38},{7,39},{8,40},{9,... | collective-permute-start | bytes 76808 | tf_op jit(solution)/shard_map/ppermute | solution.py:15
  200.9 5.3 %collective-permute-start.34 = (bf16[2,5,640]{2,0,1:T(2,128)(2,1)S(1)}, bf16[2,5,640]{2,0,1:T(2,128)(2,1)S(1)}, u32[]{:S(2)}, u32[]{:S(2)}) collective-permute-start(bf16[2,5,640]{2,0,1:T(2,128)(2,1)S(1)} %dynamic-slice_convert_fusion.13), channel_id=1, source_target_pairs={{0,128},{1,129},{2,130},{3,131},{4,132},{5,133},{6,134},{7,135},{8... | collective-permute-start | bytes 38408 | tf_op jit(solution)/shard_map/ppermute | solution.py:15
  202.7 7.7 %collective-permute-start.43 = (bf16[1,5,640]{2,0,1:T(2,128)(2,1)S(1)}, bf16[1,5,640]{2,0,1:T(2,128)(2,1)S(1)}, u32[]{:S(2)}, u32[]{:S(2)}) collective-permute-start(bf16[1,5,640]{2,0,1:T(2,128)(2,1)S(1)} %dynamic-slice_convert_fusion.14), channel_id=1, source_target_pairs={{0,8},{1,9},{2,10},{3,11},{4,12},{5,13},{6,14},{7,15},{8,0},{9,1},... | collective-permute-start | bytes 19208 | tf_op jit(solution)/shard_map/ppermute | solution.py:15
  206.2 7.7 %collective-permute-start.35 = (bf16[1,5,640]{2,0,1:T(2,128)(2,1)S(1)}, bf16[1,5,640]{2,0,1:T(2,128)(2,1)S(1)}, u32[]{:S(2)}, u32[]{:S(2)}) collective-permute-start(bf16[1,5,640]{2,0,1:T(2,128)(2,1)S(1)} %dynamic-slice_convert_fusion.15), channel_id=1, source_target_pairs={{0,8},{1,9},{2,10},{3,11},{4,12},{5,13},{6,14},{7,15},{8,0},{9,1},... | collective-permute-start | bytes 19208 | tf_op jit(solution)/shard_map/ppermute | solution.py:15
  (8 other events, 10.8 us)

commit v5 on v4

--- a/solution.py
+++ b/solution.py
@@ -48,21 +48,37 @@
     return split.transpose([0] + axes + [depth + 1]).reshape(rows, width)
 
 
+def split_pair(value):
+    high = value.astype(jnp.bfloat16)
+    low = (value - high.astype(jnp.float32)).astype(jnp.bfloat16)
+    return high, low
+
+
 def tree_scatter(partials, extra, axis):
     devices = lax.axis_size(axis)
     me = lax.axis_index(axis)
     blocks = [p.reshape(devices, p.shape[0] // devices, -1) for p in partials]
+    share, width = blocks[0].shape[1:]
     for bit in link_order(devices):
         half = blocks[0].shape[0] // 2
         upper = (me // bit) % 2
         keep = [lax.dynamic_slice_in_dim(b, upper * half, half, 0) for b in blocks]
+        high, low = split_pair(extra)
+        extra = high.astype(jnp.float32) + low.astype(jnp.float32)
+        tail = jnp.concatenate(
+            [jnp.broadcast_to(high, (half, 1, width // 2)), jnp.broadcast_to(low, (half, 1, width // 2))],
+            2,
+        )
         send = [
             lax.dynamic_slice_in_dim(b, (1 - upper) * half, half, 0).astype(jnp.bfloat16)
             for b in blocks
         ]
-        got, got_extra = swap_with((send, extra), axis, bit)
-        blocks = [k + g.astype(jnp.float32) for k, g in zip(keep, got)]
-        extra = extra + got_extra
+        got = swap_with(jnp.concatenate(send + [tail], 1), axis, bit)
+        blocks = [
+            k + got[:, i * share : (i + 1) * share].astype(jnp.float32) for i, k in enumerate(keep)
+        ]
+        got_tail = got[0, -1].astype(jnp.float32)
+        extra = extra + (got_tail[0] + got_tail[width // 2])
     return [b[0] for b in blocks], extra
 
 
@@ -137,12 +153,9 @@
     up_partial = lax.dot_general(
         columns, grad_first, (((0,), (0,)), ((), ())), preferred_element_type=jnp.float32
     )
-    (grad_down, grad_up), loss_tile = tree_scatter(
-        (down_partial, up_partial), jnp.broadcast_to(local_loss, (8, 128)), "seq"
-    )
+    (grad_down, grad_up), loss_total = tree_scatter((down_partial, up_partial), local_loss, "seq")
     grad_down = grad_down.astype(jnp.bfloat16)
     grad_up = grad_up.astype(jnp.bfloat16)
-    loss_total = loss_tile[0, 0]
     return (loss_total / mask_total, grad_up, grad_down)
 
 

time: 217 us -> 226 us (1.041)
  starting transfers between devices: 89.5 us -> 65.1 us
  waiting for transfers between devices: 80.5 us -> 95.6 us
  between operations: 4.54 us -> 16.1 us
  local copies, waits for them, and re-layouts: 17.8 us -> 21.5 us
    ppermute x36 -> x20, starting transfers between devices: 58 us -> 33.6 us  [swap_with(): return lax.ppermute(block, axis, [(i, i ^ bit) for i in range(devices)])]
    ppermute x36 -> x20, waiting for transfers between devices: 62.6 us -> 77.7 us  [swap_with(): return lax.ppermute(block, axis, [(i, i ^ bit) for i in range(devices)])]
    slice x1 -> x8, local copies, waits for them, and re-layouts: 0.51 us -> 4.68 us  [tree_scatter(): extra = extra + (got_tail[0] + got_tail[width // 2])]
    unnamed x32 -> x34, local copies, waits for them, and re-layouts: 8.4 us -> 9.86 us
    add x22 -> x7, other arithmetic: 7.03 us -> 5.64 us  [tree_scatter(): k + got[:, i * share:(i + 1) * share].astype(jnp.float32)]
  transfers between devices with their start and end apart: 44 -> 28, of which waited for: 28 -> 15; matrix products, arithmetic and copies ran while one was open for 10% -> 4% of each run, Pallas kernels for 0% -> 0%
where the time goes in v5:
time: 226 us; the launch traced here: 223 us
  waiting for transfers between devices  95.6 us (42%)
  starting transfers between devices  65.1 us (29%)
  local copies, waits for them, and re-layouts  21.5 us (10%)
  other arithmetic  16.2 us (7%)
  between operations  16.1 us (7%)
  matrix products  8.75 us (4%)
    ppermute x20, waiting for transfers between devices, swap_with(): return lax.ppermute(block, axis, [(i, i ^ bit) for i in range(devices)])  77.7 us
    ppermute x20, starting transfers between devices, swap_with(): return lax.ppermute(block, axis, [(i, i ^ bit) for i in range(devices)])  33.6 us
    ppermute x8, starting transfers between devices, from_behind(): return lax.ppermute(block, axis, route)  31.5 us
    ppermute x8, waiting for transfers between devices, from_behind(): return lax.ppermute(block, axis, route)  17.9 us
    unnamed x34, local copies, waits for them, and re-layouts  9.86 us
    add x7, other arithmetic, tree_scatter(): k + got[:, i * share:(i + 1) * share].astype(jnp.float32)  5.64 us
    slice x8, local copies, waits for them, and re-layouts, tree_scatter(): extra = extra + (got_tail[0] + got_tail[width // 2])  4.68 us
  transfers between devices with their start and end apart: 28, of which 15 were waited for; matrix products, arithmetic and copies ran while one was open for 4% of the time, Pallas kernels for 0%

profile of v5, /device:TPU:32, one launch (start us, length us, event | category | flops | bytes accessed | tf_op | source)
XLA Modules:
  0.0 223.3 jit_solution(10537270612641771647)
XLA Ops:
  0.6 1.2 convert_reduce_fusion
  1.9 1.2 fusion.14
  3.1 1.4 fusion.9
  4.5 2.1 fusion.56
  7.0 8.2 %collective-permute-start = (bf16[128,640]{1,0:T(8,128)(2,1)S(1)}, bf16[128,640]{1,0:T(8,128)(2,1)S(1)}, u32[]{:S(2)}, u32[]{:S(2)}) collective-permute-start(bf16[128,640]{1,0:T(8,128)(2,1)S(1)} %multiply_convert_fusion.1), channel_id=1, source_target_pairs={{0,8},{1,9},{2,10},{3,11},{4,12},{5,13},{6,14},{7,15},{8,16},{9,17... | collective-permute-start | bytes 491528 | tf_op jit(solution)/shard_map/ppermute | solution.py:10
  15.2 3.4 %collective-permute-start.1 = (bf16[128,640]{1,0:T(8,128)(2,1)S(1)}, bf16[128,640]{1,0:T(8,128)(2,1)S(1)}, u32[]{:S(2)}, u32[]{:S(2)}) collective-permute-start(bf16[128,640]{1,0:T(8,128)(2,1)S(1)} %multiply_convert_fusion.1), channel_id=1, source_target_pairs={{0,4},{1,5},{2,6},{3,7},{4,8},{5,9},{6,10},{7,11},{8,12},{9,13},{1... | collective-permute-start | bytes 491528 | tf_op jit(solution)/shard_map/ppermute | solution.py:10
  18.6 1.3 collective-permute-start.2
  19.9 1.3 collective-permute-start.3
  21.3 8.5 %collective-permute-done.1 = bf16[128,640]{1,0:T(8,128)(2,1)S(1)} collective-permute-done((bf16[128,640]{1,0:T(8,128)(2,1)S(1)}, bf16[128,640]{1,0:T(8,128)(2,1)S(1)}, u32[]{:S(2)}, u32[]{:S(2)}) %collective-permute-start.1) | collective-permute-done | bytes 163872 | tf_op jit(solution)/shard_map/ppermute | solution.py:10
  30.0 9.4 %collective-permute-done.3 = bf16[128,640]{1,0:T(8,128)(2,1)S(1)} collective-permute-done((bf16[128,640]{1,0:T(8,128)(2,1)S(1)}, bf16[128,640]{1,0:T(8,128)(2,1)S(1)}, u32[]{:S(2)}, u32[]{:S(2)}) %collective-permute-start.3) | collective-permute-done | bytes 163872 | tf_op jit(solution)/shard_map/ppermute | solution.py:10
  43.0 1.7 collective-permute-start.6
  44.8 1.8 collective-permute-done.5
  47.3 3.9 %collective-permute-start.7 = (f32[8,128]{1,0:T(8,128)S(1)}, f32[8,128]{1,0:T(8,128)S(1)}, u32[]{:S(2)}, u32[]{:S(2)}) collective-permute-start(f32[8,128]{1,0:T(8,128)S(1)} %add_add_fusion.5), channel_id=1, source_target_pairs={{0,16},{1,17},{2,18},{3,19},{4,20},{5,21},{6,22},{7,23},{8,24},{9,... | collective-permute-start | bytes 12296 | tf_op jit(solution)/shard_map/ppermute | solution.py:15
  51.2 1.6 collective-permute-start.8
  52.8 2.0 collective-permute-done.8
  54.8 2.5 %collective-permute-done.9 = f32[8,128]{1,0:T(8,128)S(1)} collective-permute-done((f32[8,128]{1,0:T(8,128)S(1)}, f32[8,128]{1,0:T(8,128)S(1)}, u32[]{:S(2)}, u32[]{:S(2)}) %collective-permute-start.9) | collective-permute-done | bytes 4128 | tf_op jit(solution)/shard_map/ppermute | solution.py:15
  57.3 2.7 %collective-permute-start.11 = (f32[8,128]{1,0:T(8,128)S(1)}, f32[8,128]{1,0:T(8,128)S(1)}, u32[]{:S(2)}, u32[]{:S(2)}) collective-permute-start(f32[8,128]{1,0:T(8,128)S(1)} %add_add_fusion.4), channel_id=1, source_target_pairs={{0,32},{1,33},{2,34},{3,35},{4,36},{5,37},{6,38},{7,39},{8,40},{9,... | collective-permute-start | bytes 12296 | tf_op jit(solution)/shard_map/ppermute | solution.py:15
  60.0 3.2 %collective-permute-start.12 = (f32[8,128]{1,0:T(8,128)S(1)}, f32[8,128]{1,0:T(8,128)S(1)}, u32[]{:S(2)}, u32[]{:S(2)}) collective-permute-start(f32[8,128]{1,0:T(8,128)S(1)} %add_add_fusion.4), channel_id=1, source_target_pairs={{0,36},{1,37},{2,38},{3,39},{4,32},{5,33},{6,34},{7,35},{8,44},{9,... | collective-permute-start | bytes 12296 | tf_op jit(solution)/shard_map/ppermute | solution.py:15
  63.2 3.7 %collective-permute-done.12 = f32[8,128]{1,0:T(8,128)S(1)} collective-permute-done((f32[8,128]{1,0:T(8,128)S(1)}, f32[8,128]{1,0:T(8,128)S(1)}, u32[]{:S(2)}, u32[]{:S(2)}) %collective-permute-start.12) | collective-permute-done | bytes 4128 | tf_op jit(solution)/shard_map/ppermute | solution.py:15
  66.9 1.8 collective-permute-start.13
  68.7 5.9 %collective-permute-start.14 = (f32[8,128]{1,0:T(8,128)S(1)}, f32[8,128]{1,0:T(8,128)S(1)}, u32[]{:S(2)}, u32[]{:S(2)}) collective-permute-start(f32[8,128]{1,0:T(8,128)S(1)} %add_add_fusion.3), channel_id=1, source_target_pairs={{0,8},{1,9},{2,10},{3,11},{4,12},{5,13},{6,14},{7,15},{8,0},{9,1},... | collective-permute-start | bytes 12296 | tf_op jit(solution)/shard_map/ppermute | solution.py:15
  74.5 1.6 collective-permute-start.15
  79.1 5.3 %collective-permute-done.15 = f32[8,128]{1,0:T(8,128)S(1)} collective-permute-done((f32[8,128]{1,0:T(8,128)S(1)}, f32[8,128]{1,0:T(8,128)S(1)}, u32[]{:S(2)}, u32[]{:S(2)}) %collective-permute-start.15) | collective-permute-done | bytes 4128 | tf_op jit(solution)/shard_map/ppermute | solution.py:15
  85.7 1.3 fusion
  89.1 1.5 collective-permute-start.16
  90.6 1.3 collective-permute-start.17
  91.9 6.1 %collective-permute-start.18 = (bf16[128,640]{1,0:T(8,128)(2,1)}, bf16[128,640]{1,0:T(8,128)(2,1)}, u32[]{:S(2)}, u32[]{:S(2)}) collective-permute-start(bf16[128,640]{1,0:T(8,128)(2,1)} %add_convert_fusion.1), channel_id=1, source_target_pairs={{0,4},{1,5},{2,6},{3,7},{4,8},{5,9},{6,10},{7,11},{8,12},{9,13},{1... | collective-permute-start | bytes 491528 | tf_op jit(solution)/shard_map/ppermute | solution.py:10
  98.0 8.5 %collective-permute-start.19 = (bf16[128,640]{1,0:T(8,128)(2,1)}, bf16[128,640]{1,0:T(8,128)(2,1)}, u32[]{:S(2)}, u32[]{:S(2)}) collective-permute-start(bf16[128,640]{1,0:T(8,128)(2,1)} %add_convert_fusion.1), channel_id=1, source_target_pairs={{0,8},{1,9},{2,10},{3,11},{4,12},{5,13},{6,14},{7,15},{8,16},{9,17... | collective-permute-start | bytes 491528 | tf_op jit(solution)/shard_map/ppermute | solution.py:10
  107.5 1.2 reshape.139
  109.6 1.7 copy-done.3
  115.3 1.5 multiply_reduce_fusion
  117.7 1.7 copy-done.4
  120.0 3.8 %collective-permute-done.20 = bf16[128,11,640]{2,0,1:T(8,128)(2,1)} collective-permute-done((bf16[128,11,640]{2,0,1:T(8,128)(2,1)S(1)}, bf16[128,11,640]{2,0,1:T(8,128)(2,1)}, u32[]{:S(2)}, u32[]{:S(2)}) %collective-permute-start.20) | collective-permute-done | bytes 1802272 | tf_op jit(solution)/shard_map/ppermute | solution.py:15
  126.4 2.7 %convert_add_fusion.1 = (f32[128,5,640]{2,0,1:T(8,128)S(1)}, f32[128,5,640]{2,0,1:T(8,128)S(1)}) fusion(f32[256,5,640]{2,0,1:T(8,128)} %copy-done.3, s32[]{:T(128)S(6)} %select_n.124, bf16[128,11,640]{2,0,1:T(8,128)(2,1)} %collective-permute-done.20, f32[256,5,640]{2,0,1:T(8,128)} %copy-done.4), kind=kLoop, calls=%fused_computation.6 | loop fusion | flops 1638400 | bytes 8192004 | tf_op jit(solution)/shard_map/add | solution.py:78
  129.2 1.2 copy-done.5
  130.5 1.1 pad_maximum_fusion.1
  132.1 21.8 %collective-permute-done.21 = bf16[64,11,640]{2,0,1:T(8,128)(2,1)} collective-permute-done((bf16[64,11,640]{2,0,1:T(8,128)(2,1)}, bf16[64,11,640]{2,0,1:T(8,128)(2,1)}, u32[]{:S(2)}, u32[]{:S(2)}) %collective-permute-start.21) | collective-permute-done | bytes 901152 | tf_op jit(solution)/shard_map/ppermute | solution.py:15
  153.9 1.5 convert_add_fusion.3
  159.4 4.1 %collective-permute-start.22 = (bf16[32,11,640]{2,0,1:T(8,128)(2,1)S(1)}, bf16[32,11,640]{2,0,1:T(8,128)(2,1)S(1)}, u32[]{:S(2)}, u32[]{:S(2)}) collective-permute-start(bf16[32,11,640]{2,0,1:T(8,128)(2,1)S(1)} %pad_maximum_fusion.2), channel_id=1, source_target_pairs={{0,16},{1,17},{2,18},{3,19},{4,20},{5,21},{6,22},{7,23},{8,24},{9,... | collective-permute-start | bytes 1351688 | tf_op jit(solution)/shard_map/ppermute | solution.py:15
  163.5 9.8 %collective-permute-done.22 = bf16[32,11,640]{2,0,1:T(8,128)(2,1)S(1)} collective-permute-done((bf16[32,11,640]{2,0,1:T(8,128)(2,1)S(1)}, bf16[32,11,640]{2,0,1:T(8,128)(2,1)S(1)}, u32[]{:S(2)}, u32[]{:S(2)}) %collective-permute-start.22) | collective-permute-done | bytes 450592 | tf_op jit(solution)/shard_map/ppermute | solution.py:15
  173.3 1.2 convert_add_fusion.5
  176.6 4.3 %collective-permute-start.23 = (bf16[16,11,640]{2,0,1:T(8,128)(2,1)S(1)}, bf16[16,11,640]{2,0,1:T(8,128)(2,1)S(1)}, u32[]{:S(2)}, u32[]{:S(2)}) collective-permute-start(bf16[16,11,640]{2,0,1:T(8,128)(2,1)S(1)} %pad_maximum_fusion.3), channel_id=1, source_target_pairs={{0,64},{1,65},{2,66},{3,67},{4,68},{5,69},{6,70},{7,71},{8,72},{9,... | collective-permute-start | bytes 675848 | tf_op jit(solution)/shard_map/ppermute | solution.py:15
  180.9 4.1 %collective-permute-done.23 = bf16[16,11,640]{2,0,1:T(8,128)(2,1)S(1)} collective-permute-done((bf16[16,11,640]{2,0,1:T(8,128)(2,1)S(1)}, bf16[16,11,640]{2,0,1:T(8,128)(2,1)S(1)}, u32[]{:S(2)}, u32[]{:S(2)}) %collective-permute-start.23) | collective-permute-done | bytes 225312 | tf_op jit(solution)/shard_map/ppermute | solution.py:15
  187.2 5.7 %collective-permute-done.24 = bf16[8,11,640]{2,0,1:T(8,128)(2,1)S(1)} collective-permute-done((bf16[8,11,640]{2,0,1:T(8,128)(2,1)S(1)}, bf16[8,11,640]{2,0,1:T(8,128)(2,1)S(1)}, u32[]{:S(2)}, u32[]{:S(2)}) %collective-permute-start.24) | collective-permute-done | bytes 112672 | tf_op jit(solution)/shard_map/ppermute | solution.py:15
  195.2 5.6 %collective-permute-done.25 = bf16[4,11,640]{2,0,1:T(4,128)(2,1)S(1)} collective-permute-done((bf16[4,11,640]{2,0,1:T(4,128)(2,1)S(1)}, bf16[4,11,640]{2,0,1:T(4,128)(2,1)S(1)}, u32[]{:S(2)}, u32[]{:S(2)}) %collective-permute-start.25) | collective-permute-done | bytes 56352 | tf_op jit(solution)/shard_map/ppermute | solution.py:15
  202.9 1.6 collective-permute-start.26
  204.5 3.8 %collective-permute-done.26 = bf16[2,11,640]{2,0,1:T(2,128)(2,1)S(1)} collective-permute-done((bf16[2,11,640]{2,0,1:T(2,128)(2,1)S(1)}, bf16[2,11,640]{2,0,1:T(2,128)(2,1)S(1)}, u32[]{:S(2)}, u32[]{:S(2)}) %collective-permute-start.26) | collective-permute-done | bytes 28192 | tf_op jit(solution)/shard_map/ppermute | solution.py:15
  210.6 7.7 %collective-permute-done.27 = bf16[1,11,640]{2,0,1:T(2,128)(2,1)S(1)} collective-permute-done((bf16[1,11,640]{2,0,1:T(2,128)(2,1)S(1)}, bf16[1,11,640]{2,0,1:T(2,128)(2,1)S(1)}, u32[]{:S(2)}, u32[]{:S(2)}) %collective-permute-start.27) | collective-permute-done | bytes 14112 | tf_op jit(solution)/shard_map/ppermute | solution.py:15
  (162 shorter events, 26.6 us)
Async XLA Ops:
  0.6 40.0 %copy-start = (bf16[1280,640]{1,0:T(8,128)(2,1)S(1)}, bf16[1280,640]{1,0:T(8,128)(2,1)}, u32[]{:S(2)}) copy-start(bf16[1280,640]{1,0:T(8,128)(2,1)} %param.14) | copy-start | bytes 4915204
  4.5 34.9 %copy-start.1 = (bf16[5,640,640]{2,1,0:T(8,128)(2,1)S(1)}, bf16[5,640,640]{2,1,0:T(8,128)(2,1)}, u32[]{:S(2)}) copy-start(bf16[5,640,640]{2,1,0:T(8,128)(2,1)} %param.13) | copy-start | bytes 12288004
  7.0 14.2 %collective-permute-start = (bf16[128,640]{1,0:T(8,128)(2,1)S(1)}, bf16[128,640]{1,0:T(8,128)(2,1)S(1)}, u32[]{:S(2)}, u32[]{:S(2)}) collective-permute-start(bf16[128,640]{1,0:T(8,128)(2,1)S(1)} %multiply_convert_fusion.1), channel_id=1, source_target_pairs={{0,8},{1,9},{2,10},{3,11},{4,12},{5,13},{6,14},{7,15},{8,16},{9,17... | collective-permute-start | bytes 491528 | tf_op jit(solution)/shard_map/ppermute | solution.py:10
  15.2 14.5 %collective-permute-start.1 = (bf16[128,640]{1,0:T(8,128)(2,1)S(1)}, bf16[128,640]{1,0:T(8,128)(2,1)S(1)}, u32[]{:S(2)}, u32[]{:S(2)}) collective-permute-start(bf16[128,640]{1,0:T(8,128)(2,1)S(1)} %multiply_convert_fusion.1), channel_id=1, source_target_pairs={{0,4},{1,5},{2,6},{3,7},{4,8},{5,9},{6,10},{7,11},{8,12},{9,13},{1... | collective-permute-start | bytes 491528 | tf_op jit(solution)/shard_map/ppermute | solution.py:10
  18.6 11.4 %collective-permute-start.2 = (bf16[128,640]{1,0:T(8,128)(2,1)S(1)}, bf16[128,640]{1,0:T(8,128)(2,1)S(1)}, u32[]{:S(2)}, u32[]{:S(2)}) collective-permute-start(bf16[128,640]{1,0:T(8,128)(2,1)S(1)} %multiply_convert_fusion.1), channel_id=1, source_target_pairs={{4,0},{5,1},{6,2},{7,3},{8,4},{9,5},{10,6},{11,7},{12,8},{13,9},{1... | collective-permute-start | bytes 491528 | tf_op jit(solution)/shard_map/ppermute | solution.py:10
  19.9 19.5 %collective-permute-start.3 = (bf16[128,640]{1,0:T(8,128)(2,1)S(1)}, bf16[128,640]{1,0:T(8,128)(2,1)S(1)}, u32[]{:S(2)}, u32[]{:S(2)}) collective-permute-start(bf16[128,640]{1,0:T(8,128)(2,1)S(1)} %multiply_convert_fusion.1), channel_id=1, source_target_pairs={{8,0},{9,1},{10,2},{11,3},{12,4},{13,5},{14,6},{15,7},{16,8},{17,9... | collective-permute-start | bytes 491528 | tf_op jit(solution)/shard_map/ppermute | solution.py:10
  39.4 1.2 copy-start.6
  39.5 1.2 copy-start.10
  39.5 1.2 copy-start.12
  40.4 1.2 copy-start.11
  42.8 2.0 collective-permute-start.4
  42.9 3.7 %collective-permute-start.5 = (f32[8,128]{1,0:T(8,128)S(1)}, f32[8,128]{1,0:T(8,128)S(1)}, u32[]{:S(2)}, u32[]{:S(2)}) collective-permute-start(f32[8,128]{1,0:T(8,128)S(1)} %broadcast_in_dim.26), channel_id=1, source_target_pairs={{0,2},{1,3},{2,0},{3,1},{4,6},{5,7},{6,4},{7,5},{8,10},{9,11},{10,... | collective-permute-start | bytes 12296 | tf_op jit(solution)/shard_map/ppermute | solution.py:15
  43.0 3.6 %collective-permute-start.6 = (f32[8,128]{1,0:T(8,128)S(1)}, f32[8,128]{1,0:T(8,128)S(1)}, u32[]{:S(2)}, u32[]{:S(2)}) collective-permute-start(f32[8,128]{1,0:T(8,128)S(1)} %broadcast_in_dim.26), channel_id=1, source_target_pairs={{0,3},{1,2},{2,1},{3,0},{4,7},{5,6},{6,5},{7,4},{8,11},{9,10},{10,... | collective-permute-start | bytes 12296 | tf_op jit(solution)/shard_map/ppermute | solution.py:15
  47.3 5.5 %collective-permute-start.7 = (f32[8,128]{1,0:T(8,128)S(1)}, f32[8,128]{1,0:T(8,128)S(1)}, u32[]{:S(2)}, u32[]{:S(2)}) collective-permute-start(f32[8,128]{1,0:T(8,128)S(1)} %add_add_fusion.5), channel_id=1, source_target_pairs={{0,16},{1,17},{2,18},{3,19},{4,20},{5,21},{6,22},{7,23},{8,24},{9,... | collective-permute-start | bytes 12296 | tf_op jit(solution)/shard_map/ppermute | solution.py:15
  51.2 3.6 %collective-permute-start.8 = (f32[8,128]{1,0:T(8,128)S(1)}, f32[8,128]{1,0:T(8,128)S(1)}, u32[]{:S(2)}, u32[]{:S(2)}) collective-permute-start(f32[8,128]{1,0:T(8,128)S(1)} %add_add_fusion.5), channel_id=1, source_target_pairs={{0,64},{1,65},{2,66},{3,67},{4,68},{5,69},{6,70},{7,71},{8,72},{9,... | collective-permute-start | bytes 12296 | tf_op jit(solution)/shard_map/ppermute | solution.py:15
  52.8 4.5 %collective-permute-start.9 = (f32[8,128]{1,0:T(8,128)S(1)}, f32[8,128]{1,0:T(8,128)S(1)}, u32[]{:S(2)}, u32[]{:S(2)}) collective-permute-start(f32[8,128]{1,0:T(8,128)S(1)} %add_add_fusion.5), channel_id=1, source_target_pairs={{0,80},{1,81},{2,82},{3,83},{4,84},{5,85},{6,86},{7,87},{8,88},{9,... | collective-permute-start | bytes 12296 | tf_op jit(solution)/shard_map/ppermute | solution.py:15
  57.3 5.9 %collective-permute-start.10 = (f32[8,128]{1,0:T(8,128)S(1)}, f32[8,128]{1,0:T(8,128)S(1)}, u32[]{:S(2)}, u32[]{:S(2)}) collective-permute-start(f32[8,128]{1,0:T(8,128)S(1)} %add_add_fusion.4), channel_id=1, source_target_pairs={{0,4},{1,5},{2,6},{3,7},{4,0},{5,1},{6,2},{7,3},{8,12},{9,13},{10,... | collective-permute-start | bytes 12296 | tf_op jit(solution)/shard_map/ppermute | solution.py:15
  57.3 5.9 %collective-permute-start.11 = (f32[8,128]{1,0:T(8,128)S(1)}, f32[8,128]{1,0:T(8,128)S(1)}, u32[]{:S(2)}, u32[]{:S(2)}) collective-permute-start(f32[8,128]{1,0:T(8,128)S(1)} %add_add_fusion.4), channel_id=1, source_target_pairs={{0,32},{1,33},{2,34},{3,35},{4,36},{5,37},{6,38},{7,39},{8,40},{9,... | collective-permute-start | bytes 12296 | tf_op jit(solution)/shard_map/ppermute | solution.py:15
  60.0 6.9 %collective-permute-start.12 = (f32[8,128]{1,0:T(8,128)S(1)}, f32[8,128]{1,0:T(8,128)S(1)}, u32[]{:S(2)}, u32[]{:S(2)}) collective-permute-start(f32[8,128]{1,0:T(8,128)S(1)} %add_add_fusion.4), channel_id=1, source_target_pairs={{0,36},{1,37},{2,38},{3,39},{4,32},{5,33},{6,34},{7,35},{8,44},{9,... | collective-permute-start | bytes 12296 | tf_op jit(solution)/shard_map/ppermute | solution.py:15
  66.9 12.2 %collective-permute-start.13 = (f32[8,128]{1,0:T(8,128)S(1)}, f32[8,128]{1,0:T(8,128)S(1)}, u32[]{:S(2)}, u32[]{:S(2)}) collective-permute-start(f32[8,128]{1,0:T(8,128)S(1)} %add_add_fusion.3), channel_id=1, source_target_pairs={{0,128},{1,129},{2,130},{3,131},{4,132},{5,133},{6,134},{7,135},{8... | collective-permute-start | bytes 12296 | tf_op jit(solution)/shard_map/ppermute | solution.py:15
  68.7 10.4 %collective-permute-start.14 = (f32[8,128]{1,0:T(8,128)S(1)}, f32[8,128]{1,0:T(8,128)S(1)}, u32[]{:S(2)}, u32[]{:S(2)}) collective-permute-start(f32[8,128]{1,0:T(8,128)S(1)} %add_add_fusion.3), channel_id=1, source_target_pairs={{0,8},{1,9},{2,10},{3,11},{4,12},{5,13},{6,14},{7,15},{8,0},{9,1},... | collective-permute-start | bytes 12296 | tf_op jit(solution)/shard_map/ppermute | solution.py:15
  74.5 9.9 %collective-permute-start.15 = (f32[8,128]{1,0:T(8,128)S(1)}, f32[8,128]{1,0:T(8,128)S(1)}, u32[]{:S(2)}, u32[]{:S(2)}) collective-permute-start(f32[8,128]{1,0:T(8,128)S(1)} %add_add_fusion.3), channel_id=1, source_target_pairs={{0,136},{1,137},{2,138},{3,139},{4,140},{5,141},{6,142},{7,143},{8... | collective-permute-start | bytes 12296 | tf_op jit(solution)/shard_map/ppermute | solution.py:15
  89.1 22.3 %collective-permute-start.16 = (bf16[128,640]{1,0:T(8,128)(2,1)}, bf16[128,640]{1,0:T(8,128)(2,1)}, u32[]{:S(2)}, u32[]{:S(2)}) collective-permute-start(bf16[128,640]{1,0:T(8,128)(2,1)} %add_convert_fusion.1), channel_id=1, source_target_pairs={{8,0},{9,1},{10,2},{11,3},{12,4},{13,5},{14,6},{15,7},{16,8},{17,9... | collective-permute-start | bytes 491528 | tf_op jit(solution)/shard_map/ppermute | solution.py:10
  90.6 21.8 %collective-permute-start.17 = (bf16[128,640]{1,0:T(8,128)(2,1)}, bf16[128,640]{1,0:T(8,128)(2,1)}, u32[]{:S(2)}, u32[]{:S(2)}) collective-permute-start(bf16[128,640]{1,0:T(8,128)(2,1)} %add_convert_fusion.1), channel_id=1, source_target_pairs={{4,0},{5,1},{6,2},{7,3},{8,4},{9,5},{10,6},{11,7},{12,8},{13,9},{1... | collective-permute-start | bytes 491528 | tf_op jit(solution)/shard_map/ppermute | solution.py:10
  91.9 21.5 %collective-permute-start.18 = (bf16[128,640]{1,0:T(8,128)(2,1)}, bf16[128,640]{1,0:T(8,128)(2,1)}, u32[]{:S(2)}, u32[]{:S(2)}) collective-permute-start(bf16[128,640]{1,0:T(8,128)(2,1)} %add_convert_fusion.1), channel_id=1, source_target_pairs={{0,4},{1,5},{2,6},{3,7},{4,8},{5,9},{6,10},{7,11},{8,12},{9,13},{1... | collective-permute-start | bytes 491528 | tf_op jit(solution)/shard_map/ppermute | solution.py:10
  98.0 16.3 %collective-permute-start.19 = (bf16[128,640]{1,0:T(8,128)(2,1)}, bf16[128,640]{1,0:T(8,128)(2,1)}, u32[]{:S(2)}, u32[]{:S(2)}) collective-permute-start(bf16[128,640]{1,0:T(8,128)(2,1)} %add_convert_fusion.1), channel_id=1, source_target_pairs={{0,8},{1,9},{2,10},{3,11},{4,12},{5,13},{6,14},{7,15},{8,16},{9,17... | collective-permute-start | bytes 491528 | tf_op jit(solution)/shard_map/ppermute | solution.py:10
  108.8 6.4 %copy-start.2 = (bf16[5,640,640]{2,1,0:T(8,128)(2,1)S(1)}, bf16[5,640,640]{2,1,0:T(8,128)(2,1)}, u32[]{:S(2)}) copy-start(bf16[5,640,640]{2,1,0:T(8,128)(2,1)} %param.13) | copy-start | bytes 12288004
  109.6 1.7 copy-start.3
  115.3 1.8 copy-start.9
  117.7 1.7 copy-start.4
  119.9 4.0 %collective-permute-start.20 = (bf16[128,11,640]{2,0,1:T(8,128)(2,1)S(1)}, bf16[128,11,640]{2,0,1:T(8,128)(2,1)}, u32[]{:S(2)}, u32[]{:S(2)}) collective-permute-start(bf16[128,11,640]{2,0,1:T(8,128)(2,1)S(1)} %pad_maximum_fusion), channel_id=1, source_target_pairs={{0,1},{1,0},{2,3},{3,2},{4,5},{5,4},{6,7},{7,6},{8,9},{9,8},{10,11... | collective-permute-start | bytes 5406728 | tf_op jit(solution)/shard_map/ppermute | solution.py:15
  129.2 1.2 copy-start.5
  131.5 22.4 %collective-permute-start.21 = (bf16[64,11,640]{2,0,1:T(8,128)(2,1)}, bf16[64,11,640]{2,0,1:T(8,128)(2,1)}, u32[]{:S(2)}, u32[]{:S(2)}) collective-permute-start(bf16[64,11,640]{2,0,1:T(8,128)(2,1)} %pad_maximum_fusion.1), channel_id=1, source_target_pairs={{0,2},{1,3},{2,0},{3,1},{4,6},{5,7},{6,4},{7,5},{8,10},{9,11},{10,... | collective-permute-start | bytes 2703368 | tf_op jit(solution)/shard_map/ppermute | solution.py:15
  155.4 0.9 copy-start.7
  155.5 1.2 copy-start.8
  159.4 13.9 %collective-permute-start.22 = (bf16[32,11,640]{2,0,1:T(8,128)(2,1)S(1)}, bf16[32,11,640]{2,0,1:T(8,128)(2,1)S(1)}, u32[]{:S(2)}, u32[]{:S(2)}) collective-permute-start(bf16[32,11,640]{2,0,1:T(8,128)(2,1)S(1)} %pad_maximum_fusion.2), channel_id=1, source_target_pairs={{0,16},{1,17},{2,18},{3,19},{4,20},{5,21},{6,22},{7,23},{8,24},{9,... | collective-permute-start | bytes 1351688 | tf_op jit(solution)/shard_map/ppermute | solution.py:15
  176.6 8.4 %collective-permute-start.23 = (bf16[16,11,640]{2,0,1:T(8,128)(2,1)S(1)}, bf16[16,11,640]{2,0,1:T(8,128)(2,1)S(1)}, u32[]{:S(2)}, u32[]{:S(2)}) collective-permute-start(bf16[16,11,640]{2,0,1:T(8,128)(2,1)S(1)} %pad_maximum_fusion.3), channel_id=1, source_target_pairs={{0,64},{1,65},{2,66},{3,67},{4,68},{5,69},{6,70},{7,71},{8,72},{9,... | collective-permute-start | bytes 675848 | tf_op jit(solution)/shard_map/ppermute | solution.py:15
  187.1 5.9 %collective-permute-start.24 = (bf16[8,11,640]{2,0,1:T(8,128)(2,1)S(1)}, bf16[8,11,640]{2,0,1:T(8,128)(2,1)S(1)}, u32[]{:S(2)}, u32[]{:S(2)}) collective-permute-start(bf16[8,11,640]{2,0,1:T(8,128)(2,1)S(1)} %pad_maximum_fusion.4), channel_id=1, source_target_pairs={{0,4},{1,5},{2,6},{3,7},{4,0},{5,1},{6,2},{7,3},{8,12},{9,13},{10,... | collective-permute-start | bytes 337928 | tf_op jit(solution)/shard_map/ppermute | solution.py:15
  195.0 5.8 %collective-permute-start.25 = (bf16[4,11,640]{2,0,1:T(4,128)(2,1)S(1)}, bf16[4,11,640]{2,0,1:T(4,128)(2,1)S(1)}, u32[]{:S(2)}, u32[]{:S(2)}) collective-permute-start(bf16[4,11,640]{2,0,1:T(4,128)(2,1)S(1)} %pad_maximum_fusion.5), channel_id=1, source_target_pairs={{0,32},{1,33},{2,34},{3,35},{4,36},{5,37},{6,38},{7,39},{8,40},{9,... | collective-permute-start | bytes 168968 | tf_op jit(solution)/shard_map/ppermute | solution.py:15
  202.9 5.5 %collective-permute-start.26 = (bf16[2,11,640]{2,0,1:T(2,128)(2,1)S(1)}, bf16[2,11,640]{2,0,1:T(2,128)(2,1)S(1)}, u32[]{:S(2)}, u32[]{:S(2)}) collective-permute-start(bf16[2,11,640]{2,0,1:T(2,128)(2,1)S(1)} %pad_maximum_fusion.6), channel_id=1, source_target_pairs={{0,128},{1,129},{2,130},{3,131},{4,132},{5,133},{6,134},{7,135},{8... | collective-permute-start | bytes 84488 | tf_op jit(solution)/shard_map/ppermute | solution.py:15
  210.4 7.9 %collective-permute-start.27 = (bf16[1,11,640]{2,0,1:T(2,128)(2,1)S(1)}, bf16[1,11,640]{2,0,1:T(2,128)(2,1)S(1)}, u32[]{:S(2)}, u32[]{:S(2)}) collective-permute-start(bf16[1,11,640]{2,0,1:T(2,128)(2,1)S(1)} %pad_maximum_fusion.7), channel_id=1, source_target_pairs={{0,8},{1,9},{2,10},{3,11},{4,12},{5,13},{6,14},{7,15},{8,0},{9,1},... | collective-permute-start | bytes 42248 | tf_op jit(solution)/shard_map/ppermute | solution.py:15

commit v6 on v4

--- a/solution.py
+++ b/solution.py
@@ -60,7 +60,10 @@
             lax.dynamic_slice_in_dim(b, (1 - upper) * half, half, 0).astype(jnp.bfloat16)
             for b in blocks
         ]
-        got, got_extra = swap_with((send, extra), axis, bit)
+        pieces = 2 if half >= 16 else 1
+        parts = [jnp.split(s, pieces, 0) for s in send]
+        got_parts, got_extra = swap_with((parts, extra), axis, bit)
+        got = [jnp.concatenate(g, 0) if pieces > 1 else g[0] for g in got_parts]
         blocks = [k + g.astype(jnp.float32) for k, g in zip(keep, got)]
         extra = extra + got_extra
     return [b[0] for b in blocks], extra

time: 217 us -> 204 us (0.940)
  waiting for transfers between devices: 80.5 us -> 61.6 us
  starting transfers between devices: 89.5 us -> 103 us
  other arithmetic: 14.6 us -> 11.1 us
  local copies, waits for them, and re-layouts: 17.8 us -> 15.2 us
    ppermute x36 -> x44, waiting for transfers between devices: 62.6 us -> 43.7 us  [swap_with(): return lax.ppermute(block, axis, [(i, i ^ bit) for i in range(devices)])]
    ppermute x36 -> x44, starting transfers between devices: 58 us -> 71.2 us  [swap_with(): return lax.ppermute(block, axis, [(i, i ^ bit) for i in range(devices)])]
    add x14 -> x13, other arithmetic: 5.72 us -> 2.21 us  [tree_scatter(): blocks = [k + g.astype(jnp.float32) for k, g in zip(keep, got)]]
    unnamed x32 -> x26, local copies, waits for them, and re-layouts: 8.4 us -> 5.48 us
  transfers between devices with their start and end apart: 44 -> 52, of which waited for: 28 -> 27; matrix products, arithmetic and copies ran while one was open for 10% -> 10% of each run, Pallas kernels for 0% -> 0%
where the time goes in v6:
time: 204 us
  starting transfers between devices  103 us (50%)
  waiting for transfers between devices  61.6 us (30%)
  local copies, waits for them, and re-layouts  15.2 us (7%)
  other arithmetic  11.1 us (5%)
  matrix products  8.75 us (4%)
  between operations  4.63 us (2%)
    ppermute x44, starting transfers between devices, swap_with(): return lax.ppermute(block, axis, [(i, i ^ bit) for i in range(devices)])  71.2 us
    ppermute x44, waiting for transfers between devices, swap_with(): return lax.ppermute(block, axis, [(i, i ^ bit) for i in range(devices)])  43.7 us
    ppermute x8, starting transfers between devices, from_behind(): return lax.ppermute(block, axis, route)  31.3 us
    ppermute x8, waiting for transfers between devices, from_behind(): return lax.ppermute(block, axis, route)  17.9 us
    unnamed x26, local copies, waits for them, and re-layouts  5.48 us
  transfers between devices with their start and end apart: 52, of which 27 were waited for; matrix products, arithmetic and copies ran while one was open for 10% of the time, Pallas kernels for 0%

profile of v6, /device:TPU:32, one launch (start us, length us, event | category | flops | bytes accessed | tf_op | source)
XLA Modules:
  0.0 203.8 jit_solution(6273843674392472411)
XLA Ops:
  3.1 1.4 fusion.9
  4.5 2.1 %fusion.52 = (f32[128]{0:T(128)S(1)}, f32[128,640]{1,0:T(8,128)S(1)}) fusion(bf16[128,1280]{1,0:T(8,128)(2,1)S(1)} %fusion.9, bf16[1280,640]{1,0:T(8,128)(2,1)} %param.12), kind=kOutput, calls=%fused_computation.137 | convolution fusion | flops 209796992 | bytes 2294272 | tf_op jit(solution)/shard_map/dot_general | solution.py:99
  7.0 8.2 %collective-permute-start = (bf16[128,640]{1,0:T(8,128)(2,1)S(1)}, bf16[128,640]{1,0:T(8,128)(2,1)S(1)}, u32[]{:S(2)}, u32[]{:S(2)}) collective-permute-start(bf16[128,640]{1,0:T(8,128)(2,1)S(1)} %multiply_convert_fusion.1), channel_id=1, source_target_pairs={{0,8},{1,9},{2,10},{3,11},{4,12},{5,13},{6,14},{7,15},{8,16},{9,17... | collective-permute-start | bytes 491528 | tf_op jit(solution)/shard_map/ppermute | solution.py:10
  15.2 3.4 %collective-permute-start.1 = (bf16[128,640]{1,0:T(8,128)(2,1)S(1)}, bf16[128,640]{1,0:T(8,128)(2,1)S(1)}, u32[]{:S(2)}, u32[]{:S(2)}) collective-permute-start(bf16[128,640]{1,0:T(8,128)(2,1)S(1)} %multiply_convert_fusion.1), channel_id=1, source_target_pairs={{0,4},{1,5},{2,6},{3,7},{4,8},{5,9},{6,10},{7,11},{8,12},{9,13},{1... | collective-permute-start | bytes 491528 | tf_op jit(solution)/shard_map/ppermute | solution.py:10
  21.3 8.5 %collective-permute-done.1 = bf16[128,640]{1,0:T(8,128)(2,1)S(1)} collective-permute-done((bf16[128,640]{1,0:T(8,128)(2,1)S(1)}, bf16[128,640]{1,0:T(8,128)(2,1)S(1)}, u32[]{:S(2)}, u32[]{:S(2)}) %collective-permute-start.1) | collective-permute-done | bytes 163872 | tf_op jit(solution)/shard_map/ppermute | solution.py:10
  30.0 9.4 %collective-permute-done.3 = bf16[128,640]{1,0:T(8,128)(2,1)S(1)} collective-permute-done((bf16[128,640]{1,0:T(8,128)(2,1)S(1)}, bf16[128,640]{1,0:T(8,128)(2,1)S(1)}, u32[]{:S(2)}, u32[]{:S(2)}) %collective-permute-start.3) | collective-permute-done | bytes 163872 | tf_op jit(solution)/shard_map/ppermute | solution.py:10
  42.9 1.5 collective-permute-start.13
  47.3 5.0 %collective-permute-start.17 = (f32[8,128]{1,0:T(8,128)S(1)}, f32[8,128]{1,0:T(8,128)S(1)}, u32[]{:S(2)}, u32[]{:S(2)}) collective-permute-start(f32[8,128]{1,0:T(8,128)S(1)} %add_add_fusion.5), channel_id=1, source_target_pairs={{0,80},{1,81},{2,82},{3,83},{4,84},{5,85},{6,86},{7,87},{8,88},{9,... | collective-permute-start | bytes 12296 | tf_op jit(solution)/shard_map/ppermute | solution.py:15
  53.9 2.0 collective-permute-done.16
  56.4 2.7 %collective-permute-start.19 = (f32[8,128]{1,0:T(8,128)S(1)}, f32[8,128]{1,0:T(8,128)S(1)}, u32[]{:S(2)}, u32[]{:S(2)}) collective-permute-start(f32[8,128]{1,0:T(8,128)S(1)} %add_add_fusion.4), channel_id=1, source_target_pairs={{0,32},{1,33},{2,34},{3,35},{4,36},{5,37},{6,38},{7,39},{8,40},{9,... | collective-permute-start | bytes 12296 | tf_op jit(solution)/shard_map/ppermute | solution.py:15
  59.1 3.2 %collective-permute-start.18 = (f32[8,128]{1,0:T(8,128)S(1)}, f32[8,128]{1,0:T(8,128)S(1)}, u32[]{:S(2)}, u32[]{:S(2)}) collective-permute-start(f32[8,128]{1,0:T(8,128)S(1)} %add_add_fusion.4), channel_id=1, source_target_pairs={{0,4},{1,5},{2,6},{3,7},{4,0},{5,1},{6,2},{7,3},{8,12},{9,13},{10,... | collective-permute-start | bytes 12296 | tf_op jit(solution)/shard_map/ppermute | solution.py:15
  64.6 6.2 %collective-permute-start.23 = (f32[8,128]{1,0:T(8,128)S(1)}, f32[8,128]{1,0:T(8,128)S(1)}, u32[]{:S(2)}, u32[]{:S(2)}) collective-permute-start(f32[8,128]{1,0:T(8,128)S(1)} %add_add_fusion.3), channel_id=1, source_target_pairs={{0,136},{1,137},{2,138},{3,139},{4,140},{5,141},{6,142},{7,143},{8... | collective-permute-start | bytes 12296 | tf_op jit(solution)/shard_map/ppermute | solution.py:15
  70.8 2.4 %collective-permute-start.22 = (f32[8,128]{1,0:T(8,128)S(1)}, f32[8,128]{1,0:T(8,128)S(1)}, u32[]{:S(2)}, u32[]{:S(2)}) collective-permute-start(f32[8,128]{1,0:T(8,128)S(1)} %add_add_fusion.3), channel_id=1, source_target_pairs={{0,8},{1,9},{2,10},{3,11},{4,12},{5,13},{6,14},{7,15},{8,0},{9,1},... | collective-permute-start | bytes 12296 | tf_op jit(solution)/shard_map/ppermute | solution.py:15
  75.0 3.3 %collective-permute-done.22 = f32[8,128]{1,0:T(8,128)S(1)} collective-permute-done((f32[8,128]{1,0:T(8,128)S(1)}, f32[8,128]{1,0:T(8,128)S(1)}, u32[]{:S(2)}, u32[]{:S(2)}) %collective-permute-start.22) | collective-permute-done | bytes 4128 | tf_op jit(solution)/shard_map/ppermute | solution.py:15
  84.3 1.3 collective-permute-start.25
  85.6 6.1 %collective-permute-start.26 = (bf16[128,640]{1,0:T(8,128)(2,1)}, bf16[128,640]{1,0:T(8,128)(2,1)}, u32[]{:S(2)}, u32[]{:S(2)}) collective-permute-start(bf16[128,640]{1,0:T(8,128)(2,1)} %add_convert_fusion.1), channel_id=1, source_target_pairs={{0,4},{1,5},{2,6},{3,7},{4,8},{5,9},{6,10},{7,11},{8,12},{9,13},{1... | collective-permute-start | bytes 491528 | tf_op jit(solution)/shard_map/ppermute | solution.py:10
  91.7 8.5 %collective-permute-start.27 = (bf16[128,640]{1,0:T(8,128)(2,1)}, bf16[128,640]{1,0:T(8,128)(2,1)}, u32[]{:S(2)}, u32[]{:S(2)}) collective-permute-start(bf16[128,640]{1,0:T(8,128)(2,1)} %add_convert_fusion.1), channel_id=1, source_target_pairs={{0,8},{1,9},{2,10},{3,11},{4,12},{5,13},{6,14},{7,15},{8,16},{9,17... | collective-permute-start | bytes 491528 | tf_op jit(solution)/shard_map/ppermute | solution.py:10
  108.1 1.5 multiply_reduce_fusion
  112.3 2.0 collective-permute-start.43
  116.6 2.0 collective-permute-start.31
  119.3 9.0 %collective-permute-start.6 = (f32[8,128]{1,0:T(8,128)S(1)}, f32[8,128]{1,0:T(8,128)S(1)}, u32[]{:S(2)}, u32[]{:S(2)}) collective-permute-start(f32[8,128]{1,0:T(8,128)S(1)} %fusion.65), channel_id=1, source_target_pairs={{0,16},{1,17},{2,18},{3,19},{4,20},{5,21},{6,22},{7,23},{8,24},{9,... | collective-permute-start | bytes 12296 | tf_op jit(solution)/shard_map/ppermute | solution.py:15
  128.2 1.6 collective-permute-done.6
  129.8 1.4 collective-permute-start.7
  131.3 2.2 %collective-permute-done.7 = f32[8,128]{1,0:T(8,128)S(1)} collective-permute-done((f32[8,128]{1,0:T(8,128)S(1)}, f32[8,128]{1,0:T(8,128)S(1)}, u32[]{:S(2)}, u32[]{:S(2)}) %collective-permute-start.7) | collective-permute-done | bytes 4128 | tf_op jit(solution)/shard_map/ppermute | solution.py:15
  133.4 3.1 %collective-permute-start.8 = (f32[8,128]{1,0:T(8,128)S(1)}, f32[8,128]{1,0:T(8,128)S(1)}, u32[]{:S(2)}, u32[]{:S(2)}) collective-permute-start(f32[8,128]{1,0:T(8,128)S(1)} %add.283), channel_id=1, source_target_pairs={{0,4},{1,5},{2,6},{3,7},{4,0},{5,1},{6,2},{7,3},{8,12},{9,13},{10,... | collective-permute-start | bytes 12296 | tf_op jit(solution)/shard_map/ppermute | solution.py:15
  136.5 1.6 collective-permute-done.8
  138.1 3.0 %collective-permute-start.9 = (f32[8,128]{1,0:T(8,128)S(1)}, f32[8,128]{1,0:T(8,128)S(1)}, u32[]{:S(2)}, u32[]{:S(2)}) collective-permute-start(f32[8,128]{1,0:T(8,128)S(1)} %add.284), channel_id=1, source_target_pairs={{0,32},{1,33},{2,34},{3,35},{4,36},{5,37},{6,38},{7,39},{8,40},{9,... | collective-permute-start | bytes 12296 | tf_op jit(solution)/shard_map/ppermute | solution.py:15
  141.1 2.1 %collective-permute-done.9 = f32[8,128]{1,0:T(8,128)S(1)} collective-permute-done((f32[8,128]{1,0:T(8,128)S(1)}, f32[8,128]{1,0:T(8,128)S(1)}, u32[]{:S(2)}, u32[]{:S(2)}) %collective-permute-start.9) | collective-permute-done | bytes 4128 | tf_op jit(solution)/shard_map/ppermute | solution.py:15
  143.2 6.1 %collective-permute-start.10 = (f32[8,128]{1,0:T(8,128)S(1)}, f32[8,128]{1,0:T(8,128)S(1)}, u32[]{:S(2)}, u32[]{:S(2)}) collective-permute-start(f32[8,128]{1,0:T(8,128)S(1)} %add.285), channel_id=1, source_target_pairs={{0,128},{1,129},{2,130},{3,131},{4,132},{5,133},{6,134},{7,135},{8... | collective-permute-start | bytes 12296 | tf_op jit(solution)/shard_map/ppermute | solution.py:15
  149.4 1.6 collective-permute-done.10
  151.3 7.2 %collective-permute-done.11 = f32[8,128]{1,0:T(8,128)S(1)} collective-permute-done((f32[8,128]{1,0:T(8,128)S(1)}, f32[8,128]{1,0:T(8,128)S(1)}, u32[]{:S(2)}, u32[]{:S(2)}) %collective-permute-start.11) | collective-permute-done | bytes 4128 | tf_op jit(solution)/shard_map/ppermute | solution.py:15
  160.4 1.7 convert_add_fusion.2
  162.2 2.0 collective-permute-start.32
  164.5 1.9 collective-permute-start.44
  168.1 4.0 %collective-permute-start.35 = (bf16[8,5,640]{2,0,1:T(8,128)(2,1)S(1)}, bf16[8,5,640]{2,0,1:T(8,128)(2,1)S(1)}, u32[]{:S(2)}, u32[]{:S(2)}) collective-permute-start(bf16[8,5,640]{2,0,1:T(8,128)(2,1)S(1)} %get-tuple-element.26), channel_id=1, source_target_pairs={{0,64},{1,65},{2,66},{3,67},{4,68},{5,69},{6,70},{7,71},{8,72},{9,... | collective-permute-start | bytes 153608 | tf_op jit(solution)/shard_map/ppermute | solution.py:15
  172.2 2.0 collective-permute-start.47
  174.3 1.8 collective-permute-done.34
  176.7 1.7 collective-permute-done.46
  179.3 1.9 collective-permute-done.36
  181.4 2.1 %collective-permute-done.48 = bf16[8,5,640]{2,0,1:T(8,128)(2,1)S(1)} collective-permute-done((bf16[8,5,640]{2,0,1:T(8,128)(2,1)S(1)}, bf16[8,5,640]{2,0,1:T(8,128)(2,1)S(1)}, u32[]{:S(2)}, u32[]{:S(2)}) %collective-permute-start.48) | collective-permute-done | bytes 51232 | tf_op jit(solution)/shard_map/ppermute | solution.py:15
  183.5 1.5 collective-permute-start.49
  185.1 1.7 collective-permute-done.37
  189.0 1.5 collective-permute-start.50
  190.6 1.5 collective-permute-done.38
  192.2 2.1 %collective-permute-done.50 = bf16[2,5,640]{2,0,1:T(2,128)(2,1)S(1)} collective-permute-done((bf16[2,5,640]{2,0,1:T(2,128)(2,1)S(1)}, bf16[2,5,640]{2,0,1:T(2,128)(2,1)S(1)}, u32[]{:S(2)}, u32[]{:S(2)}) %collective-permute-start.50) | collective-permute-done | bytes 12832 | tf_op jit(solution)/shard_map/ppermute | solution.py:15
  194.4 3.9 %collective-permute-start.51 = (bf16[1,5,640]{2,0,1:T(2,128)(2,1)S(1)}, bf16[1,5,640]{2,0,1:T(2,128)(2,1)S(1)}, u32[]{:S(2)}, u32[]{:S(2)}) collective-permute-start(bf16[1,5,640]{2,0,1:T(2,128)(2,1)S(1)} %dynamic-slice_convert_fusion.14), channel_id=1, source_target_pairs={{0,8},{1,9},{2,10},{3,11},{4,12},{5,13},{6,14},{7,15},{8,0},{9,1},... | collective-permute-start | bytes 19208 | tf_op jit(solution)/shard_map/ppermute | solution.py:15
  198.3 1.5 collective-permute-done.39
  200.5 1.6 collective-permute-done.51
  (180 shorter events, 45.1 us)
Async XLA Ops:
  7.0 14.2 %collective-permute-start = (bf16[128,640]{1,0:T(8,128)(2,1)S(1)}, bf16[128,640]{1,0:T(8,128)(2,1)S(1)}, u32[]{:S(2)}, u32[]{:S(2)}) collective-permute-start(bf16[128,640]{1,0:T(8,128)(2,1)S(1)} %multiply_convert_fusion.1), channel_id=1, source_target_pairs={{0,8},{1,9},{2,10},{3,11},{4,12},{5,13},{6,14},{7,15},{8,16},{9,17... | collective-permute-start | bytes 491528 | tf_op jit(solution)/shard_map/ppermute | solution.py:10
  15.2 14.5 %collective-permute-start.1 = (bf16[128,640]{1,0:T(8,128)(2,1)S(1)}, bf16[128,640]{1,0:T(8,128)(2,1)S(1)}, u32[]{:S(2)}, u32[]{:S(2)}) collective-permute-start(bf16[128,640]{1,0:T(8,128)(2,1)S(1)} %multiply_convert_fusion.1), channel_id=1, source_target_pairs={{0,4},{1,5},{2,6},{3,7},{4,8},{5,9},{6,10},{7,11},{8,12},{9,13},{1... | collective-permute-start | bytes 491528 | tf_op jit(solution)/shard_map/ppermute | solution.py:10
  18.6 11.4 %collective-permute-start.2 = (bf16[128,640]{1,0:T(8,128)(2,1)S(1)}, bf16[128,640]{1,0:T(8,128)(2,1)S(1)}, u32[]{:S(2)}, u32[]{:S(2)}) collective-permute-start(bf16[128,640]{1,0:T(8,128)(2,1)S(1)} %multiply_convert_fusion.1), channel_id=1, source_target_pairs={{4,0},{5,1},{6,2},{7,3},{8,4},{9,5},{10,6},{11,7},{12,8},{13,9},{1... | collective-permute-start | bytes 491528 | tf_op jit(solution)/shard_map/ppermute | solution.py:10
  19.9 19.5 %collective-permute-start.3 = (bf16[128,640]{1,0:T(8,128)(2,1)S(1)}, bf16[128,640]{1,0:T(8,128)(2,1)S(1)}, u32[]{:S(2)}, u32[]{:S(2)}) collective-permute-start(bf16[128,640]{1,0:T(8,128)(2,1)S(1)} %multiply_convert_fusion.1), channel_id=1, source_target_pairs={{8,0},{9,1},{10,2},{11,3},{12,4},{13,5},{14,6},{15,7},{16,8},{17,9... | collective-permute-start | bytes 491528 | tf_op jit(solution)/shard_map/ppermute | solution.py:10
  42.9 3.7 %collective-permute-start.13 = (f32[8,128]{1,0:T(8,128)S(1)}, f32[8,128]{1,0:T(8,128)S(1)}, u32[]{:S(2)}, u32[]{:S(2)}) collective-permute-start(f32[8,128]{1,0:T(8,128)S(1)} %broadcast_in_dim.13), channel_id=1, source_target_pairs={{0,2},{1,3},{2,0},{3,1},{4,6},{5,7},{6,4},{7,5},{8,10},{9,11},{10,... | collective-permute-start | bytes 12296 | tf_op jit(solution)/shard_map/ppermute | solution.py:15
  47.3 6.6 %collective-permute-start.17 = (f32[8,128]{1,0:T(8,128)S(1)}, f32[8,128]{1,0:T(8,128)S(1)}, u32[]{:S(2)}, u32[]{:S(2)}) collective-permute-start(f32[8,128]{1,0:T(8,128)S(1)} %add_add_fusion.5), channel_id=1, source_target_pairs={{0,80},{1,81},{2,82},{3,83},{4,84},{5,85},{6,86},{7,87},{8,88},{9,... | collective-permute-start | bytes 12296 | tf_op jit(solution)/shard_map/ppermute | solution.py:15
  52.3 3.6 %collective-permute-start.16 = (f32[8,128]{1,0:T(8,128)S(1)}, f32[8,128]{1,0:T(8,128)S(1)}, u32[]{:S(2)}, u32[]{:S(2)}) collective-permute-start(f32[8,128]{1,0:T(8,128)S(1)} %add_add_fusion.5), channel_id=1, source_target_pairs={{0,64},{1,65},{2,66},{3,67},{4,68},{5,69},{6,70},{7,71},{8,72},{9,... | collective-permute-start | bytes 12296 | tf_op jit(solution)/shard_map/ppermute | solution.py:15
  52.7 3.6 %collective-permute-start.15 = (f32[8,128]{1,0:T(8,128)S(1)}, f32[8,128]{1,0:T(8,128)S(1)}, u32[]{:S(2)}, u32[]{:S(2)}) collective-permute-start(f32[8,128]{1,0:T(8,128)S(1)} %add_add_fusion.5), channel_id=1, source_target_pairs={{0,16},{1,17},{2,18},{3,19},{4,20},{5,21},{6,22},{7,23},{8,24},{9,... | collective-permute-start | bytes 12296 | tf_op jit(solution)/shard_map/ppermute | solution.py:15
  56.3 8.2 %collective-permute-start.20 = (f32[8,128]{1,0:T(8,128)S(1)}, f32[8,128]{1,0:T(8,128)S(1)}, u32[]{:S(2)}, u32[]{:S(2)}) collective-permute-start(f32[8,128]{1,0:T(8,128)S(1)} %add_add_fusion.4), channel_id=1, source_target_pairs={{0,36},{1,37},{2,38},{3,39},{4,32},{5,33},{6,34},{7,35},{8,44},{9,... | collective-permute-start | bytes 12296 | tf_op jit(solution)/shard_map/ppermute | solution.py:15
  56.4 8.2 %collective-permute-start.19 = (f32[8,128]{1,0:T(8,128)S(1)}, f32[8,128]{1,0:T(8,128)S(1)}, u32[]{:S(2)}, u32[]{:S(2)}) collective-permute-start(f32[8,128]{1,0:T(8,128)S(1)} %add_add_fusion.4), channel_id=1, source_target_pairs={{0,32},{1,33},{2,34},{3,35},{4,36},{5,37},{6,38},{7,39},{8,40},{9,... | collective-permute-start | bytes 12296 | tf_op jit(solution)/shard_map/ppermute | solution.py:15
  59.1 5.5 %collective-permute-start.18 = (f32[8,128]{1,0:T(8,128)S(1)}, f32[8,128]{1,0:T(8,128)S(1)}, u32[]{:S(2)}, u32[]{:S(2)}) collective-permute-start(f32[8,128]{1,0:T(8,128)S(1)} %add_add_fusion.4), channel_id=1, source_target_pairs={{0,4},{1,5},{2,6},{3,7},{4,0},{5,1},{6,2},{7,3},{8,12},{9,13},{10,... | collective-permute-start | bytes 12296 | tf_op jit(solution)/shard_map/ppermute | solution.py:15
  64.5 9.1 %collective-permute-start.4 = (f32[8,128]{1,0:T(8,128)S(1)}, f32[8,128]{1,0:T(8,128)S(1)}, u32[]{:S(2)}, u32[]{:S(2)}) collective-permute-start(f32[8,128]{1,0:T(8,128)S(1)} %broadcast_in_dim.12), channel_id=1, source_target_pairs={{0,1},{1,0},{2,3},{3,2},{4,5},{5,4},{6,7},{7,6},{8,9},{9,8},{10,11... | collective-permute-start | bytes 12296 | tf_op jit(solution)/shard_map/ppermute | solution.py:15
  64.6 10.4 %collective-permute-start.23 = (f32[8,128]{1,0:T(8,128)S(1)}, f32[8,128]{1,0:T(8,128)S(1)}, u32[]{:S(2)}, u32[]{:S(2)}) collective-permute-start(f32[8,128]{1,0:T(8,128)S(1)} %add_add_fusion.3), channel_id=1, source_target_pairs={{0,136},{1,137},{2,138},{3,139},{4,140},{5,141},{6,142},{7,143},{8... | collective-permute-start | bytes 12296 | tf_op jit(solution)/shard_map/ppermute | solution.py:15
  70.8 7.5 %collective-permute-start.22 = (f32[8,128]{1,0:T(8,128)S(1)}, f32[8,128]{1,0:T(8,128)S(1)}, u32[]{:S(2)}, u32[]{:S(2)}) collective-permute-start(f32[8,128]{1,0:T(8,128)S(1)} %add_add_fusion.3), channel_id=1, source_target_pairs={{0,8},{1,9},{2,10},{3,11},{4,12},{5,13},{6,14},{7,15},{8,0},{9,1},... | collective-permute-start | bytes 12296 | tf_op jit(solution)/shard_map/ppermute | solution.py:15
  73.3 5.1 %collective-permute-start.21 = (f32[8,128]{1,0:T(8,128)S(1)}, f32[8,128]{1,0:T(8,128)S(1)}, u32[]{:S(2)}, u32[]{:S(2)}) collective-permute-start(f32[8,128]{1,0:T(8,128)S(1)} %add_add_fusion.3), channel_id=1, source_target_pairs={{0,128},{1,129},{2,130},{3,131},{4,132},{5,133},{6,134},{7,135},{8... | collective-permute-start | bytes 12296 | tf_op jit(solution)/shard_map/ppermute | solution.py:15
  74.3 44.4 %collective-permute-start.5 = (f32[8,128]{1,0:T(8,128)S(1)}, f32[8,128]{1,0:T(8,128)S(1)}, u32[]{:S(2)}, u32[]{:S(2)}) collective-permute-start(f32[8,128]{1,0:T(8,128)S(1)} %broadcast_add_fusion), channel_id=1, source_target_pairs={{0,2},{1,3},{2,0},{3,1},{4,6},{5,7},{6,4},{7,5},{8,10},{9,11},{10,... | collective-permute-start | bytes 12296 | tf_op jit(solution)/shard_map/ppermute | solution.py:15
  83.0 20.5 %collective-permute-start.24 = (bf16[128,640]{1,0:T(8,128)(2,1)}, bf16[128,640]{1,0:T(8,128)(2,1)}, u32[]{:S(2)}, u32[]{:S(2)}) collective-permute-start(bf16[128,640]{1,0:T(8,128)(2,1)} %add_convert_fusion.1), channel_id=1, source_target_pairs={{8,0},{9,1},{10,2},{11,3},{12,4},{13,5},{14,6},{15,7},{16,8},{17,9... | collective-permute-start | bytes 491528 | tf_op jit(solution)/shard_map/ppermute | solution.py:10
  84.3 20.4 %collective-permute-start.25 = (bf16[128,640]{1,0:T(8,128)(2,1)}, bf16[128,640]{1,0:T(8,128)(2,1)}, u32[]{:S(2)}, u32[]{:S(2)}) collective-permute-start(bf16[128,640]{1,0:T(8,128)(2,1)} %add_convert_fusion.1), channel_id=1, source_target_pairs={{4,0},{5,1},{6,2},{7,3},{8,4},{9,5},{10,6},{11,7},{12,8},{13,9},{1... | collective-permute-start | bytes 491528 | tf_op jit(solution)/shard_map/ppermute | solution.py:10
  85.6 20.6 %collective-permute-start.26 = (bf16[128,640]{1,0:T(8,128)(2,1)}, bf16[128,640]{1,0:T(8,128)(2,1)}, u32[]{:S(2)}, u32[]{:S(2)}) collective-permute-start(bf16[128,640]{1,0:T(8,128)(2,1)} %add_convert_fusion.1), channel_id=1, source_target_pairs={{0,4},{1,5},{2,6},{3,7},{4,8},{5,9},{6,10},{7,11},{8,12},{9,13},{1... | collective-permute-start | bytes 491528 | tf_op jit(solution)/shard_map/ppermute | solution.py:10
  91.7 15.5 %collective-permute-start.27 = (bf16[128,640]{1,0:T(8,128)(2,1)}, bf16[128,640]{1,0:T(8,128)(2,1)}, u32[]{:S(2)}, u32[]{:S(2)}) collective-permute-start(bf16[128,640]{1,0:T(8,128)(2,1)} %add_convert_fusion.1), channel_id=1, source_target_pairs={{0,8},{1,9},{2,10},{3,11},{4,12},{5,13},{6,14},{7,15},{8,16},{9,17... | collective-permute-start | bytes 491528 | tf_op jit(solution)/shard_map/ppermute | solution.py:10
  103.5 7.8 %collective-permute-start.41 = (bf16[64,5,640]{2,0,1:T(8,128)(2,1)S(1)}, bf16[64,5,640]{2,0,1:T(8,128)(2,1)S(1)}, u32[]{:S(2)}, u32[]{:S(2)}) collective-permute-start(bf16[64,5,640]{2,0,1:T(8,128)(2,1)S(1)} %get-tuple-element.12), channel_id=1, source_target_pairs={{0,1},{1,0},{2,3},{3,2},{4,5},{5,4},{6,7},{7,6},{8,9},{9,8},{10,11... | collective-permute-start | bytes 1228808 | tf_op jit(solution)/shard_map/ppermute | solution.py:15
  104.7 6.6 %collective-permute-start.40 = (bf16[64,5,640]{2,0,1:T(8,128)(2,1)S(1)}, bf16[64,5,640]{2,0,1:T(8,128)(2,1)S(1)}, u32[]{:S(2)}, u32[]{:S(2)}) collective-permute-start(bf16[64,5,640]{2,0,1:T(8,128)(2,1)S(1)} %get-tuple-element.11), channel_id=1, source_target_pairs={{0,1},{1,0},{2,3},{3,2},{4,5},{5,4},{6,7},{7,6},{8,9},{9,8},{10,11... | collective-permute-start | bytes 1228808 | tf_op jit(solution)/shard_map/ppermute | solution.py:15
  112.3 48.0 %collective-permute-start.43 = (bf16[32,5,640]{2,0,1:T(8,128)(2,1)}, bf16[32,5,640]{2,0,1:T(8,128)(2,1)}, u32[]{:S(2)}, u32[]{:S(2)}) collective-permute-start(bf16[32,5,640]{2,0,1:T(8,128)(2,1)} %get-tuple-element.16), channel_id=1, source_target_pairs={{0,2},{1,3},{2,0},{3,1},{4,6},{5,7},{6,4},{7,5},{8,10},{9,11},{10,... | collective-permute-start | bytes 614408 | tf_op jit(solution)/shard_map/ppermute | solution.py:15
  114.3 46.0 %collective-permute-start.42 = (bf16[32,5,640]{2,0,1:T(8,128)(2,1)S(1)}, bf16[32,5,640]{2,0,1:T(8,128)(2,1)}, u32[]{:S(2)}, u32[]{:S(2)}) collective-permute-start(bf16[32,5,640]{2,0,1:T(8,128)(2,1)S(1)} %get-tuple-element.15), channel_id=1, source_target_pairs={{0,2},{1,3},{2,0},{3,1},{4,6},{5,7},{6,4},{7,5},{8,10},{9,11},{10,... | collective-permute-start | bytes 614408 | tf_op jit(solution)/shard_map/ppermute | solution.py:15
  116.6 43.8 %collective-permute-start.31 = (bf16[32,5,640]{2,0,1:T(8,128)(2,1)}, bf16[32,5,640]{2,0,1:T(8,128)(2,1)}, u32[]{:S(2)}, u32[]{:S(2)}) collective-permute-start(bf16[32,5,640]{2,0,1:T(8,128)(2,1)} %get-tuple-element.18), channel_id=1, source_target_pairs={{0,2},{1,3},{2,0},{3,1},{4,6},{5,7},{6,4},{7,5},{8,10},{9,11},{10,... | collective-permute-start | bytes 614408 | tf_op jit(solution)/shard_map/ppermute | solution.py:15
  118.6 41.8 %collective-permute-start.30 = (bf16[32,5,640]{2,0,1:T(8,128)(2,1)}, bf16[32,5,640]{2,0,1:T(8,128)(2,1)}, u32[]{:S(2)}, u32[]{:S(2)}) collective-permute-start(bf16[32,5,640]{2,0,1:T(8,128)(2,1)} %get-tuple-element.17), channel_id=1, source_target_pairs={{0,2},{1,3},{2,0},{3,1},{4,6},{5,7},{6,4},{7,5},{8,10},{9,11},{10,... | collective-permute-start | bytes 614408 | tf_op jit(solution)/shard_map/ppermute | solution.py:15
  119.3 10.6 %collective-permute-start.6 = (f32[8,128]{1,0:T(8,128)S(1)}, f32[8,128]{1,0:T(8,128)S(1)}, u32[]{:S(2)}, u32[]{:S(2)}) collective-permute-start(f32[8,128]{1,0:T(8,128)S(1)} %fusion.65), channel_id=1, source_target_pairs={{0,16},{1,17},{2,18},{3,19},{4,20},{5,21},{6,22},{7,23},{8,24},{9,... | collective-permute-start | bytes 12296 | tf_op jit(solution)/shard_map/ppermute | solution.py:15
  129.8 3.6 %collective-permute-start.7 = (f32[8,128]{1,0:T(8,128)S(1)}, f32[8,128]{1,0:T(8,128)S(1)}, u32[]{:S(2)}, u32[]{:S(2)}) collective-permute-start(f32[8,128]{1,0:T(8,128)S(1)} %add.282), channel_id=1, source_target_pairs={{0,64},{1,65},{2,66},{3,67},{4,68},{5,69},{6,70},{7,71},{8,72},{9,... | collective-permute-start | bytes 12296 | tf_op jit(solution)/shard_map/ppermute | solution.py:15
  133.4 4.7 %collective-permute-start.8 = (f32[8,128]{1,0:T(8,128)S(1)}, f32[8,128]{1,0:T(8,128)S(1)}, u32[]{:S(2)}, u32[]{:S(2)}) collective-permute-start(f32[8,128]{1,0:T(8,128)S(1)} %add.283), channel_id=1, source_target_pairs={{0,4},{1,5},{2,6},{3,7},{4,0},{5,1},{6,2},{7,3},{8,12},{9,13},{10,... | collective-permute-start | bytes 12296 | tf_op jit(solution)/shard_map/ppermute | solution.py:15
  138.1 5.1 %collective-permute-start.9 = (f32[8,128]{1,0:T(8,128)S(1)}, f32[8,128]{1,0:T(8,128)S(1)}, u32[]{:S(2)}, u32[]{:S(2)}) collective-permute-start(f32[8,128]{1,0:T(8,128)S(1)} %add.284), channel_id=1, source_target_pairs={{0,32},{1,33},{2,34},{3,35},{4,36},{5,37},{6,38},{7,39},{8,40},{9,... | collective-permute-start | bytes 12296 | tf_op jit(solution)/shard_map/ppermute | solution.py:15
  143.2 7.7 %collective-permute-start.10 = (f32[8,128]{1,0:T(8,128)S(1)}, f32[8,128]{1,0:T(8,128)S(1)}, u32[]{:S(2)}, u32[]{:S(2)}) collective-permute-start(f32[8,128]{1,0:T(8,128)S(1)} %add.285), channel_id=1, source_target_pairs={{0,128},{1,129},{2,130},{3,131},{4,132},{5,133},{6,134},{7,135},{8... | collective-permute-start | bytes 12296 | tf_op jit(solution)/shard_map/ppermute | solution.py:15
  150.9 7.5 %collective-permute-start.11 = (f32[8,128]{1,0:T(8,128)S(1)}, f32[8,128]{1,0:T(8,128)S(1)}, u32[]{:S(2)}, u32[]{:S(2)}) collective-permute-start(f32[8,128]{1,0:T(8,128)S(1)} %add.286), channel_id=1, source_target_pairs={{0,8},{1,9},{2,10},{3,11},{4,12},{5,13},{6,14},{7,15},{8,0},{9,1},... | collective-permute-start | bytes 12296 | tf_op jit(solution)/shard_map/ppermute | solution.py:15
  162.1 4.7 %collective-permute-start.33 = (bf16[16,5,640]{2,0,1:T(8,128)(2,1)S(1)}, bf16[16,5,640]{2,0,1:T(8,128)(2,1)S(1)}, u32[]{:S(2)}, u32[]{:S(2)}) collective-permute-start(bf16[16,5,640]{2,0,1:T(8,128)(2,1)S(1)} %get-tuple-element.22), channel_id=1, source_target_pairs={{0,16},{1,17},{2,18},{3,19},{4,20},{5,21},{6,22},{7,23},{8,24},{9,... | collective-permute-start | bytes 307208 | tf_op jit(solution)/shard_map/ppermute | solution.py:15
  162.2 5.7 %collective-permute-start.32 = (bf16[16,5,640]{2,0,1:T(8,128)(2,1)S(1)}, bf16[16,5,640]{2,0,1:T(8,128)(2,1)S(1)}, u32[]{:S(2)}, u32[]{:S(2)}) collective-permute-start(bf16[16,5,640]{2,0,1:T(8,128)(2,1)S(1)} %get-tuple-element.21), channel_id=1, source_target_pairs={{0,16},{1,17},{2,18},{3,19},{4,20},{5,21},{6,22},{7,23},{8,24},{9,... | collective-permute-start | bytes 307208 | tf_op jit(solution)/shard_map/ppermute | solution.py:15
  164.3 7.8 %collective-permute-start.45 = (bf16[16,5,640]{2,0,1:T(8,128)(2,1)S(1)}, bf16[16,5,640]{2,0,1:T(8,128)(2,1)S(1)}, u32[]{:S(2)}, u32[]{:S(2)}) collective-permute-start(bf16[16,5,640]{2,0,1:T(8,128)(2,1)S(1)} %get-tuple-element.20), channel_id=1, source_target_pairs={{0,16},{1,17},{2,18},{3,19},{4,20},{5,21},{6,22},{7,23},{8,24},{9,... | collective-permute-start | bytes 307208 | tf_op jit(solution)/shard_map/ppermute | solution.py:15
  164.5 7.6 %collective-permute-start.44 = (bf16[16,5,640]{2,0,1:T(8,128)(2,1)S(1)}, bf16[16,5,640]{2,0,1:T(8,128)(2,1)S(1)}, u32[]{:S(2)}, u32[]{:S(2)}) collective-permute-start(bf16[16,5,640]{2,0,1:T(8,128)(2,1)S(1)} %get-tuple-element.19), channel_id=1, source_target_pairs={{0,16},{1,17},{2,18},{3,19},{4,20},{5,21},{6,22},{7,23},{8,24},{9,... | collective-permute-start | bytes 307208 | tf_op jit(solution)/shard_map/ppermute | solution.py:15
  168.1 6.3 %collective-permute-start.35 = (bf16[8,5,640]{2,0,1:T(8,128)(2,1)S(1)}, bf16[8,5,640]{2,0,1:T(8,128)(2,1)S(1)}, u32[]{:S(2)}, u32[]{:S(2)}) collective-permute-start(bf16[8,5,640]{2,0,1:T(8,128)(2,1)S(1)} %get-tuple-element.26), channel_id=1, source_target_pairs={{0,64},{1,65},{2,66},{3,67},{4,68},{5,69},{6,70},{7,71},{8,72},{9,... | collective-permute-start | bytes 153608 | tf_op jit(solution)/shard_map/ppermute | solution.py:15
  172.0 4.1 %collective-permute-start.34 = (bf16[8,5,640]{2,0,1:T(8,128)(2,1)S(1)}, bf16[8,5,640]{2,0,1:T(8,128)(2,1)S(1)}, u32[]{:S(2)}, u32[]{:S(2)}) collective-permute-start(bf16[8,5,640]{2,0,1:T(8,128)(2,1)S(1)} %get-tuple-element.25), channel_id=1, source_target_pairs={{0,64},{1,65},{2,66},{3,67},{4,68},{5,69},{6,70},{7,71},{8,72},{9,... | collective-permute-start | bytes 153608 | tf_op jit(solution)/shard_map/ppermute | solution.py:15
  172.2 4.5 %collective-permute-start.47 = (bf16[8,5,640]{2,0,1:T(8,128)(2,1)S(1)}, bf16[8,5,640]{2,0,1:T(8,128)(2,1)S(1)}, u32[]{:S(2)}, u32[]{:S(2)}) collective-permute-start(bf16[8,5,640]{2,0,1:T(8,128)(2,1)S(1)} %get-tuple-element.24), channel_id=1, source_target_pairs={{0,64},{1,65},{2,66},{3,67},{4,68},{5,69},{6,70},{7,71},{8,72},{9,... | collective-permute-start | bytes 153608 | tf_op jit(solution)/shard_map/ppermute | solution.py:15
  174.2 4.1 %collective-permute-start.46 = (bf16[8,5,640]{2,0,1:T(8,128)(2,1)S(1)}, bf16[8,5,640]{2,0,1:T(8,128)(2,1)S(1)}, u32[]{:S(2)}, u32[]{:S(2)}) collective-permute-start(bf16[8,5,640]{2,0,1:T(8,128)(2,1)S(1)} %get-tuple-element.23), channel_id=1, source_target_pairs={{0,64},{1,65},{2,66},{3,67},{4,68},{5,69},{6,70},{7,71},{8,72},{9,... | collective-permute-start | bytes 153608 | tf_op jit(solution)/shard_map/ppermute | solution.py:15
  176.2 5.1 %collective-permute-start.36 = (bf16[8,5,640]{2,0,1:T(8,128)(2,1)S(1)}, bf16[8,5,640]{2,0,1:T(8,128)(2,1)S(1)}, u32[]{:S(2)}, u32[]{:S(2)}) collective-permute-start(bf16[8,5,640]{2,0,1:T(8,128)(2,1)S(1)} %dynamic-slice_convert_fusion.9), channel_id=1, source_target_pairs={{0,4},{1,5},{2,6},{3,7},{4,0},{5,1},{6,2},{7,3},{8,12},{9,13},{10,... | collective-permute-start | bytes 153608 | tf_op jit(solution)/shard_map/ppermute | solution.py:15
  178.4 5.1 %collective-permute-start.48 = (bf16[8,5,640]{2,0,1:T(8,128)(2,1)S(1)}, bf16[8,5,640]{2,0,1:T(8,128)(2,1)S(1)}, u32[]{:S(2)}, u32[]{:S(2)}) collective-permute-start(bf16[8,5,640]{2,0,1:T(8,128)(2,1)S(1)} %dynamic-slice_convert_fusion.8), channel_id=1, source_target_pairs={{0,4},{1,5},{2,6},{3,7},{4,0},{5,1},{6,2},{7,3},{8,12},{9,13},{10,... | collective-permute-start | bytes 153608 | tf_op jit(solution)/shard_map/ppermute | solution.py:15
  181.3 5.4 %collective-permute-start.37 = (bf16[4,5,640]{2,0,1:T(4,128)(2,1)S(1)}, bf16[4,5,640]{2,0,1:T(4,128)(2,1)S(1)}, u32[]{:S(2)}, u32[]{:S(2)}) collective-permute-start(bf16[4,5,640]{2,0,1:T(4,128)(2,1)S(1)} %dynamic-slice_convert_fusion.11), channel_id=1, source_target_pairs={{0,32},{1,33},{2,34},{3,35},{4,36},{5,37},{6,38},{7,39},{8,40},{9,... | collective-permute-start | bytes 76808 | tf_op jit(solution)/shard_map/ppermute | solution.py:15
  183.5 5.4 %collective-permute-start.49 = (bf16[4,5,640]{2,0,1:T(4,128)(2,1)S(1)}, bf16[4,5,640]{2,0,1:T(4,128)(2,1)S(1)}, u32[]{:S(2)}, u32[]{:S(2)}) collective-permute-start(bf16[4,5,640]{2,0,1:T(4,128)(2,1)S(1)} %dynamic-slice_convert_fusion.10), channel_id=1, source_target_pairs={{0,32},{1,33},{2,34},{3,35},{4,36},{5,37},{6,38},{7,39},{8,40},{9,... | collective-permute-start | bytes 76808 | tf_op jit(solution)/shard_map/ppermute | solution.py:15
  186.8 5.3 %collective-permute-start.38 = (bf16[2,5,640]{2,0,1:T(2,128)(2,1)S(1)}, bf16[2,5,640]{2,0,1:T(2,128)(2,1)S(1)}, u32[]{:S(2)}, u32[]{:S(2)}) collective-permute-start(bf16[2,5,640]{2,0,1:T(2,128)(2,1)S(1)} %dynamic-slice_convert_fusion.13), channel_id=1, source_target_pairs={{0,128},{1,129},{2,130},{3,131},{4,132},{5,133},{6,134},{7,135},{8... | collective-permute-start | bytes 38408 | tf_op jit(solution)/shard_map/ppermute | solution.py:15
  189.0 5.3 %collective-permute-start.50 = (bf16[2,5,640]{2,0,1:T(2,128)(2,1)S(1)}, bf16[2,5,640]{2,0,1:T(2,128)(2,1)S(1)}, u32[]{:S(2)}, u32[]{:S(2)}) collective-permute-start(bf16[2,5,640]{2,0,1:T(2,128)(2,1)S(1)} %dynamic-slice_convert_fusion.12), channel_id=1, source_target_pairs={{0,128},{1,129},{2,130},{3,131},{4,132},{5,133},{6,134},{7,135},{8... | collective-permute-start | bytes 38408 | tf_op jit(solution)/shard_map/ppermute | solution.py:15
  192.1 7.7 %collective-permute-start.39 = (bf16[1,5,640]{2,0,1:T(2,128)(2,1)S(1)}, bf16[1,5,640]{2,0,1:T(2,128)(2,1)S(1)}, u32[]{:S(2)}, u32[]{:S(2)}) collective-permute-start(bf16[1,5,640]{2,0,1:T(2,128)(2,1)S(1)} %dynamic-slice_convert_fusion.15), channel_id=1, source_target_pairs={{0,8},{1,9},{2,10},{3,11},{4,12},{5,13},{6,14},{7,15},{8,0},{9,1},... | collective-permute-start | bytes 19208 | tf_op jit(solution)/shard_map/ppermute | solution.py:15
  194.4 7.7 %collective-permute-start.51 = (bf16[1,5,640]{2,0,1:T(2,128)(2,1)S(1)}, bf16[1,5,640]{2,0,1:T(2,128)(2,1)S(1)}, u32[]{:S(2)}, u32[]{:S(2)}) collective-permute-start(bf16[1,5,640]{2,0,1:T(2,128)(2,1)S(1)} %dynamic-slice_convert_fusion.14), channel_id=1, source_target_pairs={{0,8},{1,9},{2,10},{3,11},{4,12},{5,13},{6,14},{7,15},{8,0},{9,1},... | collective-permute-start | bytes 19208 | tf_op jit(solution)/shard_map/ppermute | solution.py:15
  (13 other events, 99.7 us)

commit v7 on v6

--- a/solution.py
+++ b/solution.py
@@ -7,7 +7,7 @@
 def from_behind(block, axis, distance):
     devices = range(lax.axis_size(axis))
     route = [(i - distance, i) for i in devices if i - distance in devices]
-    return lax.ppermute(block, axis, route)
+    return jnp.concatenate(lax.ppermute(jnp.split(block, 2, 0), axis, route), 0)
 
 
 def swap_with(block, axis, bit):

time: 204 us -> 250 us (1.23)
  starting transfers between devices: 103 us -> 139 us
  waiting for transfers between devices: 61.6 us -> 67.8 us
  other arithmetic: 11.1 us -> 14.7 us
    ppermute x8 -> x16, starting transfers between devices: 31.3 us -> 53.7 us  [from_behind(): return jnp.concatenate(lax.ppermute(jnp.split(block, 2, 0), axis, route), 0)]
    ppermute x44, starting transfers between devices: 71.2 us -> 84.9 us  [swap_with(): return lax.ppermute(block, axis, [(i, i ^ bit) for i in range(devices)])]
    ppermute x8 -> x16, waiting for transfers between devices: 17.9 us -> 23.9 us  [from_behind(): return jnp.concatenate(lax.ppermute(jnp.split(block, 2, 0), axis, route), 0)]
    unnamed x26 -> x42, local copies, waits for them, and re-layouts: 5.48 us -> 4.77 us
  transfers between devices with their start and end apart: 52 -> 60, of which waited for: 27 -> 32; matrix products, arithmetic and copies ran while one was open for 10% -> 8% of each run, Pallas kernels for 0% -> 0%
where the time goes in v7:
time: 250 us; the launch traced here: 249 us
  starting transfers between devices  139 us (56%)
  waiting for transfers between devices  67.8 us (27%)
  other arithmetic  14.7 us (6%)
  local copies, waits for them, and re-layouts  13.3 us (5%)
  matrix products  9.4 us (4%)
  between operations  4.81 us (2%)
    ppermute x44, starting transfers between devices, swap_with(): return lax.ppermute(block, axis, [(i, i ^ bit) for i in range(devices)])  84.9 us
    ppermute x16, starting transfers between devices, from_behind(): return jnp.concatenate(lax.ppermute(jnp.split(block, 2, 0), axis, route), 0)  53.7 us
    ppermute x44, waiting for transfers between devices, swap_with(): return lax.ppermute(block, axis, [(i, i ^ bit) for i in range(devices)])  43.8 us
    ppermute x16, waiting for transfers between devices, from_behind(): return jnp.concatenate(lax.ppermute(jnp.split(block, 2, 0), axis, route), 0)  23.9 us
  transfers between devices with their start and end apart: 60, of which 32 were waited for; matrix products, arithmetic and copies ran while one was open for 8% of the time, Pallas kernels for 0%

profile of v7, /device:TPU:32, one launch (start us, length us, event | category | flops | bytes accessed | tf_op | source)
XLA Modules:
  0.0 248.6 jit_solution(15486651040979000980)
XLA Ops:
  4.5 2.1 fusion.62
  7.6 8.2 %collective-permute-start.1 = (bf16[64,640]{1,0:T(8,128)(2,1)S(1)}, bf16[64,640]{1,0:T(8,128)(2,1)S(1)}, u32[]{:S(2)}, u32[]{:S(2)}) collective-permute-start(bf16[64,640]{1,0:T(8,128)(2,1)S(1)} %get-tuple-element.26), channel_id=1, source_target_pairs={{0,8},{1,9},{2,10},{3,11},{4,12},{5,13},{6,14},{7,15},{8,16},{9,17... | collective-permute-start | bytes 245768 | tf_op jit(solution)/shard_map/ppermute | solution.py:10
  15.8 2.5 collective-permute-start
  18.3 5.2 %collective-permute-start.3 = (bf16[64,640]{1,0:T(8,128)(2,1)S(1)}, bf16[64,640]{1,0:T(8,128)(2,1)S(1)}, u32[]{:S(2)}, u32[]{:S(2)}) collective-permute-start(bf16[64,640]{1,0:T(8,128)(2,1)S(1)} %get-tuple-element.26), channel_id=1, source_target_pairs={{0,4},{1,5},{2,6},{3,7},{4,8},{5,9},{6,10},{7,11},{8,12},{9,13},{1... | collective-permute-start | bytes 245768 | tf_op jit(solution)/shard_map/ppermute | solution.py:10
  23.4 5.5 %collective-permute-start.2 = (bf16[64,640]{1,0:T(8,128)(2,1)S(1)}, bf16[64,640]{1,0:T(8,128)(2,1)S(1)}, u32[]{:S(2)}, u32[]{:S(2)}) collective-permute-start(bf16[64,640]{1,0:T(8,128)(2,1)S(1)} %get-tuple-element.25), channel_id=1, source_target_pairs={{0,4},{1,5},{2,6},{3,7},{4,8},{5,9},{6,10},{7,11},{8,12},{9,13},{1... | collective-permute-start | bytes 245768 | tf_op jit(solution)/shard_map/ppermute | solution.py:10
  34.5 3.4 %collective-permute-done.5 = bf16[64,640]{1,0:T(8,128)(2,1)S(1)} collective-permute-done((bf16[64,640]{1,0:T(8,128)(2,1)S(1)}, bf16[64,640]{1,0:T(8,128)(2,1)S(1)}, u32[]{:S(2)}, u32[]{:S(2)}) %collective-permute-start.5) | collective-permute-done | bytes 81952 | tf_op jit(solution)/shard_map/ppermute | solution.py:10
  38.8 9.6 %collective-permute-done.7 = bf16[64,640]{1,0:T(8,128)(2,1)S(1)} collective-permute-done((bf16[64,640]{1,0:T(8,128)(2,1)S(1)}, bf16[64,640]{1,0:T(8,128)(2,1)S(1)}, u32[]{:S(2)}, u32[]{:S(2)}) %collective-permute-start.7) | collective-permute-done | bytes 81952 | tf_op jit(solution)/shard_map/ppermute | solution.py:10
  57.2 4.9 %collective-permute-start.21 = (f32[8,128]{1,0:T(8,128)S(1)}, f32[8,128]{1,0:T(8,128)S(1)}, u32[]{:S(2)}, u32[]{:S(2)}) collective-permute-start(f32[8,128]{1,0:T(8,128)S(1)} %add_add_fusion.5), channel_id=1, source_target_pairs={{0,80},{1,81},{2,82},{3,83},{4,84},{5,85},{6,86},{7,87},{8,88},{9,... | collective-permute-start | bytes 12296 | tf_op jit(solution)/shard_map/ppermute | solution.py:15
  67.0 3.6 %collective-permute-start.24 = (f32[8,128]{1,0:T(8,128)S(1)}, f32[8,128]{1,0:T(8,128)S(1)}, u32[]{:S(2)}, u32[]{:S(2)}) collective-permute-start(f32[8,128]{1,0:T(8,128)S(1)} %add_add_fusion.4), channel_id=1, source_target_pairs={{0,36},{1,37},{2,38},{3,39},{4,32},{5,33},{6,34},{7,35},{8,44},{9,... | collective-permute-start | bytes 12296 | tf_op jit(solution)/shard_map/ppermute | solution.py:15
  70.6 1.6 collective-permute-start.23
  73.9 1.8 collective-permute-done.23
  76.6 8.9 %collective-permute-start.27 = (f32[8,128]{1,0:T(8,128)S(1)}, f32[8,128]{1,0:T(8,128)S(1)}, u32[]{:S(2)}, u32[]{:S(2)}) collective-permute-start(f32[8,128]{1,0:T(8,128)S(1)} %add_add_fusion.3), channel_id=1, source_target_pairs={{0,136},{1,137},{2,138},{3,139},{4,140},{5,141},{6,142},{7,143},{8... | collective-permute-start | bytes 12296 | tf_op jit(solution)/shard_map/ppermute | solution.py:15
  85.6 5.5 %collective-permute-start.26 = (f32[8,128]{1,0:T(8,128)S(1)}, f32[8,128]{1,0:T(8,128)S(1)}, u32[]{:S(2)}, u32[]{:S(2)}) collective-permute-start(f32[8,128]{1,0:T(8,128)S(1)} %add_add_fusion.3), channel_id=1, source_target_pairs={{0,8},{1,9},{2,10},{3,11},{4,12},{5,13},{6,14},{7,15},{8,0},{9,1},... | collective-permute-start | bytes 12296 | tf_op jit(solution)/shard_map/ppermute | solution.py:15
  91.1 3.1 %collective-permute-start.25 = (f32[8,128]{1,0:T(8,128)S(1)}, f32[8,128]{1,0:T(8,128)S(1)}, u32[]{:S(2)}, u32[]{:S(2)}) collective-permute-start(f32[8,128]{1,0:T(8,128)S(1)} %add_add_fusion.3), channel_id=1, source_target_pairs={{0,128},{1,129},{2,130},{3,131},{4,132},{5,133},{6,134},{7,135},{8... | collective-permute-start | bytes 12296 | tf_op jit(solution)/shard_map/ppermute | solution.py:15
  112.4 2.9 %collective-permute-done.29 = bf16[64,640]{1,0:T(8,128)(2,1)} collective-permute-done((bf16[64,640]{1,0:T(8,128)(2,1)}, bf16[64,640]{1,0:T(8,128)(2,1)}, u32[]{:S(2)}, u32[]{:S(2)}) %collective-permute-start.29) | collective-permute-done | bytes 81952 | tf_op jit(solution)/shard_map/ppermute | solution.py:10
  115.3 3.3 %collective-permute-start.33 = (bf16[64,640]{1,0:T(8,128)(2,1)}, bf16[64,640]{1,0:T(8,128)(2,1)S(1)}, u32[]{:S(2)}, u32[]{:S(2)}) collective-permute-start(bf16[64,640]{1,0:T(8,128)(2,1)} %get-tuple-element.24), channel_id=1, source_target_pairs={{0,4},{1,5},{2,6},{3,7},{4,8},{5,9},{6,10},{7,11},{8,12},{9,13},{1... | collective-permute-start | bytes 245768 | tf_op jit(solution)/shard_map/ppermute | solution.py:10
  118.6 5.1 %collective-permute-done.28 = bf16[64,640]{1,0:T(8,128)(2,1)} collective-permute-done((bf16[64,640]{1,0:T(8,128)(2,1)S(1)}, bf16[64,640]{1,0:T(8,128)(2,1)}, u32[]{:S(2)}, u32[]{:S(2)}) %collective-permute-start.28) | collective-permute-done | bytes 81952 | tf_op jit(solution)/shard_map/ppermute | solution.py:10
  123.7 1.6 collective-permute-start.32
  126.3 9.3 %collective-permute-start.35 = (bf16[64,640]{1,0:T(8,128)(2,1)}, bf16[64,640]{1,0:T(8,128)(2,1)S(1)}, u32[]{:S(2)}, u32[]{:S(2)}) collective-permute-start(bf16[64,640]{1,0:T(8,128)(2,1)} %get-tuple-element.24), channel_id=1, source_target_pairs={{0,8},{1,9},{2,10},{3,11},{4,12},{5,13},{6,14},{7,15},{8,16},{9,17... | collective-permute-start | bytes 245768 | tf_op jit(solution)/shard_map/ppermute | solution.py:10
  135.6 7.8 %collective-permute-start.34 = (bf16[64,640]{1,0:T(8,128)(2,1)S(1)}, bf16[64,640]{1,0:T(8,128)(2,1)S(1)}, u32[]{:S(2)}, u32[]{:S(2)}) collective-permute-start(bf16[64,640]{1,0:T(8,128)(2,1)S(1)} %get-tuple-element.23), channel_id=1, source_target_pairs={{0,8},{1,9},{2,10},{3,11},{4,12},{5,13},{6,14},{7,15},{8,16},{9,17... | collective-permute-start | bytes 245768 | tf_op jit(solution)/shard_map/ppermute | solution.py:10
  146.3 1.5 multiply_reduce_fusion
  153.6 2.3 collective-permute-done.9
  157.3 3.5 %collective-permute-start.10 = (f32[8,128]{1,0:T(8,128)S(1)}, f32[8,128]{1,0:T(8,128)S(1)}, u32[]{:S(2)}, u32[]{:S(2)}) collective-permute-start(f32[8,128]{1,0:T(8,128)S(1)} %fusion.75), channel_id=1, source_target_pairs={{0,16},{1,17},{2,18},{3,19},{4,20},{5,21},{6,22},{7,23},{8,24},{9,... | collective-permute-start | bytes 12296 | tf_op jit(solution)/shard_map/ppermute | solution.py:15
  160.7 1.6 collective-permute-done.10
  162.3 6.3 %collective-permute-start.11 = (f32[8,128]{1,0:T(8,128)S(1)}, f32[8,128]{1,0:T(8,128)S(1)}, u32[]{:S(2)}, u32[]{:S(2)}) collective-permute-start(f32[8,128]{1,0:T(8,128)S(1)} %add.282), channel_id=1, source_target_pairs={{0,64},{1,65},{2,66},{3,67},{4,68},{5,69},{6,70},{7,71},{8,72},{9,... | collective-permute-start | bytes 12296 | tf_op jit(solution)/shard_map/ppermute | solution.py:15
  168.6 1.6 collective-permute-done.11
  170.2 1.9 collective-permute-start.12
  172.1 2.6 %collective-permute-done.12 = f32[8,128]{1,0:T(8,128)S(1)} collective-permute-done((f32[8,128]{1,0:T(8,128)S(1)}, f32[8,128]{1,0:T(8,128)S(1)}, u32[]{:S(2)}, u32[]{:S(2)}) %collective-permute-start.12) | collective-permute-done | bytes 4128 | tf_op jit(solution)/shard_map/ppermute | solution.py:15
  175.9 3.9 %collective-permute-done.13 = f32[8,128]{1,0:T(8,128)S(1)} collective-permute-done((f32[8,128]{1,0:T(8,128)S(1)}, f32[8,128]{1,0:T(8,128)S(1)}, u32[]{:S(2)}, u32[]{:S(2)}) %collective-permute-start.13) | collective-permute-done | bytes 4128 | tf_op jit(solution)/shard_map/ppermute | solution.py:15
  179.8 4.5 %collective-permute-start.14 = (f32[8,128]{1,0:T(8,128)S(1)}, f32[8,128]{1,0:T(8,128)S(1)}, u32[]{:S(2)}, u32[]{:S(2)}) collective-permute-start(f32[8,128]{1,0:T(8,128)S(1)} %add.285), channel_id=1, source_target_pairs={{0,128},{1,129},{2,130},{3,131},{4,132},{5,133},{6,134},{7,135},{8... | collective-permute-start | bytes 12296 | tf_op jit(solution)/shard_map/ppermute | solution.py:15
  184.3 1.6 collective-permute-done.14
  186.3 7.1 %collective-permute-done.15 = f32[8,128]{1,0:T(8,128)S(1)} collective-permute-done((f32[8,128]{1,0:T(8,128)S(1)}, f32[8,128]{1,0:T(8,128)S(1)}, u32[]{:S(2)}, u32[]{:S(2)}) %collective-permute-start.15) | collective-permute-done | bytes 4128 | tf_op jit(solution)/shard_map/ppermute | solution.py:15
  195.3 2.7 %convert_add_fusion = (f32[128,5,640]{2,0,1:T(8,128)S(1)}, f32[128,5,640]{2,0,1:T(8,128)S(1)}) fusion(f32[256,5,640]{2,0,1:T(8,128)} %copy-done.3, s32[]{:T(128)S(6)} %select_n.123, bf16[64,5,640]{2,0,1:T(8,128)(2,1)} %collective-permute-done.49, bf16[64,5,640]{2,0,1:T(8,128)(2,1)} %collective-permute-done.48, ...), kind=kLoop, calls=%fused_computation.4 | loop fusion | flops 4096000 | bytes 8192004 | tf_op jit(solution)/shard_map/add | solution.py:67
  198.7 1.6 collective-permute-start.38
  200.9 1.6 collective-permute-start.50
  202.5 1.5 collective-permute-done.39
  204.0 2.2 collective-permute-done.38
  206.7 1.7 collective-permute-start.40
  208.5 2.1 collective-permute-done.50
  211.1 1.7 collective-permute-start.52
  222.4 1.9 collective-permute-start.56
  224.4 1.6 collective-permute-start.45
  226.0 1.6 collective-permute-done.56
  227.6 2.4 collective-permute-start.57
  230.1 3.7 %collective-permute-start.46 = (bf16[2,5,640]{2,0,1:T(2,128)(2,1)S(1)}, bf16[2,5,640]{2,0,1:T(2,128)(2,1)S(1)}, u32[]{:S(2)}, u32[]{:S(2)}) collective-permute-start(bf16[2,5,640]{2,0,1:T(2,128)(2,1)S(1)} %dynamic-slice_convert_fusion.13), channel_id=1, source_target_pairs={{0,128},{1,129},{2,130},{3,131},{4,132},{5,133},{6,134},{7,135},{8... | collective-permute-start | bytes 38408 | tf_op jit(solution)/shard_map/ppermute | solution.py:15
  233.8 3.4 %collective-permute-start.58 = (bf16[2,5,640]{2,0,1:T(2,128)(2,1)S(1)}, bf16[2,5,640]{2,0,1:T(2,128)(2,1)S(1)}, u32[]{:S(2)}, u32[]{:S(2)}) collective-permute-start(bf16[2,5,640]{2,0,1:T(2,128)(2,1)S(1)} %dynamic-slice_convert_fusion.12), channel_id=1, source_target_pairs={{0,128},{1,129},{2,130},{3,131},{4,132},{5,133},{6,134},{7,135},{8... | collective-permute-start | bytes 38408 | tf_op jit(solution)/shard_map/ppermute | solution.py:15
  239.1 4.3 %collective-permute-start.59 = (bf16[1,5,640]{2,0,1:T(2,128)(2,1)S(1)}, bf16[1,5,640]{2,0,1:T(2,128)(2,1)S(1)}, u32[]{:S(2)}, u32[]{:S(2)}) collective-permute-start(bf16[1,5,640]{2,0,1:T(2,128)(2,1)S(1)} %dynamic-slice_convert_fusion.14), channel_id=1, source_target_pairs={{0,8},{1,9},{2,10},{3,11},{4,12},{5,13},{6,14},{7,15},{8,0},{9,1},... | collective-permute-start | bytes 19208 | tf_op jit(solution)/shard_map/ppermute | solution.py:15
  243.4 1.5 collective-permute-done.47
  (220 shorter events, 73.8 us)
Async XLA Ops:
  7.6 22.7 %collective-permute-start.1 = (bf16[64,640]{1,0:T(8,128)(2,1)S(1)}, bf16[64,640]{1,0:T(8,128)(2,1)S(1)}, u32[]{:S(2)}, u32[]{:S(2)}) collective-permute-start(bf16[64,640]{1,0:T(8,128)(2,1)S(1)} %get-tuple-element.26), channel_id=1, source_target_pairs={{0,8},{1,9},{2,10},{3,11},{4,12},{5,13},{6,14},{7,15},{8,16},{9,17... | collective-permute-start | bytes 245768 | tf_op jit(solution)/shard_map/ppermute | solution.py:10
  15.8 15.8 %collective-permute-start = (bf16[64,640]{1,0:T(8,128)(2,1)S(1)}, bf16[64,640]{1,0:T(8,128)(2,1)S(1)}, u32[]{:S(2)}, u32[]{:S(2)}) collective-permute-start(bf16[64,640]{1,0:T(8,128)(2,1)S(1)} %get-tuple-element.25), channel_id=1, source_target_pairs={{0,8},{1,9},{2,10},{3,11},{4,12},{5,13},{6,14},{7,15},{8,16},{9,17... | collective-permute-start | bytes 245768 | tf_op jit(solution)/shard_map/ppermute | solution.py:10
  18.3 14.6 %collective-permute-start.3 = (bf16[64,640]{1,0:T(8,128)(2,1)S(1)}, bf16[64,640]{1,0:T(8,128)(2,1)S(1)}, u32[]{:S(2)}, u32[]{:S(2)}) collective-permute-start(bf16[64,640]{1,0:T(8,128)(2,1)S(1)} %get-tuple-element.26), channel_id=1, source_target_pairs={{0,4},{1,5},{2,6},{3,7},{4,8},{5,9},{6,10},{7,11},{8,12},{9,13},{1... | collective-permute-start | bytes 245768 | tf_op jit(solution)/shard_map/ppermute | solution.py:10
  23.4 10.8 %collective-permute-start.2 = (bf16[64,640]{1,0:T(8,128)(2,1)S(1)}, bf16[64,640]{1,0:T(8,128)(2,1)S(1)}, u32[]{:S(2)}, u32[]{:S(2)}) collective-permute-start(bf16[64,640]{1,0:T(8,128)(2,1)S(1)} %get-tuple-element.25), channel_id=1, source_target_pairs={{0,4},{1,5},{2,6},{3,7},{4,8},{5,9},{6,10},{7,11},{8,12},{9,13},{1... | collective-permute-start | bytes 245768 | tf_op jit(solution)/shard_map/ppermute | solution.py:10
  28.9 9.0 %collective-permute-start.5 = (bf16[64,640]{1,0:T(8,128)(2,1)S(1)}, bf16[64,640]{1,0:T(8,128)(2,1)S(1)}, u32[]{:S(2)}, u32[]{:S(2)}) collective-permute-start(bf16[64,640]{1,0:T(8,128)(2,1)S(1)} %get-tuple-element.26), channel_id=1, source_target_pairs={{4,0},{5,1},{6,2},{7,3},{8,4},{9,5},{10,6},{11,7},{12,8},{13,9},{1... | collective-permute-start | bytes 245768 | tf_op jit(solution)/shard_map/ppermute | solution.py:10
  30.3 8.5 %collective-permute-start.4 = (bf16[64,640]{1,0:T(8,128)(2,1)S(1)}, bf16[64,640]{1,0:T(8,128)(2,1)S(1)}, u32[]{:S(2)}, u32[]{:S(2)}) collective-permute-start(bf16[64,640]{1,0:T(8,128)(2,1)S(1)} %get-tuple-element.25), channel_id=1, source_target_pairs={{4,0},{5,1},{6,2},{7,3},{8,4},{9,5},{10,6},{11,7},{12,8},{13,9},{1... | collective-permute-start | bytes 245768 | tf_op jit(solution)/shard_map/ppermute | solution.py:10
  31.6 16.8 %collective-permute-start.7 = (bf16[64,640]{1,0:T(8,128)(2,1)S(1)}, bf16[64,640]{1,0:T(8,128)(2,1)S(1)}, u32[]{:S(2)}, u32[]{:S(2)}) collective-permute-start(bf16[64,640]{1,0:T(8,128)(2,1)S(1)} %get-tuple-element.26), channel_id=1, source_target_pairs={{8,0},{9,1},{10,2},{11,3},{12,4},{13,5},{14,6},{15,7},{16,8},{17,9... | collective-permute-start | bytes 245768 | tf_op jit(solution)/shard_map/ppermute | solution.py:10
  32.9 16.4 %collective-permute-start.6 = (bf16[64,640]{1,0:T(8,128)(2,1)S(1)}, bf16[64,640]{1,0:T(8,128)(2,1)S(1)}, u32[]{:S(2)}, u32[]{:S(2)}) collective-permute-start(bf16[64,640]{1,0:T(8,128)(2,1)S(1)} %get-tuple-element.25), channel_id=1, source_target_pairs={{8,0},{9,1},{10,2},{11,3},{12,4},{13,5},{14,6},{15,7},{16,8},{17,9... | collective-permute-start | bytes 245768 | tf_op jit(solution)/shard_map/ppermute | solution.py:10
  57.2 7.6 %collective-permute-start.21 = (f32[8,128]{1,0:T(8,128)S(1)}, f32[8,128]{1,0:T(8,128)S(1)}, u32[]{:S(2)}, u32[]{:S(2)}) collective-permute-start(f32[8,128]{1,0:T(8,128)S(1)} %add_add_fusion.5), channel_id=1, source_target_pairs={{0,80},{1,81},{2,82},{3,83},{4,84},{5,85},{6,86},{7,87},{8,88},{9,... | collective-permute-start | bytes 12296 | tf_op jit(solution)/shard_map/ppermute | solution.py:15
  67.0 6.9 %collective-permute-start.24 = (f32[8,128]{1,0:T(8,128)S(1)}, f32[8,128]{1,0:T(8,128)S(1)}, u32[]{:S(2)}, u32[]{:S(2)}) collective-permute-start(f32[8,128]{1,0:T(8,128)S(1)} %add_add_fusion.4), channel_id=1, source_target_pairs={{0,36},{1,37},{2,38},{3,39},{4,32},{5,33},{6,34},{7,35},{8,44},{9,... | collective-permute-start | bytes 12296 | tf_op jit(solution)/shard_map/ppermute | solution.py:15
  70.6 5.1 %collective-permute-start.23 = (f32[8,128]{1,0:T(8,128)S(1)}, f32[8,128]{1,0:T(8,128)S(1)}, u32[]{:S(2)}, u32[]{:S(2)}) collective-permute-start(f32[8,128]{1,0:T(8,128)S(1)} %add_add_fusion.4), channel_id=1, source_target_pairs={{0,32},{1,33},{2,34},{3,35},{4,36},{5,37},{6,38},{7,39},{8,40},{9,... | collective-permute-start | bytes 12296 | tf_op jit(solution)/shard_map/ppermute | solution.py:15
  76.6 20.4 %collective-permute-start.27 = (f32[8,128]{1,0:T(8,128)S(1)}, f32[8,128]{1,0:T(8,128)S(1)}, u32[]{:S(2)}, u32[]{:S(2)}) collective-permute-start(f32[8,128]{1,0:T(8,128)S(1)} %add_add_fusion.3), channel_id=1, source_target_pairs={{0,136},{1,137},{2,138},{3,139},{4,140},{5,141},{6,142},{7,143},{8... | collective-permute-start | bytes 12296 | tf_op jit(solution)/shard_map/ppermute | solution.py:15
  85.6 11.5 %collective-permute-start.26 = (f32[8,128]{1,0:T(8,128)S(1)}, f32[8,128]{1,0:T(8,128)S(1)}, u32[]{:S(2)}, u32[]{:S(2)}) collective-permute-start(f32[8,128]{1,0:T(8,128)S(1)} %add_add_fusion.3), channel_id=1, source_target_pairs={{0,8},{1,9},{2,10},{3,11},{4,12},{5,13},{6,14},{7,15},{8,0},{9,1},... | collective-permute-start | bytes 12296 | tf_op jit(solution)/shard_map/ppermute | solution.py:15
  91.1 5.9 %collective-permute-start.25 = (f32[8,128]{1,0:T(8,128)S(1)}, f32[8,128]{1,0:T(8,128)S(1)}, u32[]{:S(2)}, u32[]{:S(2)}) collective-permute-start(f32[8,128]{1,0:T(8,128)S(1)} %add_add_fusion.3), channel_id=1, source_target_pairs={{0,128},{1,129},{2,130},{3,131},{4,132},{5,133},{6,134},{7,135},{8... | collective-permute-start | bytes 12296 | tf_op jit(solution)/shard_map/ppermute | solution.py:15
  97.0 54.0 %collective-permute-start.8 = (f32[8,128]{1,0:T(8,128)}, f32[8,128]{1,0:T(8,128)}, u32[]{:S(2)}, u32[]{:S(2)}) collective-permute-start(f32[8,128]{1,0:T(8,128)} %broadcast_in_dim.12), channel_id=1, source_target_pairs={{0,1},{1,0},{2,3},{3,2},{4,5},{5,4},{6,7},{7,6},{8,9},{9,8},{10,11... | collective-permute-start | bytes 12296 | tf_op jit(solution)/shard_map/ppermute | solution.py:15
  101.7 13.6 %collective-permute-start.29 = (bf16[64,640]{1,0:T(8,128)(2,1)}, bf16[64,640]{1,0:T(8,128)(2,1)}, u32[]{:S(2)}, u32[]{:S(2)}) collective-permute-start(bf16[64,640]{1,0:T(8,128)(2,1)} %get-tuple-element.24), channel_id=1, source_target_pairs={{8,0},{9,1},{10,2},{11,3},{12,4},{13,5},{14,6},{15,7},{16,8},{17,9... | collective-permute-start | bytes 245768 | tf_op jit(solution)/shard_map/ppermute | solution.py:10
  103.0 23.3 %collective-permute-start.31 = (bf16[64,640]{1,0:T(8,128)(2,1)}, bf16[64,640]{1,0:T(8,128)(2,1)}, u32[]{:S(2)}, u32[]{:S(2)}) collective-permute-start(bf16[64,640]{1,0:T(8,128)(2,1)} %get-tuple-element.24), channel_id=1, source_target_pairs={{4,0},{5,1},{6,2},{7,3},{8,4},{9,5},{10,6},{11,7},{12,8},{13,9},{1... | collective-permute-start | bytes 245768 | tf_op jit(solution)/shard_map/ppermute | solution.py:10
  104.3 19.4 %collective-permute-start.28 = (bf16[64,640]{1,0:T(8,128)(2,1)S(1)}, bf16[64,640]{1,0:T(8,128)(2,1)}, u32[]{:S(2)}, u32[]{:S(2)}) collective-permute-start(bf16[64,640]{1,0:T(8,128)(2,1)S(1)} %get-tuple-element.23), channel_id=1, source_target_pairs={{8,0},{9,1},{10,2},{11,3},{12,4},{13,5},{14,6},{15,7},{16,8},{17,9... | collective-permute-start | bytes 245768 | tf_op jit(solution)/shard_map/ppermute | solution.py:10
  105.6 30.0 %collective-permute-start.30 = (bf16[64,640]{1,0:T(8,128)(2,1)S(1)}, bf16[64,640]{1,0:T(8,128)(2,1)}, u32[]{:S(2)}, u32[]{:S(2)}) collective-permute-start(bf16[64,640]{1,0:T(8,128)(2,1)S(1)} %get-tuple-element.23), channel_id=1, source_target_pairs={{4,0},{5,1},{6,2},{7,3},{8,4},{9,5},{10,6},{11,7},{12,8},{13,9},{1... | collective-permute-start | bytes 245768 | tf_op jit(solution)/shard_map/ppermute | solution.py:10
  115.3 29.2 %collective-permute-start.33 = (bf16[64,640]{1,0:T(8,128)(2,1)}, bf16[64,640]{1,0:T(8,128)(2,1)S(1)}, u32[]{:S(2)}, u32[]{:S(2)}) collective-permute-start(bf16[64,640]{1,0:T(8,128)(2,1)} %get-tuple-element.24), channel_id=1, source_target_pairs={{0,4},{1,5},{2,6},{3,7},{4,8},{5,9},{6,10},{7,11},{8,12},{9,13},{1... | collective-permute-start | bytes 245768 | tf_op jit(solution)/shard_map/ppermute | solution.py:10
  123.7 20.9 %collective-permute-start.32 = (bf16[64,640]{1,0:T(8,128)(2,1)S(1)}, bf16[64,640]{1,0:T(8,128)(2,1)S(1)}, u32[]{:S(2)}, u32[]{:S(2)}) collective-permute-start(bf16[64,640]{1,0:T(8,128)(2,1)S(1)} %get-tuple-element.23), channel_id=1, source_target_pairs={{0,4},{1,5},{2,6},{3,7},{4,8},{5,9},{6,10},{7,11},{8,12},{9,13},{1... | collective-permute-start | bytes 245768 | tf_op jit(solution)/shard_map/ppermute | solution.py:10
  126.3 18.8 %collective-permute-start.35 = (bf16[64,640]{1,0:T(8,128)(2,1)}, bf16[64,640]{1,0:T(8,128)(2,1)S(1)}, u32[]{:S(2)}, u32[]{:S(2)}) collective-permute-start(bf16[64,640]{1,0:T(8,128)(2,1)} %get-tuple-element.24), channel_id=1, source_target_pairs={{0,8},{1,9},{2,10},{3,11},{4,12},{5,13},{6,14},{7,15},{8,16},{9,17... | collective-permute-start | bytes 245768 | tf_op jit(solution)/shard_map/ppermute | solution.py:10
  135.6 10.7 %collective-permute-start.34 = (bf16[64,640]{1,0:T(8,128)(2,1)S(1)}, bf16[64,640]{1,0:T(8,128)(2,1)S(1)}, u32[]{:S(2)}, u32[]{:S(2)}) collective-permute-start(bf16[64,640]{1,0:T(8,128)(2,1)S(1)} %get-tuple-element.23), channel_id=1, source_target_pairs={{0,8},{1,9},{2,10},{3,11},{4,12},{5,13},{6,14},{7,15},{8,16},{9,17... | collective-permute-start | bytes 245768 | tf_op jit(solution)/shard_map/ppermute | solution.py:10
  144.5 50.8 %collective-permute-start.49 = (bf16[64,5,640]{2,0,1:T(8,128)(2,1)S(1)}, bf16[64,5,640]{2,0,1:T(8,128)(2,1)}, u32[]{:S(2)}, u32[]{:S(2)}) collective-permute-start(bf16[64,5,640]{2,0,1:T(8,128)(2,1)S(1)} %get-tuple-element.12), channel_id=1, source_target_pairs={{0,1},{1,0},{2,3},{3,2},{4,5},{5,4},{6,7},{7,6},{8,9},{9,8},{10,11... | collective-permute-start | bytes 1228808 | tf_op jit(solution)/shard_map/ppermute | solution.py:15
  144.6 50.7 %collective-permute-start.48 = (bf16[64,5,640]{2,0,1:T(8,128)(2,1)S(1)}, bf16[64,5,640]{2,0,1:T(8,128)(2,1)}, u32[]{:S(2)}, u32[]{:S(2)}) collective-permute-start(bf16[64,5,640]{2,0,1:T(8,128)(2,1)S(1)} %get-tuple-element.11), channel_id=1, source_target_pairs={{0,1},{1,0},{2,3},{3,2},{4,5},{5,4},{6,7},{7,6},{8,9},{9,8},{10,11... | collective-permute-start | bytes 1228808 | tf_op jit(solution)/shard_map/ppermute | solution.py:15
  150.5 44.8 %collective-permute-start.37 = (bf16[64,5,640]{2,0,1:T(8,128)(2,1)S(1)}, bf16[64,5,640]{2,0,1:T(8,128)(2,1)}, u32[]{:S(2)}, u32[]{:S(2)}) collective-permute-start(bf16[64,5,640]{2,0,1:T(8,128)(2,1)S(1)} %get-tuple-element.14), channel_id=1, source_target_pairs={{0,1},{1,0},{2,3},{3,2},{4,5},{5,4},{6,7},{7,6},{8,9},{9,8},{10,11... | collective-permute-start | bytes 1228808 | tf_op jit(solution)/shard_map/ppermute | solution.py:15
  150.5 44.8 %collective-permute-start.36 = (bf16[64,5,640]{2,0,1:T(8,128)(2,1)S(1)}, bf16[64,5,640]{2,0,1:T(8,128)(2,1)}, u32[]{:S(2)}, u32[]{:S(2)}) collective-permute-start(bf16[64,5,640]{2,0,1:T(8,128)(2,1)S(1)} %get-tuple-element.13), channel_id=1, source_target_pairs={{0,1},{1,0},{2,3},{3,2},{4,5},{5,4},{6,7},{7,6},{8,9},{9,8},{10,11... | collective-permute-start | bytes 1228808 | tf_op jit(solution)/shard_map/ppermute | solution.py:15
  157.3 5.1 %collective-permute-start.10 = (f32[8,128]{1,0:T(8,128)S(1)}, f32[8,128]{1,0:T(8,128)S(1)}, u32[]{:S(2)}, u32[]{:S(2)}) collective-permute-start(f32[8,128]{1,0:T(8,128)S(1)} %fusion.75), channel_id=1, source_target_pairs={{0,16},{1,17},{2,18},{3,19},{4,20},{5,21},{6,22},{7,23},{8,24},{9,... | collective-permute-start | bytes 12296 | tf_op jit(solution)/shard_map/ppermute | solution.py:15
  162.3 7.9 %collective-permute-start.11 = (f32[8,128]{1,0:T(8,128)S(1)}, f32[8,128]{1,0:T(8,128)S(1)}, u32[]{:S(2)}, u32[]{:S(2)}) collective-permute-start(f32[8,128]{1,0:T(8,128)S(1)} %add.282), channel_id=1, source_target_pairs={{0,64},{1,65},{2,66},{3,67},{4,68},{5,69},{6,70},{7,71},{8,72},{9,... | collective-permute-start | bytes 12296 | tf_op jit(solution)/shard_map/ppermute | solution.py:15
  174.7 5.1 %collective-permute-start.13 = (f32[8,128]{1,0:T(8,128)S(1)}, f32[8,128]{1,0:T(8,128)S(1)}, u32[]{:S(2)}, u32[]{:S(2)}) collective-permute-start(f32[8,128]{1,0:T(8,128)S(1)} %add.284), channel_id=1, source_target_pairs={{0,32},{1,33},{2,34},{3,35},{4,36},{5,37},{6,38},{7,39},{8,40},{9,... | collective-permute-start | bytes 12296 | tf_op jit(solution)/shard_map/ppermute | solution.py:15
  179.8 6.1 %collective-permute-start.14 = (f32[8,128]{1,0:T(8,128)S(1)}, f32[8,128]{1,0:T(8,128)S(1)}, u32[]{:S(2)}, u32[]{:S(2)}) collective-permute-start(f32[8,128]{1,0:T(8,128)S(1)} %add.285), channel_id=1, source_target_pairs={{0,128},{1,129},{2,130},{3,131},{4,132},{5,133},{6,134},{7,135},{8... | collective-permute-start | bytes 12296 | tf_op jit(solution)/shard_map/ppermute | solution.py:15
  185.9 7.6 %collective-permute-start.15 = (f32[8,128]{1,0:T(8,128)S(1)}, f32[8,128]{1,0:T(8,128)S(1)}, u32[]{:S(2)}, u32[]{:S(2)}) collective-permute-start(f32[8,128]{1,0:T(8,128)S(1)} %add.286), channel_id=1, source_target_pairs={{0,8},{1,9},{2,10},{3,11},{4,12},{5,13},{6,14},{7,15},{8,0},{9,1},... | collective-permute-start | bytes 12296 | tf_op jit(solution)/shard_map/ppermute | solution.py:15
  198.2 5.8 %collective-permute-start.39 = (bf16[32,5,640]{2,0,1:T(8,128)(2,1)S(1)}, bf16[32,5,640]{2,0,1:T(8,128)(2,1)S(1)}, u32[]{:S(2)}, u32[]{:S(2)}) collective-permute-start(bf16[32,5,640]{2,0,1:T(8,128)(2,1)S(1)} %get-tuple-element.18), channel_id=1, source_target_pairs={{0,2},{1,3},{2,0},{3,1},{4,6},{5,7},{6,4},{7,5},{8,10},{9,11},{10,... | collective-permute-start | bytes 614408 | tf_op jit(solution)/shard_map/ppermute | solution.py:15
  198.7 7.6 %collective-permute-start.38 = (bf16[32,5,640]{2,0,1:T(8,128)(2,1)S(1)}, bf16[32,5,640]{2,0,1:T(8,128)(2,1)S(1)}, u32[]{:S(2)}, u32[]{:S(2)}) collective-permute-start(bf16[32,5,640]{2,0,1:T(8,128)(2,1)S(1)} %get-tuple-element.17), channel_id=1, source_target_pairs={{0,2},{1,3},{2,0},{3,1},{4,6},{5,7},{6,4},{7,5},{8,10},{9,11},{10,... | collective-permute-start | bytes 614408 | tf_op jit(solution)/shard_map/ppermute | solution.py:15
  200.4 8.1 %collective-permute-start.51 = (bf16[32,5,640]{2,0,1:T(8,128)(2,1)S(1)}, bf16[32,5,640]{2,0,1:T(8,128)(2,1)S(1)}, u32[]{:S(2)}, u32[]{:S(2)}) collective-permute-start(bf16[32,5,640]{2,0,1:T(8,128)(2,1)S(1)} %get-tuple-element.16), channel_id=1, source_target_pairs={{0,2},{1,3},{2,0},{3,1},{4,6},{5,7},{6,4},{7,5},{8,10},{9,11},{10,... | collective-permute-start | bytes 614408 | tf_op jit(solution)/shard_map/ppermute | solution.py:15
  200.9 9.7 %collective-permute-start.50 = (bf16[32,5,640]{2,0,1:T(8,128)(2,1)S(1)}, bf16[32,5,640]{2,0,1:T(8,128)(2,1)S(1)}, u32[]{:S(2)}, u32[]{:S(2)}) collective-permute-start(bf16[32,5,640]{2,0,1:T(8,128)(2,1)S(1)} %get-tuple-element.15), channel_id=1, source_target_pairs={{0,2},{1,3},{2,0},{3,1},{4,6},{5,7},{6,4},{7,5},{8,10},{9,11},{10,... | collective-permute-start | bytes 614408 | tf_op jit(solution)/shard_map/ppermute | solution.py:15
  206.4 6.5 %collective-permute-start.41 = (bf16[16,5,640]{2,0,1:T(8,128)(2,1)S(1)}, bf16[16,5,640]{2,0,1:T(8,128)(2,1)S(1)}, u32[]{:S(2)}, u32[]{:S(2)}) collective-permute-start(bf16[16,5,640]{2,0,1:T(8,128)(2,1)S(1)} %get-tuple-element.22), channel_id=1, source_target_pairs={{0,16},{1,17},{2,18},{3,19},{4,20},{5,21},{6,22},{7,23},{8,24},{9,... | collective-permute-start | bytes 307208 | tf_op jit(solution)/shard_map/ppermute | solution.py:15
  206.7 6.1 %collective-permute-start.40 = (bf16[16,5,640]{2,0,1:T(8,128)(2,1)S(1)}, bf16[16,5,640]{2,0,1:T(8,128)(2,1)S(1)}, u32[]{:S(2)}, u32[]{:S(2)}) collective-permute-start(bf16[16,5,640]{2,0,1:T(8,128)(2,1)S(1)} %get-tuple-element.21), channel_id=1, source_target_pairs={{0,16},{1,17},{2,18},{3,19},{4,20},{5,21},{6,22},{7,23},{8,24},{9,... | collective-permute-start | bytes 307208 | tf_op jit(solution)/shard_map/ppermute | solution.py:15
  211.1 5.7 %collective-permute-start.52 = (bf16[16,5,640]{2,0,1:T(8,128)(2,1)S(1)}, bf16[16,5,640]{2,0,1:T(8,128)(2,1)S(1)}, u32[]{:S(2)}, u32[]{:S(2)}) collective-permute-start(bf16[16,5,640]{2,0,1:T(8,128)(2,1)S(1)} %get-tuple-element.19), channel_id=1, source_target_pairs={{0,16},{1,17},{2,18},{3,19},{4,20},{5,21},{6,22},{7,23},{8,24},{9,... | collective-permute-start | bytes 307208 | tf_op jit(solution)/shard_map/ppermute | solution.py:15
  213.0 6.1 %collective-permute-start.43 = (bf16[8,5,640]{2,0,1:T(8,128)(2,1)S(1)}, bf16[8,5,640]{2,0,1:T(8,128)(2,1)S(1)}, u32[]{:S(2)}, u32[]{:S(2)}) collective-permute-start(bf16[8,5,640]{2,0,1:T(8,128)(2,1)S(1)} %get-tuple-element.30), channel_id=1, source_target_pairs={{0,64},{1,65},{2,66},{3,67},{4,68},{5,69},{6,70},{7,71},{8,72},{9,... | collective-permute-start | bytes 153608 | tf_op jit(solution)/shard_map/ppermute | solution.py:15
  219.1 5.2 %collective-permute-start.44 = (bf16[8,5,640]{2,0,1:T(8,128)(2,1)S(1)}, bf16[8,5,640]{2,0,1:T(8,128)(2,1)S(1)}, u32[]{:S(2)}, u32[]{:S(2)}) collective-permute-start(bf16[8,5,640]{2,0,1:T(8,128)(2,1)S(1)} %dynamic-slice_convert_fusion.9), channel_id=1, source_target_pairs={{0,4},{1,5},{2,6},{3,7},{4,0},{5,1},{6,2},{7,3},{8,12},{9,13},{10,... | collective-permute-start | bytes 153608 | tf_op jit(solution)/shard_map/ppermute | solution.py:15
  222.4 5.2 %collective-permute-start.56 = (bf16[8,5,640]{2,0,1:T(8,128)(2,1)S(1)}, bf16[8,5,640]{2,0,1:T(8,128)(2,1)S(1)}, u32[]{:S(2)}, u32[]{:S(2)}) collective-permute-start(bf16[8,5,640]{2,0,1:T(8,128)(2,1)S(1)} %dynamic-slice_convert_fusion.8), channel_id=1, source_target_pairs={{0,4},{1,5},{2,6},{3,7},{4,0},{5,1},{6,2},{7,3},{8,12},{9,13},{10,... | collective-permute-start | bytes 153608 | tf_op jit(solution)/shard_map/ppermute | solution.py:15
  224.4 5.7 %collective-permute-start.45 = (bf16[4,5,640]{2,0,1:T(4,128)(2,1)S(1)}, bf16[4,5,640]{2,0,1:T(4,128)(2,1)S(1)}, u32[]{:S(2)}, u32[]{:S(2)}) collective-permute-start(bf16[4,5,640]{2,0,1:T(4,128)(2,1)S(1)} %dynamic-slice_convert_fusion.11), channel_id=1, source_target_pairs={{0,32},{1,33},{2,34},{3,35},{4,36},{5,37},{6,38},{7,39},{8,40},{9,... | collective-permute-start | bytes 76808 | tf_op jit(solution)/shard_map/ppermute | solution.py:15
  227.6 6.1 %collective-permute-start.57 = (bf16[4,5,640]{2,0,1:T(4,128)(2,1)S(1)}, bf16[4,5,640]{2,0,1:T(4,128)(2,1)S(1)}, u32[]{:S(2)}, u32[]{:S(2)}) collective-permute-start(bf16[4,5,640]{2,0,1:T(4,128)(2,1)S(1)} %dynamic-slice_convert_fusion.10), channel_id=1, source_target_pairs={{0,32},{1,33},{2,34},{3,35},{4,36},{5,37},{6,38},{7,39},{8,40},{9,... | collective-permute-start | bytes 76808 | tf_op jit(solution)/shard_map/ppermute | solution.py:15
  230.1 7.2 %collective-permute-start.46 = (bf16[2,5,640]{2,0,1:T(2,128)(2,1)S(1)}, bf16[2,5,640]{2,0,1:T(2,128)(2,1)S(1)}, u32[]{:S(2)}, u32[]{:S(2)}) collective-permute-start(bf16[2,5,640]{2,0,1:T(2,128)(2,1)S(1)} %dynamic-slice_convert_fusion.13), channel_id=1, source_target_pairs={{0,128},{1,129},{2,130},{3,131},{4,132},{5,133},{6,134},{7,135},{8... | collective-permute-start | bytes 38408 | tf_op jit(solution)/shard_map/ppermute | solution.py:15
  233.8 5.3 %collective-permute-start.58 = (bf16[2,5,640]{2,0,1:T(2,128)(2,1)S(1)}, bf16[2,5,640]{2,0,1:T(2,128)(2,1)S(1)}, u32[]{:S(2)}, u32[]{:S(2)}) collective-permute-start(bf16[2,5,640]{2,0,1:T(2,128)(2,1)S(1)} %dynamic-slice_convert_fusion.12), channel_id=1, source_target_pairs={{0,128},{1,129},{2,130},{3,131},{4,132},{5,133},{6,134},{7,135},{8... | collective-permute-start | bytes 38408 | tf_op jit(solution)/shard_map/ppermute | solution.py:15
  237.3 7.7 %collective-permute-start.47 = (bf16[1,5,640]{2,0,1:T(2,128)(2,1)S(1)}, bf16[1,5,640]{2,0,1:T(2,128)(2,1)S(1)}, u32[]{:S(2)}, u32[]{:S(2)}) collective-permute-start(bf16[1,5,640]{2,0,1:T(2,128)(2,1)S(1)} %dynamic-slice_convert_fusion.15), channel_id=1, source_target_pairs={{0,8},{1,9},{2,10},{3,11},{4,12},{5,13},{6,14},{7,15},{8,0},{9,1},... | collective-permute-start | bytes 19208 | tf_op jit(solution)/shard_map/ppermute | solution.py:15
  239.1 7.7 %collective-permute-start.59 = (bf16[1,5,640]{2,0,1:T(2,128)(2,1)S(1)}, bf16[1,5,640]{2,0,1:T(2,128)(2,1)S(1)}, u32[]{:S(2)}, u32[]{:S(2)}) collective-permute-start(bf16[1,5,640]{2,0,1:T(2,128)(2,1)S(1)} %dynamic-slice_convert_fusion.14), channel_id=1, source_target_pairs={{0,8},{1,9},{2,10},{3,11},{4,12},{5,13},{6,14},{7,15},{8,0},{9,1},... | collective-permute-start | bytes 19208 | tf_op jit(solution)/shard_map/ppermute | solution.py:15
  (32 other events, 485.8 us)

commit v8 on v6

--- a/solution.py
+++ b/solution.py
@@ -48,10 +48,17 @@
     return split.transpose([0] + axes + [depth + 1]).reshape(rows, width)
 
 
+def split_pair(value):
+    high = value.astype(jnp.bfloat16)
+    low = (value - high.astype(jnp.float32)).astype(jnp.bfloat16)
+    return high, low
+
+
 def tree_scatter(partials, extra, axis):
     devices = lax.axis_size(axis)
     me = lax.axis_index(axis)
     blocks = [p.reshape(devices, p.shape[0] // devices, -1) for p in partials]
+    share, width = blocks[0].shape[1:]
     for bit in link_order(devices):
         half = blocks[0].shape[0] // 2
         upper = (me // bit) % 2
@@ -61,11 +68,21 @@
             for b in blocks
         ]
         pieces = 2 if half >= 16 else 1
-        parts = [jnp.split(s, pieces, 0) for s in send]
-        got_parts, got_extra = swap_with((parts, extra), axis, bit)
+        parts = [list(jnp.split(s, pieces, 0)) for s in send]
+        high, low = split_pair(extra)
+        extra = high.astype(jnp.float32) + low.astype(jnp.float32)
+        rows = parts[0][0].shape[0]
+        tail = jnp.concatenate(
+            [jnp.broadcast_to(high, (rows, 1, width // 2)), jnp.broadcast_to(low, (rows, 1, width // 2))],
+            2,
+        )
+        parts[0][0] = jnp.concatenate([parts[0][0], tail], 1)
+        got_parts = swap_with(parts, axis, bit)
+        got_tail = got_parts[0][0][0, share].astype(jnp.float32)
+        extra = extra + (got_tail[0] + got_tail[width // 2])
+        got_parts[0][0] = got_parts[0][0][:, :share]
         got = [jnp.concatenate(g, 0) if pieces > 1 else g[0] for g in got_parts]
         blocks = [k + g.astype(jnp.float32) for k, g in zip(keep, got)]
-        extra = extra + got_extra
     return [b[0] for b in blocks], extra
 
 
@@ -140,12 +157,9 @@
     up_partial = lax.dot_general(
         columns, grad_first, (((0,), (0,)), ((), ())), preferred_element_type=jnp.float32
     )
-    (grad_down, grad_up), loss_tile = tree_scatter(
-        (down_partial, up_partial), jnp.broadcast_to(local_loss, (8, 128)), "seq"
-    )
+    (grad_down, grad_up), loss_total = tree_scatter((down_partial, up_partial), local_loss, "seq")
     grad_down = grad_down.astype(jnp.bfloat16)
     grad_up = grad_up.astype(jnp.bfloat16)
-    loss_total = loss_tile[0, 0]
     return (loss_total / mask_total, grad_up, grad_down)
 
 

time: 204 us -> 208 us (1.020)
  starting transfers between devices: 103 us -> 88.8 us
  between operations: 4.63 us -> 15.9 us
  local copies, waits for them, and re-layouts: 15.2 us -> 22.3 us
    ppermute x44 -> x36, waiting for transfers between devices: 43.7 us -> 32.1 us  [swap_with(): return lax.ppermute(block, axis, [(i, i ^ bit) for i in range(devices)])]
    ppermute x44 -> x36, starting transfers between devices: 71.2 us -> 60.1 us  [swap_with(): return lax.ppermute(block, axis, [(i, i ^ bit) for i in range(devices)])]
    ppermute x8, waiting for transfers between devices: 17.9 us -> 27.5 us  [from_behind(): return lax.ppermute(block, axis, route)]
    slice x1 -> x12, local copies, waits for them, and re-layouts: 0.51 us -> 5.75 us  [the longest x8 4.67 us: tree_scatter(): extra = extra + (got_tail[0] + got_tail[width // 2])]
    ppermute x8, starting transfers between devices: 31.3 us -> 28.6 us  [from_behind(): return lax.ppermute(block, axis, route)]
    unnamed x26 -> x30, local copies, waits for them, and re-layouts: 5.48 us -> 6.93 us
  transfers between devices with their start and end apart: 52 -> 44, of which waited for: 27 -> 18; matrix products, arithmetic and copies ran while one was open for 10% -> 11% of each run, Pallas kernels for 0% -> 0%
where the time goes in v8:
time: 208 us; the launch traced here: 207 us
  starting transfers between devices  88.8 us (43%)
  waiting for transfers between devices  59.6 us (29%)
  local copies, waits for them, and re-layouts  22.3 us (11%)
  between operations  15.9 us (8%)
  other arithmetic  11.9 us (6%)
  matrix products  8.77 us (4%)
    ppermute x36, starting transfers between devices, swap_with(): return lax.ppermute(block, axis, [(i, i ^ bit) for i in range(devices)])  60.1 us
    ppermute x36, waiting for transfers between devices, swap_with(): return lax.ppermute(block, axis, [(i, i ^ bit) for i in range(devices)])  32.1 us
    ppermute x8, starting transfers between devices, from_behind(): return lax.ppermute(block, axis, route)  28.6 us
    ppermute x8, waiting for transfers between devices, from_behind(): return lax.ppermute(block, axis, route)  27.5 us
    unnamed x30, local copies, waits for them, and re-layouts  6.93 us
    slice x8, local copies, waits for them, and re-layouts, tree_scatter(): extra = extra + (got_tail[0] + got_tail[width // 2])  4.67 us
  transfers between devices with their start and end apart: 44, of which 18 were waited for; matrix products, arithmetic and copies ran while one was open for 11% of the time, Pallas kernels for 0%

profile of v8, /device:TPU:32, one launch (start us, length us, event | category | flops | bytes accessed | tf_op | source)
XLA Modules:
  0.0 207.3 jit_solution(1385239170161894316)
XLA Ops:
  0.6 1.2 convert_reduce_fusion
  3.1 1.4 fusion.9
  4.5 2.1 %fusion.62 = (f32[128]{0:T(128)S(1)}, f32[128,640]{1,0:T(8,128)S(1)}) fusion(bf16[128,1280]{1,0:T(8,128)(2,1)S(1)} %fusion.9, bf16[1280,640]{1,0:T(8,128)(2,1)} %param.12), kind=kOutput, calls=%fused_computation.162 | convolution fusion | flops 209796992 | bytes 2294272 | tf_op jit(solution)/shard_map/dot_general | solution.py:116
  7.0 8.2 %collective-permute-start = (bf16[128,640]{1,0:T(8,128)(2,1)S(1)}, bf16[128,640]{1,0:T(8,128)(2,1)S(1)}, u32[]{:S(2)}, u32[]{:S(2)}) collective-permute-start(bf16[128,640]{1,0:T(8,128)(2,1)S(1)} %multiply_convert_fusion.1), channel_id=1, source_target_pairs={{0,8},{1,9},{2,10},{3,11},{4,12},{5,13},{6,14},{7,15},{8,16},{9,17... | collective-permute-start | bytes 491528 | tf_op jit(solution)/shard_map/ppermute | solution.py:10
  15.2 1.3 collective-permute-start.2
  16.5 1.3 collective-permute-start.3
  17.8 5.5 %collective-permute-start.1 = (bf16[128,640]{1,0:T(8,128)(2,1)S(1)}, bf16[128,640]{1,0:T(8,128)(2,1)S(1)}, u32[]{:S(2)}, u32[]{:S(2)}) collective-permute-start(bf16[128,640]{1,0:T(8,128)(2,1)S(1)} %multiply_convert_fusion.1), channel_id=1, source_target_pairs={{0,4},{1,5},{2,6},{3,7},{4,8},{5,9},{6,10},{7,11},{8,12},{9,13},{1... | collective-permute-start | bytes 491528 | tf_op jit(solution)/shard_map/ppermute | solution.py:10
  23.3 8.9 %collective-permute-done.1 = bf16[128,640]{1,0:T(8,128)(2,1)S(1)} collective-permute-done((bf16[128,640]{1,0:T(8,128)(2,1)S(1)}, bf16[128,640]{1,0:T(8,128)(2,1)S(1)}, u32[]{:S(2)}, u32[]{:S(2)}) %collective-permute-start.1) | collective-permute-done | bytes 163872 | tf_op jit(solution)/shard_map/ppermute | solution.py:10
  32.5 5.1 %collective-permute-done.3 = bf16[128,640]{1,0:T(8,128)(2,1)S(1)} collective-permute-done((bf16[128,640]{1,0:T(8,128)(2,1)S(1)}, bf16[128,640]{1,0:T(8,128)(2,1)S(1)}, u32[]{:S(2)}, u32[]{:S(2)}) %collective-permute-start.3) | collective-permute-done | bytes 163872 | tf_op jit(solution)/shard_map/ppermute | solution.py:10
  41.2 2.0 collective-permute-start.4
  43.3 1.5 collective-permute-done.5
  45.4 6.2 %collective-permute-start.9 = (f32[8,128]{1,0:T(8,128)S(1)}, f32[8,128]{1,0:T(8,128)S(1)}, u32[]{:S(2)}, u32[]{:S(2)}) collective-permute-start(f32[8,128]{1,0:T(8,128)S(1)} %add_add_fusion.5), channel_id=1, source_target_pairs={{0,80},{1,81},{2,82},{3,83},{4,84},{5,85},{6,86},{7,87},{8,88},{9,... | collective-permute-start | bytes 12296 | tf_op jit(solution)/shard_map/ppermute | solution.py:15
  51.6 1.8 collective-permute-start.8
  53.5 1.4 collective-permute-start.7
  55.2 1.8 collective-permute-done.7
  57.1 1.5 collective-permute-start.12
  59.1 3.9 %collective-permute-start.10 = (f32[8,128]{1,0:T(8,128)S(1)}, f32[8,128]{1,0:T(8,128)S(1)}, u32[]{:S(2)}, u32[]{:S(2)}) collective-permute-start(f32[8,128]{1,0:T(8,128)S(1)} %add_add_fusion.4), channel_id=1, source_target_pairs={{0,4},{1,5},{2,6},{3,7},{4,0},{5,1},{6,2},{7,3},{8,12},{9,13},{10,... | collective-permute-start | bytes 12296 | tf_op jit(solution)/shard_map/ppermute | solution.py:15
  64.6 4.8 %collective-permute-start.15 = (f32[8,128]{1,0:T(8,128)S(1)}, f32[8,128]{1,0:T(8,128)S(1)}, u32[]{:S(2)}, u32[]{:S(2)}) collective-permute-start(f32[8,128]{1,0:T(8,128)S(1)} %add_add_fusion.3), channel_id=1, source_target_pairs={{0,136},{1,137},{2,138},{3,139},{4,140},{5,141},{6,142},{7,143},{8... | collective-permute-start | bytes 12296 | tf_op jit(solution)/shard_map/ppermute | solution.py:15
  69.4 3.9 %collective-permute-start.14 = (f32[8,128]{1,0:T(8,128)S(1)}, f32[8,128]{1,0:T(8,128)S(1)}, u32[]{:S(2)}, u32[]{:S(2)}) collective-permute-start(f32[8,128]{1,0:T(8,128)S(1)} %add_add_fusion.3), channel_id=1, source_target_pairs={{0,8},{1,9},{2,10},{3,11},{4,12},{5,13},{6,14},{7,15},{8,0},{9,1},... | collective-permute-start | bytes 12296 | tf_op jit(solution)/shard_map/ppermute | solution.py:15
  76.9 1.5 collective-permute-done.13
  79.6 1.3 fusion
  83.0 5.5 %collective-permute-start.30 = (bf16[128,640]{1,0:T(8,128)(2,1)}, bf16[128,640]{1,0:T(8,128)(2,1)}, u32[]{:S(2)}, u32[]{:S(2)}) collective-permute-start(bf16[128,640]{1,0:T(8,128)(2,1)} %add_convert_fusion.1), channel_id=1, source_target_pairs={{0,4},{1,5},{2,6},{3,7},{4,8},{5,9},{6,10},{7,11},{8,12},{9,13},{1... | collective-permute-start | bytes 491528 | tf_op jit(solution)/shard_map/ppermute | solution.py:10
  88.5 4.3 %collective-permute-start.31 = (bf16[128,640]{1,0:T(8,128)(2,1)}, bf16[128,640]{1,0:T(8,128)(2,1)}, u32[]{:S(2)}, u32[]{:S(2)}) collective-permute-start(bf16[128,640]{1,0:T(8,128)(2,1)} %add_convert_fusion.1), channel_id=1, source_target_pairs={{0,8},{1,9},{2,10},{3,11},{4,12},{5,13},{6,14},{7,15},{8,16},{9,17... | collective-permute-start | bytes 491528 | tf_op jit(solution)/shard_map/ppermute | solution.py:10
  92.9 1.3 collective-permute-start.29
  94.1 1.3 collective-permute-start.28
  98.8 1.5 copy-done.3
  100.4 13.6 %collective-permute-done.28 = bf16[128,640]{1,0:T(8,128)(2,1)} collective-permute-done((bf16[128,640]{1,0:T(8,128)(2,1)}, bf16[128,640]{1,0:T(8,128)(2,1)}, u32[]{:S(2)}, u32[]{:S(2)}) %collective-permute-start.28) | collective-permute-done | bytes 163872 | tf_op jit(solution)/shard_map/ppermute | solution.py:10
  117.8 1.5 multiply_reduce_fusion
  126.5 1.8 convert_add_fusion.1
  129.4 2.0 collective-permute-start.35
  131.6 2.0 collective-permute-start.18
  133.6 3.6 %collective-permute-done.34 = bf16[32,5,640]{2,0,1:T(8,128)(2,1)S(1)} collective-permute-done((bf16[32,5,640]{2,0,1:T(8,128)(2,1)S(1)}, bf16[32,5,640]{2,0,1:T(8,128)(2,1)S(1)}, u32[]{:S(2)}, u32[]{:S(2)}) %collective-permute-start.34) | collective-permute-done | bytes 204832 | tf_op jit(solution)/shard_map/ppermute | solution.py:15
  137.3 4.4 %collective-permute-done.35 = bf16[32,5,640]{2,0,1:T(8,128)(2,1)S(1)} collective-permute-done((bf16[32,5,640]{2,0,1:T(8,128)(2,1)S(1)}, bf16[32,5,640]{2,0,1:T(8,128)(2,1)S(1)}, u32[]{:S(2)}, u32[]{:S(2)}) %collective-permute-start.35) | collective-permute-done | bytes 204832 | tf_op jit(solution)/shard_map/ppermute | solution.py:15
  142.5 2.0 collective-permute-start.37
  144.5 6.3 %collective-permute-done.18 = bf16[32,6,640]{2,0,1:T(8,128)(2,1)S(1)} collective-permute-done((bf16[32,6,640]{2,0,1:T(8,128)(2,1)S(1)}, bf16[32,6,640]{2,0,1:T(8,128)(2,1)S(1)}, u32[]{:S(2)}, u32[]{:S(2)}) %collective-permute-start.18) | collective-permute-done | bytes 245792 | tf_op jit(solution)/shard_map/ppermute | solution.py:15
  157.0 2.1 %collective-permute-start.20 = (bf16[16,6,640]{2,0,1:T(8,128)(2,1)S(1)}, bf16[16,6,640]{2,0,1:T(8,128)(2,1)S(1)}, u32[]{:S(2)}, u32[]{:S(2)}) collective-permute-start(bf16[16,6,640]{2,0,1:T(8,128)(2,1)S(1)} %pad_maximum_fusion.2), channel_id=1, source_target_pairs={{0,16},{1,17},{2,18},{3,19},{4,20},{5,21},{6,22},{7,23},{8,24},{9,... | collective-permute-start | bytes 368648 | tf_op jit(solution)/shard_map/ppermute | solution.py:15
  159.9 2.2 %collective-permute-start.40 = (bf16[8,5,640]{2,0,1:T(8,128)(2,1)S(1)}, bf16[8,5,640]{2,0,1:T(8,128)(2,1)S(1)}, u32[]{:S(2)}, u32[]{:S(2)}) collective-permute-start(bf16[8,5,640]{2,0,1:T(8,128)(2,1)S(1)} %dynamic-slice_convert_fusion.8), channel_id=1, source_target_pairs={{0,4},{1,5},{2,6},{3,7},{4,0},{5,1},{6,2},{7,3},{8,12},{9,13},{10,... | collective-permute-start | bytes 153608 | tf_op jit(solution)/shard_map/ppermute | solution.py:15
  164.2 1.6 collective-permute-start.23
  166.5 3.2 %collective-permute-start.41 = (bf16[4,5,640]{2,0,1:T(4,128)(2,1)S(1)}, bf16[4,5,640]{2,0,1:T(4,128)(2,1)S(1)}, u32[]{:S(2)}, u32[]{:S(2)}) collective-permute-start(bf16[4,5,640]{2,0,1:T(4,128)(2,1)S(1)} %dynamic-slice_convert_fusion.10), channel_id=1, source_target_pairs={{0,32},{1,33},{2,34},{3,35},{4,36},{5,37},{6,38},{7,39},{8,40},{9,... | collective-permute-start | bytes 76808 | tf_op jit(solution)/shard_map/ppermute | solution.py:15
  172.2 1.3 collective-permute-start.24
  173.5 1.4 collective-permute-start.42
  174.9 2.5 %collective-permute-done.24 = bf16[8,6,640]{2,0,1:T(8,128)(2,1)S(1)} collective-permute-done((bf16[8,6,640]{2,0,1:T(8,128)(2,1)S(1)}, bf16[8,6,640]{2,0,1:T(8,128)(2,1)S(1)}, u32[]{:S(2)}, u32[]{:S(2)}) %collective-permute-start.24) | collective-permute-done | bytes 61472 | tf_op jit(solution)/shard_map/ppermute | solution.py:15
  179.4 3.0 %collective-permute-start.25 = (bf16[4,6,640]{2,0,1:T(4,128)(2,1)S(1)}, bf16[4,6,640]{2,0,1:T(4,128)(2,1)S(1)}, u32[]{:S(2)}, u32[]{:S(2)}) collective-permute-start(bf16[4,6,640]{2,0,1:T(4,128)(2,1)S(1)} %pad_maximum_fusion.5), channel_id=1, source_target_pairs={{0,32},{1,33},{2,34},{3,35},{4,36},{5,37},{6,38},{7,39},{8,40},{9,... | collective-permute-start | bytes 92168 | tf_op jit(solution)/shard_map/ppermute | solution.py:15
  182.4 2.5 %collective-permute-done.25 = bf16[4,6,640]{2,0,1:T(4,128)(2,1)S(1)} collective-permute-done((bf16[4,6,640]{2,0,1:T(4,128)(2,1)S(1)}, bf16[4,6,640]{2,0,1:T(4,128)(2,1)S(1)}, u32[]{:S(2)}, u32[]{:S(2)}) %collective-permute-start.25) | collective-permute-done | bytes 30752 | tf_op jit(solution)/shard_map/ppermute | solution.py:15
  186.9 1.9 collective-permute-start.26
  188.8 4.5 %collective-permute-start.43 = (bf16[1,5,640]{2,0,1:T(2,128)(2,1)S(1)}, bf16[1,5,640]{2,0,1:T(2,128)(2,1)S(1)}, u32[]{:S(2)}, u32[]{:S(2)}) collective-permute-start(bf16[1,5,640]{2,0,1:T(2,128)(2,1)S(1)} %dynamic-slice_convert_fusion.14), channel_id=1, source_target_pairs={{0,8},{1,9},{2,10},{3,11},{4,12},{5,13},{6,14},{7,15},{8,0},{9,1},... | collective-permute-start | bytes 19208 | tf_op jit(solution)/shard_map/ppermute | solution.py:15
  195.3 2.9 %collective-permute-start.27 = (bf16[1,6,640]{2,0,1:T(2,128)(2,1)S(1)}, bf16[1,6,640]{2,0,1:T(2,128)(2,1)S(1)}, u32[]{:S(2)}, u32[]{:S(2)}) collective-permute-start(bf16[1,6,640]{2,0,1:T(2,128)(2,1)S(1)} %pad_maximum_fusion.7), channel_id=1, source_target_pairs={{0,8},{1,9},{2,10},{3,11},{4,12},{5,13},{6,14},{7,15},{8,0},{9,1},... | collective-permute-start | bytes 23048 | tf_op jit(solution)/shard_map/ppermute | solution.py:15
  198.9 4.2 %collective-permute-done.27 = bf16[1,6,640]{2,0,1:T(2,128)(2,1)S(1)} collective-permute-done((bf16[1,6,640]{2,0,1:T(2,128)(2,1)S(1)}, bf16[1,6,640]{2,0,1:T(2,128)(2,1)S(1)}, u32[]{:S(2)}, u32[]{:S(2)}) %collective-permute-start.27) | collective-permute-done | bytes 7712 | tf_op jit(solution)/shard_map/ppermute | solution.py:15
  (210 shorter events, 40.6 us)
Async XLA Ops:
  0.6 38.2 %copy-start = (bf16[1280,640]{1,0:T(8,128)(2,1)S(1)}, bf16[1280,640]{1,0:T(8,128)(2,1)}, u32[]{:S(2)}) copy-start(bf16[1280,640]{1,0:T(8,128)(2,1)} %param.14) | copy-start | bytes 4915204
  4.5 33.1 %copy-start.1 = (bf16[5,640,640]{2,1,0:T(8,128)(2,1)S(1)}, bf16[5,640,640]{2,1,0:T(8,128)(2,1)}, u32[]{:S(2)}) copy-start(bf16[5,640,640]{2,1,0:T(8,128)(2,1)} %param.13) | copy-start | bytes 12288004
  7.0 16.3 %collective-permute-start = (bf16[128,640]{1,0:T(8,128)(2,1)S(1)}, bf16[128,640]{1,0:T(8,128)(2,1)S(1)}, u32[]{:S(2)}, u32[]{:S(2)}) collective-permute-start(bf16[128,640]{1,0:T(8,128)(2,1)S(1)} %multiply_convert_fusion.1), channel_id=1, source_target_pairs={{0,8},{1,9},{2,10},{3,11},{4,12},{5,13},{6,14},{7,15},{8,16},{9,17... | collective-permute-start | bytes 491528 | tf_op jit(solution)/shard_map/ppermute | solution.py:10
  15.2 17.3 %collective-permute-start.2 = (bf16[128,640]{1,0:T(8,128)(2,1)S(1)}, bf16[128,640]{1,0:T(8,128)(2,1)S(1)}, u32[]{:S(2)}, u32[]{:S(2)}) collective-permute-start(bf16[128,640]{1,0:T(8,128)(2,1)S(1)} %multiply_convert_fusion.1), channel_id=1, source_target_pairs={{4,0},{5,1},{6,2},{7,3},{8,4},{9,5},{10,6},{11,7},{12,8},{13,9},{1... | collective-permute-start | bytes 491528 | tf_op jit(solution)/shard_map/ppermute | solution.py:10
  16.5 21.1 %collective-permute-start.3 = (bf16[128,640]{1,0:T(8,128)(2,1)S(1)}, bf16[128,640]{1,0:T(8,128)(2,1)S(1)}, u32[]{:S(2)}, u32[]{:S(2)}) collective-permute-start(bf16[128,640]{1,0:T(8,128)(2,1)S(1)} %multiply_convert_fusion.1), channel_id=1, source_target_pairs={{8,0},{9,1},{10,2},{11,3},{12,4},{13,5},{14,6},{15,7},{16,8},{17,9... | collective-permute-start | bytes 491528 | tf_op jit(solution)/shard_map/ppermute | solution.py:10
  17.8 14.4 %collective-permute-start.1 = (bf16[128,640]{1,0:T(8,128)(2,1)S(1)}, bf16[128,640]{1,0:T(8,128)(2,1)S(1)}, u32[]{:S(2)}, u32[]{:S(2)}) collective-permute-start(bf16[128,640]{1,0:T(8,128)(2,1)S(1)} %multiply_convert_fusion.1), channel_id=1, source_target_pairs={{0,4},{1,5},{2,6},{3,7},{4,8},{5,9},{6,10},{7,11},{8,12},{9,13},{1... | collective-permute-start | bytes 491528 | tf_op jit(solution)/shard_map/ppermute | solution.py:10
  41.0 3.7 %collective-permute-start.5 = (f32[8,128]{1,0:T(8,128)S(1)}, f32[8,128]{1,0:T(8,128)S(1)}, u32[]{:S(2)}, u32[]{:S(2)}) collective-permute-start(f32[8,128]{1,0:T(8,128)S(1)} %broadcast_in_dim.26), channel_id=1, source_target_pairs={{0,2},{1,3},{2,0},{3,1},{4,6},{5,7},{6,4},{7,5},{8,10},{9,11},{10,... | collective-permute-start | bytes 12296 | tf_op jit(solution)/shard_map/ppermute | solution.py:15
  41.1 3.6 %collective-permute-start.6 = (f32[8,128]{1,0:T(8,128)S(1)}, f32[8,128]{1,0:T(8,128)S(1)}, u32[]{:S(2)}, u32[]{:S(2)}) collective-permute-start(f32[8,128]{1,0:T(8,128)S(1)} %broadcast_in_dim.26), channel_id=1, source_target_pairs={{0,3},{1,2},{2,1},{3,0},{4,7},{5,6},{6,5},{7,4},{8,11},{9,10},{10,... | collective-permute-start | bytes 12296 | tf_op jit(solution)/shard_map/ppermute | solution.py:15
  41.2 3.5 %collective-permute-start.4 = (f32[8,128]{1,0:T(8,128)S(1)}, f32[8,128]{1,0:T(8,128)S(1)}, u32[]{:S(2)}, u32[]{:S(2)}) collective-permute-start(f32[8,128]{1,0:T(8,128)S(1)} %broadcast_in_dim.26), channel_id=1, source_target_pairs={{0,1},{1,0},{2,3},{3,2},{4,5},{5,4},{6,7},{7,6},{8,9},{9,8},{10,11... | collective-permute-start | bytes 12296 | tf_op jit(solution)/shard_map/ppermute | solution.py:15
  45.4 9.5 %collective-permute-start.9 = (f32[8,128]{1,0:T(8,128)S(1)}, f32[8,128]{1,0:T(8,128)S(1)}, u32[]{:S(2)}, u32[]{:S(2)}) collective-permute-start(f32[8,128]{1,0:T(8,128)S(1)} %add_add_fusion.5), channel_id=1, source_target_pairs={{0,80},{1,81},{2,82},{3,83},{4,84},{5,85},{6,86},{7,87},{8,88},{9,... | collective-permute-start | bytes 12296 | tf_op jit(solution)/shard_map/ppermute | solution.py:15
  51.6 3.6 %collective-permute-start.8 = (f32[8,128]{1,0:T(8,128)S(1)}, f32[8,128]{1,0:T(8,128)S(1)}, u32[]{:S(2)}, u32[]{:S(2)}) collective-permute-start(f32[8,128]{1,0:T(8,128)S(1)} %add_add_fusion.5), channel_id=1, source_target_pairs={{0,64},{1,65},{2,66},{3,67},{4,68},{5,69},{6,70},{7,71},{8,72},{9,... | collective-permute-start | bytes 12296 | tf_op jit(solution)/shard_map/ppermute | solution.py:15
  53.5 3.6 %collective-permute-start.7 = (f32[8,128]{1,0:T(8,128)S(1)}, f32[8,128]{1,0:T(8,128)S(1)}, u32[]{:S(2)}, u32[]{:S(2)}) collective-permute-start(f32[8,128]{1,0:T(8,128)S(1)} %add_add_fusion.5), channel_id=1, source_target_pairs={{0,16},{1,17},{2,18},{3,19},{4,20},{5,21},{6,22},{7,23},{8,24},{9,... | collective-permute-start | bytes 12296 | tf_op jit(solution)/shard_map/ppermute | solution.py:15
  57.1 6.9 %collective-permute-start.12 = (f32[8,128]{1,0:T(8,128)S(1)}, f32[8,128]{1,0:T(8,128)S(1)}, u32[]{:S(2)}, u32[]{:S(2)}) collective-permute-start(f32[8,128]{1,0:T(8,128)S(1)} %add_add_fusion.4), channel_id=1, source_target_pairs={{0,36},{1,37},{2,38},{3,39},{4,32},{5,33},{6,34},{7,35},{8,44},{9,... | collective-permute-start | bytes 12296 | tf_op jit(solution)/shard_map/ppermute | solution.py:15
  58.6 5.4 %collective-permute-start.11 = (f32[8,128]{1,0:T(8,128)S(1)}, f32[8,128]{1,0:T(8,128)S(1)}, u32[]{:S(2)}, u32[]{:S(2)}) collective-permute-start(f32[8,128]{1,0:T(8,128)S(1)} %add_add_fusion.4), channel_id=1, source_target_pairs={{0,32},{1,33},{2,34},{3,35},{4,36},{5,37},{6,38},{7,39},{8,40},{9,... | collective-permute-start | bytes 12296 | tf_op jit(solution)/shard_map/ppermute | solution.py:15
  59.1 5.5 %collective-permute-start.10 = (f32[8,128]{1,0:T(8,128)S(1)}, f32[8,128]{1,0:T(8,128)S(1)}, u32[]{:S(2)}, u32[]{:S(2)}) collective-permute-start(f32[8,128]{1,0:T(8,128)S(1)} %add_add_fusion.4), channel_id=1, source_target_pairs={{0,4},{1,5},{2,6},{3,7},{4,0},{5,1},{6,2},{7,3},{8,12},{9,13},{10,... | collective-permute-start | bytes 12296 | tf_op jit(solution)/shard_map/ppermute | solution.py:15
  64.6 11.8 %collective-permute-start.15 = (f32[8,128]{1,0:T(8,128)S(1)}, f32[8,128]{1,0:T(8,128)S(1)}, u32[]{:S(2)}, u32[]{:S(2)}) collective-permute-start(f32[8,128]{1,0:T(8,128)S(1)} %add_add_fusion.3), channel_id=1, source_target_pairs={{0,136},{1,137},{2,138},{3,139},{4,140},{5,141},{6,142},{7,143},{8... | collective-permute-start | bytes 12296 | tf_op jit(solution)/shard_map/ppermute | solution.py:15
  69.4 7.5 %collective-permute-start.14 = (f32[8,128]{1,0:T(8,128)S(1)}, f32[8,128]{1,0:T(8,128)S(1)}, u32[]{:S(2)}, u32[]{:S(2)}) collective-permute-start(f32[8,128]{1,0:T(8,128)S(1)} %add_add_fusion.3), channel_id=1, source_target_pairs={{0,8},{1,9},{2,10},{3,11},{4,12},{5,13},{6,14},{7,15},{8,0},{9,1},... | collective-permute-start | bytes 12296 | tf_op jit(solution)/shard_map/ppermute | solution.py:15
  73.3 5.1 %collective-permute-start.13 = (f32[8,128]{1,0:T(8,128)S(1)}, f32[8,128]{1,0:T(8,128)S(1)}, u32[]{:S(2)}, u32[]{:S(2)}) collective-permute-start(f32[8,128]{1,0:T(8,128)S(1)} %add_add_fusion.3), channel_id=1, source_target_pairs={{0,128},{1,129},{2,130},{3,131},{4,132},{5,133},{6,134},{7,135},{8... | collective-permute-start | bytes 12296 | tf_op jit(solution)/shard_map/ppermute | solution.py:15
  83.0 32.9 %collective-permute-start.30 = (bf16[128,640]{1,0:T(8,128)(2,1)}, bf16[128,640]{1,0:T(8,128)(2,1)}, u32[]{:S(2)}, u32[]{:S(2)}) collective-permute-start(bf16[128,640]{1,0:T(8,128)(2,1)} %add_convert_fusion.1), channel_id=1, source_target_pairs={{0,4},{1,5},{2,6},{3,7},{4,8},{5,9},{6,10},{7,11},{8,12},{9,13},{1... | collective-permute-start | bytes 491528 | tf_op jit(solution)/shard_map/ppermute | solution.py:10
  88.5 28.3 %collective-permute-start.31 = (bf16[128,640]{1,0:T(8,128)(2,1)}, bf16[128,640]{1,0:T(8,128)(2,1)}, u32[]{:S(2)}, u32[]{:S(2)}) collective-permute-start(bf16[128,640]{1,0:T(8,128)(2,1)} %add_convert_fusion.1), channel_id=1, source_target_pairs={{0,8},{1,9},{2,10},{3,11},{4,12},{5,13},{6,14},{7,15},{8,16},{9,17... | collective-permute-start | bytes 491528 | tf_op jit(solution)/shard_map/ppermute | solution.py:10
  92.9 22.0 %collective-permute-start.29 = (bf16[128,640]{1,0:T(8,128)(2,1)}, bf16[128,640]{1,0:T(8,128)(2,1)}, u32[]{:S(2)}, u32[]{:S(2)}) collective-permute-start(bf16[128,640]{1,0:T(8,128)(2,1)} %add_convert_fusion.1), channel_id=1, source_target_pairs={{4,0},{5,1},{6,2},{7,3},{8,4},{9,5},{10,6},{11,7},{12,8},{13,9},{1... | collective-permute-start | bytes 491528 | tf_op jit(solution)/shard_map/ppermute | solution.py:10
  94.1 19.8 %collective-permute-start.28 = (bf16[128,640]{1,0:T(8,128)(2,1)}, bf16[128,640]{1,0:T(8,128)(2,1)}, u32[]{:S(2)}, u32[]{:S(2)}) collective-permute-start(bf16[128,640]{1,0:T(8,128)(2,1)} %add_convert_fusion.1), channel_id=1, source_target_pairs={{8,0},{9,1},{10,2},{11,3},{12,4},{13,5},{14,6},{15,7},{16,8},{17,9... | collective-permute-start | bytes 491528 | tf_op jit(solution)/shard_map/ppermute | solution.py:10
  98.7 19.1 %copy-start.2 = (bf16[5,640,640]{2,1,0:T(8,128)(2,1)S(1)}, bf16[5,640,640]{2,1,0:T(8,128)(2,1)}, u32[]{:S(2)}) copy-start(bf16[5,640,640]{2,1,0:T(8,128)(2,1)} %param.13) | copy-start | bytes 12288004
  100.3 26.2 %collective-permute-start.17 = (bf16[64,5,640]{2,0,1:T(8,128)(2,1)S(1)}, bf16[64,5,640]{2,0,1:T(8,128)(2,1)S(1)}, u32[]{:S(2)}, u32[]{:S(2)}) collective-permute-start(bf16[64,5,640]{2,0,1:T(8,128)(2,1)S(1)} %get-tuple-element.13), channel_id=1, source_target_pairs={{0,1},{1,0},{2,3},{3,2},{4,5},{5,4},{6,7},{7,6},{8,9},{9,8},{10,11... | collective-permute-start | bytes 1228808 | tf_op jit(solution)/shard_map/ppermute | solution.py:15
  113.9 8.9 %collective-permute-start.16 = (bf16[64,6,640]{2,0,1:T(8,128)(2,1)S(1)}, bf16[64,6,640]{2,0,1:T(8,128)(2,1)}, u32[]{:S(2)}, u32[]{:S(2)}) collective-permute-start(bf16[64,6,640]{2,0,1:T(8,128)(2,1)S(1)} %pad_maximum_fusion), channel_id=1, source_target_pairs={{0,1},{1,0},{2,3},{3,2},{4,5},{5,4},{6,7},{7,6},{8,9},{9,8},{10,11... | collective-permute-start | bytes 1474568 | tf_op jit(solution)/shard_map/ppermute | solution.py:15
  122.3 6.0 %collective-permute-start.32 = (bf16[64,5,640]{2,0,1:T(8,128)(2,1)}, bf16[64,5,640]{2,0,1:T(8,128)(2,1)S(1)}, u32[]{:S(2)}, u32[]{:S(2)}) collective-permute-start(bf16[64,5,640]{2,0,1:T(8,128)(2,1)} %get-tuple-element.11), channel_id=1, source_target_pairs={{0,1},{1,0},{2,3},{3,2},{4,5},{5,4},{6,7},{7,6},{8,9},{9,8},{10,11... | collective-permute-start | bytes 1228808 | tf_op jit(solution)/shard_map/ppermute | solution.py:15
  122.8 5.5 %collective-permute-start.33 = (bf16[64,5,640]{2,0,1:T(8,128)(2,1)}, bf16[64,5,640]{2,0,1:T(8,128)(2,1)S(1)}, u32[]{:S(2)}, u32[]{:S(2)}) collective-permute-start(bf16[64,5,640]{2,0,1:T(8,128)(2,1)} %get-tuple-element.12), channel_id=1, source_target_pairs={{0,1},{1,0},{2,3},{3,2},{4,5},{5,4},{6,7},{7,6},{8,9},{9,8},{10,11... | collective-permute-start | bytes 1228808 | tf_op jit(solution)/shard_map/ppermute | solution.py:15
  126.5 2.4 %copy-start.5 = (f32[256,5,640]{2,0,1:T(8,128)S(1)}, f32[256,5,640]{2,0,1:T(8,128)}, u32[]{:S(2)}) copy-start(f32[256,5,640]{2,0,1:T(8,128)} %copy-done.4) | copy-start | bytes 9830404
  129.3 8.0 %collective-permute-start.34 = (bf16[32,5,640]{2,0,1:T(8,128)(2,1)S(1)}, bf16[32,5,640]{2,0,1:T(8,128)(2,1)S(1)}, u32[]{:S(2)}, u32[]{:S(2)}) collective-permute-start(bf16[32,5,640]{2,0,1:T(8,128)(2,1)S(1)} %get-tuple-element.15), channel_id=1, source_target_pairs={{0,2},{1,3},{2,0},{3,1},{4,6},{5,7},{6,4},{7,5},{8,10},{9,11},{10,... | collective-permute-start | bytes 614408 | tf_op jit(solution)/shard_map/ppermute | solution.py:15
  129.4 12.3 %collective-permute-start.35 = (bf16[32,5,640]{2,0,1:T(8,128)(2,1)S(1)}, bf16[32,5,640]{2,0,1:T(8,128)(2,1)S(1)}, u32[]{:S(2)}, u32[]{:S(2)}) collective-permute-start(bf16[32,5,640]{2,0,1:T(8,128)(2,1)S(1)} %get-tuple-element.16), channel_id=1, source_target_pairs={{0,2},{1,3},{2,0},{3,1},{4,6},{5,7},{6,4},{7,5},{8,10},{9,11},{10,... | collective-permute-start | bytes 614408 | tf_op jit(solution)/shard_map/ppermute | solution.py:15
  131.4 19.5 %collective-permute-start.19 = (bf16[32,5,640]{2,0,1:T(8,128)(2,1)S(1)}, bf16[32,5,640]{2,0,1:T(8,128)(2,1)S(1)}, u32[]{:S(2)}, u32[]{:S(2)}) collective-permute-start(bf16[32,5,640]{2,0,1:T(8,128)(2,1)S(1)} %get-tuple-element.17), channel_id=1, source_target_pairs={{0,2},{1,3},{2,0},{3,1},{4,6},{5,7},{6,4},{7,5},{8,10},{9,11},{10,... | collective-permute-start | bytes 614408 | tf_op jit(solution)/shard_map/ppermute | solution.py:15
  131.6 19.2 %collective-permute-start.18 = (bf16[32,6,640]{2,0,1:T(8,128)(2,1)S(1)}, bf16[32,6,640]{2,0,1:T(8,128)(2,1)S(1)}, u32[]{:S(2)}, u32[]{:S(2)}) collective-permute-start(bf16[32,6,640]{2,0,1:T(8,128)(2,1)S(1)} %pad_maximum_fusion.1), channel_id=1, source_target_pairs={{0,2},{1,3},{2,0},{3,1},{4,6},{5,7},{6,4},{7,5},{8,10},{9,11},{10,... | collective-permute-start | bytes 737288 | tf_op jit(solution)/shard_map/ppermute | solution.py:15
  142.5 11.2 %collective-permute-start.36 = (bf16[16,5,640]{2,0,1:T(8,128)(2,1)}, bf16[16,5,640]{2,0,1:T(8,128)(2,1)}, u32[]{:S(2)}, u32[]{:S(2)}) collective-permute-start(bf16[16,5,640]{2,0,1:T(8,128)(2,1)} %get-tuple-element.19), channel_id=1, source_target_pairs={{0,16},{1,17},{2,18},{3,19},{4,20},{5,21},{6,22},{7,23},{8,24},{9,... | collective-permute-start | bytes 307208 | tf_op jit(solution)/shard_map/ppermute | solution.py:15
  142.5 11.2 %collective-permute-start.37 = (bf16[16,5,640]{2,0,1:T(8,128)(2,1)}, bf16[16,5,640]{2,0,1:T(8,128)(2,1)}, u32[]{:S(2)}, u32[]{:S(2)}) collective-permute-start(bf16[16,5,640]{2,0,1:T(8,128)(2,1)} %get-tuple-element.20), channel_id=1, source_target_pairs={{0,16},{1,17},{2,18},{3,19},{4,20},{5,21},{6,22},{7,23},{8,24},{9,... | collective-permute-start | bytes 307208 | tf_op jit(solution)/shard_map/ppermute | solution.py:15
  153.6 10.5 %collective-permute-start.21 = (bf16[16,5,640]{2,0,1:T(8,128)(2,1)}, bf16[16,5,640]{2,0,1:T(8,128)(2,1)S(1)}, u32[]{:S(2)}, u32[]{:S(2)}) collective-permute-start(bf16[16,5,640]{2,0,1:T(8,128)(2,1)} %get-tuple-element.21), channel_id=1, source_target_pairs={{0,16},{1,17},{2,18},{3,19},{4,20},{5,21},{6,22},{7,23},{8,24},{9,... | collective-permute-start | bytes 307208 | tf_op jit(solution)/shard_map/ppermute | solution.py:15
  154.8 4.2 %collective-permute-start.38 = (bf16[8,5,640]{2,0,1:T(8,128)(2,1)S(1)}, bf16[8,5,640]{2,0,1:T(8,128)(2,1)S(1)}, u32[]{:S(2)}, u32[]{:S(2)}) collective-permute-start(bf16[8,5,640]{2,0,1:T(8,128)(2,1)S(1)} %get-tuple-element.23), channel_id=1, source_target_pairs={{0,64},{1,65},{2,66},{3,67},{4,68},{5,69},{6,70},{7,71},{8,72},{9,... | collective-permute-start | bytes 153608 | tf_op jit(solution)/shard_map/ppermute | solution.py:15
  155.8 4.1 %collective-permute-start.39 = (bf16[8,5,640]{2,0,1:T(8,128)(2,1)S(1)}, bf16[8,5,640]{2,0,1:T(8,128)(2,1)S(1)}, u32[]{:S(2)}, u32[]{:S(2)}) collective-permute-start(bf16[8,5,640]{2,0,1:T(8,128)(2,1)S(1)} %get-tuple-element.24), channel_id=1, source_target_pairs={{0,64},{1,65},{2,66},{3,67},{4,68},{5,69},{6,70},{7,71},{8,72},{9,... | collective-permute-start | bytes 153608 | tf_op jit(solution)/shard_map/ppermute | solution.py:15
  157.0 5.2 %collective-permute-start.20 = (bf16[16,6,640]{2,0,1:T(8,128)(2,1)S(1)}, bf16[16,6,640]{2,0,1:T(8,128)(2,1)S(1)}, u32[]{:S(2)}, u32[]{:S(2)}) collective-permute-start(bf16[16,6,640]{2,0,1:T(8,128)(2,1)S(1)} %pad_maximum_fusion.2), channel_id=1, source_target_pairs={{0,16},{1,17},{2,18},{3,19},{4,20},{5,21},{6,22},{7,23},{8,24},{9,... | collective-permute-start | bytes 368648 | tf_op jit(solution)/shard_map/ppermute | solution.py:15
  159.9 6.5 %collective-permute-start.40 = (bf16[8,5,640]{2,0,1:T(8,128)(2,1)S(1)}, bf16[8,5,640]{2,0,1:T(8,128)(2,1)S(1)}, u32[]{:S(2)}, u32[]{:S(2)}) collective-permute-start(bf16[8,5,640]{2,0,1:T(8,128)(2,1)S(1)} %dynamic-slice_convert_fusion.8), channel_id=1, source_target_pairs={{0,4},{1,5},{2,6},{3,7},{4,0},{5,1},{6,2},{7,3},{8,12},{9,13},{10,... | collective-permute-start | bytes 153608 | tf_op jit(solution)/shard_map/ppermute | solution.py:15
  164.2 7.8 %collective-permute-start.23 = (bf16[8,5,640]{2,0,1:T(8,128)(2,1)S(1)}, bf16[8,5,640]{2,0,1:T(8,128)(2,1)S(1)}, u32[]{:S(2)}, u32[]{:S(2)}) collective-permute-start(bf16[8,5,640]{2,0,1:T(8,128)(2,1)S(1)} %get-tuple-element.25), channel_id=1, source_target_pairs={{0,64},{1,65},{2,66},{3,67},{4,68},{5,69},{6,70},{7,71},{8,72},{9,... | collective-permute-start | bytes 153608 | tf_op jit(solution)/shard_map/ppermute | solution.py:15
  165.8 4.3 %collective-permute-start.22 = (bf16[8,6,640]{2,0,1:T(8,128)(2,1)S(1)}, bf16[8,6,640]{2,0,1:T(8,128)(2,1)S(1)}, u32[]{:S(2)}, u32[]{:S(2)}) collective-permute-start(bf16[8,6,640]{2,0,1:T(8,128)(2,1)S(1)} %pad_maximum_fusion.3), channel_id=1, source_target_pairs={{0,64},{1,65},{2,66},{3,67},{4,68},{5,69},{6,70},{7,71},{8,72},{9,... | collective-permute-start | bytes 184328 | tf_op jit(solution)/shard_map/ppermute | solution.py:15
  166.5 7.0 %collective-permute-start.41 = (bf16[4,5,640]{2,0,1:T(4,128)(2,1)S(1)}, bf16[4,5,640]{2,0,1:T(4,128)(2,1)S(1)}, u32[]{:S(2)}, u32[]{:S(2)}) collective-permute-start(bf16[4,5,640]{2,0,1:T(4,128)(2,1)S(1)} %dynamic-slice_convert_fusion.10), channel_id=1, source_target_pairs={{0,32},{1,33},{2,34},{3,35},{4,36},{5,37},{6,38},{7,39},{8,40},{9,... | collective-permute-start | bytes 76808 | tf_op jit(solution)/shard_map/ppermute | solution.py:15
  172.2 5.2 %collective-permute-start.24 = (bf16[8,6,640]{2,0,1:T(8,128)(2,1)S(1)}, bf16[8,6,640]{2,0,1:T(8,128)(2,1)S(1)}, u32[]{:S(2)}, u32[]{:S(2)}) collective-permute-start(bf16[8,6,640]{2,0,1:T(8,128)(2,1)S(1)} %pad_maximum_fusion.4), channel_id=1, source_target_pairs={{0,4},{1,5},{2,6},{3,7},{4,0},{5,1},{6,2},{7,3},{8,12},{9,13},{10,... | collective-permute-start | bytes 184328 | tf_op jit(solution)/shard_map/ppermute | solution.py:15
  173.5 8.9 %collective-permute-start.42 = (bf16[2,5,640]{2,0,1:T(2,128)(2,1)S(1)}, bf16[2,5,640]{2,0,1:T(2,128)(2,1)S(1)}, u32[]{:S(2)}, u32[]{:S(2)}) collective-permute-start(bf16[2,5,640]{2,0,1:T(2,128)(2,1)S(1)} %dynamic-slice_convert_fusion.12), channel_id=1, source_target_pairs={{0,128},{1,129},{2,130},{3,131},{4,132},{5,133},{6,134},{7,135},{8... | collective-permute-start | bytes 38408 | tf_op jit(solution)/shard_map/ppermute | solution.py:15
  179.4 5.5 %collective-permute-start.25 = (bf16[4,6,640]{2,0,1:T(4,128)(2,1)S(1)}, bf16[4,6,640]{2,0,1:T(4,128)(2,1)S(1)}, u32[]{:S(2)}, u32[]{:S(2)}) collective-permute-start(bf16[4,6,640]{2,0,1:T(4,128)(2,1)S(1)} %pad_maximum_fusion.5), channel_id=1, source_target_pairs={{0,32},{1,33},{2,34},{3,35},{4,36},{5,37},{6,38},{7,39},{8,40},{9,... | collective-permute-start | bytes 92168 | tf_op jit(solution)/shard_map/ppermute | solution.py:15
  186.9 6.4 %collective-permute-start.26 = (bf16[2,6,640]{2,0,1:T(2,128)(2,1)S(1)}, bf16[2,6,640]{2,0,1:T(2,128)(2,1)S(1)}, u32[]{:S(2)}, u32[]{:S(2)}) collective-permute-start(bf16[2,6,640]{2,0,1:T(2,128)(2,1)S(1)} %pad_maximum_fusion.6), channel_id=1, source_target_pairs={{0,128},{1,129},{2,130},{3,131},{4,132},{5,133},{6,134},{7,135},{8... | collective-permute-start | bytes 46088 | tf_op jit(solution)/shard_map/ppermute | solution.py:15
  188.8 9.4 %collective-permute-start.43 = (bf16[1,5,640]{2,0,1:T(2,128)(2,1)S(1)}, bf16[1,5,640]{2,0,1:T(2,128)(2,1)S(1)}, u32[]{:S(2)}, u32[]{:S(2)}) collective-permute-start(bf16[1,5,640]{2,0,1:T(2,128)(2,1)S(1)} %dynamic-slice_convert_fusion.14), channel_id=1, source_target_pairs={{0,8},{1,9},{2,10},{3,11},{4,12},{5,13},{6,14},{7,15},{8,0},{9,1},... | collective-permute-start | bytes 19208 | tf_op jit(solution)/shard_map/ppermute | solution.py:15
  195.3 7.7 %collective-permute-start.27 = (bf16[1,6,640]{2,0,1:T(2,128)(2,1)S(1)}, bf16[1,6,640]{2,0,1:T(2,128)(2,1)S(1)}, u32[]{:S(2)}, u32[]{:S(2)}) collective-permute-start(bf16[1,6,640]{2,0,1:T(2,128)(2,1)S(1)} %pad_maximum_fusion.7), channel_id=1, source_target_pairs={{0,8},{1,9},{2,10},{3,11},{4,12},{5,13},{6,14},{7,15},{8,0},{9,1},... | collective-permute-start | bytes 23048 | tf_op jit(solution)/shard_map/ppermute | solution.py:15
  (7 other events, 10.2 us)

commit v9 on v6

--- a/solution.py
+++ b/solution.py
@@ -93,11 +93,13 @@
     context_rows = float(local_rows * seq_devices)
     masked = mask_flags.astype(jnp.float32)
     local_count = jnp.sum(masked)
-    mask_total = count_sum(jnp.broadcast_to(local_count, (8, 128)), "seq")[0, 0]
+    count_tile = count_sum(jnp.broadcast_to(local_count, (8, 128)), "seq")
     alphabet = jnp.arange(vocab_size, dtype=jnp.int32)
     first_act = norm_gelu(hidden_in.astype(jnp.float32)).astype(jnp.bfloat16)
     first_pre = jnp.dot(first_act, w_in, preferred_element_type=jnp.float32)
     narrow_activation = norm_gelu(first_pre).astype(jnp.bfloat16)
+    count_tile, narrow_activation = lax.optimization_barrier((count_tile, narrow_activation))
+    mask_total = count_tile[0, 0]
     kernel_tap_pile = jnp.stack(spread(narrow_activation, shard_reach))
     conv_pre = jnp.einsum(
         "krc,kcb->rb", kernel_tap_pile, conv_weight, preferred_element_type=jnp.float32

time: 204 us -> 200 us (0.980)
  starting transfers between devices: 103 us -> 98.7 us
  waiting for transfers between devices: 61.6 us -> 59 us
    ppermute x8, waiting for transfers between devices: 17.9 us -> 13.1 us  [from_behind(): return lax.ppermute(block, axis, route)]
    ppermute x8, starting transfers between devices: 31.3 us -> 28.5 us  [from_behind(): return lax.ppermute(block, axis, route)]
    dot_general x1, matrix products: 0.92 us -> 3.13 us  [shards(): jnp.einsum('krc,kcb->rb', kernel_tap_pile, conv_weight, preferred_element...]
    ppermute x44, waiting for transfers between devices: 43.7 us -> 45.9 us  [swap_with(): return lax.ppermute(block, axis, [(i, i ^ bit) for i in range(devices)])]
    unnamed x26 -> x27, local copies, waits for them, and re-layouts: 5.48 us -> 5.35 us
  transfers between devices with their start and end apart: 52 -> 52, of which waited for: 27 -> 28; matrix products, arithmetic and copies ran while one was open for 10% -> 12% of each run, Pallas kernels for 0% -> 0%
where the time goes in v9:
time: 200 us
  starting transfers between devices  98.7 us (49%)
  waiting for transfers between devices  59 us (30%)
  local copies, waits for them, and re-layouts  15.1 us (8%)
  other arithmetic  12.5 us (6%)
  matrix products  9.85 us (5%)
  between operations  4.66 us (2%)
    ppermute x44, starting transfers between devices, swap_with(): return lax.ppermute(block, axis, [(i, i ^ bit) for i in range(devices)])  70.1 us
    ppermute x44, waiting for transfers between devices, swap_with(): return lax.ppermute(block, axis, [(i, i ^ bit) for i in range(devices)])  45.9 us
    ppermute x8, starting transfers between devices, from_behind(): return lax.ppermute(block, axis, route)  28.5 us
    ppermute x8, waiting for transfers between devices, from_behind(): return lax.ppermute(block, axis, route)  13.1 us
    unnamed x27, local copies, waits for them, and re-layouts  5.35 us
  transfers between devices with their start and end apart: 52, of which 28 were waited for; matrix products, arithmetic and copies ran while one was open for 12% of the time, Pallas kernels for 0%

profile of v9, /device:TPU:32, one launch (start us, length us, event | category | flops | bytes accessed | tf_op | source)
XLA Modules:
  0.0 199.7 jit_solution(8429463760026644672)
XLA Ops:
  0.6 1.4 convert_reduce_fusion.1
  2.8 1.9 collective-permute-start.1
  7.0 1.4 fusion.9
  8.4 1.9 fusion.53
  11.1 2.5 %collective-permute-start.5 = (f32[8,128]{1,0:T(8,128)S(1)}, f32[8,128]{1,0:T(8,128)S(1)}, u32[]{:S(2)}, u32[]{:S(2)}) collective-permute-start(f32[8,128]{1,0:T(8,128)S(1)} %add_add_fusion.5), channel_id=1, source_target_pairs={{0,80},{1,81},{2,82},{3,83},{4,84},{5,85},{6,86},{7,87},{8,88},{9,... | collective-permute-start | bytes 12296 | tf_op jit(solution)/shard_map/ppermute | solution.py:15
  15.7 1.5 collective-permute-done.4
  17.7 5.4 %collective-permute-start.8 = (f32[8,128]{1,0:T(8,128)S(1)}, f32[8,128]{1,0:T(8,128)S(1)}, u32[]{:S(2)}, u32[]{:S(2)}) collective-permute-start(f32[8,128]{1,0:T(8,128)S(1)} %add_add_fusion.4), channel_id=1, source_target_pairs={{0,36},{1,37},{2,38},{3,39},{4,32},{5,33},{6,34},{7,35},{8,44},{9,... | collective-permute-start | bytes 12296 | tf_op jit(solution)/shard_map/ppermute | solution.py:15
  24.7 3.5 %collective-permute-done.7 = f32[8,128]{1,0:T(8,128)S(1)} collective-permute-done((f32[8,128]{1,0:T(8,128)S(1)}, f32[8,128]{1,0:T(8,128)S(1)}, u32[]{:S(2)}, u32[]{:S(2)}) %collective-permute-start.7) | collective-permute-done | bytes 4128 | tf_op jit(solution)/shard_map/ppermute | solution.py:15
  28.4 7.1 %collective-permute-start.11 = (f32[8,128]{1,0:T(8,128)S(1)}, f32[8,128]{1,0:T(8,128)S(1)}, u32[]{:S(2)}, u32[]{:S(2)}) collective-permute-start(f32[8,128]{1,0:T(8,128)S(1)} %add_add_fusion.3), channel_id=1, source_target_pairs={{0,136},{1,137},{2,138},{3,139},{4,140},{5,141},{6,142},{7,143},{8... | collective-permute-start | bytes 12296 | tf_op jit(solution)/shard_map/ppermute | solution.py:15
  35.5 1.5 collective-permute-start.10
  38.3 4.7 %collective-permute-done.10 = f32[8,128]{1,0:T(8,128)S(1)} collective-permute-done((f32[8,128]{1,0:T(8,128)S(1)}, f32[8,128]{1,0:T(8,128)S(1)}, u32[]{:S(2)}, u32[]{:S(2)}) %collective-permute-start.10) | collective-permute-done | bytes 4128 | tf_op jit(solution)/shard_map/ppermute | solution.py:15
  43.1 5.4 %collective-permute-start.12 = (bf16[128,640]{1,0:T(8,128)(2,1)S(1)}, bf16[128,640]{1,0:T(8,128)(2,1)S(1)}, u32[]{:S(2)}, u32[]{:S(2)}) collective-permute-start(bf16[128,640]{1,0:T(8,128)(2,1)S(1)} %multiply_convert_fusion.1), channel_id=1, source_target_pairs={{0,8},{1,9},{2,10},{3,11},{4,12},{5,13},{6,14},{7,15},{8,16},{9,17... | collective-permute-start | bytes 491528 | tf_op jit(solution)/shard_map/ppermute | solution.py:10
  50.1 3.4 %collective-permute-start.13 = (bf16[128,640]{1,0:T(8,128)(2,1)S(1)}, bf16[128,640]{1,0:T(8,128)(2,1)S(1)}, u32[]{:S(2)}, u32[]{:S(2)}) collective-permute-start(bf16[128,640]{1,0:T(8,128)(2,1)S(1)} %multiply_convert_fusion.1), channel_id=1, source_target_pairs={{0,4},{1,5},{2,6},{3,7},{4,8},{5,9},{6,10},{7,11},{8,12},{9,13},{1... | collective-permute-start | bytes 491528 | tf_op jit(solution)/shard_map/ppermute | solution.py:10
  57.3 2.8 %collective-permute-done.13 = bf16[128,640]{1,0:T(8,128)(2,1)S(1)} collective-permute-done((bf16[128,640]{1,0:T(8,128)(2,1)S(1)}, bf16[128,640]{1,0:T(8,128)(2,1)S(1)}, u32[]{:S(2)}, u32[]{:S(2)}) %collective-permute-start.13) | collective-permute-done | bytes 163872 | tf_op jit(solution)/shard_map/ppermute | solution.py:10
  60.2 2.3 %collective-permute-done.14 = bf16[128,640]{1,0:T(8,128)(2,1)S(1)} collective-permute-done((bf16[128,640]{1,0:T(8,128)(2,1)S(1)}, bf16[128,640]{1,0:T(8,128)(2,1)S(1)}, u32[]{:S(2)}, u32[]{:S(2)}) %collective-permute-start.14) | collective-permute-done | bytes 163872 | tf_op jit(solution)/shard_map/ppermute | solution.py:10
  62.5 7.9 %collective-permute-done.15 = bf16[128,640]{1,0:T(8,128)(2,1)S(1)} collective-permute-done((bf16[128,640]{1,0:T(8,128)(2,1)S(1)}, bf16[128,640]{1,0:T(8,128)(2,1)S(1)}, u32[]{:S(2)}, u32[]{:S(2)}) %collective-permute-start.15) | collective-permute-done | bytes 163872 | tf_op jit(solution)/shard_map/ppermute | solution.py:10
  70.5 3.1 %fusion.54 = (f32[128]{0:T(128)S(1)}, f32[128,640]{1,0:T(8,128)S(1)}) fusion(bf16[5,128,640]{2,1,0:T(8,128)(2,1)S(1)} %bitcast_dynamic-update-slice_fusion.5, bf16[5,640,640]{2,1,0:T(8,128)(2,1)} %param.13), kind=kOutput, calls=%fused_computation.139 | convolution fusion | flops 524369792 | bytes 5243392 | tf_op jit(solution)/shard_map/krc,kcb->rb/dot_general | solution.py:104
  80.5 6.1 %collective-permute-start.26 = (bf16[128,640]{1,0:T(8,128)(2,1)}, bf16[128,640]{1,0:T(8,128)(2,1)}, u32[]{:S(2)}, u32[]{:S(2)}) collective-permute-start(bf16[128,640]{1,0:T(8,128)(2,1)} %add_convert_fusion.1), channel_id=1, source_target_pairs={{0,4},{1,5},{2,6},{3,7},{4,8},{5,9},{6,10},{7,11},{8,12},{9,13},{1... | collective-permute-start | bytes 491528 | tf_op jit(solution)/shard_map/ppermute | solution.py:10
  86.6 8.5 %collective-permute-start.27 = (bf16[128,640]{1,0:T(8,128)(2,1)}, bf16[128,640]{1,0:T(8,128)(2,1)}, u32[]{:S(2)}, u32[]{:S(2)}) collective-permute-start(bf16[128,640]{1,0:T(8,128)(2,1)} %add_convert_fusion.1), channel_id=1, source_target_pairs={{0,8},{1,9},{2,10},{3,11},{4,12},{5,13},{6,14},{7,15},{8,16},{9,17... | collective-permute-start | bytes 491528 | tf_op jit(solution)/shard_map/ppermute | solution.py:10
  104.9 1.5 multiply_reduce_fusion
  109.2 1.9 collective-permute-start.43
  113.5 1.9 collective-permute-start.31
  116.1 4.9 %collective-permute-start.18 = (f32[8,128]{1,0:T(8,128)S(1)}, f32[8,128]{1,0:T(8,128)S(1)}, u32[]{:S(2)}, u32[]{:S(2)}) collective-permute-start(f32[8,128]{1,0:T(8,128)S(1)} %fusion.66), channel_id=1, source_target_pairs={{0,16},{1,17},{2,18},{3,19},{4,20},{5,21},{6,22},{7,23},{8,24},{9,... | collective-permute-start | bytes 12296 | tf_op jit(solution)/shard_map/ppermute | solution.py:15
  121.0 1.6 collective-permute-done.18
  122.6 5.8 %collective-permute-start.19 = (f32[8,128]{1,0:T(8,128)S(1)}, f32[8,128]{1,0:T(8,128)S(1)}, u32[]{:S(2)}, u32[]{:S(2)}) collective-permute-start(f32[8,128]{1,0:T(8,128)S(1)} %add.294), channel_id=1, source_target_pairs={{0,64},{1,65},{2,66},{3,67},{4,68},{5,69},{6,70},{7,71},{8,72},{9,... | collective-permute-start | bytes 12296 | tf_op jit(solution)/shard_map/ppermute | solution.py:15
  128.4 1.6 collective-permute-done.19
  130.8 3.6 %collective-permute-done.20 = f32[8,128]{1,0:T(8,128)S(1)} collective-permute-done((f32[8,128]{1,0:T(8,128)S(1)}, f32[8,128]{1,0:T(8,128)S(1)}, u32[]{:S(2)}, u32[]{:S(2)}) %collective-permute-start.20) | collective-permute-done | bytes 4128 | tf_op jit(solution)/shard_map/ppermute | solution.py:15
  134.5 1.7 collective-permute-start.21
  136.2 3.4 %collective-permute-done.21 = f32[8,128]{1,0:T(8,128)S(1)} collective-permute-done((f32[8,128]{1,0:T(8,128)S(1)}, f32[8,128]{1,0:T(8,128)S(1)}, u32[]{:S(2)}, u32[]{:S(2)}) %collective-permute-start.21) | collective-permute-done | bytes 4128 | tf_op jit(solution)/shard_map/ppermute | solution.py:15
  139.6 4.3 %collective-permute-start.22 = (f32[8,128]{1,0:T(8,128)S(1)}, f32[8,128]{1,0:T(8,128)S(1)}, u32[]{:S(2)}, u32[]{:S(2)}) collective-permute-start(f32[8,128]{1,0:T(8,128)S(1)} %add.297), channel_id=1, source_target_pairs={{0,128},{1,129},{2,130},{3,131},{4,132},{5,133},{6,134},{7,135},{8... | collective-permute-start | bytes 12296 | tf_op jit(solution)/shard_map/ppermute | solution.py:15
  143.8 1.6 collective-permute-done.22
  145.4 1.6 collective-permute-start.23
  147.0 5.9 %collective-permute-done.23 = f32[8,128]{1,0:T(8,128)S(1)} collective-permute-done((f32[8,128]{1,0:T(8,128)S(1)}, f32[8,128]{1,0:T(8,128)S(1)}, u32[]{:S(2)}, u32[]{:S(2)}) %collective-permute-start.23) | collective-permute-done | bytes 4128 | tf_op jit(solution)/shard_map/ppermute | solution.py:15
  154.8 1.7 convert_add_fusion.2
  162.5 4.0 %collective-permute-start.35 = (bf16[8,5,640]{2,0,1:T(8,128)(2,1)S(1)}, bf16[8,5,640]{2,0,1:T(8,128)(2,1)S(1)}, u32[]{:S(2)}, u32[]{:S(2)}) collective-permute-start(bf16[8,5,640]{2,0,1:T(8,128)(2,1)S(1)} %get-tuple-element.28), channel_id=1, source_target_pairs={{0,64},{1,65},{2,66},{3,67},{4,68},{5,69},{6,70},{7,71},{8,72},{9,... | collective-permute-start | bytes 153608 | tf_op jit(solution)/shard_map/ppermute | solution.py:15
  166.7 2.0 %collective-permute-start.47 = (bf16[8,5,640]{2,0,1:T(8,128)(2,1)S(1)}, bf16[8,5,640]{2,0,1:T(8,128)(2,1)S(1)}, u32[]{:S(2)}, u32[]{:S(2)}) collective-permute-start(bf16[8,5,640]{2,0,1:T(8,128)(2,1)S(1)} %get-tuple-element.26), channel_id=1, source_target_pairs={{0,64},{1,65},{2,66},{3,67},{4,68},{5,69},{6,70},{7,71},{8,72},{9,... | collective-permute-start | bytes 153608 | tf_op jit(solution)/shard_map/ppermute | solution.py:15
  168.9 1.8 collective-permute-done.34
  171.2 1.7 collective-permute-done.46
  173.9 1.9 collective-permute-done.36
  176.5 1.5 collective-permute-done.48
  178.1 1.5 collective-permute-start.49
  179.6 1.7 collective-permute-done.37
  181.3 3.5 %collective-permute-start.38 = (bf16[2,5,640]{2,0,1:T(2,128)(2,1)S(1)}, bf16[2,5,640]{2,0,1:T(2,128)(2,1)S(1)}, u32[]{:S(2)}, u32[]{:S(2)}) collective-permute-start(bf16[2,5,640]{2,0,1:T(2,128)(2,1)S(1)} %dynamic-slice_convert_fusion.13), channel_id=1, source_target_pairs={{0,128},{1,129},{2,130},{3,131},{4,132},{5,133},{6,134},{7,135},{8... | collective-permute-start | bytes 38408 | tf_op jit(solution)/shard_map/ppermute | solution.py:15
  184.9 2.1 %collective-permute-start.50 = (bf16[2,5,640]{2,0,1:T(2,128)(2,1)S(1)}, bf16[2,5,640]{2,0,1:T(2,128)(2,1)S(1)}, u32[]{:S(2)}, u32[]{:S(2)}) collective-permute-start(bf16[2,5,640]{2,0,1:T(2,128)(2,1)S(1)} %dynamic-slice_convert_fusion.12), channel_id=1, source_target_pairs={{0,128},{1,129},{2,130},{3,131},{4,132},{5,133},{6,134},{7,135},{8... | collective-permute-start | bytes 38408 | tf_op jit(solution)/shard_map/ppermute | solution.py:15
  187.0 2.5 %collective-permute-start.39 = (bf16[1,5,640]{2,0,1:T(2,128)(2,1)S(1)}, bf16[1,5,640]{2,0,1:T(2,128)(2,1)S(1)}, u32[]{:S(2)}, u32[]{:S(2)}) collective-permute-start(bf16[1,5,640]{2,0,1:T(2,128)(2,1)S(1)} %dynamic-slice_convert_fusion.15), channel_id=1, source_target_pairs={{0,8},{1,9},{2,10},{3,11},{4,12},{5,13},{6,14},{7,15},{8,0},{9,1},... | collective-permute-start | bytes 19208 | tf_op jit(solution)/shard_map/ppermute | solution.py:15
  190.3 2.9 %collective-permute-start.51 = (bf16[1,5,640]{2,0,1:T(2,128)(2,1)S(1)}, bf16[1,5,640]{2,0,1:T(2,128)(2,1)S(1)}, u32[]{:S(2)}, u32[]{:S(2)}) collective-permute-start(bf16[1,5,640]{2,0,1:T(2,128)(2,1)S(1)} %dynamic-slice_convert_fusion.14), channel_id=1, source_target_pairs={{0,8},{1,9},{2,10},{3,11},{4,12},{5,13},{6,14},{7,15},{8,0},{9,1},... | collective-permute-start | bytes 19208 | tf_op jit(solution)/shard_map/ppermute | solution.py:15
  193.2 1.5 collective-permute-done.39
  195.4 2.6 %collective-permute-done.51 = bf16[1,5,640]{2,0,1:T(2,128)(2,1)S(1)} collective-permute-done((bf16[1,5,640]{2,0,1:T(2,128)(2,1)S(1)}, bf16[1,5,640]{2,0,1:T(2,128)(2,1)S(1)}, u32[]{:S(2)}, u32[]{:S(2)}) %collective-permute-start.51) | collective-permute-done | bytes 6432 | tf_op jit(solution)/shard_map/ppermute | solution.py:15
  (181 shorter events, 48.3 us)
Async XLA Ops:
  2.7 7.7 %collective-permute-start.2 = (f32[8,128]{1,0:T(8,128)S(1)}, f32[8,128]{1,0:T(8,128)S(1)}, u32[]{:S(2)}, u32[]{:S(2)}) collective-permute-start(f32[8,128]{1,0:T(8,128)S(1)} %broadcast_in_dim.12), channel_id=1, source_target_pairs={{0,3},{1,2},{2,1},{3,0},{4,7},{5,6},{6,5},{7,4},{8,11},{9,10},{10,... | collective-permute-start | bytes 12296 | tf_op jit(solution)/shard_map/ppermute | solution.py:15
  2.8 7.6 %collective-permute-start.1 = (f32[8,128]{1,0:T(8,128)S(1)}, f32[8,128]{1,0:T(8,128)S(1)}, u32[]{:S(2)}, u32[]{:S(2)}) collective-permute-start(f32[8,128]{1,0:T(8,128)S(1)} %broadcast_in_dim.12), channel_id=1, source_target_pairs={{0,2},{1,3},{2,0},{3,1},{4,6},{5,7},{6,4},{7,5},{8,10},{9,11},{10,... | collective-permute-start | bytes 12296 | tf_op jit(solution)/shard_map/ppermute | solution.py:15
  4.7 5.7 %collective-permute-start = (f32[8,128]{1,0:T(8,128)S(1)}, f32[8,128]{1,0:T(8,128)S(1)}, u32[]{:S(2)}, u32[]{:S(2)}) collective-permute-start(f32[8,128]{1,0:T(8,128)S(1)} %broadcast_in_dim.12), channel_id=1, source_target_pairs={{0,1},{1,0},{2,3},{3,2},{4,5},{5,4},{6,7},{7,6},{8,9},{9,8},{10,11... | collective-permute-start | bytes 12296 | tf_op jit(solution)/shard_map/ppermute | solution.py:15
  11.1 4.6 %collective-permute-start.5 = (f32[8,128]{1,0:T(8,128)S(1)}, f32[8,128]{1,0:T(8,128)S(1)}, u32[]{:S(2)}, u32[]{:S(2)}) collective-permute-start(f32[8,128]{1,0:T(8,128)S(1)} %add_add_fusion.5), channel_id=1, source_target_pairs={{0,80},{1,81},{2,82},{3,83},{4,84},{5,85},{6,86},{7,87},{8,88},{9,... | collective-permute-start | bytes 12296 | tf_op jit(solution)/shard_map/ppermute | solution.py:15
  17.7 7.0 %collective-permute-start.8 = (f32[8,128]{1,0:T(8,128)S(1)}, f32[8,128]{1,0:T(8,128)S(1)}, u32[]{:S(2)}, u32[]{:S(2)}) collective-permute-start(f32[8,128]{1,0:T(8,128)S(1)} %add_add_fusion.4), channel_id=1, source_target_pairs={{0,36},{1,37},{2,38},{3,39},{4,32},{5,33},{6,34},{7,35},{8,44},{9,... | collective-permute-start | bytes 12296 | tf_op jit(solution)/shard_map/ppermute | solution.py:15
  23.1 5.1 %collective-permute-start.7 = (f32[8,128]{1,0:T(8,128)S(1)}, f32[8,128]{1,0:T(8,128)S(1)}, u32[]{:S(2)}, u32[]{:S(2)}) collective-permute-start(f32[8,128]{1,0:T(8,128)S(1)} %add_add_fusion.4), channel_id=1, source_target_pairs={{0,32},{1,33},{2,34},{3,35},{4,36},{5,37},{6,38},{7,39},{8,40},{9,... | collective-permute-start | bytes 12296 | tf_op jit(solution)/shard_map/ppermute | solution.py:15
  23.9 4.5 %collective-permute-start.6 = (f32[8,128]{1,0:T(8,128)S(1)}, f32[8,128]{1,0:T(8,128)S(1)}, u32[]{:S(2)}, u32[]{:S(2)}) collective-permute-start(f32[8,128]{1,0:T(8,128)S(1)} %add_add_fusion.4), channel_id=1, source_target_pairs={{0,4},{1,5},{2,6},{3,7},{4,0},{5,1},{6,2},{7,3},{8,12},{9,13},{10,... | collective-permute-start | bytes 12296 | tf_op jit(solution)/shard_map/ppermute | solution.py:15
  28.4 9.9 %collective-permute-start.11 = (f32[8,128]{1,0:T(8,128)S(1)}, f32[8,128]{1,0:T(8,128)S(1)}, u32[]{:S(2)}, u32[]{:S(2)}) collective-permute-start(f32[8,128]{1,0:T(8,128)S(1)} %add_add_fusion.3), channel_id=1, source_target_pairs={{0,136},{1,137},{2,138},{3,139},{4,140},{5,141},{6,142},{7,143},{8... | collective-permute-start | bytes 12296 | tf_op jit(solution)/shard_map/ppermute | solution.py:15
  35.5 7.5 %collective-permute-start.10 = (f32[8,128]{1,0:T(8,128)S(1)}, f32[8,128]{1,0:T(8,128)S(1)}, u32[]{:S(2)}, u32[]{:S(2)}) collective-permute-start(f32[8,128]{1,0:T(8,128)S(1)} %add_add_fusion.3), channel_id=1, source_target_pairs={{0,8},{1,9},{2,10},{3,11},{4,12},{5,13},{6,14},{7,15},{8,0},{9,1},... | collective-permute-start | bytes 12296 | tf_op jit(solution)/shard_map/ppermute | solution.py:15
  37.0 6.1 %collective-permute-start.9 = (f32[8,128]{1,0:T(8,128)S(1)}, f32[8,128]{1,0:T(8,128)S(1)}, u32[]{:S(2)}, u32[]{:S(2)}) collective-permute-start(f32[8,128]{1,0:T(8,128)S(1)} %add_add_fusion.3), channel_id=1, source_target_pairs={{0,128},{1,129},{2,130},{3,131},{4,132},{5,133},{6,134},{7,135},{8... | collective-permute-start | bytes 12296 | tf_op jit(solution)/shard_map/ppermute | solution.py:15
  43.1 14.2 %collective-permute-start.12 = (bf16[128,640]{1,0:T(8,128)(2,1)S(1)}, bf16[128,640]{1,0:T(8,128)(2,1)S(1)}, u32[]{:S(2)}, u32[]{:S(2)}) collective-permute-start(bf16[128,640]{1,0:T(8,128)(2,1)S(1)} %multiply_convert_fusion.1), channel_id=1, source_target_pairs={{0,8},{1,9},{2,10},{3,11},{4,12},{5,13},{6,14},{7,15},{8,16},{9,17... | collective-permute-start | bytes 491528 | tf_op jit(solution)/shard_map/ppermute | solution.py:10
  50.1 10.0 %collective-permute-start.13 = (bf16[128,640]{1,0:T(8,128)(2,1)S(1)}, bf16[128,640]{1,0:T(8,128)(2,1)S(1)}, u32[]{:S(2)}, u32[]{:S(2)}) collective-permute-start(bf16[128,640]{1,0:T(8,128)(2,1)S(1)} %multiply_convert_fusion.1), channel_id=1, source_target_pairs={{0,4},{1,5},{2,6},{3,7},{4,8},{5,9},{6,10},{7,11},{8,12},{9,13},{1... | collective-permute-start | bytes 491528 | tf_op jit(solution)/shard_map/ppermute | solution.py:10
  53.5 9.0 %collective-permute-start.14 = (bf16[128,640]{1,0:T(8,128)(2,1)S(1)}, bf16[128,640]{1,0:T(8,128)(2,1)S(1)}, u32[]{:S(2)}, u32[]{:S(2)}) collective-permute-start(bf16[128,640]{1,0:T(8,128)(2,1)S(1)} %multiply_convert_fusion.1), channel_id=1, source_target_pairs={{4,0},{5,1},{6,2},{7,3},{8,4},{9,5},{10,6},{11,7},{12,8},{13,9},{1... | collective-permute-start | bytes 491528 | tf_op jit(solution)/shard_map/ppermute | solution.py:10
  54.8 15.7 %collective-permute-start.15 = (bf16[128,640]{1,0:T(8,128)(2,1)S(1)}, bf16[128,640]{1,0:T(8,128)(2,1)S(1)}, u32[]{:S(2)}, u32[]{:S(2)}) collective-permute-start(bf16[128,640]{1,0:T(8,128)(2,1)S(1)} %multiply_convert_fusion.1), channel_id=1, source_target_pairs={{8,0},{9,1},{10,2},{11,3},{12,4},{13,5},{14,6},{15,7},{16,8},{17,9... | collective-permute-start | bytes 491528 | tf_op jit(solution)/shard_map/ppermute | solution.py:10
  77.9 22.9 %collective-permute-start.24 = (bf16[128,640]{1,0:T(8,128)(2,1)}, bf16[128,640]{1,0:T(8,128)(2,1)}, u32[]{:S(2)}, u32[]{:S(2)}) collective-permute-start(bf16[128,640]{1,0:T(8,128)(2,1)} %add_convert_fusion.1), channel_id=1, source_target_pairs={{8,0},{9,1},{10,2},{11,3},{12,4},{13,5},{14,6},{15,7},{16,8},{17,9... | collective-permute-start | bytes 491528 | tf_op jit(solution)/shard_map/ppermute | solution.py:10
  79.2 22.7 %collective-permute-start.25 = (bf16[128,640]{1,0:T(8,128)(2,1)}, bf16[128,640]{1,0:T(8,128)(2,1)}, u32[]{:S(2)}, u32[]{:S(2)}) collective-permute-start(bf16[128,640]{1,0:T(8,128)(2,1)} %add_convert_fusion.1), channel_id=1, source_target_pairs={{4,0},{5,1},{6,2},{7,3},{8,4},{9,5},{10,6},{11,7},{12,8},{13,9},{1... | collective-permute-start | bytes 491528 | tf_op jit(solution)/shard_map/ppermute | solution.py:10
  80.5 22.5 %collective-permute-start.26 = (bf16[128,640]{1,0:T(8,128)(2,1)}, bf16[128,640]{1,0:T(8,128)(2,1)}, u32[]{:S(2)}, u32[]{:S(2)}) collective-permute-start(bf16[128,640]{1,0:T(8,128)(2,1)} %add_convert_fusion.1), channel_id=1, source_target_pairs={{0,4},{1,5},{2,6},{3,7},{4,8},{5,9},{6,10},{7,11},{8,12},{9,13},{1... | collective-permute-start | bytes 491528 | tf_op jit(solution)/shard_map/ppermute | solution.py:10
  86.6 17.4 %collective-permute-start.27 = (bf16[128,640]{1,0:T(8,128)(2,1)}, bf16[128,640]{1,0:T(8,128)(2,1)}, u32[]{:S(2)}, u32[]{:S(2)}) collective-permute-start(bf16[128,640]{1,0:T(8,128)(2,1)} %add_convert_fusion.1), channel_id=1, source_target_pairs={{0,8},{1,9},{2,10},{3,11},{4,12},{5,13},{6,14},{7,15},{8,16},{9,17... | collective-permute-start | bytes 491528 | tf_op jit(solution)/shard_map/ppermute | solution.py:10
  99.2 9.1 %collective-permute-start.41 = (bf16[64,5,640]{2,0,1:T(8,128)(2,1)S(1)}, bf16[64,5,640]{2,0,1:T(8,128)(2,1)S(1)}, u32[]{:S(2)}, u32[]{:S(2)}) collective-permute-start(bf16[64,5,640]{2,0,1:T(8,128)(2,1)S(1)} %get-tuple-element.14), channel_id=1, source_target_pairs={{0,1},{1,0},{2,3},{3,2},{4,5},{5,4},{6,7},{7,6},{8,9},{9,8},{10,11... | collective-permute-start | bytes 1228808 | tf_op jit(solution)/shard_map/ppermute | solution.py:15
  100.8 7.4 %collective-permute-start.40 = (bf16[64,5,640]{2,0,1:T(8,128)(2,1)S(1)}, bf16[64,5,640]{2,0,1:T(8,128)(2,1)S(1)}, u32[]{:S(2)}, u32[]{:S(2)}) collective-permute-start(bf16[64,5,640]{2,0,1:T(8,128)(2,1)S(1)} %get-tuple-element.13), channel_id=1, source_target_pairs={{0,1},{1,0},{2,3},{3,2},{4,5},{5,4},{6,7},{7,6},{8,9},{9,8},{10,11... | collective-permute-start | bytes 1228808 | tf_op jit(solution)/shard_map/ppermute | solution.py:15
  101.9 13.6 %collective-permute-start.17 = (f32[8,128]{1,0:T(8,128)S(1)}, f32[8,128]{1,0:T(8,128)S(1)}, u32[]{:S(2)}, u32[]{:S(2)}) collective-permute-start(f32[8,128]{1,0:T(8,128)S(1)} %broadcast_add_fusion), channel_id=1, source_target_pairs={{0,2},{1,3},{2,0},{3,1},{4,6},{5,7},{6,4},{7,5},{8,10},{9,11},{10,... | collective-permute-start | bytes 12296 | tf_op jit(solution)/shard_map/ppermute | solution.py:15
  107.6 3.7 %collective-permute-start.29 = (bf16[64,5,640]{2,0,1:T(8,128)(2,1)S(1)}, bf16[64,5,640]{2,0,1:T(8,128)(2,1)S(1)}, u32[]{:S(2)}, u32[]{:S(2)}) collective-permute-start(bf16[64,5,640]{2,0,1:T(8,128)(2,1)S(1)} %get-tuple-element.16), channel_id=1, source_target_pairs={{0,1},{1,0},{2,3},{3,2},{4,5},{5,4},{6,7},{7,6},{8,9},{9,8},{10,11... | collective-permute-start | bytes 1228808 | tf_op jit(solution)/shard_map/ppermute | solution.py:15
  109.2 45.6 %collective-permute-start.43 = (bf16[32,5,640]{2,0,1:T(8,128)(2,1)}, bf16[32,5,640]{2,0,1:T(8,128)(2,1)}, u32[]{:S(2)}, u32[]{:S(2)}) collective-permute-start(bf16[32,5,640]{2,0,1:T(8,128)(2,1)} %get-tuple-element.18), channel_id=1, source_target_pairs={{0,2},{1,3},{2,0},{3,1},{4,6},{5,7},{6,4},{7,5},{8,10},{9,11},{10,... | collective-permute-start | bytes 614408 | tf_op jit(solution)/shard_map/ppermute | solution.py:15
  111.1 43.7 %collective-permute-start.42 = (bf16[32,5,640]{2,0,1:T(8,128)(2,1)S(1)}, bf16[32,5,640]{2,0,1:T(8,128)(2,1)}, u32[]{:S(2)}, u32[]{:S(2)}) collective-permute-start(bf16[32,5,640]{2,0,1:T(8,128)(2,1)S(1)} %get-tuple-element.17), channel_id=1, source_target_pairs={{0,2},{1,3},{2,0},{3,1},{4,6},{5,7},{6,4},{7,5},{8,10},{9,11},{10,... | collective-permute-start | bytes 614408 | tf_op jit(solution)/shard_map/ppermute | solution.py:15
  113.5 41.4 %collective-permute-start.31 = (bf16[32,5,640]{2,0,1:T(8,128)(2,1)}, bf16[32,5,640]{2,0,1:T(8,128)(2,1)}, u32[]{:S(2)}, u32[]{:S(2)}) collective-permute-start(bf16[32,5,640]{2,0,1:T(8,128)(2,1)} %get-tuple-element.20), channel_id=1, source_target_pairs={{0,2},{1,3},{2,0},{3,1},{4,6},{5,7},{6,4},{7,5},{8,10},{9,11},{10,... | collective-permute-start | bytes 614408 | tf_op jit(solution)/shard_map/ppermute | solution.py:15
  115.4 39.4 %collective-permute-start.30 = (bf16[32,5,640]{2,0,1:T(8,128)(2,1)}, bf16[32,5,640]{2,0,1:T(8,128)(2,1)}, u32[]{:S(2)}, u32[]{:S(2)}) collective-permute-start(bf16[32,5,640]{2,0,1:T(8,128)(2,1)} %get-tuple-element.19), channel_id=1, source_target_pairs={{0,2},{1,3},{2,0},{3,1},{4,6},{5,7},{6,4},{7,5},{8,10},{9,11},{10,... | collective-permute-start | bytes 614408 | tf_op jit(solution)/shard_map/ppermute | solution.py:15
  116.1 6.4 %collective-permute-start.18 = (f32[8,128]{1,0:T(8,128)S(1)}, f32[8,128]{1,0:T(8,128)S(1)}, u32[]{:S(2)}, u32[]{:S(2)}) collective-permute-start(f32[8,128]{1,0:T(8,128)S(1)} %fusion.66), channel_id=1, source_target_pairs={{0,16},{1,17},{2,18},{3,19},{4,20},{5,21},{6,22},{7,23},{8,24},{9,... | collective-permute-start | bytes 12296 | tf_op jit(solution)/shard_map/ppermute | solution.py:15
  122.6 7.3 %collective-permute-start.19 = (f32[8,128]{1,0:T(8,128)S(1)}, f32[8,128]{1,0:T(8,128)S(1)}, u32[]{:S(2)}, u32[]{:S(2)}) collective-permute-start(f32[8,128]{1,0:T(8,128)S(1)} %add.294), channel_id=1, source_target_pairs={{0,64},{1,65},{2,66},{3,67},{4,68},{5,69},{6,70},{7,71},{8,72},{9,... | collective-permute-start | bytes 12296 | tf_op jit(solution)/shard_map/ppermute | solution.py:15
  129.9 4.5 %collective-permute-start.20 = (f32[8,128]{1,0:T(8,128)S(1)}, f32[8,128]{1,0:T(8,128)S(1)}, u32[]{:S(2)}, u32[]{:S(2)}) collective-permute-start(f32[8,128]{1,0:T(8,128)S(1)} %add.295), channel_id=1, source_target_pairs={{0,4},{1,5},{2,6},{3,7},{4,0},{5,1},{6,2},{7,3},{8,12},{9,13},{10,... | collective-permute-start | bytes 12296 | tf_op jit(solution)/shard_map/ppermute | solution.py:15
  134.5 5.1 %collective-permute-start.21 = (f32[8,128]{1,0:T(8,128)S(1)}, f32[8,128]{1,0:T(8,128)S(1)}, u32[]{:S(2)}, u32[]{:S(2)}) collective-permute-start(f32[8,128]{1,0:T(8,128)S(1)} %add.296), channel_id=1, source_target_pairs={{0,32},{1,33},{2,34},{3,35},{4,36},{5,37},{6,38},{7,39},{8,40},{9,... | collective-permute-start | bytes 12296 | tf_op jit(solution)/shard_map/ppermute | solution.py:15
  139.6 5.8 %collective-permute-start.22 = (f32[8,128]{1,0:T(8,128)S(1)}, f32[8,128]{1,0:T(8,128)S(1)}, u32[]{:S(2)}, u32[]{:S(2)}) collective-permute-start(f32[8,128]{1,0:T(8,128)S(1)} %add.297), channel_id=1, source_target_pairs={{0,128},{1,129},{2,130},{3,131},{4,132},{5,133},{6,134},{7,135},{8... | collective-permute-start | bytes 12296 | tf_op jit(solution)/shard_map/ppermute | solution.py:15
  145.4 7.5 %collective-permute-start.23 = (f32[8,128]{1,0:T(8,128)S(1)}, f32[8,128]{1,0:T(8,128)S(1)}, u32[]{:S(2)}, u32[]{:S(2)}) collective-permute-start(f32[8,128]{1,0:T(8,128)S(1)} %add.298), channel_id=1, source_target_pairs={{0,8},{1,9},{2,10},{3,11},{4,12},{5,13},{6,14},{7,15},{8,0},{9,1},... | collective-permute-start | bytes 12296 | tf_op jit(solution)/shard_map/ppermute | solution.py:15
  156.6 4.7 %collective-permute-start.33 = (bf16[16,5,640]{2,0,1:T(8,128)(2,1)S(1)}, bf16[16,5,640]{2,0,1:T(8,128)(2,1)S(1)}, u32[]{:S(2)}, u32[]{:S(2)}) collective-permute-start(bf16[16,5,640]{2,0,1:T(8,128)(2,1)S(1)} %get-tuple-element.24), channel_id=1, source_target_pairs={{0,16},{1,17},{2,18},{3,19},{4,20},{5,21},{6,22},{7,23},{8,24},{9,... | collective-permute-start | bytes 307208 | tf_op jit(solution)/shard_map/ppermute | solution.py:15
  157.5 4.9 %collective-permute-start.32 = (bf16[16,5,640]{2,0,1:T(8,128)(2,1)S(1)}, bf16[16,5,640]{2,0,1:T(8,128)(2,1)S(1)}, u32[]{:S(2)}, u32[]{:S(2)}) collective-permute-start(bf16[16,5,640]{2,0,1:T(8,128)(2,1)S(1)} %get-tuple-element.23), channel_id=1, source_target_pairs={{0,16},{1,17},{2,18},{3,19},{4,20},{5,21},{6,22},{7,23},{8,24},{9,... | collective-permute-start | bytes 307208 | tf_op jit(solution)/shard_map/ppermute | solution.py:15
  158.8 7.9 %collective-permute-start.45 = (bf16[16,5,640]{2,0,1:T(8,128)(2,1)S(1)}, bf16[16,5,640]{2,0,1:T(8,128)(2,1)S(1)}, u32[]{:S(2)}, u32[]{:S(2)}) collective-permute-start(bf16[16,5,640]{2,0,1:T(8,128)(2,1)S(1)} %get-tuple-element.22), channel_id=1, source_target_pairs={{0,16},{1,17},{2,18},{3,19},{4,20},{5,21},{6,22},{7,23},{8,24},{9,... | collective-permute-start | bytes 307208 | tf_op jit(solution)/shard_map/ppermute | solution.py:15
  159.7 6.9 %collective-permute-start.44 = (bf16[16,5,640]{2,0,1:T(8,128)(2,1)S(1)}, bf16[16,5,640]{2,0,1:T(8,128)(2,1)S(1)}, u32[]{:S(2)}, u32[]{:S(2)}) collective-permute-start(bf16[16,5,640]{2,0,1:T(8,128)(2,1)S(1)} %get-tuple-element.21), channel_id=1, source_target_pairs={{0,16},{1,17},{2,18},{3,19},{4,20},{5,21},{6,22},{7,23},{8,24},{9,... | collective-permute-start | bytes 307208 | tf_op jit(solution)/shard_map/ppermute | solution.py:15
  162.5 6.3 %collective-permute-start.35 = (bf16[8,5,640]{2,0,1:T(8,128)(2,1)S(1)}, bf16[8,5,640]{2,0,1:T(8,128)(2,1)S(1)}, u32[]{:S(2)}, u32[]{:S(2)}) collective-permute-start(bf16[8,5,640]{2,0,1:T(8,128)(2,1)S(1)} %get-tuple-element.28), channel_id=1, source_target_pairs={{0,64},{1,65},{2,66},{3,67},{4,68},{5,69},{6,70},{7,71},{8,72},{9,... | collective-permute-start | bytes 153608 | tf_op jit(solution)/shard_map/ppermute | solution.py:15
  166.5 4.1 %collective-permute-start.34 = (bf16[8,5,640]{2,0,1:T(8,128)(2,1)S(1)}, bf16[8,5,640]{2,0,1:T(8,128)(2,1)S(1)}, u32[]{:S(2)}, u32[]{:S(2)}) collective-permute-start(bf16[8,5,640]{2,0,1:T(8,128)(2,1)S(1)} %get-tuple-element.27), channel_id=1, source_target_pairs={{0,64},{1,65},{2,66},{3,67},{4,68},{5,69},{6,70},{7,71},{8,72},{9,... | collective-permute-start | bytes 153608 | tf_op jit(solution)/shard_map/ppermute | solution.py:15
  166.7 4.5 %collective-permute-start.47 = (bf16[8,5,640]{2,0,1:T(8,128)(2,1)S(1)}, bf16[8,5,640]{2,0,1:T(8,128)(2,1)S(1)}, u32[]{:S(2)}, u32[]{:S(2)}) collective-permute-start(bf16[8,5,640]{2,0,1:T(8,128)(2,1)S(1)} %get-tuple-element.26), channel_id=1, source_target_pairs={{0,64},{1,65},{2,66},{3,67},{4,68},{5,69},{6,70},{7,71},{8,72},{9,... | collective-permute-start | bytes 153608 | tf_op jit(solution)/shard_map/ppermute | solution.py:15
  168.8 4.1 %collective-permute-start.46 = (bf16[8,5,640]{2,0,1:T(8,128)(2,1)S(1)}, bf16[8,5,640]{2,0,1:T(8,128)(2,1)S(1)}, u32[]{:S(2)}, u32[]{:S(2)}) collective-permute-start(bf16[8,5,640]{2,0,1:T(8,128)(2,1)S(1)} %get-tuple-element.25), channel_id=1, source_target_pairs={{0,64},{1,65},{2,66},{3,67},{4,68},{5,69},{6,70},{7,71},{8,72},{9,... | collective-permute-start | bytes 153608 | tf_op jit(solution)/shard_map/ppermute | solution.py:15
  170.7 5.1 %collective-permute-start.36 = (bf16[8,5,640]{2,0,1:T(8,128)(2,1)S(1)}, bf16[8,5,640]{2,0,1:T(8,128)(2,1)S(1)}, u32[]{:S(2)}, u32[]{:S(2)}) collective-permute-start(bf16[8,5,640]{2,0,1:T(8,128)(2,1)S(1)} %dynamic-slice_convert_fusion.9), channel_id=1, source_target_pairs={{0,4},{1,5},{2,6},{3,7},{4,0},{5,1},{6,2},{7,3},{8,12},{9,13},{10,... | collective-permute-start | bytes 153608 | tf_op jit(solution)/shard_map/ppermute | solution.py:15
  172.9 5.1 %collective-permute-start.48 = (bf16[8,5,640]{2,0,1:T(8,128)(2,1)S(1)}, bf16[8,5,640]{2,0,1:T(8,128)(2,1)S(1)}, u32[]{:S(2)}, u32[]{:S(2)}) collective-permute-start(bf16[8,5,640]{2,0,1:T(8,128)(2,1)S(1)} %dynamic-slice_convert_fusion.8), channel_id=1, source_target_pairs={{0,4},{1,5},{2,6},{3,7},{4,0},{5,1},{6,2},{7,3},{8,12},{9,13},{10,... | collective-permute-start | bytes 153608 | tf_op jit(solution)/shard_map/ppermute | solution.py:15
  175.8 5.4 %collective-permute-start.37 = (bf16[4,5,640]{2,0,1:T(4,128)(2,1)S(1)}, bf16[4,5,640]{2,0,1:T(4,128)(2,1)S(1)}, u32[]{:S(2)}, u32[]{:S(2)}) collective-permute-start(bf16[4,5,640]{2,0,1:T(4,128)(2,1)S(1)} %dynamic-slice_convert_fusion.11), channel_id=1, source_target_pairs={{0,32},{1,33},{2,34},{3,35},{4,36},{5,37},{6,38},{7,39},{8,40},{9,... | collective-permute-start | bytes 76808 | tf_op jit(solution)/shard_map/ppermute | solution.py:15
  178.1 6.8 %collective-permute-start.49 = (bf16[4,5,640]{2,0,1:T(4,128)(2,1)S(1)}, bf16[4,5,640]{2,0,1:T(4,128)(2,1)S(1)}, u32[]{:S(2)}, u32[]{:S(2)}) collective-permute-start(bf16[4,5,640]{2,0,1:T(4,128)(2,1)S(1)} %dynamic-slice_convert_fusion.10), channel_id=1, source_target_pairs={{0,32},{1,33},{2,34},{3,35},{4,36},{5,37},{6,38},{7,39},{8,40},{9,... | collective-permute-start | bytes 76808 | tf_op jit(solution)/shard_map/ppermute | solution.py:15
  181.3 5.7 %collective-permute-start.38 = (bf16[2,5,640]{2,0,1:T(2,128)(2,1)S(1)}, bf16[2,5,640]{2,0,1:T(2,128)(2,1)S(1)}, u32[]{:S(2)}, u32[]{:S(2)}) collective-permute-start(bf16[2,5,640]{2,0,1:T(2,128)(2,1)S(1)} %dynamic-slice_convert_fusion.13), channel_id=1, source_target_pairs={{0,128},{1,129},{2,130},{3,131},{4,132},{5,133},{6,134},{7,135},{8... | collective-permute-start | bytes 38408 | tf_op jit(solution)/shard_map/ppermute | solution.py:15
  184.9 5.3 %collective-permute-start.50 = (bf16[2,5,640]{2,0,1:T(2,128)(2,1)S(1)}, bf16[2,5,640]{2,0,1:T(2,128)(2,1)S(1)}, u32[]{:S(2)}, u32[]{:S(2)}) collective-permute-start(bf16[2,5,640]{2,0,1:T(2,128)(2,1)S(1)} %dynamic-slice_convert_fusion.12), channel_id=1, source_target_pairs={{0,128},{1,129},{2,130},{3,131},{4,132},{5,133},{6,134},{7,135},{8... | collective-permute-start | bytes 38408 | tf_op jit(solution)/shard_map/ppermute | solution.py:15
  187.0 7.7 %collective-permute-start.39 = (bf16[1,5,640]{2,0,1:T(2,128)(2,1)S(1)}, bf16[1,5,640]{2,0,1:T(2,128)(2,1)S(1)}, u32[]{:S(2)}, u32[]{:S(2)}) collective-permute-start(bf16[1,5,640]{2,0,1:T(2,128)(2,1)S(1)} %dynamic-slice_convert_fusion.15), channel_id=1, source_target_pairs={{0,8},{1,9},{2,10},{3,11},{4,12},{5,13},{6,14},{7,15},{8,0},{9,1},... | collective-permute-start | bytes 19208 | tf_op jit(solution)/shard_map/ppermute | solution.py:15
  190.3 7.7 %collective-permute-start.51 = (bf16[1,5,640]{2,0,1:T(2,128)(2,1)S(1)}, bf16[1,5,640]{2,0,1:T(2,128)(2,1)S(1)}, u32[]{:S(2)}, u32[]{:S(2)}) collective-permute-start(bf16[1,5,640]{2,0,1:T(2,128)(2,1)S(1)} %dynamic-slice_convert_fusion.14), channel_id=1, source_target_pairs={{0,8},{1,9},{2,10},{3,11},{4,12},{5,13},{6,14},{7,15},{8,0},{9,1},... | collective-permute-start | bytes 19208 | tf_op jit(solution)/shard_map/ppermute | solution.py:15
  (13 other events, 148.0 us)

commit v10 on v9

--- a/solution.py
+++ b/solution.py
@@ -65,7 +65,8 @@
         got_parts, got_extra = swap_with((parts, extra), axis, bit)
         got = [jnp.concatenate(g, 0) if pieces > 1 else g[0] for g in got_parts]
         blocks = [k + g.astype(jnp.float32) for k, g in zip(keep, got)]
-        extra = extra + got_extra
+        if extra is not None:
+            extra = extra + got_extra
     return [b[0] for b in blocks], extra
 
 
@@ -134,6 +135,12 @@
     )
     back_pieces = spread(gradient_before_activation, shard_reach)
     backward_tap_pile = jnp.stack(back_pieces[::-1])
+    (grad_down,), loss_tile = tree_scatter(
+        (down_partial,), jnp.broadcast_to(local_loss, (8, 128)), "seq"
+    )
+    grad_down, loss_tile, backward_tap_pile = lax.optimization_barrier(
+        (grad_down, loss_tile, backward_tap_pile)
+    )
     grad_neck = jnp.einsum(
         "krc,kbc->rb", backward_tap_pile, conv_weight, preferred_element_type=jnp.float32
     )
@@ -142,9 +149,7 @@
     up_partial = lax.dot_general(
         columns, grad_first, (((0,), (0,)), ((), ())), preferred_element_type=jnp.float32
     )
-    (grad_down, grad_up), loss_tile = tree_scatter(
-        (down_partial, up_partial), jnp.broadcast_to(local_loss, (8, 128)), "seq"
-    )
+    (grad_up,), _ = tree_scatter((up_partial,), None, "seq")
     grad_down = grad_down.astype(jnp.bfloat16)
     grad_up = grad_up.astype(jnp.bfloat16)
     loss_total = loss_tile[0, 0]

time: 200 us -> 226 us (1.13)
  waiting for transfers between devices: 59 us -> 101 us
  starting transfers between devices: 98.7 us -> 89 us
  local copies, waits for them, and re-layouts: 15.1 us -> 9.32 us
  other arithmetic: 12.5 us -> 9.94 us
    ppermute x44, waiting for transfers between devices: 45.9 us -> 87.6 us  [swap_with(): return lax.ppermute(block, axis, [(i, i ^ bit) for i in range(devices)])]
    ppermute x44, starting transfers between devices: 70.1 us -> 61.1 us  [swap_with(): return lax.ppermute(block, axis, [(i, i ^ bit) for i in range(devices)])]
    unnamed x27 -> x29, local copies, waits for them, and re-layouts: 5.35 us -> 2.13 us
  transfers between devices with their start and end apart: 52 -> 52, of which waited for: 28 -> 37; matrix products, arithmetic and copies ran while one was open for 12% -> 5% of each run, Pallas kernels for 0% -> 0%
where the time goes in v10:
time: 226 us; the launch traced here: 224 us
  waiting for transfers between devices  101 us (45%)
  starting transfers between devices  89 us (39%)
  other arithmetic  9.94 us (4%)
  matrix products  9.85 us (4%)
  local copies, waits for them, and re-layouts  9.32 us (4%)
  between operations  4.86 us (2%)
    ppermute x44, waiting for transfers between devices, swap_with(): return lax.ppermute(block, axis, [(i, i ^ bit) for i in range(devices)])  87.6 us
    ppermute x44, starting transfers between devices, swap_with(): return lax.ppermute(block, axis, [(i, i ^ bit) for i in range(devices)])  61.1 us
    ppermute x8, starting transfers between devices, from_behind(): return lax.ppermute(block, axis, route)  27.9 us
    ppermute x8, waiting for transfers between devices, from_behind(): return lax.ppermute(block, axis, route)  13.1 us
  transfers between devices with their start and end apart: 52, of which 37 were waited for; matrix products, arithmetic and copies ran while one was open for 5% of the time, Pallas kernels for 0%

profile of v10, /device:TPU:32, one launch (start us, length us, event | category | flops | bytes accessed | tf_op | source)
XLA Modules:
  0.0 223.6 jit_solution(13979596201660877917)
XLA Ops:
  2.8 1.9 collective-permute-start.1
  8.4 1.9 fusion.52
  11.1 2.5 %collective-permute-start.5 = (f32[8,128]{1,0:T(8,128)S(1)}, f32[8,128]{1,0:T(8,128)S(1)}, u32[]{:S(2)}, u32[]{:S(2)}) collective-permute-start(f32[8,128]{1,0:T(8,128)S(1)} %add_add_fusion.5), channel_id=1, source_target_pairs={{0,80},{1,81},{2,82},{3,83},{4,84},{5,85},{6,86},{7,87},{8,88},{9,... | collective-permute-start | bytes 12296 | tf_op jit(solution)/shard_map/ppermute | solution.py:15
  15.7 1.5 collective-permute-done.4
  17.7 5.4 %collective-permute-start.8 = (f32[8,128]{1,0:T(8,128)S(1)}, f32[8,128]{1,0:T(8,128)S(1)}, u32[]{:S(2)}, u32[]{:S(2)}) collective-permute-start(f32[8,128]{1,0:T(8,128)S(1)} %add_add_fusion.4), channel_id=1, source_target_pairs={{0,36},{1,37},{2,38},{3,39},{4,32},{5,33},{6,34},{7,35},{8,44},{9,... | collective-permute-start | bytes 12296 | tf_op jit(solution)/shard_map/ppermute | solution.py:15
  24.7 3.5 %collective-permute-done.7 = f32[8,128]{1,0:T(8,128)S(1)} collective-permute-done((f32[8,128]{1,0:T(8,128)S(1)}, f32[8,128]{1,0:T(8,128)S(1)}, u32[]{:S(2)}, u32[]{:S(2)}) %collective-permute-start.7) | collective-permute-done | bytes 4128 | tf_op jit(solution)/shard_map/ppermute | solution.py:15
  28.4 7.1 %collective-permute-start.11 = (f32[8,128]{1,0:T(8,128)S(1)}, f32[8,128]{1,0:T(8,128)S(1)}, u32[]{:S(2)}, u32[]{:S(2)}) collective-permute-start(f32[8,128]{1,0:T(8,128)S(1)} %add_add_fusion.3), channel_id=1, source_target_pairs={{0,136},{1,137},{2,138},{3,139},{4,140},{5,141},{6,142},{7,143},{8... | collective-permute-start | bytes 12296 | tf_op jit(solution)/shard_map/ppermute | solution.py:15
  35.5 1.4 collective-permute-start.10
  38.3 4.7 %collective-permute-done.10 = f32[8,128]{1,0:T(8,128)S(1)} collective-permute-done((f32[8,128]{1,0:T(8,128)S(1)}, f32[8,128]{1,0:T(8,128)S(1)}, u32[]{:S(2)}, u32[]{:S(2)}) %collective-permute-start.10) | collective-permute-done | bytes 4128 | tf_op jit(solution)/shard_map/ppermute | solution.py:15
  43.1 5.4 %collective-permute-start.12 = (bf16[128,640]{1,0:T(8,128)(2,1)S(1)}, bf16[128,640]{1,0:T(8,128)(2,1)S(1)}, u32[]{:S(2)}, u32[]{:S(2)}) collective-permute-start(bf16[128,640]{1,0:T(8,128)(2,1)S(1)} %multiply_convert_fusion.1), channel_id=1, source_target_pairs={{0,8},{1,9},{2,10},{3,11},{4,12},{5,13},{6,14},{7,15},{8,16},{9,17... | collective-permute-start | bytes 491528 | tf_op jit(solution)/shard_map/ppermute | solution.py:10
  50.3 3.4 %collective-permute-start.13 = (bf16[128,640]{1,0:T(8,128)(2,1)S(1)}, bf16[128,640]{1,0:T(8,128)(2,1)S(1)}, u32[]{:S(2)}, u32[]{:S(2)}) collective-permute-start(bf16[128,640]{1,0:T(8,128)(2,1)S(1)} %multiply_convert_fusion.1), channel_id=1, source_target_pairs={{0,4},{1,5},{2,6},{3,7},{4,8},{5,9},{6,10},{7,11},{8,12},{9,13},{1... | collective-permute-start | bytes 491528 | tf_op jit(solution)/shard_map/ppermute | solution.py:10
  57.5 2.6 %collective-permute-done.13 = bf16[128,640]{1,0:T(8,128)(2,1)S(1)} collective-permute-done((bf16[128,640]{1,0:T(8,128)(2,1)S(1)}, bf16[128,640]{1,0:T(8,128)(2,1)S(1)}, u32[]{:S(2)}, u32[]{:S(2)}) %collective-permute-start.13) | collective-permute-done | bytes 163872 | tf_op jit(solution)/shard_map/ppermute | solution.py:10
  60.2 2.4 %collective-permute-done.14 = bf16[128,640]{1,0:T(8,128)(2,1)S(1)} collective-permute-done((bf16[128,640]{1,0:T(8,128)(2,1)S(1)}, bf16[128,640]{1,0:T(8,128)(2,1)S(1)}, u32[]{:S(2)}, u32[]{:S(2)}) %collective-permute-start.14) | collective-permute-done | bytes 163872 | tf_op jit(solution)/shard_map/ppermute | solution.py:10
  62.6 8.0 %collective-permute-done.15 = bf16[128,640]{1,0:T(8,128)(2,1)S(1)} collective-permute-done((bf16[128,640]{1,0:T(8,128)(2,1)S(1)}, bf16[128,640]{1,0:T(8,128)(2,1)S(1)}, u32[]{:S(2)}, u32[]{:S(2)}) %collective-permute-start.15) | collective-permute-done | bytes 163872 | tf_op jit(solution)/shard_map/ppermute | solution.py:10
  70.7 3.1 %fusion.53 = (f32[128]{0:T(128)S(1)}, f32[128,640]{1,0:T(8,128)S(1)}) fusion(bf16[5,128,640]{2,1,0:T(8,128)(2,1)S(1)} %bitcast_dynamic-update-slice_fusion.5, bf16[5,640,640]{2,1,0:T(8,128)(2,1)} %param.13), kind=kOutput, calls=%fused_computation.138 | convolution fusion | flops 524369792 | bytes 5243392 | tf_op jit(solution)/shard_map/krc,kcb->rb/dot_general | solution.py:105
  82.7 2.9 %collective-permute-done.29 = f32[8,128]{1,0:T(8,128)S(1)} collective-permute-done((f32[8,128]{1,0:T(8,128)S(1)}, f32[8,128]{1,0:T(8,128)S(1)}, u32[]{:S(2)}, u32[]{:S(2)}) %collective-permute-start.29) | collective-permute-done | bytes 4128 | tf_op jit(solution)/shard_map/ppermute | solution.py:15
  86.2 2.5 %collective-permute-start.30 = (f32[8,128]{1,0:T(8,128)S(1)}, f32[8,128]{1,0:T(8,128)S(1)}, u32[]{:S(2)}, u32[]{:S(2)}) collective-permute-start(f32[8,128]{1,0:T(8,128)S(1)} %fusion.65), channel_id=1, source_target_pairs={{0,16},{1,17},{2,18},{3,19},{4,20},{5,21},{6,22},{7,23},{8,24},{9,... | collective-permute-start | bytes 12296 | tf_op jit(solution)/shard_map/ppermute | solution.py:15
  88.8 1.5 collective-permute-done.30
  90.3 2.5 %collective-permute-start.31 = (f32[8,128]{1,0:T(8,128)S(1)}, f32[8,128]{1,0:T(8,128)S(1)}, u32[]{:S(2)}, u32[]{:S(2)}) collective-permute-start(f32[8,128]{1,0:T(8,128)S(1)} %add.335), channel_id=1, source_target_pairs={{0,64},{1,65},{2,66},{3,67},{4,68},{5,69},{6,70},{7,71},{8,72},{9,... | collective-permute-start | bytes 12296 | tf_op jit(solution)/shard_map/ppermute | solution.py:15
  94.5 4.5 %collective-permute-done.32 = f32[8,128]{1,0:T(8,128)S(1)} collective-permute-done((f32[8,128]{1,0:T(8,128)S(1)}, f32[8,128]{1,0:T(8,128)S(1)}, u32[]{:S(2)}, u32[]{:S(2)}) %collective-permute-start.32) | collective-permute-done | bytes 4128 | tf_op jit(solution)/shard_map/ppermute | solution.py:15
  99.0 2.8 %collective-permute-start.33 = (f32[8,128]{1,0:T(8,128)S(1)}, f32[8,128]{1,0:T(8,128)S(1)}, u32[]{:S(2)}, u32[]{:S(2)}) collective-permute-start(f32[8,128]{1,0:T(8,128)S(1)} %add.337), channel_id=1, source_target_pairs={{0,32},{1,33},{2,34},{3,35},{4,36},{5,37},{6,38},{7,39},{8,40},{9,... | collective-permute-start | bytes 12296 | tf_op jit(solution)/shard_map/ppermute | solution.py:15
  102.3 1.8 collective-permute-done.33
  104.1 1.8 collective-permute-start.34
  106.2 2.1 collective-permute-start.19
  109.2 4.0 %collective-permute-start.35 = (f32[8,128]{1,0:T(8,128)S(1)}, f32[8,128]{1,0:T(8,128)S(1)}, u32[]{:S(2)}, u32[]{:S(2)}) collective-permute-start(f32[8,128]{1,0:T(8,128)S(1)} %add.339), channel_id=1, source_target_pairs={{0,8},{1,9},{2,10},{3,11},{4,12},{5,13},{6,14},{7,15},{8,0},{9,1},... | collective-permute-start | bytes 12296 | tf_op jit(solution)/shard_map/ppermute | solution.py:15
  113.2 1.4 collective-permute-done.18
  115.1 1.8 collective-permute-start.20
  119.6 5.5 %collective-permute-start.38 = (bf16[128,640]{1,0:T(8,128)(2,1)S(1)}, bf16[128,640]{1,0:T(8,128)(2,1)S(1)}, u32[]{:S(2)}, u32[]{:S(2)}) collective-permute-start(bf16[128,640]{1,0:T(8,128)(2,1)S(1)} %add_convert_fusion.1), channel_id=1, source_target_pairs={{0,4},{1,5},{2,6},{3,7},{4,8},{5,9},{6,10},{7,11},{8,12},{9,13},{1... | collective-permute-start | bytes 491528 | tf_op jit(solution)/shard_map/ppermute | solution.py:10
  125.1 8.5 %collective-permute-start.39 = (bf16[128,640]{1,0:T(8,128)(2,1)S(1)}, bf16[128,640]{1,0:T(8,128)(2,1)S(1)}, u32[]{:S(2)}, u32[]{:S(2)}) collective-permute-start(bf16[128,640]{1,0:T(8,128)(2,1)S(1)} %add_convert_fusion.1), channel_id=1, source_target_pairs={{0,8},{1,9},{2,10},{3,11},{4,12},{5,13},{6,14},{7,15},{8,16},{9,17... | collective-permute-start | bytes 491528 | tf_op jit(solution)/shard_map/ppermute | solution.py:10
  133.7 5.9 %collective-permute-start.23 = (bf16[8,5,640]{2,0,1:T(8,128)(2,1)S(1)}, bf16[8,5,640]{2,0,1:T(8,128)(2,1)S(1)}, u32[]{:S(2)}, u32[]{:S(2)}) collective-permute-start(bf16[8,5,640]{2,0,1:T(8,128)(2,1)S(1)} %get-tuple-element.34), channel_id=1, source_target_pairs={{0,64},{1,65},{2,66},{3,67},{4,68},{5,69},{6,70},{7,71},{8,72},{9,... | collective-permute-start | bytes 153608 | tf_op jit(solution)/shard_map/ppermute | solution.py:15
  139.7 2.0 collective-permute-done.23
  141.7 2.0 collective-permute-done.22
  144.4 4.4 %collective-permute-done.24 = bf16[8,5,640]{2,0,1:T(8,128)(2,1)S(1)} collective-permute-done((bf16[8,5,640]{2,0,1:T(8,128)(2,1)S(1)}, bf16[8,5,640]{2,0,1:T(8,128)(2,1)S(1)}, u32[]{:S(2)}, u32[]{:S(2)}) %collective-permute-start.24) | collective-permute-done | bytes 51232 | tf_op jit(solution)/shard_map/ppermute | solution.py:15
  149.3 5.2 %collective-permute-done.25 = bf16[4,5,640]{2,0,1:T(4,128)(2,1)S(1)} collective-permute-done((bf16[4,5,640]{2,0,1:T(4,128)(2,1)S(1)}, bf16[4,5,640]{2,0,1:T(4,128)(2,1)S(1)}, u32[]{:S(2)}, u32[]{:S(2)}) %collective-permute-start.25) | collective-permute-done | bytes 25632 | tf_op jit(solution)/shard_map/ppermute | solution.py:15
  155.6 4.3 %collective-permute-done.26 = bf16[2,5,640]{2,0,1:T(2,128)(2,1)S(1)} collective-permute-done((bf16[2,5,640]{2,0,1:T(2,128)(2,1)S(1)}, bf16[2,5,640]{2,0,1:T(2,128)(2,1)S(1)}, u32[]{:S(2)}, u32[]{:S(2)}) %collective-permute-start.26) | collective-permute-done | bytes 12832 | tf_op jit(solution)/shard_map/ppermute | solution.py:15
  160.2 7.6 %collective-permute-done.27 = bf16[1,5,640]{2,0,1:T(2,128)(2,1)S(1)} collective-permute-done((bf16[1,5,640]{2,0,1:T(2,128)(2,1)S(1)}, bf16[1,5,640]{2,0,1:T(2,128)(2,1)S(1)}, u32[]{:S(2)}, u32[]{:S(2)}) %collective-permute-start.27) | collective-permute-done | bytes 6432 | tf_op jit(solution)/shard_map/ppermute | solution.py:15
  168.4 1.5 multiply_reduce_fusion
  173.7 2.6 %collective-permute-start.43 = (bf16[32,5,640]{2,0,1:T(8,128)(2,1)S(1)}, bf16[32,5,640]{2,0,1:T(8,128)(2,1)S(1)}, u32[]{:S(2)}, u32[]{:S(2)}) collective-permute-start(bf16[32,5,640]{2,0,1:T(8,128)(2,1)S(1)} %get-tuple-element.24), channel_id=1, source_target_pairs={{0,2},{1,3},{2,0},{3,1},{4,6},{5,7},{6,4},{7,5},{8,10},{9,11},{10,... | collective-permute-start | bytes 614408 | tf_op jit(solution)/shard_map/ppermute | solution.py:15
  176.4 5.8 %collective-permute-done.43 = bf16[32,5,640]{2,0,1:T(8,128)(2,1)S(1)} collective-permute-done((bf16[32,5,640]{2,0,1:T(8,128)(2,1)S(1)}, bf16[32,5,640]{2,0,1:T(8,128)(2,1)S(1)}, u32[]{:S(2)}, u32[]{:S(2)}) %collective-permute-start.43) | collective-permute-done | bytes 204832 | tf_op jit(solution)/shard_map/ppermute | solution.py:15
  182.2 3.8 %collective-permute-done.42 = bf16[32,5,640]{2,0,1:T(8,128)(2,1)S(1)} collective-permute-done((bf16[32,5,640]{2,0,1:T(8,128)(2,1)S(1)}, bf16[32,5,640]{2,0,1:T(8,128)(2,1)S(1)}, u32[]{:S(2)}, u32[]{:S(2)}) %collective-permute-start.42) | collective-permute-done | bytes 204832 | tf_op jit(solution)/shard_map/ppermute | solution.py:15
  186.3 2.0 collective-permute-start.44
  188.3 3.4 %collective-permute-done.45 = bf16[16,5,640]{2,0,1:T(8,128)(2,1)S(1)} collective-permute-done((bf16[16,5,640]{2,0,1:T(8,128)(2,1)S(1)}, bf16[16,5,640]{2,0,1:T(8,128)(2,1)S(1)}, u32[]{:S(2)}, u32[]{:S(2)}) %collective-permute-start.45) | collective-permute-done | bytes 102432 | tf_op jit(solution)/shard_map/ppermute | solution.py:15
  195.1 2.1 collective-permute-done.47
  198.4 4.8 %collective-permute-done.48 = bf16[8,5,640]{2,0,1:T(8,128)(2,1)S(1)} collective-permute-done((bf16[8,5,640]{2,0,1:T(8,128)(2,1)S(1)}, bf16[8,5,640]{2,0,1:T(8,128)(2,1)S(1)}, u32[]{:S(2)}, u32[]{:S(2)}) %collective-permute-start.48) | collective-permute-done | bytes 51232 | tf_op jit(solution)/shard_map/ppermute | solution.py:15
  204.6 4.0 %collective-permute-done.49 = bf16[4,5,640]{2,0,1:T(4,128)(2,1)S(1)} collective-permute-done((bf16[4,5,640]{2,0,1:T(4,128)(2,1)S(1)}, bf16[4,5,640]{2,0,1:T(4,128)(2,1)S(1)}, u32[]{:S(2)}, u32[]{:S(2)}) %collective-permute-start.49) | collective-permute-done | bytes 25632 | tf_op jit(solution)/shard_map/ppermute | solution.py:15
  209.4 4.6 %collective-permute-done.50 = bf16[2,5,640]{2,0,1:T(2,128)(2,1)S(1)} collective-permute-done((bf16[2,5,640]{2,0,1:T(2,128)(2,1)S(1)}, bf16[2,5,640]{2,0,1:T(2,128)(2,1)S(1)}, u32[]{:S(2)}, u32[]{:S(2)}) %collective-permute-start.50) | collective-permute-done | bytes 12832 | tf_op jit(solution)/shard_map/ppermute | solution.py:15
  214.0 3.3 %collective-permute-start.51 = (bf16[1,5,640]{2,0,1:T(2,128)(2,1)S(1)}, bf16[1,5,640]{2,0,1:T(2,128)(2,1)S(1)}, u32[]{:S(2)}, u32[]{:S(2)}) collective-permute-start(bf16[1,5,640]{2,0,1:T(2,128)(2,1)S(1)} %dynamic-slice_convert_fusion.14), channel_id=1, source_target_pairs={{0,8},{1,9},{2,10},{3,11},{4,12},{5,13},{6,14},{7,15},{8,0},{9,1},... | collective-permute-start | bytes 19208 | tf_op jit(solution)/shard_map/ppermute | solution.py:15
  219.2 2.6 %collective-permute-done.51 = bf16[1,5,640]{2,0,1:T(2,128)(2,1)S(1)} collective-permute-done((bf16[1,5,640]{2,0,1:T(2,128)(2,1)S(1)}, bf16[1,5,640]{2,0,1:T(2,128)(2,1)S(1)}, u32[]{:S(2)}, u32[]{:S(2)}) %collective-permute-start.51) | collective-permute-done | bytes 6432 | tf_op jit(solution)/shard_map/ppermute | solution.py:15
  (184 shorter events, 47.9 us)
Async XLA Ops:
  2.7 7.7 %collective-permute-start.2 = (f32[8,128]{1,0:T(8,128)S(1)}, f32[8,128]{1,0:T(8,128)S(1)}, u32[]{:S(2)}, u32[]{:S(2)}) collective-permute-start(f32[8,128]{1,0:T(8,128)S(1)} %broadcast_in_dim.12), channel_id=1, source_target_pairs={{0,3},{1,2},{2,1},{3,0},{4,7},{5,6},{6,5},{7,4},{8,11},{9,10},{10,... | collective-permute-start | bytes 12296 | tf_op jit(solution)/shard_map/ppermute | solution.py:15
  2.8 7.6 %collective-permute-start.1 = (f32[8,128]{1,0:T(8,128)S(1)}, f32[8,128]{1,0:T(8,128)S(1)}, u32[]{:S(2)}, u32[]{:S(2)}) collective-permute-start(f32[8,128]{1,0:T(8,128)S(1)} %broadcast_in_dim.12), channel_id=1, source_target_pairs={{0,2},{1,3},{2,0},{3,1},{4,6},{5,7},{6,4},{7,5},{8,10},{9,11},{10,... | collective-permute-start | bytes 12296 | tf_op jit(solution)/shard_map/ppermute | solution.py:15
  4.7 5.7 %collective-permute-start = (f32[8,128]{1,0:T(8,128)S(1)}, f32[8,128]{1,0:T(8,128)S(1)}, u32[]{:S(2)}, u32[]{:S(2)}) collective-permute-start(f32[8,128]{1,0:T(8,128)S(1)} %broadcast_in_dim.12), channel_id=1, source_target_pairs={{0,1},{1,0},{2,3},{3,2},{4,5},{5,4},{6,7},{7,6},{8,9},{9,8},{10,11... | collective-permute-start | bytes 12296 | tf_op jit(solution)/shard_map/ppermute | solution.py:15
  11.1 4.6 %collective-permute-start.5 = (f32[8,128]{1,0:T(8,128)S(1)}, f32[8,128]{1,0:T(8,128)S(1)}, u32[]{:S(2)}, u32[]{:S(2)}) collective-permute-start(f32[8,128]{1,0:T(8,128)S(1)} %add_add_fusion.5), channel_id=1, source_target_pairs={{0,80},{1,81},{2,82},{3,83},{4,84},{5,85},{6,86},{7,87},{8,88},{9,... | collective-permute-start | bytes 12296 | tf_op jit(solution)/shard_map/ppermute | solution.py:15
  13.6 3.6 %collective-permute-start.4 = (f32[8,128]{1,0:T(8,128)S(1)}, f32[8,128]{1,0:T(8,128)S(1)}, u32[]{:S(2)}, u32[]{:S(2)}) collective-permute-start(f32[8,128]{1,0:T(8,128)S(1)} %add_add_fusion.5), channel_id=1, source_target_pairs={{0,64},{1,65},{2,66},{3,67},{4,68},{5,69},{6,70},{7,71},{8,72},{9,... | collective-permute-start | bytes 12296 | tf_op jit(solution)/shard_map/ppermute | solution.py:15
  17.7 7.0 %collective-permute-start.8 = (f32[8,128]{1,0:T(8,128)S(1)}, f32[8,128]{1,0:T(8,128)S(1)}, u32[]{:S(2)}, u32[]{:S(2)}) collective-permute-start(f32[8,128]{1,0:T(8,128)S(1)} %add_add_fusion.4), channel_id=1, source_target_pairs={{0,36},{1,37},{2,38},{3,39},{4,32},{5,33},{6,34},{7,35},{8,44},{9,... | collective-permute-start | bytes 12296 | tf_op jit(solution)/shard_map/ppermute | solution.py:15
  23.1 5.1 %collective-permute-start.7 = (f32[8,128]{1,0:T(8,128)S(1)}, f32[8,128]{1,0:T(8,128)S(1)}, u32[]{:S(2)}, u32[]{:S(2)}) collective-permute-start(f32[8,128]{1,0:T(8,128)S(1)} %add_add_fusion.4), channel_id=1, source_target_pairs={{0,32},{1,33},{2,34},{3,35},{4,36},{5,37},{6,38},{7,39},{8,40},{9,... | collective-permute-start | bytes 12296 | tf_op jit(solution)/shard_map/ppermute | solution.py:15
  23.9 4.5 %collective-permute-start.6 = (f32[8,128]{1,0:T(8,128)S(1)}, f32[8,128]{1,0:T(8,128)S(1)}, u32[]{:S(2)}, u32[]{:S(2)}) collective-permute-start(f32[8,128]{1,0:T(8,128)S(1)} %add_add_fusion.4), channel_id=1, source_target_pairs={{0,4},{1,5},{2,6},{3,7},{4,0},{5,1},{6,2},{7,3},{8,12},{9,13},{10,... | collective-permute-start | bytes 12296 | tf_op jit(solution)/shard_map/ppermute | solution.py:15
  28.4 9.9 %collective-permute-start.11 = (f32[8,128]{1,0:T(8,128)S(1)}, f32[8,128]{1,0:T(8,128)S(1)}, u32[]{:S(2)}, u32[]{:S(2)}) collective-permute-start(f32[8,128]{1,0:T(8,128)S(1)} %add_add_fusion.3), channel_id=1, source_target_pairs={{0,136},{1,137},{2,138},{3,139},{4,140},{5,141},{6,142},{7,143},{8... | collective-permute-start | bytes 12296 | tf_op jit(solution)/shard_map/ppermute | solution.py:15
  35.5 7.5 %collective-permute-start.10 = (f32[8,128]{1,0:T(8,128)S(1)}, f32[8,128]{1,0:T(8,128)S(1)}, u32[]{:S(2)}, u32[]{:S(2)}) collective-permute-start(f32[8,128]{1,0:T(8,128)S(1)} %add_add_fusion.3), channel_id=1, source_target_pairs={{0,8},{1,9},{2,10},{3,11},{4,12},{5,13},{6,14},{7,15},{8,0},{9,1},... | collective-permute-start | bytes 12296 | tf_op jit(solution)/shard_map/ppermute | solution.py:15
  37.0 6.1 %collective-permute-start.9 = (f32[8,128]{1,0:T(8,128)S(1)}, f32[8,128]{1,0:T(8,128)S(1)}, u32[]{:S(2)}, u32[]{:S(2)}) collective-permute-start(f32[8,128]{1,0:T(8,128)S(1)} %add_add_fusion.3), channel_id=1, source_target_pairs={{0,128},{1,129},{2,130},{3,131},{4,132},{5,133},{6,134},{7,135},{8... | collective-permute-start | bytes 12296 | tf_op jit(solution)/shard_map/ppermute | solution.py:15
  43.1 14.4 %collective-permute-start.12 = (bf16[128,640]{1,0:T(8,128)(2,1)S(1)}, bf16[128,640]{1,0:T(8,128)(2,1)S(1)}, u32[]{:S(2)}, u32[]{:S(2)}) collective-permute-start(bf16[128,640]{1,0:T(8,128)(2,1)S(1)} %multiply_convert_fusion.1), channel_id=1, source_target_pairs={{0,8},{1,9},{2,10},{3,11},{4,12},{5,13},{6,14},{7,15},{8,16},{9,17... | collective-permute-start | bytes 491528 | tf_op jit(solution)/shard_map/ppermute | solution.py:10
  50.3 9.8 %collective-permute-start.13 = (bf16[128,640]{1,0:T(8,128)(2,1)S(1)}, bf16[128,640]{1,0:T(8,128)(2,1)S(1)}, u32[]{:S(2)}, u32[]{:S(2)}) collective-permute-start(bf16[128,640]{1,0:T(8,128)(2,1)S(1)} %multiply_convert_fusion.1), channel_id=1, source_target_pairs={{0,4},{1,5},{2,6},{3,7},{4,8},{5,9},{6,10},{7,11},{8,12},{9,13},{1... | collective-permute-start | bytes 491528 | tf_op jit(solution)/shard_map/ppermute | solution.py:10
  53.7 8.9 %collective-permute-start.14 = (bf16[128,640]{1,0:T(8,128)(2,1)S(1)}, bf16[128,640]{1,0:T(8,128)(2,1)S(1)}, u32[]{:S(2)}, u32[]{:S(2)}) collective-permute-start(bf16[128,640]{1,0:T(8,128)(2,1)S(1)} %multiply_convert_fusion.1), channel_id=1, source_target_pairs={{4,0},{5,1},{6,2},{7,3},{8,4},{9,5},{10,6},{11,7},{12,8},{13,9},{1... | collective-permute-start | bytes 491528 | tf_op jit(solution)/shard_map/ppermute | solution.py:10
  55.0 15.7 %collective-permute-start.15 = (bf16[128,640]{1,0:T(8,128)(2,1)S(1)}, bf16[128,640]{1,0:T(8,128)(2,1)S(1)}, u32[]{:S(2)}, u32[]{:S(2)}) collective-permute-start(bf16[128,640]{1,0:T(8,128)(2,1)S(1)} %multiply_convert_fusion.1), channel_id=1, source_target_pairs={{8,0},{9,1},{10,2},{11,3},{12,4},{13,5},{14,6},{15,7},{16,8},{17,9... | collective-permute-start | bytes 491528 | tf_op jit(solution)/shard_map/ppermute | solution.py:10
  81.9 3.7 %collective-permute-start.29 = (f32[8,128]{1,0:T(8,128)S(1)}, f32[8,128]{1,0:T(8,128)S(1)}, u32[]{:S(2)}, u32[]{:S(2)}) collective-permute-start(f32[8,128]{1,0:T(8,128)S(1)} %broadcast_add_fusion), channel_id=1, source_target_pairs={{0,2},{1,3},{2,0},{3,1},{4,6},{5,7},{6,4},{7,5},{8,10},{9,11},{10,... | collective-permute-start | bytes 12296 | tf_op jit(solution)/shard_map/ppermute | solution.py:15
  86.2 4.1 %collective-permute-start.30 = (f32[8,128]{1,0:T(8,128)S(1)}, f32[8,128]{1,0:T(8,128)S(1)}, u32[]{:S(2)}, u32[]{:S(2)}) collective-permute-start(f32[8,128]{1,0:T(8,128)S(1)} %fusion.65), channel_id=1, source_target_pairs={{0,16},{1,17},{2,18},{3,19},{4,20},{5,21},{6,22},{7,23},{8,24},{9,... | collective-permute-start | bytes 12296 | tf_op jit(solution)/shard_map/ppermute | solution.py:15
  90.3 4.1 %collective-permute-start.31 = (f32[8,128]{1,0:T(8,128)S(1)}, f32[8,128]{1,0:T(8,128)S(1)}, u32[]{:S(2)}, u32[]{:S(2)}) collective-permute-start(f32[8,128]{1,0:T(8,128)S(1)} %add.335), channel_id=1, source_target_pairs={{0,64},{1,65},{2,66},{3,67},{4,68},{5,69},{6,70},{7,71},{8,72},{9,... | collective-permute-start | bytes 12296 | tf_op jit(solution)/shard_map/ppermute | solution.py:15
  92.9 13.0 %collective-permute-start.17 = (bf16[64,5,640]{2,0,1:T(8,128)(2,1)S(1)}, bf16[64,5,640]{2,0,1:T(8,128)(2,1)S(1)}, u32[]{:S(2)}, u32[]{:S(2)}) collective-permute-start(bf16[64,5,640]{2,0,1:T(8,128)(2,1)S(1)} %get-tuple-element.22), channel_id=1, source_target_pairs={{0,1},{1,0},{2,3},{3,2},{4,5},{5,4},{6,7},{7,6},{8,9},{9,8},{10,11... | collective-permute-start | bytes 1228808 | tf_op jit(solution)/shard_map/ppermute | solution.py:15
  93.0 12.9 %collective-permute-start.16 = (bf16[64,5,640]{2,0,1:T(8,128)(2,1)S(1)}, bf16[64,5,640]{2,0,1:T(8,128)(2,1)S(1)}, u32[]{:S(2)}, u32[]{:S(2)}) collective-permute-start(bf16[64,5,640]{2,0,1:T(8,128)(2,1)S(1)} %get-tuple-element.21), channel_id=1, source_target_pairs={{0,1},{1,0},{2,3},{3,2},{4,5},{5,4},{6,7},{7,6},{8,9},{9,8},{10,11... | collective-permute-start | bytes 1228808 | tf_op jit(solution)/shard_map/ppermute | solution.py:15
  94.4 4.5 %collective-permute-start.32 = (f32[8,128]{1,0:T(8,128)S(1)}, f32[8,128]{1,0:T(8,128)S(1)}, u32[]{:S(2)}, u32[]{:S(2)}) collective-permute-start(f32[8,128]{1,0:T(8,128)S(1)} %add.336), channel_id=1, source_target_pairs={{0,4},{1,5},{2,6},{3,7},{4,0},{5,1},{6,2},{7,3},{8,12},{9,13},{10,... | collective-permute-start | bytes 12296 | tf_op jit(solution)/shard_map/ppermute | solution.py:15
  99.0 5.1 %collective-permute-start.33 = (f32[8,128]{1,0:T(8,128)S(1)}, f32[8,128]{1,0:T(8,128)S(1)}, u32[]{:S(2)}, u32[]{:S(2)}) collective-permute-start(f32[8,128]{1,0:T(8,128)S(1)} %add.337), channel_id=1, source_target_pairs={{0,32},{1,33},{2,34},{3,35},{4,36},{5,37},{6,38},{7,39},{8,40},{9,... | collective-permute-start | bytes 12296 | tf_op jit(solution)/shard_map/ppermute | solution.py:15
  104.1 5.1 %collective-permute-start.34 = (f32[8,128]{1,0:T(8,128)S(1)}, f32[8,128]{1,0:T(8,128)S(1)}, u32[]{:S(2)}, u32[]{:S(2)}) collective-permute-start(f32[8,128]{1,0:T(8,128)S(1)} %add.338), channel_id=1, source_target_pairs={{0,128},{1,129},{2,130},{3,131},{4,132},{5,133},{6,134},{7,135},{8... | collective-permute-start | bytes 12296 | tf_op jit(solution)/shard_map/ppermute | solution.py:15
  106.2 7.0 %collective-permute-start.19 = (bf16[32,5,640]{2,0,1:T(8,128)(2,1)S(1)}, bf16[32,5,640]{2,0,1:T(8,128)(2,1)S(1)}, u32[]{:S(2)}, u32[]{:S(2)}) collective-permute-start(bf16[32,5,640]{2,0,1:T(8,128)(2,1)S(1)} %get-tuple-element.26), channel_id=1, source_target_pairs={{0,2},{1,3},{2,0},{3,1},{4,6},{5,7},{6,4},{7,5},{8,10},{9,11},{10,... | collective-permute-start | bytes 614408 | tf_op jit(solution)/shard_map/ppermute | solution.py:15
  108.3 6.3 %collective-permute-start.18 = (bf16[32,5,640]{2,0,1:T(8,128)(2,1)S(1)}, bf16[32,5,640]{2,0,1:T(8,128)(2,1)S(1)}, u32[]{:S(2)}, u32[]{:S(2)}) collective-permute-start(bf16[32,5,640]{2,0,1:T(8,128)(2,1)S(1)} %get-tuple-element.25), channel_id=1, source_target_pairs={{0,2},{1,3},{2,0},{3,1},{4,6},{5,7},{6,4},{7,5},{8,10},{9,11},{10,... | collective-permute-start | bytes 614408 | tf_op jit(solution)/shard_map/ppermute | solution.py:15
  109.2 10.4 %collective-permute-start.35 = (f32[8,128]{1,0:T(8,128)S(1)}, f32[8,128]{1,0:T(8,128)S(1)}, u32[]{:S(2)}, u32[]{:S(2)}) collective-permute-start(f32[8,128]{1,0:T(8,128)S(1)} %add.339), channel_id=1, source_target_pairs={{0,8},{1,9},{2,10},{3,11},{4,12},{5,13},{6,14},{7,15},{8,0},{9,1},... | collective-permute-start | bytes 12296 | tf_op jit(solution)/shard_map/ppermute | solution.py:15
  114.8 10.3 %collective-permute-start.21 = (bf16[16,5,640]{2,0,1:T(8,128)(2,1)S(1)}, bf16[16,5,640]{2,0,1:T(8,128)(2,1)S(1)}, u32[]{:S(2)}, u32[]{:S(2)}) collective-permute-start(bf16[16,5,640]{2,0,1:T(8,128)(2,1)S(1)} %get-tuple-element.30), channel_id=1, source_target_pairs={{0,16},{1,17},{2,18},{3,19},{4,20},{5,21},{6,22},{7,23},{8,24},{9,... | collective-permute-start | bytes 307208 | tf_op jit(solution)/shard_map/ppermute | solution.py:15
  115.1 18.5 %collective-permute-start.20 = (bf16[16,5,640]{2,0,1:T(8,128)(2,1)S(1)}, bf16[16,5,640]{2,0,1:T(8,128)(2,1)S(1)}, u32[]{:S(2)}, u32[]{:S(2)}) collective-permute-start(bf16[16,5,640]{2,0,1:T(8,128)(2,1)S(1)} %get-tuple-element.29), channel_id=1, source_target_pairs={{0,16},{1,17},{2,18},{3,19},{4,20},{5,21},{6,22},{7,23},{8,24},{9,... | collective-permute-start | bytes 307208 | tf_op jit(solution)/shard_map/ppermute | solution.py:15
  117.0 22.6 %collective-permute-start.36 = (bf16[128,640]{1,0:T(8,128)(2,1)S(1)}, bf16[128,640]{1,0:T(8,128)(2,1)S(1)}, u32[]{:S(2)}, u32[]{:S(2)}) collective-permute-start(bf16[128,640]{1,0:T(8,128)(2,1)S(1)} %add_convert_fusion.1), channel_id=1, source_target_pairs={{8,0},{9,1},{10,2},{11,3},{12,4},{13,5},{14,6},{15,7},{16,8},{17,9... | collective-permute-start | bytes 491528 | tf_op jit(solution)/shard_map/ppermute | solution.py:10
  118.3 26.1 %collective-permute-start.37 = (bf16[128,640]{1,0:T(8,128)(2,1)S(1)}, bf16[128,640]{1,0:T(8,128)(2,1)S(1)}, u32[]{:S(2)}, u32[]{:S(2)}) collective-permute-start(bf16[128,640]{1,0:T(8,128)(2,1)S(1)} %add_convert_fusion.1), channel_id=1, source_target_pairs={{4,0},{5,1},{6,2},{7,3},{8,4},{9,5},{10,6},{11,7},{12,8},{13,9},{1... | collective-permute-start | bytes 491528 | tf_op jit(solution)/shard_map/ppermute | solution.py:10
  119.6 35.9 %collective-permute-start.38 = (bf16[128,640]{1,0:T(8,128)(2,1)S(1)}, bf16[128,640]{1,0:T(8,128)(2,1)S(1)}, u32[]{:S(2)}, u32[]{:S(2)}) collective-permute-start(bf16[128,640]{1,0:T(8,128)(2,1)S(1)} %add_convert_fusion.1), channel_id=1, source_target_pairs={{0,4},{1,5},{2,6},{3,7},{4,8},{5,9},{6,10},{7,11},{8,12},{9,13},{1... | collective-permute-start | bytes 491528 | tf_op jit(solution)/shard_map/ppermute | solution.py:10
  125.1 35.1 %collective-permute-start.39 = (bf16[128,640]{1,0:T(8,128)(2,1)S(1)}, bf16[128,640]{1,0:T(8,128)(2,1)S(1)}, u32[]{:S(2)}, u32[]{:S(2)}) collective-permute-start(bf16[128,640]{1,0:T(8,128)(2,1)S(1)} %add_convert_fusion.1), channel_id=1, source_target_pairs={{0,8},{1,9},{2,10},{3,11},{4,12},{5,13},{6,14},{7,15},{8,16},{9,17... | collective-permute-start | bytes 491528 | tf_op jit(solution)/shard_map/ppermute | solution.py:10
  133.7 8.0 %collective-permute-start.23 = (bf16[8,5,640]{2,0,1:T(8,128)(2,1)S(1)}, bf16[8,5,640]{2,0,1:T(8,128)(2,1)S(1)}, u32[]{:S(2)}, u32[]{:S(2)}) collective-permute-start(bf16[8,5,640]{2,0,1:T(8,128)(2,1)S(1)} %get-tuple-element.34), channel_id=1, source_target_pairs={{0,64},{1,65},{2,66},{3,67},{4,68},{5,69},{6,70},{7,71},{8,72},{9,... | collective-permute-start | bytes 153608 | tf_op jit(solution)/shard_map/ppermute | solution.py:15
  139.6 4.1 %collective-permute-start.22 = (bf16[8,5,640]{2,0,1:T(8,128)(2,1)S(1)}, bf16[8,5,640]{2,0,1:T(8,128)(2,1)S(1)}, u32[]{:S(2)}, u32[]{:S(2)}) collective-permute-start(bf16[8,5,640]{2,0,1:T(8,128)(2,1)S(1)} %get-tuple-element.33), channel_id=1, source_target_pairs={{0,64},{1,65},{2,66},{3,67},{4,68},{5,69},{6,70},{7,71},{8,72},{9,... | collective-permute-start | bytes 153608 | tf_op jit(solution)/shard_map/ppermute | solution.py:15
  143.7 5.1 %collective-permute-start.24 = (bf16[8,5,640]{2,0,1:T(8,128)(2,1)S(1)}, bf16[8,5,640]{2,0,1:T(8,128)(2,1)S(1)}, u32[]{:S(2)}, u32[]{:S(2)}) collective-permute-start(bf16[8,5,640]{2,0,1:T(8,128)(2,1)S(1)} %dynamic-slice_convert_fusion.9), channel_id=1, source_target_pairs={{0,4},{1,5},{2,6},{3,7},{4,0},{5,1},{6,2},{7,3},{8,12},{9,13},{10,... | collective-permute-start | bytes 153608 | tf_op jit(solution)/shard_map/ppermute | solution.py:15
  148.9 5.6 %collective-permute-start.25 = (bf16[4,5,640]{2,0,1:T(4,128)(2,1)S(1)}, bf16[4,5,640]{2,0,1:T(4,128)(2,1)S(1)}, u32[]{:S(2)}, u32[]{:S(2)}) collective-permute-start(bf16[4,5,640]{2,0,1:T(4,128)(2,1)S(1)} %dynamic-slice_convert_fusion.11), channel_id=1, source_target_pairs={{0,32},{1,33},{2,34},{3,35},{4,36},{5,37},{6,38},{7,39},{8,40},{9,... | collective-permute-start | bytes 76808 | tf_op jit(solution)/shard_map/ppermute | solution.py:15
  154.6 5.3 %collective-permute-start.26 = (bf16[2,5,640]{2,0,1:T(2,128)(2,1)S(1)}, bf16[2,5,640]{2,0,1:T(2,128)(2,1)S(1)}, u32[]{:S(2)}, u32[]{:S(2)}) collective-permute-start(bf16[2,5,640]{2,0,1:T(2,128)(2,1)S(1)} %dynamic-slice_convert_fusion.13), channel_id=1, source_target_pairs={{0,128},{1,129},{2,130},{3,131},{4,132},{5,133},{6,134},{7,135},{8... | collective-permute-start | bytes 38408 | tf_op jit(solution)/shard_map/ppermute | solution.py:15
  159.9 7.8 %collective-permute-start.27 = (bf16[1,5,640]{2,0,1:T(2,128)(2,1)S(1)}, bf16[1,5,640]{2,0,1:T(2,128)(2,1)S(1)}, u32[]{:S(2)}, u32[]{:S(2)}) collective-permute-start(bf16[1,5,640]{2,0,1:T(2,128)(2,1)S(1)} %dynamic-slice_convert_fusion.15), channel_id=1, source_target_pairs={{0,8},{1,9},{2,10},{3,11},{4,12},{5,13},{6,14},{7,15},{8,0},{9,1},... | collective-permute-start | bytes 19208 | tf_op jit(solution)/shard_map/ppermute | solution.py:15
  173.7 8.5 %collective-permute-start.43 = (bf16[32,5,640]{2,0,1:T(8,128)(2,1)S(1)}, bf16[32,5,640]{2,0,1:T(8,128)(2,1)S(1)}, u32[]{:S(2)}, u32[]{:S(2)}) collective-permute-start(bf16[32,5,640]{2,0,1:T(8,128)(2,1)S(1)} %get-tuple-element.24), channel_id=1, source_target_pairs={{0,2},{1,3},{2,0},{3,1},{4,6},{5,7},{6,4},{7,5},{8,10},{9,11},{10,... | collective-permute-start | bytes 614408 | tf_op jit(solution)/shard_map/ppermute | solution.py:15
  176.3 9.8 %collective-permute-start.42 = (bf16[32,5,640]{2,0,1:T(8,128)(2,1)S(1)}, bf16[32,5,640]{2,0,1:T(8,128)(2,1)S(1)}, u32[]{:S(2)}, u32[]{:S(2)}) collective-permute-start(bf16[32,5,640]{2,0,1:T(8,128)(2,1)S(1)} %get-tuple-element.23), channel_id=1, source_target_pairs={{0,2},{1,3},{2,0},{3,1},{4,6},{5,7},{6,4},{7,5},{8,10},{9,11},{10,... | collective-permute-start | bytes 614408 | tf_op jit(solution)/shard_map/ppermute | solution.py:15
  186.2 5.5 %collective-permute-start.45 = (bf16[16,5,640]{2,0,1:T(8,128)(2,1)S(1)}, bf16[16,5,640]{2,0,1:T(8,128)(2,1)S(1)}, u32[]{:S(2)}, u32[]{:S(2)}) collective-permute-start(bf16[16,5,640]{2,0,1:T(8,128)(2,1)S(1)} %get-tuple-element.28), channel_id=1, source_target_pairs={{0,16},{1,17},{2,18},{3,19},{4,20},{5,21},{6,22},{7,23},{8,24},{9,... | collective-permute-start | bytes 307208 | tf_op jit(solution)/shard_map/ppermute | solution.py:15
  186.3 6.5 %collective-permute-start.44 = (bf16[16,5,640]{2,0,1:T(8,128)(2,1)S(1)}, bf16[16,5,640]{2,0,1:T(8,128)(2,1)S(1)}, u32[]{:S(2)}, u32[]{:S(2)}) collective-permute-start(bf16[16,5,640]{2,0,1:T(8,128)(2,1)S(1)} %get-tuple-element.27), channel_id=1, source_target_pairs={{0,16},{1,17},{2,18},{3,19},{4,20},{5,21},{6,22},{7,23},{8,24},{9,... | collective-permute-start | bytes 307208 | tf_op jit(solution)/shard_map/ppermute | solution.py:15
  192.9 4.2 %collective-permute-start.47 = (bf16[8,5,640]{2,0,1:T(8,128)(2,1)S(1)}, bf16[8,5,640]{2,0,1:T(8,128)(2,1)S(1)}, u32[]{:S(2)}, u32[]{:S(2)}) collective-permute-start(bf16[8,5,640]{2,0,1:T(8,128)(2,1)S(1)} %get-tuple-element.32), channel_id=1, source_target_pairs={{0,64},{1,65},{2,66},{3,67},{4,68},{5,69},{6,70},{7,71},{8,72},{9,... | collective-permute-start | bytes 153608 | tf_op jit(solution)/shard_map/ppermute | solution.py:15
  193.8 4.1 %collective-permute-start.46 = (bf16[8,5,640]{2,0,1:T(8,128)(2,1)S(1)}, bf16[8,5,640]{2,0,1:T(8,128)(2,1)S(1)}, u32[]{:S(2)}, u32[]{:S(2)}) collective-permute-start(bf16[8,5,640]{2,0,1:T(8,128)(2,1)S(1)} %get-tuple-element.31), channel_id=1, source_target_pairs={{0,64},{1,65},{2,66},{3,67},{4,68},{5,69},{6,70},{7,71},{8,72},{9,... | collective-permute-start | bytes 153608 | tf_op jit(solution)/shard_map/ppermute | solution.py:15
  198.0 5.1 %collective-permute-start.48 = (bf16[8,5,640]{2,0,1:T(8,128)(2,1)S(1)}, bf16[8,5,640]{2,0,1:T(8,128)(2,1)S(1)}, u32[]{:S(2)}, u32[]{:S(2)}) collective-permute-start(bf16[8,5,640]{2,0,1:T(8,128)(2,1)S(1)} %dynamic-slice_convert_fusion.8), channel_id=1, source_target_pairs={{0,4},{1,5},{2,6},{3,7},{4,0},{5,1},{6,2},{7,3},{8,12},{9,13},{10,... | collective-permute-start | bytes 153608 | tf_op jit(solution)/shard_map/ppermute | solution.py:15
  203.2 5.4 %collective-permute-start.49 = (bf16[4,5,640]{2,0,1:T(4,128)(2,1)S(1)}, bf16[4,5,640]{2,0,1:T(4,128)(2,1)S(1)}, u32[]{:S(2)}, u32[]{:S(2)}) collective-permute-start(bf16[4,5,640]{2,0,1:T(4,128)(2,1)S(1)} %dynamic-slice_convert_fusion.10), channel_id=1, source_target_pairs={{0,32},{1,33},{2,34},{3,35},{4,36},{5,37},{6,38},{7,39},{8,40},{9,... | collective-permute-start | bytes 76808 | tf_op jit(solution)/shard_map/ppermute | solution.py:15
  208.7 5.3 %collective-permute-start.50 = (bf16[2,5,640]{2,0,1:T(2,128)(2,1)S(1)}, bf16[2,5,640]{2,0,1:T(2,128)(2,1)S(1)}, u32[]{:S(2)}, u32[]{:S(2)}) collective-permute-start(bf16[2,5,640]{2,0,1:T(2,128)(2,1)S(1)} %dynamic-slice_convert_fusion.12), channel_id=1, source_target_pairs={{0,128},{1,129},{2,130},{3,131},{4,132},{5,133},{6,134},{7,135},{8... | collective-permute-start | bytes 38408 | tf_op jit(solution)/shard_map/ppermute | solution.py:15
  214.0 7.8 %collective-permute-start.51 = (bf16[1,5,640]{2,0,1:T(2,128)(2,1)S(1)}, bf16[1,5,640]{2,0,1:T(2,128)(2,1)S(1)}, u32[]{:S(2)}, u32[]{:S(2)}) collective-permute-start(bf16[1,5,640]{2,0,1:T(2,128)(2,1)S(1)} %dynamic-slice_convert_fusion.14), channel_id=1, source_target_pairs={{0,8},{1,9},{2,10},{3,11},{4,12},{5,13},{6,14},{7,15},{8,0},{9,1},... | collective-permute-start | bytes 19208 | tf_op jit(solution)/shard_map/ppermute | solution.py:15
  (14 other events, 174.3 us)

commit v11 on v9

--- a/solution.py
+++ b/solution.py
@@ -98,9 +98,9 @@
     first_act = norm_gelu(hidden_in.astype(jnp.float32)).astype(jnp.bfloat16)
     first_pre = jnp.dot(first_act, w_in, preferred_element_type=jnp.float32)
     narrow_activation = norm_gelu(first_pre).astype(jnp.bfloat16)
-    count_tile, narrow_activation = lax.optimization_barrier((count_tile, narrow_activation))
+    kernel_tap_pile = jnp.stack(spread(narrow_activation, shard_reach))
+    count_tile, kernel_tap_pile = lax.optimization_barrier((count_tile, kernel_tap_pile))
     mask_total = count_tile[0, 0]
-    kernel_tap_pile = jnp.stack(spread(narrow_activation, shard_reach))
     conv_pre = jnp.einsum(
         "krc,kcb->rb", kernel_tap_pile, conv_weight, preferred_element_type=jnp.float32
     )

time: 200 us -> 198 us (0.990)
  waiting for transfers between devices: 59 us -> 55.6 us
    ppermute x44, waiting for transfers between devices: 45.9 us -> 41 us  [swap_with(): return lax.ppermute(block, axis, [(i, i ^ bit) for i in range(devices)])]
    unnamed x27 -> x26, local copies, waits for them, and re-layouts: 5.35 us -> 5.33 us
  transfers between devices with their start and end apart: 52 -> 52, of which waited for: 28 -> 26; matrix products, arithmetic and copies ran while one was open for 12% -> 12% of each run, Pallas kernels for 0% -> 0%
where the time goes in v11:
time: 198 us
  starting transfers between devices  99.6 us (50%)
  waiting for transfers between devices  55.6 us (28%)
  local copies, waits for them, and re-layouts  15 us (8%)
  other arithmetic  12.8 us (6%)
  matrix products  9.85 us (5%)
  between operations  4.67 us (2%)
    ppermute x44, starting transfers between devices, swap_with(): return lax.ppermute(block, axis, [(i, i ^ bit) for i in range(devices)])  69.9 us
    ppermute x44, waiting for transfers between devices, swap_with(): return lax.ppermute(block, axis, [(i, i ^ bit) for i in range(devices)])  41 us
    ppermute x8, starting transfers between devices, from_behind(): return lax.ppermute(block, axis, route)  29.7 us
    ppermute x8, waiting for transfers between devices, from_behind(): return lax.ppermute(block, axis, route)  14.5 us
    unnamed x26, local copies, waits for them, and re-layouts  5.33 us
  transfers between devices with their start and end apart: 52, of which 26 were waited for; matrix products, arithmetic and copies ran while one was open for 12% of the time, Pallas kernels for 0%

profile of v11, /device:TPU:32, one launch (start us, length us, event | category | flops | bytes accessed | tf_op | source)
XLA Modules:
  0.0 197.5 jit_solution(10102679706997268268)
XLA Ops:
  0.6 1.4 convert_reduce_fusion.1
  2.8 1.9 collective-permute-start.1
  7.0 1.4 fusion.9
  8.4 1.9 fusion.53
  11.1 2.5 %collective-permute-start.5 = (f32[8,128]{1,0:T(8,128)S(1)}, f32[8,128]{1,0:T(8,128)S(1)}, u32[]{:S(2)}, u32[]{:S(2)}) collective-permute-start(f32[8,128]{1,0:T(8,128)S(1)} %add_add_fusion.5), channel_id=1, source_target_pairs={{0,80},{1,81},{2,82},{3,83},{4,84},{5,85},{6,86},{7,87},{8,88},{9,... | collective-permute-start | bytes 12296 | tf_op jit(solution)/shard_map/ppermute | solution.py:15
  15.7 1.5 collective-permute-done.4
  17.7 5.4 %collective-permute-start.8 = (f32[8,128]{1,0:T(8,128)S(1)}, f32[8,128]{1,0:T(8,128)S(1)}, u32[]{:S(2)}, u32[]{:S(2)}) collective-permute-start(f32[8,128]{1,0:T(8,128)S(1)} %add_add_fusion.4), channel_id=1, source_target_pairs={{0,36},{1,37},{2,38},{3,39},{4,32},{5,33},{6,34},{7,35},{8,44},{9,... | collective-permute-start | bytes 12296 | tf_op jit(solution)/shard_map/ppermute | solution.py:15
  24.7 3.5 %collective-permute-done.7 = f32[8,128]{1,0:T(8,128)S(1)} collective-permute-done((f32[8,128]{1,0:T(8,128)S(1)}, f32[8,128]{1,0:T(8,128)S(1)}, u32[]{:S(2)}, u32[]{:S(2)}) %collective-permute-start.7) | collective-permute-done | bytes 4128 | tf_op jit(solution)/shard_map/ppermute | solution.py:15
  28.4 7.1 %collective-permute-start.11 = (f32[8,128]{1,0:T(8,128)S(1)}, f32[8,128]{1,0:T(8,128)S(1)}, u32[]{:S(2)}, u32[]{:S(2)}) collective-permute-start(f32[8,128]{1,0:T(8,128)S(1)} %add_add_fusion.3), channel_id=1, source_target_pairs={{0,136},{1,137},{2,138},{3,139},{4,140},{5,141},{6,142},{7,143},{8... | collective-permute-start | bytes 12296 | tf_op jit(solution)/shard_map/ppermute | solution.py:15
  35.5 1.5 collective-permute-start.10
  37.5 6.4 %collective-permute-start.12 = (bf16[128,640]{1,0:T(8,128)(2,1)S(1)}, bf16[128,640]{1,0:T(8,128)(2,1)S(1)}, u32[]{:S(2)}, u32[]{:S(2)}) collective-permute-start(bf16[128,640]{1,0:T(8,128)(2,1)S(1)} %multiply_convert_fusion.1), channel_id=1, source_target_pairs={{0,8},{1,9},{2,10},{3,11},{4,12},{5,13},{6,14},{7,15},{8,16},{9,17... | collective-permute-start | bytes 491528 | tf_op jit(solution)/shard_map/ppermute | solution.py:10
  43.9 3.4 %collective-permute-start.13 = (bf16[128,640]{1,0:T(8,128)(2,1)S(1)}, bf16[128,640]{1,0:T(8,128)(2,1)S(1)}, u32[]{:S(2)}, u32[]{:S(2)}) collective-permute-start(bf16[128,640]{1,0:T(8,128)(2,1)S(1)} %multiply_convert_fusion.1), channel_id=1, source_target_pairs={{0,4},{1,5},{2,6},{3,7},{4,8},{5,9},{6,10},{7,11},{8,12},{9,13},{1... | collective-permute-start | bytes 491528 | tf_op jit(solution)/shard_map/ppermute | solution.py:10
  51.6 2.5 %collective-permute-done.13 = bf16[128,640]{1,0:T(8,128)(2,1)S(1)} collective-permute-done((bf16[128,640]{1,0:T(8,128)(2,1)S(1)}, bf16[128,640]{1,0:T(8,128)(2,1)S(1)}, u32[]{:S(2)}, u32[]{:S(2)}) %collective-permute-start.13) | collective-permute-done | bytes 163872 | tf_op jit(solution)/shard_map/ppermute | solution.py:10
  54.4 4.6 %collective-permute-done.14 = bf16[128,640]{1,0:T(8,128)(2,1)S(1)} collective-permute-done((bf16[128,640]{1,0:T(8,128)(2,1)S(1)}, bf16[128,640]{1,0:T(8,128)(2,1)S(1)}, u32[]{:S(2)}, u32[]{:S(2)}) %collective-permute-start.14) | collective-permute-done | bytes 163872 | tf_op jit(solution)/shard_map/ppermute | solution.py:10
  59.1 7.4 %collective-permute-done.15 = bf16[128,640]{1,0:T(8,128)(2,1)S(1)} collective-permute-done((bf16[128,640]{1,0:T(8,128)(2,1)S(1)}, bf16[128,640]{1,0:T(8,128)(2,1)S(1)}, u32[]{:S(2)}, u32[]{:S(2)}) %collective-permute-start.15) | collective-permute-done | bytes 163872 | tf_op jit(solution)/shard_map/ppermute | solution.py:10
  66.5 3.1 %fusion.54 = (f32[128]{0:T(128)S(1)}, f32[128,640]{1,0:T(8,128)S(1)}) fusion(bf16[5,128,640]{2,1,0:T(8,128)(2,1)S(1)} %bitcast_dynamic-update-slice_fusion.5, bf16[5,640,640]{2,1,0:T(8,128)(2,1)} %param.13), kind=kOutput, calls=%fused_computation.139 | convolution fusion | flops 524369792 | bytes 5243392 | tf_op jit(solution)/shard_map/krc,kcb->rb/dot_general | solution.py:104
  75.0 1.5 collective-permute-start.24
  77.8 6.1 %collective-permute-start.26 = (bf16[128,640]{1,0:T(8,128)(2,1)}, bf16[128,640]{1,0:T(8,128)(2,1)}, u32[]{:S(2)}, u32[]{:S(2)}) collective-permute-start(bf16[128,640]{1,0:T(8,128)(2,1)} %add_convert_fusion.1), channel_id=1, source_target_pairs={{0,4},{1,5},{2,6},{3,7},{4,8},{5,9},{6,10},{7,11},{8,12},{9,13},{1... | collective-permute-start | bytes 491528 | tf_op jit(solution)/shard_map/ppermute | solution.py:10
  83.9 8.5 %collective-permute-start.27 = (bf16[128,640]{1,0:T(8,128)(2,1)}, bf16[128,640]{1,0:T(8,128)(2,1)}, u32[]{:S(2)}, u32[]{:S(2)}) collective-permute-start(bf16[128,640]{1,0:T(8,128)(2,1)} %add_convert_fusion.1), channel_id=1, source_target_pairs={{0,8},{1,9},{2,10},{3,11},{4,12},{5,13},{6,14},{7,15},{8,16},{9,17... | collective-permute-start | bytes 491528 | tf_op jit(solution)/shard_map/ppermute | solution.py:10
  102.3 1.5 multiply_reduce_fusion
  106.5 1.9 collective-permute-start.43
  110.8 1.9 collective-permute-start.31
  113.5 2.9 %collective-permute-start.18 = (f32[8,128]{1,0:T(8,128)S(1)}, f32[8,128]{1,0:T(8,128)S(1)}, u32[]{:S(2)}, u32[]{:S(2)}) collective-permute-start(f32[8,128]{1,0:T(8,128)S(1)} %fusion.66), channel_id=1, source_target_pairs={{0,16},{1,17},{2,18},{3,19},{4,20},{5,21},{6,22},{7,23},{8,24},{9,... | collective-permute-start | bytes 12296 | tf_op jit(solution)/shard_map/ppermute | solution.py:15
  116.4 1.6 collective-permute-done.18
  118.0 7.7 %collective-permute-start.19 = (f32[8,128]{1,0:T(8,128)S(1)}, f32[8,128]{1,0:T(8,128)S(1)}, u32[]{:S(2)}, u32[]{:S(2)}) collective-permute-start(f32[8,128]{1,0:T(8,128)S(1)} %add.294), channel_id=1, source_target_pairs={{0,64},{1,65},{2,66},{3,67},{4,68},{5,69},{6,70},{7,71},{8,72},{9,... | collective-permute-start | bytes 12296 | tf_op jit(solution)/shard_map/ppermute | solution.py:15
  125.7 1.6 collective-permute-done.19
  127.3 1.6 collective-permute-start.20
  128.9 2.9 %collective-permute-done.20 = f32[8,128]{1,0:T(8,128)S(1)} collective-permute-done((f32[8,128]{1,0:T(8,128)S(1)}, f32[8,128]{1,0:T(8,128)S(1)}, u32[]{:S(2)}, u32[]{:S(2)}) %collective-permute-start.20) | collective-permute-done | bytes 4128 | tf_op jit(solution)/shard_map/ppermute | solution.py:15
  132.8 4.1 %collective-permute-done.21 = f32[8,128]{1,0:T(8,128)S(1)} collective-permute-done((f32[8,128]{1,0:T(8,128)S(1)}, f32[8,128]{1,0:T(8,128)S(1)}, u32[]{:S(2)}, u32[]{:S(2)}) %collective-permute-start.21) | collective-permute-done | bytes 4128 | tf_op jit(solution)/shard_map/ppermute | solution.py:15
  136.9 7.0 %collective-permute-start.22 = (f32[8,128]{1,0:T(8,128)S(1)}, f32[8,128]{1,0:T(8,128)S(1)}, u32[]{:S(2)}, u32[]{:S(2)}) collective-permute-start(f32[8,128]{1,0:T(8,128)S(1)} %add.297), channel_id=1, source_target_pairs={{0,128},{1,129},{2,130},{3,131},{4,132},{5,133},{6,134},{7,135},{8... | collective-permute-start | bytes 12296 | tf_op jit(solution)/shard_map/ppermute | solution.py:15
  143.9 1.6 collective-permute-done.22
  145.5 7.5 %collective-permute-done.23 = f32[8,128]{1,0:T(8,128)S(1)} collective-permute-done((f32[8,128]{1,0:T(8,128)S(1)}, f32[8,128]{1,0:T(8,128)S(1)}, u32[]{:S(2)}, u32[]{:S(2)}) %collective-permute-start.23) | collective-permute-done | bytes 4128 | tf_op jit(solution)/shard_map/ppermute | solution.py:15
  154.9 1.7 convert_add_fusion.2
  156.8 2.0 %collective-permute-start.32 = (bf16[16,5,640]{2,0,1:T(8,128)(2,1)S(1)}, bf16[16,5,640]{2,0,1:T(8,128)(2,1)S(1)}, u32[]{:S(2)}, u32[]{:S(2)}) collective-permute-start(bf16[16,5,640]{2,0,1:T(8,128)(2,1)S(1)} %get-tuple-element.23), channel_id=1, source_target_pairs={{0,16},{1,17},{2,18},{3,19},{4,20},{5,21},{6,22},{7,23},{8,24},{9,... | collective-permute-start | bytes 307208 | tf_op jit(solution)/shard_map/ppermute | solution.py:15
  159.0 1.9 collective-permute-start.44
  162.6 2.0 %collective-permute-start.35 = (bf16[8,5,640]{2,0,1:T(8,128)(2,1)S(1)}, bf16[8,5,640]{2,0,1:T(8,128)(2,1)S(1)}, u32[]{:S(2)}, u32[]{:S(2)}) collective-permute-start(bf16[8,5,640]{2,0,1:T(8,128)(2,1)S(1)} %get-tuple-element.28), channel_id=1, source_target_pairs={{0,64},{1,65},{2,66},{3,67},{4,68},{5,69},{6,70},{7,71},{8,72},{9,... | collective-permute-start | bytes 153608 | tf_op jit(solution)/shard_map/ppermute | solution.py:15
  164.8 2.0 %collective-permute-start.47 = (bf16[8,5,640]{2,0,1:T(8,128)(2,1)S(1)}, bf16[8,5,640]{2,0,1:T(8,128)(2,1)S(1)}, u32[]{:S(2)}, u32[]{:S(2)}) collective-permute-start(bf16[8,5,640]{2,0,1:T(8,128)(2,1)S(1)} %get-tuple-element.26), channel_id=1, source_target_pairs={{0,64},{1,65},{2,66},{3,67},{4,68},{5,69},{6,70},{7,71},{8,72},{9,... | collective-permute-start | bytes 153608 | tf_op jit(solution)/shard_map/ppermute | solution.py:15
  167.0 1.8 collective-permute-done.34
  169.3 1.7 collective-permute-done.46
  171.9 2.0 %collective-permute-done.36 = bf16[8,5,640]{2,0,1:T(8,128)(2,1)S(1)} collective-permute-done((bf16[8,5,640]{2,0,1:T(8,128)(2,1)S(1)}, bf16[8,5,640]{2,0,1:T(8,128)(2,1)S(1)}, u32[]{:S(2)}, u32[]{:S(2)}) %collective-permute-start.36) | collective-permute-done | bytes 51232 | tf_op jit(solution)/shard_map/ppermute | solution.py:15
  174.8 1.3 collective-permute-done.48
  176.1 1.6 collective-permute-start.49
  177.7 1.7 collective-permute-done.37
  179.5 3.0 %collective-permute-start.38 = (bf16[2,5,640]{2,0,1:T(2,128)(2,1)S(1)}, bf16[2,5,640]{2,0,1:T(2,128)(2,1)S(1)}, u32[]{:S(2)}, u32[]{:S(2)}) collective-permute-start(bf16[2,5,640]{2,0,1:T(2,128)(2,1)S(1)} %dynamic-slice_convert_fusion.13), channel_id=1, source_target_pairs={{0,128},{1,129},{2,130},{3,131},{4,132},{5,133},{6,134},{7,135},{8... | collective-permute-start | bytes 38408 | tf_op jit(solution)/shard_map/ppermute | solution.py:15
  182.5 2.1 %collective-permute-start.50 = (bf16[2,5,640]{2,0,1:T(2,128)(2,1)S(1)}, bf16[2,5,640]{2,0,1:T(2,128)(2,1)S(1)}, u32[]{:S(2)}, u32[]{:S(2)}) collective-permute-start(bf16[2,5,640]{2,0,1:T(2,128)(2,1)S(1)} %dynamic-slice_convert_fusion.12), channel_id=1, source_target_pairs={{0,128},{1,129},{2,130},{3,131},{4,132},{5,133},{6,134},{7,135},{8... | collective-permute-start | bytes 38408 | tf_op jit(solution)/shard_map/ppermute | solution.py:15
  184.8 3.2 %collective-permute-start.39 = (bf16[1,5,640]{2,0,1:T(2,128)(2,1)S(1)}, bf16[1,5,640]{2,0,1:T(2,128)(2,1)S(1)}, u32[]{:S(2)}, u32[]{:S(2)}) collective-permute-start(bf16[1,5,640]{2,0,1:T(2,128)(2,1)S(1)} %dynamic-slice_convert_fusion.15), channel_id=1, source_target_pairs={{0,8},{1,9},{2,10},{3,11},{4,12},{5,13},{6,14},{7,15},{8,0},{9,1},... | collective-permute-start | bytes 19208 | tf_op jit(solution)/shard_map/ppermute | solution.py:15
  188.1 3.2 %collective-permute-start.51 = (bf16[1,5,640]{2,0,1:T(2,128)(2,1)S(1)}, bf16[1,5,640]{2,0,1:T(2,128)(2,1)S(1)}, u32[]{:S(2)}, u32[]{:S(2)}) collective-permute-start(bf16[1,5,640]{2,0,1:T(2,128)(2,1)S(1)} %dynamic-slice_convert_fusion.14), channel_id=1, source_target_pairs={{0,8},{1,9},{2,10},{3,11},{4,12},{5,13},{6,14},{7,15},{8,0},{9,1},... | collective-permute-start | bytes 19208 | tf_op jit(solution)/shard_map/ppermute | solution.py:15
  193.1 2.7 %collective-permute-done.51 = bf16[1,5,640]{2,0,1:T(2,128)(2,1)S(1)} collective-permute-done((bf16[1,5,640]{2,0,1:T(2,128)(2,1)S(1)}, bf16[1,5,640]{2,0,1:T(2,128)(2,1)S(1)}, u32[]{:S(2)}, u32[]{:S(2)}) %collective-permute-start.51) | collective-permute-done | bytes 6432 | tf_op jit(solution)/shard_map/ppermute | solution.py:15
  (181 shorter events, 43.5 us)
Async XLA Ops:
  2.7 7.7 %collective-permute-start.2 = (f32[8,128]{1,0:T(8,128)S(1)}, f32[8,128]{1,0:T(8,128)S(1)}, u32[]{:S(2)}, u32[]{:S(2)}) collective-permute-start(f32[8,128]{1,0:T(8,128)S(1)} %broadcast_in_dim.12), channel_id=1, source_target_pairs={{0,3},{1,2},{2,1},{3,0},{4,7},{5,6},{6,5},{7,4},{8,11},{9,10},{10,... | collective-permute-start | bytes 12296 | tf_op jit(solution)/shard_map/ppermute | solution.py:15
  2.8 7.6 %collective-permute-start.1 = (f32[8,128]{1,0:T(8,128)S(1)}, f32[8,128]{1,0:T(8,128)S(1)}, u32[]{:S(2)}, u32[]{:S(2)}) collective-permute-start(f32[8,128]{1,0:T(8,128)S(1)} %broadcast_in_dim.12), channel_id=1, source_target_pairs={{0,2},{1,3},{2,0},{3,1},{4,6},{5,7},{6,4},{7,5},{8,10},{9,11},{10,... | collective-permute-start | bytes 12296 | tf_op jit(solution)/shard_map/ppermute | solution.py:15
  4.7 5.7 %collective-permute-start = (f32[8,128]{1,0:T(8,128)S(1)}, f32[8,128]{1,0:T(8,128)S(1)}, u32[]{:S(2)}, u32[]{:S(2)}) collective-permute-start(f32[8,128]{1,0:T(8,128)S(1)} %broadcast_in_dim.12), channel_id=1, source_target_pairs={{0,1},{1,0},{2,3},{3,2},{4,5},{5,4},{6,7},{7,6},{8,9},{9,8},{10,11... | collective-permute-start | bytes 12296 | tf_op jit(solution)/shard_map/ppermute | solution.py:15
  11.1 4.6 %collective-permute-start.5 = (f32[8,128]{1,0:T(8,128)S(1)}, f32[8,128]{1,0:T(8,128)S(1)}, u32[]{:S(2)}, u32[]{:S(2)}) collective-permute-start(f32[8,128]{1,0:T(8,128)S(1)} %add_add_fusion.5), channel_id=1, source_target_pairs={{0,80},{1,81},{2,82},{3,83},{4,84},{5,85},{6,86},{7,87},{8,88},{9,... | collective-permute-start | bytes 12296 | tf_op jit(solution)/shard_map/ppermute | solution.py:15
  17.7 7.0 %collective-permute-start.8 = (f32[8,128]{1,0:T(8,128)S(1)}, f32[8,128]{1,0:T(8,128)S(1)}, u32[]{:S(2)}, u32[]{:S(2)}) collective-permute-start(f32[8,128]{1,0:T(8,128)S(1)} %add_add_fusion.4), channel_id=1, source_target_pairs={{0,36},{1,37},{2,38},{3,39},{4,32},{5,33},{6,34},{7,35},{8,44},{9,... | collective-permute-start | bytes 12296 | tf_op jit(solution)/shard_map/ppermute | solution.py:15
  23.1 5.1 %collective-permute-start.7 = (f32[8,128]{1,0:T(8,128)S(1)}, f32[8,128]{1,0:T(8,128)S(1)}, u32[]{:S(2)}, u32[]{:S(2)}) collective-permute-start(f32[8,128]{1,0:T(8,128)S(1)} %add_add_fusion.4), channel_id=1, source_target_pairs={{0,32},{1,33},{2,34},{3,35},{4,36},{5,37},{6,38},{7,39},{8,40},{9,... | collective-permute-start | bytes 12296 | tf_op jit(solution)/shard_map/ppermute | solution.py:15
  23.9 4.5 %collective-permute-start.6 = (f32[8,128]{1,0:T(8,128)S(1)}, f32[8,128]{1,0:T(8,128)S(1)}, u32[]{:S(2)}, u32[]{:S(2)}) collective-permute-start(f32[8,128]{1,0:T(8,128)S(1)} %add_add_fusion.4), channel_id=1, source_target_pairs={{0,4},{1,5},{2,6},{3,7},{4,0},{5,1},{6,2},{7,3},{8,12},{9,13},{10,... | collective-permute-start | bytes 12296 | tf_op jit(solution)/shard_map/ppermute | solution.py:15
  28.4 20.5 %collective-permute-start.11 = (f32[8,128]{1,0:T(8,128)S(1)}, f32[8,128]{1,0:T(8,128)S(1)}, u32[]{:S(2)}, u32[]{:S(2)}) collective-permute-start(f32[8,128]{1,0:T(8,128)S(1)} %add_add_fusion.3), channel_id=1, source_target_pairs={{0,136},{1,137},{2,138},{3,139},{4,140},{5,141},{6,142},{7,143},{8... | collective-permute-start | bytes 12296 | tf_op jit(solution)/shard_map/ppermute | solution.py:15
  35.5 14.7 %collective-permute-start.10 = (f32[8,128]{1,0:T(8,128)S(1)}, f32[8,128]{1,0:T(8,128)S(1)}, u32[]{:S(2)}, u32[]{:S(2)}) collective-permute-start(f32[8,128]{1,0:T(8,128)S(1)} %add_add_fusion.3), channel_id=1, source_target_pairs={{0,8},{1,9},{2,10},{3,11},{4,12},{5,13},{6,14},{7,15},{8,0},{9,1},... | collective-permute-start | bytes 12296 | tf_op jit(solution)/shard_map/ppermute | solution.py:15
  37.0 14.6 %collective-permute-start.9 = (f32[8,128]{1,0:T(8,128)S(1)}, f32[8,128]{1,0:T(8,128)S(1)}, u32[]{:S(2)}, u32[]{:S(2)}) collective-permute-start(f32[8,128]{1,0:T(8,128)S(1)} %add_add_fusion.3), channel_id=1, source_target_pairs={{0,128},{1,129},{2,130},{3,131},{4,132},{5,133},{6,134},{7,135},{8... | collective-permute-start | bytes 12296 | tf_op jit(solution)/shard_map/ppermute | solution.py:15
  37.5 14.1 %collective-permute-start.12 = (bf16[128,640]{1,0:T(8,128)(2,1)S(1)}, bf16[128,640]{1,0:T(8,128)(2,1)S(1)}, u32[]{:S(2)}, u32[]{:S(2)}) collective-permute-start(bf16[128,640]{1,0:T(8,128)(2,1)S(1)} %multiply_convert_fusion.1), channel_id=1, source_target_pairs={{0,8},{1,9},{2,10},{3,11},{4,12},{5,13},{6,14},{7,15},{8,16},{9,17... | collective-permute-start | bytes 491528 | tf_op jit(solution)/shard_map/ppermute | solution.py:10
  43.9 10.2 %collective-permute-start.13 = (bf16[128,640]{1,0:T(8,128)(2,1)S(1)}, bf16[128,640]{1,0:T(8,128)(2,1)S(1)}, u32[]{:S(2)}, u32[]{:S(2)}) collective-permute-start(bf16[128,640]{1,0:T(8,128)(2,1)S(1)} %multiply_convert_fusion.1), channel_id=1, source_target_pairs={{0,4},{1,5},{2,6},{3,7},{4,8},{5,9},{6,10},{7,11},{8,12},{9,13},{1... | collective-permute-start | bytes 491528 | tf_op jit(solution)/shard_map/ppermute | solution.py:10
  49.0 10.1 %collective-permute-start.14 = (bf16[128,640]{1,0:T(8,128)(2,1)S(1)}, bf16[128,640]{1,0:T(8,128)(2,1)S(1)}, u32[]{:S(2)}, u32[]{:S(2)}) collective-permute-start(bf16[128,640]{1,0:T(8,128)(2,1)S(1)} %multiply_convert_fusion.1), channel_id=1, source_target_pairs={{4,0},{5,1},{6,2},{7,3},{8,4},{9,5},{10,6},{11,7},{12,8},{13,9},{1... | collective-permute-start | bytes 491528 | tf_op jit(solution)/shard_map/ppermute | solution.py:10
  50.3 16.2 %collective-permute-start.15 = (bf16[128,640]{1,0:T(8,128)(2,1)S(1)}, bf16[128,640]{1,0:T(8,128)(2,1)S(1)}, u32[]{:S(2)}, u32[]{:S(2)}) collective-permute-start(bf16[128,640]{1,0:T(8,128)(2,1)S(1)} %multiply_convert_fusion.1), channel_id=1, source_target_pairs={{8,0},{9,1},{10,2},{11,3},{12,4},{13,5},{14,6},{15,7},{16,8},{17,9... | collective-permute-start | bytes 491528 | tf_op jit(solution)/shard_map/ppermute | solution.py:10
  75.0 23.1 %collective-permute-start.24 = (bf16[128,640]{1,0:T(8,128)(2,1)}, bf16[128,640]{1,0:T(8,128)(2,1)}, u32[]{:S(2)}, u32[]{:S(2)}) collective-permute-start(bf16[128,640]{1,0:T(8,128)(2,1)} %add_convert_fusion.1), channel_id=1, source_target_pairs={{8,0},{9,1},{10,2},{11,3},{12,4},{13,5},{14,6},{15,7},{16,8},{17,9... | collective-permute-start | bytes 491528 | tf_op jit(solution)/shard_map/ppermute | solution.py:10
  76.5 22.7 %collective-permute-start.25 = (bf16[128,640]{1,0:T(8,128)(2,1)}, bf16[128,640]{1,0:T(8,128)(2,1)}, u32[]{:S(2)}, u32[]{:S(2)}) collective-permute-start(bf16[128,640]{1,0:T(8,128)(2,1)} %add_convert_fusion.1), channel_id=1, source_target_pairs={{4,0},{5,1},{6,2},{7,3},{8,4},{9,5},{10,6},{11,7},{12,8},{13,9},{1... | collective-permute-start | bytes 491528 | tf_op jit(solution)/shard_map/ppermute | solution.py:10
  77.8 22.5 %collective-permute-start.26 = (bf16[128,640]{1,0:T(8,128)(2,1)}, bf16[128,640]{1,0:T(8,128)(2,1)}, u32[]{:S(2)}, u32[]{:S(2)}) collective-permute-start(bf16[128,640]{1,0:T(8,128)(2,1)} %add_convert_fusion.1), channel_id=1, source_target_pairs={{0,4},{1,5},{2,6},{3,7},{4,8},{5,9},{6,10},{7,11},{8,12},{9,13},{1... | collective-permute-start | bytes 491528 | tf_op jit(solution)/shard_map/ppermute | solution.py:10
  83.9 17.4 %collective-permute-start.27 = (bf16[128,640]{1,0:T(8,128)(2,1)}, bf16[128,640]{1,0:T(8,128)(2,1)}, u32[]{:S(2)}, u32[]{:S(2)}) collective-permute-start(bf16[128,640]{1,0:T(8,128)(2,1)} %add_convert_fusion.1), channel_id=1, source_target_pairs={{0,8},{1,9},{2,10},{3,11},{4,12},{5,13},{6,14},{7,15},{8,16},{9,17... | collective-permute-start | bytes 491528 | tf_op jit(solution)/shard_map/ppermute | solution.py:10
  96.5 9.1 %collective-permute-start.41 = (bf16[64,5,640]{2,0,1:T(8,128)(2,1)S(1)}, bf16[64,5,640]{2,0,1:T(8,128)(2,1)S(1)}, u32[]{:S(2)}, u32[]{:S(2)}) collective-permute-start(bf16[64,5,640]{2,0,1:T(8,128)(2,1)S(1)} %get-tuple-element.14), channel_id=1, source_target_pairs={{0,1},{1,0},{2,3},{3,2},{4,5},{5,4},{6,7},{7,6},{8,9},{9,8},{10,11... | collective-permute-start | bytes 1228808 | tf_op jit(solution)/shard_map/ppermute | solution.py:15
  98.2 7.4 %collective-permute-start.40 = (bf16[64,5,640]{2,0,1:T(8,128)(2,1)S(1)}, bf16[64,5,640]{2,0,1:T(8,128)(2,1)S(1)}, u32[]{:S(2)}, u32[]{:S(2)}) collective-permute-start(bf16[64,5,640]{2,0,1:T(8,128)(2,1)S(1)} %get-tuple-element.13), channel_id=1, source_target_pairs={{0,1},{1,0},{2,3},{3,2},{4,5},{5,4},{6,7},{7,6},{8,9},{9,8},{10,11... | collective-permute-start | bytes 1228808 | tf_op jit(solution)/shard_map/ppermute | solution.py:15
  99.2 13.6 %collective-permute-start.17 = (f32[8,128]{1,0:T(8,128)S(1)}, f32[8,128]{1,0:T(8,128)S(1)}, u32[]{:S(2)}, u32[]{:S(2)}) collective-permute-start(f32[8,128]{1,0:T(8,128)S(1)} %broadcast_add_fusion), channel_id=1, source_target_pairs={{0,2},{1,3},{2,0},{3,1},{4,6},{5,7},{6,4},{7,5},{8,10},{9,11},{10,... | collective-permute-start | bytes 12296 | tf_op jit(solution)/shard_map/ppermute | solution.py:15
  104.9 3.7 %collective-permute-start.29 = (bf16[64,5,640]{2,0,1:T(8,128)(2,1)S(1)}, bf16[64,5,640]{2,0,1:T(8,128)(2,1)S(1)}, u32[]{:S(2)}, u32[]{:S(2)}) collective-permute-start(bf16[64,5,640]{2,0,1:T(8,128)(2,1)S(1)} %get-tuple-element.16), channel_id=1, source_target_pairs={{0,1},{1,0},{2,3},{3,2},{4,5},{5,4},{6,7},{7,6},{8,9},{9,8},{10,11... | collective-permute-start | bytes 1228808 | tf_op jit(solution)/shard_map/ppermute | solution.py:15
  106.5 48.4 %collective-permute-start.43 = (bf16[32,5,640]{2,0,1:T(8,128)(2,1)}, bf16[32,5,640]{2,0,1:T(8,128)(2,1)}, u32[]{:S(2)}, u32[]{:S(2)}) collective-permute-start(bf16[32,5,640]{2,0,1:T(8,128)(2,1)} %get-tuple-element.18), channel_id=1, source_target_pairs={{0,2},{1,3},{2,0},{3,1},{4,6},{5,7},{6,4},{7,5},{8,10},{9,11},{10,... | collective-permute-start | bytes 614408 | tf_op jit(solution)/shard_map/ppermute | solution.py:15
  108.5 46.4 %collective-permute-start.42 = (bf16[32,5,640]{2,0,1:T(8,128)(2,1)S(1)}, bf16[32,5,640]{2,0,1:T(8,128)(2,1)}, u32[]{:S(2)}, u32[]{:S(2)}) collective-permute-start(bf16[32,5,640]{2,0,1:T(8,128)(2,1)S(1)} %get-tuple-element.17), channel_id=1, source_target_pairs={{0,2},{1,3},{2,0},{3,1},{4,6},{5,7},{6,4},{7,5},{8,10},{9,11},{10,... | collective-permute-start | bytes 614408 | tf_op jit(solution)/shard_map/ppermute | solution.py:15
  110.8 44.1 %collective-permute-start.31 = (bf16[32,5,640]{2,0,1:T(8,128)(2,1)}, bf16[32,5,640]{2,0,1:T(8,128)(2,1)}, u32[]{:S(2)}, u32[]{:S(2)}) collective-permute-start(bf16[32,5,640]{2,0,1:T(8,128)(2,1)} %get-tuple-element.20), channel_id=1, source_target_pairs={{0,2},{1,3},{2,0},{3,1},{4,6},{5,7},{6,4},{7,5},{8,10},{9,11},{10,... | collective-permute-start | bytes 614408 | tf_op jit(solution)/shard_map/ppermute | solution.py:15
  112.7 42.2 %collective-permute-start.30 = (bf16[32,5,640]{2,0,1:T(8,128)(2,1)}, bf16[32,5,640]{2,0,1:T(8,128)(2,1)}, u32[]{:S(2)}, u32[]{:S(2)}) collective-permute-start(bf16[32,5,640]{2,0,1:T(8,128)(2,1)} %get-tuple-element.19), channel_id=1, source_target_pairs={{0,2},{1,3},{2,0},{3,1},{4,6},{5,7},{6,4},{7,5},{8,10},{9,11},{10,... | collective-permute-start | bytes 614408 | tf_op jit(solution)/shard_map/ppermute | solution.py:15
  113.5 4.5 %collective-permute-start.18 = (f32[8,128]{1,0:T(8,128)S(1)}, f32[8,128]{1,0:T(8,128)S(1)}, u32[]{:S(2)}, u32[]{:S(2)}) collective-permute-start(f32[8,128]{1,0:T(8,128)S(1)} %fusion.66), channel_id=1, source_target_pairs={{0,16},{1,17},{2,18},{3,19},{4,20},{5,21},{6,22},{7,23},{8,24},{9,... | collective-permute-start | bytes 12296 | tf_op jit(solution)/shard_map/ppermute | solution.py:15
  118.0 9.3 %collective-permute-start.19 = (f32[8,128]{1,0:T(8,128)S(1)}, f32[8,128]{1,0:T(8,128)S(1)}, u32[]{:S(2)}, u32[]{:S(2)}) collective-permute-start(f32[8,128]{1,0:T(8,128)S(1)} %add.294), channel_id=1, source_target_pairs={{0,64},{1,65},{2,66},{3,67},{4,68},{5,69},{6,70},{7,71},{8,72},{9,... | collective-permute-start | bytes 12296 | tf_op jit(solution)/shard_map/ppermute | solution.py:15
  127.3 4.5 %collective-permute-start.20 = (f32[8,128]{1,0:T(8,128)S(1)}, f32[8,128]{1,0:T(8,128)S(1)}, u32[]{:S(2)}, u32[]{:S(2)}) collective-permute-start(f32[8,128]{1,0:T(8,128)S(1)} %add.295), channel_id=1, source_target_pairs={{0,4},{1,5},{2,6},{3,7},{4,0},{5,1},{6,2},{7,3},{8,12},{9,13},{10,... | collective-permute-start | bytes 12296 | tf_op jit(solution)/shard_map/ppermute | solution.py:15
  131.8 5.1 %collective-permute-start.21 = (f32[8,128]{1,0:T(8,128)S(1)}, f32[8,128]{1,0:T(8,128)S(1)}, u32[]{:S(2)}, u32[]{:S(2)}) collective-permute-start(f32[8,128]{1,0:T(8,128)S(1)} %add.296), channel_id=1, source_target_pairs={{0,32},{1,33},{2,34},{3,35},{4,36},{5,37},{6,38},{7,39},{8,40},{9,... | collective-permute-start | bytes 12296 | tf_op jit(solution)/shard_map/ppermute | solution.py:15
  136.9 8.6 %collective-permute-start.22 = (f32[8,128]{1,0:T(8,128)S(1)}, f32[8,128]{1,0:T(8,128)S(1)}, u32[]{:S(2)}, u32[]{:S(2)}) collective-permute-start(f32[8,128]{1,0:T(8,128)S(1)} %add.297), channel_id=1, source_target_pairs={{0,128},{1,129},{2,130},{3,131},{4,132},{5,133},{6,134},{7,135},{8... | collective-permute-start | bytes 12296 | tf_op jit(solution)/shard_map/ppermute | solution.py:15
  145.5 7.5 %collective-permute-start.23 = (f32[8,128]{1,0:T(8,128)S(1)}, f32[8,128]{1,0:T(8,128)S(1)}, u32[]{:S(2)}, u32[]{:S(2)}) collective-permute-start(f32[8,128]{1,0:T(8,128)S(1)} %add.298), channel_id=1, source_target_pairs={{0,8},{1,9},{2,10},{3,11},{4,12},{5,13},{6,14},{7,15},{8,0},{9,1},... | collective-permute-start | bytes 12296 | tf_op jit(solution)/shard_map/ppermute | solution.py:15
  156.7 4.7 %collective-permute-start.33 = (bf16[16,5,640]{2,0,1:T(8,128)(2,1)S(1)}, bf16[16,5,640]{2,0,1:T(8,128)(2,1)S(1)}, u32[]{:S(2)}, u32[]{:S(2)}) collective-permute-start(bf16[16,5,640]{2,0,1:T(8,128)(2,1)S(1)} %get-tuple-element.24), channel_id=1, source_target_pairs={{0,16},{1,17},{2,18},{3,19},{4,20},{5,21},{6,22},{7,23},{8,24},{9,... | collective-permute-start | bytes 307208 | tf_op jit(solution)/shard_map/ppermute | solution.py:15
  156.8 5.7 %collective-permute-start.32 = (bf16[16,5,640]{2,0,1:T(8,128)(2,1)S(1)}, bf16[16,5,640]{2,0,1:T(8,128)(2,1)S(1)}, u32[]{:S(2)}, u32[]{:S(2)}) collective-permute-start(bf16[16,5,640]{2,0,1:T(8,128)(2,1)S(1)} %get-tuple-element.23), channel_id=1, source_target_pairs={{0,16},{1,17},{2,18},{3,19},{4,20},{5,21},{6,22},{7,23},{8,24},{9,... | collective-permute-start | bytes 307208 | tf_op jit(solution)/shard_map/ppermute | solution.py:15
  158.9 5.9 %collective-permute-start.45 = (bf16[16,5,640]{2,0,1:T(8,128)(2,1)S(1)}, bf16[16,5,640]{2,0,1:T(8,128)(2,1)S(1)}, u32[]{:S(2)}, u32[]{:S(2)}) collective-permute-start(bf16[16,5,640]{2,0,1:T(8,128)(2,1)S(1)} %get-tuple-element.22), channel_id=1, source_target_pairs={{0,16},{1,17},{2,18},{3,19},{4,20},{5,21},{6,22},{7,23},{8,24},{9,... | collective-permute-start | bytes 307208 | tf_op jit(solution)/shard_map/ppermute | solution.py:15
  159.0 5.7 %collective-permute-start.44 = (bf16[16,5,640]{2,0,1:T(8,128)(2,1)S(1)}, bf16[16,5,640]{2,0,1:T(8,128)(2,1)S(1)}, u32[]{:S(2)}, u32[]{:S(2)}) collective-permute-start(bf16[16,5,640]{2,0,1:T(8,128)(2,1)S(1)} %get-tuple-element.21), channel_id=1, source_target_pairs={{0,16},{1,17},{2,18},{3,19},{4,20},{5,21},{6,22},{7,23},{8,24},{9,... | collective-permute-start | bytes 307208 | tf_op jit(solution)/shard_map/ppermute | solution.py:15
  162.6 4.3 %collective-permute-start.35 = (bf16[8,5,640]{2,0,1:T(8,128)(2,1)S(1)}, bf16[8,5,640]{2,0,1:T(8,128)(2,1)S(1)}, u32[]{:S(2)}, u32[]{:S(2)}) collective-permute-start(bf16[8,5,640]{2,0,1:T(8,128)(2,1)S(1)} %get-tuple-element.28), channel_id=1, source_target_pairs={{0,64},{1,65},{2,66},{3,67},{4,68},{5,69},{6,70},{7,71},{8,72},{9,... | collective-permute-start | bytes 153608 | tf_op jit(solution)/shard_map/ppermute | solution.py:15
  164.6 4.1 %collective-permute-start.34 = (bf16[8,5,640]{2,0,1:T(8,128)(2,1)S(1)}, bf16[8,5,640]{2,0,1:T(8,128)(2,1)S(1)}, u32[]{:S(2)}, u32[]{:S(2)}) collective-permute-start(bf16[8,5,640]{2,0,1:T(8,128)(2,1)S(1)} %get-tuple-element.27), channel_id=1, source_target_pairs={{0,64},{1,65},{2,66},{3,67},{4,68},{5,69},{6,70},{7,71},{8,72},{9,... | collective-permute-start | bytes 153608 | tf_op jit(solution)/shard_map/ppermute | solution.py:15
  164.8 4.4 %collective-permute-start.47 = (bf16[8,5,640]{2,0,1:T(8,128)(2,1)S(1)}, bf16[8,5,640]{2,0,1:T(8,128)(2,1)S(1)}, u32[]{:S(2)}, u32[]{:S(2)}) collective-permute-start(bf16[8,5,640]{2,0,1:T(8,128)(2,1)S(1)} %get-tuple-element.26), channel_id=1, source_target_pairs={{0,64},{1,65},{2,66},{3,67},{4,68},{5,69},{6,70},{7,71},{8,72},{9,... | collective-permute-start | bytes 153608 | tf_op jit(solution)/shard_map/ppermute | solution.py:15
  166.8 4.1 %collective-permute-start.46 = (bf16[8,5,640]{2,0,1:T(8,128)(2,1)S(1)}, bf16[8,5,640]{2,0,1:T(8,128)(2,1)S(1)}, u32[]{:S(2)}, u32[]{:S(2)}) collective-permute-start(bf16[8,5,640]{2,0,1:T(8,128)(2,1)S(1)} %get-tuple-element.25), channel_id=1, source_target_pairs={{0,64},{1,65},{2,66},{3,67},{4,68},{5,69},{6,70},{7,71},{8,72},{9,... | collective-permute-start | bytes 153608 | tf_op jit(solution)/shard_map/ppermute | solution.py:15
  168.8 5.2 %collective-permute-start.36 = (bf16[8,5,640]{2,0,1:T(8,128)(2,1)S(1)}, bf16[8,5,640]{2,0,1:T(8,128)(2,1)S(1)}, u32[]{:S(2)}, u32[]{:S(2)}) collective-permute-start(bf16[8,5,640]{2,0,1:T(8,128)(2,1)S(1)} %dynamic-slice_convert_fusion.9), channel_id=1, source_target_pairs={{0,4},{1,5},{2,6},{3,7},{4,0},{5,1},{6,2},{7,3},{8,12},{9,13},{10,... | collective-permute-start | bytes 153608 | tf_op jit(solution)/shard_map/ppermute | solution.py:15
  171.0 5.1 %collective-permute-start.48 = (bf16[8,5,640]{2,0,1:T(8,128)(2,1)S(1)}, bf16[8,5,640]{2,0,1:T(8,128)(2,1)S(1)}, u32[]{:S(2)}, u32[]{:S(2)}) collective-permute-start(bf16[8,5,640]{2,0,1:T(8,128)(2,1)S(1)} %dynamic-slice_convert_fusion.8), channel_id=1, source_target_pairs={{0,4},{1,5},{2,6},{3,7},{4,0},{5,1},{6,2},{7,3},{8,12},{9,13},{10,... | collective-permute-start | bytes 153608 | tf_op jit(solution)/shard_map/ppermute | solution.py:15
  174.0 5.4 %collective-permute-start.37 = (bf16[4,5,640]{2,0,1:T(4,128)(2,1)S(1)}, bf16[4,5,640]{2,0,1:T(4,128)(2,1)S(1)}, u32[]{:S(2)}, u32[]{:S(2)}) collective-permute-start(bf16[4,5,640]{2,0,1:T(4,128)(2,1)S(1)} %dynamic-slice_convert_fusion.11), channel_id=1, source_target_pairs={{0,32},{1,33},{2,34},{3,35},{4,36},{5,37},{6,38},{7,39},{8,40},{9,... | collective-permute-start | bytes 76808 | tf_op jit(solution)/shard_map/ppermute | solution.py:15
  176.1 6.3 %collective-permute-start.49 = (bf16[4,5,640]{2,0,1:T(4,128)(2,1)S(1)}, bf16[4,5,640]{2,0,1:T(4,128)(2,1)S(1)}, u32[]{:S(2)}, u32[]{:S(2)}) collective-permute-start(bf16[4,5,640]{2,0,1:T(4,128)(2,1)S(1)} %dynamic-slice_convert_fusion.10), channel_id=1, source_target_pairs={{0,32},{1,33},{2,34},{3,35},{4,36},{5,37},{6,38},{7,39},{8,40},{9,... | collective-permute-start | bytes 76808 | tf_op jit(solution)/shard_map/ppermute | solution.py:15
  179.5 5.3 %collective-permute-start.38 = (bf16[2,5,640]{2,0,1:T(2,128)(2,1)S(1)}, bf16[2,5,640]{2,0,1:T(2,128)(2,1)S(1)}, u32[]{:S(2)}, u32[]{:S(2)}) collective-permute-start(bf16[2,5,640]{2,0,1:T(2,128)(2,1)S(1)} %dynamic-slice_convert_fusion.13), channel_id=1, source_target_pairs={{0,128},{1,129},{2,130},{3,131},{4,132},{5,133},{6,134},{7,135},{8... | collective-permute-start | bytes 38408 | tf_op jit(solution)/shard_map/ppermute | solution.py:15
  182.5 5.5 %collective-permute-start.50 = (bf16[2,5,640]{2,0,1:T(2,128)(2,1)S(1)}, bf16[2,5,640]{2,0,1:T(2,128)(2,1)S(1)}, u32[]{:S(2)}, u32[]{:S(2)}) collective-permute-start(bf16[2,5,640]{2,0,1:T(2,128)(2,1)S(1)} %dynamic-slice_convert_fusion.12), channel_id=1, source_target_pairs={{0,128},{1,129},{2,130},{3,131},{4,132},{5,133},{6,134},{7,135},{8... | collective-permute-start | bytes 38408 | tf_op jit(solution)/shard_map/ppermute | solution.py:15
  184.8 7.7 %collective-permute-start.39 = (bf16[1,5,640]{2,0,1:T(2,128)(2,1)S(1)}, bf16[1,5,640]{2,0,1:T(2,128)(2,1)S(1)}, u32[]{:S(2)}, u32[]{:S(2)}) collective-permute-start(bf16[1,5,640]{2,0,1:T(2,128)(2,1)S(1)} %dynamic-slice_convert_fusion.15), channel_id=1, source_target_pairs={{0,8},{1,9},{2,10},{3,11},{4,12},{5,13},{6,14},{7,15},{8,0},{9,1},... | collective-permute-start | bytes 19208 | tf_op jit(solution)/shard_map/ppermute | solution.py:15
  188.1 7.7 %collective-permute-start.51 = (bf16[1,5,640]{2,0,1:T(2,128)(2,1)S(1)}, bf16[1,5,640]{2,0,1:T(2,128)(2,1)S(1)}, u32[]{:S(2)}, u32[]{:S(2)}) collective-permute-start(bf16[1,5,640]{2,0,1:T(2,128)(2,1)S(1)} %dynamic-slice_convert_fusion.14), channel_id=1, source_target_pairs={{0,8},{1,9},{2,10},{3,11},{4,12},{5,13},{6,14},{7,15},{8,0},{9,1},... | collective-permute-start | bytes 19208 | tf_op jit(solution)/shard_map/ppermute | solution.py:15
  (13 other events, 146.0 us)

commit v12 on v11

--- a/solution.py
+++ b/solution.py
@@ -93,7 +93,7 @@
     context_rows = float(local_rows * seq_devices)
     masked = mask_flags.astype(jnp.float32)
     local_count = jnp.sum(masked)
-    count_tile = count_sum(jnp.broadcast_to(local_count, (8, 128)), "seq")
+    count_tile = tree_sum(jnp.broadcast_to(local_count, (8, 128)), "seq")
     alphabet = jnp.arange(vocab_size, dtype=jnp.int32)
     first_act = norm_gelu(hidden_in.astype(jnp.float32)).astype(jnp.bfloat16)
     first_pre = jnp.dot(first_act, w_in, preferred_element_type=jnp.float32)

time: 198 us -> 198 us (level)
  starting transfers between devices: 99.6 us -> 97 us
    ppermute x44 -> x40, starting transfers between devices: 69.9 us -> 64.4 us  [swap_with(): return lax.ppermute(block, axis, [(i, i ^ bit) for i in range(devices)])]
    ppermute x8, waiting for transfers between devices: 14.5 us -> 11.3 us  [from_behind(): return lax.ppermute(block, axis, route)]
    ppermute x8, starting transfers between devices: 29.7 us -> 32.6 us  [from_behind(): return lax.ppermute(block, axis, route)]
    ppermute x44 -> x40, waiting for transfers between devices: 41 us -> 43.9 us  [swap_with(): return lax.ppermute(block, axis, [(i, i ^ bit) for i in range(devices)])]
  transfers between devices with their start and end apart: 52 -> 48, of which waited for: 26 -> 22; matrix products, arithmetic and copies ran while one was open for 12% -> 13% of each run, Pallas kernels for 0% -> 0%
where the time goes in v12:
time: 198 us; the launch traced here: 197 us
  starting transfers between devices  97 us (49%)
  waiting for transfers between devices  55.2 us (28%)
  local copies, waits for them, and re-layouts  15.9 us (8%)
  other arithmetic  14.1 us (7%)
  matrix products  9.84 us (5%)
  between operations  4.63 us (2%)
    ppermute x40, starting transfers between devices, swap_with(): return lax.ppermute(block, axis, [(i, i ^ bit) for i in range(devices)])  64.4 us
    ppermute x40, waiting for transfers between devices, swap_with(): return lax.ppermute(block, axis, [(i, i ^ bit) for i in range(devices)])  43.9 us
    ppermute x8, starting transfers between devices, from_behind(): return lax.ppermute(block, axis, route)  32.6 us
    ppermute x8, waiting for transfers between devices, from_behind(): return lax.ppermute(block, axis, route)  11.3 us
    unnamed x26, local copies, waits for them, and re-layouts  6.22 us
  transfers between devices with their start and end apart: 48, of which 22 were waited for; matrix products, arithmetic and copies ran while one was open for 13% of the time, Pallas kernels for 0%

profile of v12, /device:TPU:32, one launch (start us, length us, event | category | flops | bytes accessed | tf_op | source)
XLA Modules:
  0.0 196.7 jit_solution(3004945034182702094)
XLA Ops:
  0.6 1.4 convert_reduce_fusion.1
  5.1 1.4 fusion.9
  6.5 1.9 fusion.53
  9.3 1.9 collective-permute-start.1
  12.1 7.4 %collective-permute-start.8 = (bf16[128,640]{1,0:T(8,128)(2,1)}, bf16[128,640]{1,0:T(8,128)(2,1)S(1)}, u32[]{:S(2)}, u32[]{:S(2)}) collective-permute-start(bf16[128,640]{1,0:T(8,128)(2,1)} %multiply_convert_fusion.1), channel_id=1, source_target_pairs={{0,8},{1,9},{2,10},{3,11},{4,12},{5,13},{6,14},{7,15},{8,16},{9,17... | collective-permute-start | bytes 491528 | tf_op jit(solution)/shard_map/ppermute | solution.py:10
  20.2 1.6 collective-permute-start.2
  21.8 2.1 %collective-permute-done.2 = f32[8,128]{1,0:T(8,128)S(1)} collective-permute-done((f32[8,128]{1,0:T(8,128)S(1)}, f32[8,128]{1,0:T(8,128)S(1)}, u32[]{:S(2)}, u32[]{:S(2)}) %collective-permute-start.2) | collective-permute-done | bytes 4128 | tf_op jit(solution)/shard_map/ppermute | solution.py:15
  23.9 1.6 collective-permute-start.3
  25.4 2.0 %collective-permute-done.3 = f32[8,128]{1,0:T(8,128)S(1)} collective-permute-done((f32[8,128]{1,0:T(8,128)S(1)}, f32[8,128]{1,0:T(8,128)S(1)}, u32[]{:S(2)}, u32[]{:S(2)}) %collective-permute-start.3) | collective-permute-done | bytes 4128 | tf_op jit(solution)/shard_map/ppermute | solution.py:15
  27.5 1.5 collective-permute-start.4
  29.0 3.0 %collective-permute-done.4 = f32[8,128]{1,0:T(8,128)S(1)} collective-permute-done((f32[8,128]{1,0:T(8,128)S(1)}, f32[8,128]{1,0:T(8,128)S(1)}, u32[]{:S(2)}, u32[]{:S(2)}) %collective-permute-start.4) | collective-permute-done | bytes 4128 | tf_op jit(solution)/shard_map/ppermute | solution.py:15
  32.0 3.0 %collective-permute-start.5 = (f32[8,128]{1,0:T(8,128)S(1)}, f32[8,128]{1,0:T(8,128)S(1)}, u32[]{:S(2)}, u32[]{:S(2)}) collective-permute-start(f32[8,128]{1,0:T(8,128)S(1)} %add.261), channel_id=1, source_target_pairs={{0,32},{1,33},{2,34},{3,35},{4,36},{5,37},{6,38},{7,39},{8,40},{9,... | collective-permute-start | bytes 12296 | tf_op jit(solution)/shard_map/ppermute | solution.py:15
  35.0 2.1 %collective-permute-done.5 = f32[8,128]{1,0:T(8,128)S(1)} collective-permute-done((f32[8,128]{1,0:T(8,128)S(1)}, f32[8,128]{1,0:T(8,128)S(1)}, u32[]{:S(2)}, u32[]{:S(2)}) %collective-permute-start.5) | collective-permute-done | bytes 4128 | tf_op jit(solution)/shard_map/ppermute | solution.py:15
  37.1 3.2 %collective-permute-start.6 = (f32[8,128]{1,0:T(8,128)S(1)}, f32[8,128]{1,0:T(8,128)S(1)}, u32[]{:S(2)}, u32[]{:S(2)}) collective-permute-start(f32[8,128]{1,0:T(8,128)S(1)} %add.262), channel_id=1, source_target_pairs={{0,128},{1,129},{2,130},{3,131},{4,132},{5,133},{6,134},{7,135},{8... | collective-permute-start | bytes 12296 | tf_op jit(solution)/shard_map/ppermute | solution.py:15
  40.3 1.9 collective-permute-done.6
  42.6 5.5 %collective-permute-start.9 = (bf16[128,640]{1,0:T(8,128)(2,1)}, bf16[128,640]{1,0:T(8,128)(2,1)}, u32[]{:S(2)}, u32[]{:S(2)}) collective-permute-start(bf16[128,640]{1,0:T(8,128)(2,1)} %multiply_convert_fusion.1), channel_id=1, source_target_pairs={{0,4},{1,5},{2,6},{3,7},{4,8},{5,9},{6,10},{7,11},{8,12},{9,13},{1... | collective-permute-start | bytes 491528 | tf_op jit(solution)/shard_map/ppermute | solution.py:10
  53.6 3.4 %collective-permute-done.10 = bf16[128,640]{1,0:T(8,128)(2,1)S(1)} collective-permute-done((bf16[128,640]{1,0:T(8,128)(2,1)}, bf16[128,640]{1,0:T(8,128)(2,1)S(1)}, u32[]{:S(2)}, u32[]{:S(2)}) %collective-permute-start.10) | collective-permute-done | bytes 163872 | tf_op jit(solution)/shard_map/ppermute | solution.py:10
  57.0 7.9 %collective-permute-done.11 = bf16[128,640]{1,0:T(8,128)(2,1)S(1)} collective-permute-done((bf16[128,640]{1,0:T(8,128)(2,1)}, bf16[128,640]{1,0:T(8,128)(2,1)S(1)}, u32[]{:S(2)}, u32[]{:S(2)}) %collective-permute-start.11) | collective-permute-done | bytes 163872 | tf_op jit(solution)/shard_map/ppermute | solution.py:10
  65.0 3.1 %fusion.54 = (f32[128]{0:T(128)S(1)}, f32[128,640]{1,0:T(8,128)S(1)}) fusion(bf16[5,128,640]{2,1,0:T(8,128)(2,1)S(1)} %bitcast_dynamic-update-slice_fusion.5, bf16[5,640,640]{2,1,0:T(8,128)(2,1)} %param.13), kind=kOutput, calls=%fused_computation.136 | convolution fusion | flops 524369792 | bytes 5243392 | tf_op jit(solution)/shard_map/krc,kcb->rb/dot_general | solution.py:104
  76.1 6.1 %collective-permute-start.22 = (bf16[128,640]{1,0:T(8,128)(2,1)}, bf16[128,640]{1,0:T(8,128)(2,1)}, u32[]{:S(2)}, u32[]{:S(2)}) collective-permute-start(bf16[128,640]{1,0:T(8,128)(2,1)} %add_convert_fusion.1), channel_id=1, source_target_pairs={{0,4},{1,5},{2,6},{3,7},{4,8},{5,9},{6,10},{7,11},{8,12},{9,13},{1... | collective-permute-start | bytes 491528 | tf_op jit(solution)/shard_map/ppermute | solution.py:10
  82.2 8.5 %collective-permute-start.23 = (bf16[128,640]{1,0:T(8,128)(2,1)}, bf16[128,640]{1,0:T(8,128)(2,1)}, u32[]{:S(2)}, u32[]{:S(2)}) collective-permute-start(bf16[128,640]{1,0:T(8,128)(2,1)} %add_convert_fusion.1), channel_id=1, source_target_pairs={{0,8},{1,9},{2,10},{3,11},{4,12},{5,13},{6,14},{7,15},{8,16},{9,17... | collective-permute-start | bytes 491528 | tf_op jit(solution)/shard_map/ppermute | solution.py:10
  100.8 1.5 multiply_reduce_fusion
  105.0 1.9 collective-permute-start.39
  109.2 1.9 collective-permute-start.27
  111.9 3.6 %collective-permute-start.14 = (f32[8,128]{1,0:T(8,128)S(1)}, f32[8,128]{1,0:T(8,128)S(1)}, u32[]{:S(2)}, u32[]{:S(2)}) collective-permute-start(f32[8,128]{1,0:T(8,128)S(1)} %fusion.66), channel_id=1, source_target_pairs={{0,16},{1,17},{2,18},{3,19},{4,20},{5,21},{6,22},{7,23},{8,24},{9,... | collective-permute-start | bytes 12296 | tf_op jit(solution)/shard_map/ppermute | solution.py:15
  115.5 1.6 collective-permute-done.14
  117.1 8.0 %collective-permute-start.15 = (f32[8,128]{1,0:T(8,128)S(1)}, f32[8,128]{1,0:T(8,128)S(1)}, u32[]{:S(2)}, u32[]{:S(2)}) collective-permute-start(f32[8,128]{1,0:T(8,128)S(1)} %add.278), channel_id=1, source_target_pairs={{0,64},{1,65},{2,66},{3,67},{4,68},{5,69},{6,70},{7,71},{8,72},{9,... | collective-permute-start | bytes 12296 | tf_op jit(solution)/shard_map/ppermute | solution.py:15
  125.1 1.6 collective-permute-done.15
  126.9 4.3 %collective-permute-done.16 = f32[8,128]{1,0:T(8,128)S(1)} collective-permute-done((f32[8,128]{1,0:T(8,128)S(1)}, f32[8,128]{1,0:T(8,128)S(1)}, u32[]{:S(2)}, u32[]{:S(2)}) %collective-permute-start.16) | collective-permute-done | bytes 4128 | tf_op jit(solution)/shard_map/ppermute | solution.py:15
  131.6 4.7 %collective-permute-done.17 = f32[8,128]{1,0:T(8,128)S(1)} collective-permute-done((f32[8,128]{1,0:T(8,128)S(1)}, f32[8,128]{1,0:T(8,128)S(1)}, u32[]{:S(2)}, u32[]{:S(2)}) %collective-permute-start.17) | collective-permute-done | bytes 4128 | tf_op jit(solution)/shard_map/ppermute | solution.py:15
  136.3 5.9 %collective-permute-start.18 = (f32[8,128]{1,0:T(8,128)S(1)}, f32[8,128]{1,0:T(8,128)S(1)}, u32[]{:S(2)}, u32[]{:S(2)}) collective-permute-start(f32[8,128]{1,0:T(8,128)S(1)} %add.281), channel_id=1, source_target_pairs={{0,128},{1,129},{2,130},{3,131},{4,132},{5,133},{6,134},{7,135},{8... | collective-permute-start | bytes 12296 | tf_op jit(solution)/shard_map/ppermute | solution.py:15
  142.1 1.6 collective-permute-done.18
  144.1 7.1 %collective-permute-done.19 = f32[8,128]{1,0:T(8,128)S(1)} collective-permute-done((f32[8,128]{1,0:T(8,128)S(1)}, f32[8,128]{1,0:T(8,128)S(1)}, u32[]{:S(2)}, u32[]{:S(2)}) %collective-permute-start.19) | collective-permute-done | bytes 4128 | tf_op jit(solution)/shard_map/ppermute | solution.py:15
  153.1 1.7 convert_add_fusion.2
  155.0 2.0 %collective-permute-start.28 = (bf16[16,5,640]{2,0,1:T(8,128)(2,1)S(1)}, bf16[16,5,640]{2,0,1:T(8,128)(2,1)S(1)}, u32[]{:S(2)}, u32[]{:S(2)}) collective-permute-start(bf16[16,5,640]{2,0,1:T(8,128)(2,1)S(1)} %get-tuple-element.23), channel_id=1, source_target_pairs={{0,16},{1,17},{2,18},{3,19},{4,20},{5,21},{6,22},{7,23},{8,24},{9,... | collective-permute-start | bytes 307208 | tf_op jit(solution)/shard_map/ppermute | solution.py:15
  157.3 1.9 collective-permute-start.40
  160.8 1.8 collective-permute-start.31
  163.1 1.8 collective-permute-start.43
  165.2 1.6 collective-permute-done.30
  167.3 1.7 collective-permute-done.42
  170.0 1.9 collective-permute-done.32
  171.9 2.5 %collective-permute-start.33 = (bf16[4,5,640]{2,0,1:T(4,128)(2,1)S(1)}, bf16[4,5,640]{2,0,1:T(4,128)(2,1)S(1)}, u32[]{:S(2)}, u32[]{:S(2)}) collective-permute-start(bf16[4,5,640]{2,0,1:T(4,128)(2,1)S(1)} %dynamic-slice_convert_fusion.11), channel_id=1, source_target_pairs={{0,32},{1,33},{2,34},{3,35},{4,36},{5,37},{6,38},{7,39},{8,40},{9,... | collective-permute-start | bytes 76808 | tf_op jit(solution)/shard_map/ppermute | solution.py:15
  174.5 2.2 %collective-permute-start.45 = (bf16[4,5,640]{2,0,1:T(4,128)(2,1)S(1)}, bf16[4,5,640]{2,0,1:T(4,128)(2,1)S(1)}, u32[]{:S(2)}, u32[]{:S(2)}) collective-permute-start(bf16[4,5,640]{2,0,1:T(4,128)(2,1)S(1)} %dynamic-slice_convert_fusion.10), channel_id=1, source_target_pairs={{0,32},{1,33},{2,34},{3,35},{4,36},{5,37},{6,38},{7,39},{8,40},{9,... | collective-permute-start | bytes 76808 | tf_op jit(solution)/shard_map/ppermute | solution.py:15
  177.4 3.5 %collective-permute-start.34 = (bf16[2,5,640]{2,0,1:T(2,128)(2,1)S(1)}, bf16[2,5,640]{2,0,1:T(2,128)(2,1)S(1)}, u32[]{:S(2)}, u32[]{:S(2)}) collective-permute-start(bf16[2,5,640]{2,0,1:T(2,128)(2,1)S(1)} %dynamic-slice_convert_fusion.13), channel_id=1, source_target_pairs={{0,128},{1,129},{2,130},{3,131},{4,132},{5,133},{6,134},{7,135},{8... | collective-permute-start | bytes 38408 | tf_op jit(solution)/shard_map/ppermute | solution.py:15
  180.9 2.2 %collective-permute-start.46 = (bf16[2,5,640]{2,0,1:T(2,128)(2,1)S(1)}, bf16[2,5,640]{2,0,1:T(2,128)(2,1)S(1)}, u32[]{:S(2)}, u32[]{:S(2)}) collective-permute-start(bf16[2,5,640]{2,0,1:T(2,128)(2,1)S(1)} %dynamic-slice_convert_fusion.12), channel_id=1, source_target_pairs={{0,128},{1,129},{2,130},{3,131},{4,132},{5,133},{6,134},{7,135},{8... | collective-permute-start | bytes 38408 | tf_op jit(solution)/shard_map/ppermute | solution.py:15
  183.2 4.0 %collective-permute-start.35 = (bf16[1,5,640]{2,0,1:T(2,128)(2,1)S(1)}, bf16[1,5,640]{2,0,1:T(2,128)(2,1)S(1)}, u32[]{:S(2)}, u32[]{:S(2)}) collective-permute-start(bf16[1,5,640]{2,0,1:T(2,128)(2,1)S(1)} %dynamic-slice_convert_fusion.15), channel_id=1, source_target_pairs={{0,8},{1,9},{2,10},{3,11},{4,12},{5,13},{6,14},{7,15},{8,0},{9,1},... | collective-permute-start | bytes 19208 | tf_op jit(solution)/shard_map/ppermute | solution.py:15
  187.2 3.2 %collective-permute-start.47 = (bf16[1,5,640]{2,0,1:T(2,128)(2,1)S(1)}, bf16[1,5,640]{2,0,1:T(2,128)(2,1)S(1)}, u32[]{:S(2)}, u32[]{:S(2)}) collective-permute-start(bf16[1,5,640]{2,0,1:T(2,128)(2,1)S(1)} %dynamic-slice_convert_fusion.14), channel_id=1, source_target_pairs={{0,8},{1,9},{2,10},{3,11},{4,12},{5,13},{6,14},{7,15},{8,0},{9,1},... | collective-permute-start | bytes 19208 | tf_op jit(solution)/shard_map/ppermute | solution.py:15
  191.5 3.4 %collective-permute-done.47 = bf16[1,5,640]{2,0,1:T(2,128)(2,1)S(1)} collective-permute-done((bf16[1,5,640]{2,0,1:T(2,128)(2,1)S(1)}, bf16[1,5,640]{2,0,1:T(2,128)(2,1)S(1)}, u32[]{:S(2)}, u32[]{:S(2)}) %collective-permute-start.47) | collective-permute-done | bytes 6432 | tf_op jit(solution)/shard_map/ppermute | solution.py:15
  (177 shorter events, 42.5 us)
Async XLA Ops:
  2.7 6.0 %collective-permute-start = (f32[8,128]{1,0:T(8,128)S(1)}, f32[8,128]{1,0:T(8,128)S(1)}, u32[]{:S(2)}, u32[]{:S(2)}) collective-permute-start(f32[8,128]{1,0:T(8,128)S(1)} %broadcast_in_dim.12), channel_id=1, source_target_pairs={{0,1},{1,0},{2,3},{3,2},{4,5},{5,4},{6,7},{7,6},{8,9},{9,8},{10,11... | collective-permute-start | bytes 12296 | tf_op jit(solution)/shard_map/ppermute | solution.py:15
  9.3 10.2 %collective-permute-start.1 = (f32[8,128]{1,0:T(8,128)S(1)}, f32[8,128]{1,0:T(8,128)S(1)}, u32[]{:S(2)}, u32[]{:S(2)}) collective-permute-start(f32[8,128]{1,0:T(8,128)S(1)} %broadcast_add_fusion.1), channel_id=1, source_target_pairs={{0,2},{1,3},{2,0},{3,1},{4,6},{5,7},{6,4},{7,5},{8,10},{9,11},{10,... | collective-permute-start | bytes 12296 | tf_op jit(solution)/shard_map/ppermute | solution.py:15
  12.1 40.3 %collective-permute-start.8 = (bf16[128,640]{1,0:T(8,128)(2,1)}, bf16[128,640]{1,0:T(8,128)(2,1)S(1)}, u32[]{:S(2)}, u32[]{:S(2)}) collective-permute-start(bf16[128,640]{1,0:T(8,128)(2,1)} %multiply_convert_fusion.1), channel_id=1, source_target_pairs={{0,8},{1,9},{2,10},{3,11},{4,12},{5,13},{6,14},{7,15},{8,16},{9,17... | collective-permute-start | bytes 491528 | tf_op jit(solution)/shard_map/ppermute | solution.py:10
  20.2 3.7 %collective-permute-start.2 = (f32[8,128]{1,0:T(8,128)S(1)}, f32[8,128]{1,0:T(8,128)S(1)}, u32[]{:S(2)}, u32[]{:S(2)}) collective-permute-start(f32[8,128]{1,0:T(8,128)S(1)} %fusion.67), channel_id=1, source_target_pairs={{0,16},{1,17},{2,18},{3,19},{4,20},{5,21},{6,22},{7,23},{8,24},{9,... | collective-permute-start | bytes 12296 | tf_op jit(solution)/shard_map/ppermute | solution.py:15
  23.9 3.6 %collective-permute-start.3 = (f32[8,128]{1,0:T(8,128)S(1)}, f32[8,128]{1,0:T(8,128)S(1)}, u32[]{:S(2)}, u32[]{:S(2)}) collective-permute-start(f32[8,128]{1,0:T(8,128)S(1)} %add.259), channel_id=1, source_target_pairs={{0,64},{1,65},{2,66},{3,67},{4,68},{5,69},{6,70},{7,71},{8,72},{9,... | collective-permute-start | bytes 12296 | tf_op jit(solution)/shard_map/ppermute | solution.py:15
  27.5 4.5 %collective-permute-start.4 = (f32[8,128]{1,0:T(8,128)S(1)}, f32[8,128]{1,0:T(8,128)S(1)}, u32[]{:S(2)}, u32[]{:S(2)}) collective-permute-start(f32[8,128]{1,0:T(8,128)S(1)} %add.260), channel_id=1, source_target_pairs={{0,4},{1,5},{2,6},{3,7},{4,0},{5,1},{6,2},{7,3},{8,12},{9,13},{10,... | collective-permute-start | bytes 12296 | tf_op jit(solution)/shard_map/ppermute | solution.py:15
  32.0 5.1 %collective-permute-start.5 = (f32[8,128]{1,0:T(8,128)S(1)}, f32[8,128]{1,0:T(8,128)S(1)}, u32[]{:S(2)}, u32[]{:S(2)}) collective-permute-start(f32[8,128]{1,0:T(8,128)S(1)} %add.261), channel_id=1, source_target_pairs={{0,32},{1,33},{2,34},{3,35},{4,36},{5,37},{6,38},{7,39},{8,40},{9,... | collective-permute-start | bytes 12296 | tf_op jit(solution)/shard_map/ppermute | solution.py:15
  37.1 5.1 %collective-permute-start.6 = (f32[8,128]{1,0:T(8,128)S(1)}, f32[8,128]{1,0:T(8,128)S(1)}, u32[]{:S(2)}, u32[]{:S(2)}) collective-permute-start(f32[8,128]{1,0:T(8,128)S(1)} %add.262), channel_id=1, source_target_pairs={{0,128},{1,129},{2,130},{3,131},{4,132},{5,133},{6,134},{7,135},{8... | collective-permute-start | bytes 12296 | tf_op jit(solution)/shard_map/ppermute | solution.py:15
  42.2 10.1 %collective-permute-start.7 = (f32[8,128]{1,0:T(8,128)S(1)}, f32[8,128]{1,0:T(8,128)S(1)}, u32[]{:S(2)}, u32[]{:S(2)}) collective-permute-start(f32[8,128]{1,0:T(8,128)S(1)} %add.263), channel_id=1, source_target_pairs={{0,8},{1,9},{2,10},{3,11},{4,12},{5,13},{6,14},{7,15},{8,0},{9,1},... | collective-permute-start | bytes 12296 | tf_op jit(solution)/shard_map/ppermute | solution.py:15
  42.6 9.8 %collective-permute-start.9 = (bf16[128,640]{1,0:T(8,128)(2,1)}, bf16[128,640]{1,0:T(8,128)(2,1)}, u32[]{:S(2)}, u32[]{:S(2)}) collective-permute-start(bf16[128,640]{1,0:T(8,128)(2,1)} %multiply_convert_fusion.1), channel_id=1, source_target_pairs={{0,4},{1,5},{2,6},{3,7},{4,8},{5,9},{6,10},{7,11},{8,12},{9,13},{1... | collective-permute-start | bytes 491528 | tf_op jit(solution)/shard_map/ppermute | solution.py:10
  48.1 8.9 %collective-permute-start.10 = (bf16[128,640]{1,0:T(8,128)(2,1)}, bf16[128,640]{1,0:T(8,128)(2,1)S(1)}, u32[]{:S(2)}, u32[]{:S(2)}) collective-permute-start(bf16[128,640]{1,0:T(8,128)(2,1)} %multiply_convert_fusion.1), channel_id=1, source_target_pairs={{4,0},{5,1},{6,2},{7,3},{8,4},{9,5},{10,6},{11,7},{12,8},{13,9},{1... | collective-permute-start | bytes 491528 | tf_op jit(solution)/shard_map/ppermute | solution.py:10
  49.4 15.5 %collective-permute-start.11 = (bf16[128,640]{1,0:T(8,128)(2,1)}, bf16[128,640]{1,0:T(8,128)(2,1)S(1)}, u32[]{:S(2)}, u32[]{:S(2)}) collective-permute-start(bf16[128,640]{1,0:T(8,128)(2,1)} %multiply_convert_fusion.1), channel_id=1, source_target_pairs={{8,0},{9,1},{10,2},{11,3},{12,4},{13,5},{14,6},{15,7},{16,8},{17,9... | collective-permute-start | bytes 491528 | tf_op jit(solution)/shard_map/ppermute | solution.py:10
  73.5 23.1 %collective-permute-start.20 = (bf16[128,640]{1,0:T(8,128)(2,1)}, bf16[128,640]{1,0:T(8,128)(2,1)}, u32[]{:S(2)}, u32[]{:S(2)}) collective-permute-start(bf16[128,640]{1,0:T(8,128)(2,1)} %add_convert_fusion.1), channel_id=1, source_target_pairs={{8,0},{9,1},{10,2},{11,3},{12,4},{13,5},{14,6},{15,7},{16,8},{17,9... | collective-permute-start | bytes 491528 | tf_op jit(solution)/shard_map/ppermute | solution.py:10
  74.8 22.9 %collective-permute-start.21 = (bf16[128,640]{1,0:T(8,128)(2,1)}, bf16[128,640]{1,0:T(8,128)(2,1)}, u32[]{:S(2)}, u32[]{:S(2)}) collective-permute-start(bf16[128,640]{1,0:T(8,128)(2,1)} %add_convert_fusion.1), channel_id=1, source_target_pairs={{4,0},{5,1},{6,2},{7,3},{8,4},{9,5},{10,6},{11,7},{12,8},{13,9},{1... | collective-permute-start | bytes 491528 | tf_op jit(solution)/shard_map/ppermute | solution.py:10
  76.1 22.8 %collective-permute-start.22 = (bf16[128,640]{1,0:T(8,128)(2,1)}, bf16[128,640]{1,0:T(8,128)(2,1)}, u32[]{:S(2)}, u32[]{:S(2)}) collective-permute-start(bf16[128,640]{1,0:T(8,128)(2,1)} %add_convert_fusion.1), channel_id=1, source_target_pairs={{0,4},{1,5},{2,6},{3,7},{4,8},{5,9},{6,10},{7,11},{8,12},{9,13},{1... | collective-permute-start | bytes 491528 | tf_op jit(solution)/shard_map/ppermute | solution.py:10
  82.2 17.6 %collective-permute-start.23 = (bf16[128,640]{1,0:T(8,128)(2,1)}, bf16[128,640]{1,0:T(8,128)(2,1)}, u32[]{:S(2)}, u32[]{:S(2)}) collective-permute-start(bf16[128,640]{1,0:T(8,128)(2,1)} %add_convert_fusion.1), channel_id=1, source_target_pairs={{0,8},{1,9},{2,10},{3,11},{4,12},{5,13},{6,14},{7,15},{8,16},{9,17... | collective-permute-start | bytes 491528 | tf_op jit(solution)/shard_map/ppermute | solution.py:10
  91.4 3.6 %collective-permute-start.12 = (f32[8,128]{1,0:T(8,128)S(1)}, f32[8,128]{1,0:T(8,128)S(1)}, u32[]{:S(2)}, u32[]{:S(2)}) collective-permute-start(f32[8,128]{1,0:T(8,128)S(1)} %broadcast_in_dim.13), channel_id=1, source_target_pairs={{0,1},{1,0},{2,3},{3,2},{4,5},{5,4},{6,7},{7,6},{8,9},{9,8},{10,11... | collective-permute-start | bytes 12296 | tf_op jit(solution)/shard_map/ppermute | solution.py:15
  95.0 9.1 %collective-permute-start.37 = (bf16[64,5,640]{2,0,1:T(8,128)(2,1)S(1)}, bf16[64,5,640]{2,0,1:T(8,128)(2,1)S(1)}, u32[]{:S(2)}, u32[]{:S(2)}) collective-permute-start(bf16[64,5,640]{2,0,1:T(8,128)(2,1)S(1)} %get-tuple-element.14), channel_id=1, source_target_pairs={{0,1},{1,0},{2,3},{3,2},{4,5},{5,4},{6,7},{7,6},{8,9},{9,8},{10,11... | collective-permute-start | bytes 1228808 | tf_op jit(solution)/shard_map/ppermute | solution.py:15
  96.7 7.4 %collective-permute-start.36 = (bf16[64,5,640]{2,0,1:T(8,128)(2,1)S(1)}, bf16[64,5,640]{2,0,1:T(8,128)(2,1)S(1)}, u32[]{:S(2)}, u32[]{:S(2)}) collective-permute-start(bf16[64,5,640]{2,0,1:T(8,128)(2,1)S(1)} %get-tuple-element.13), channel_id=1, source_target_pairs={{0,1},{1,0},{2,3},{3,2},{4,5},{5,4},{6,7},{7,6},{8,9},{9,8},{10,11... | collective-permute-start | bytes 1228808 | tf_op jit(solution)/shard_map/ppermute | solution.py:15
  97.7 13.6 %collective-permute-start.13 = (f32[8,128]{1,0:T(8,128)S(1)}, f32[8,128]{1,0:T(8,128)S(1)}, u32[]{:S(2)}, u32[]{:S(2)}) collective-permute-start(f32[8,128]{1,0:T(8,128)S(1)} %broadcast_add_fusion), channel_id=1, source_target_pairs={{0,2},{1,3},{2,0},{3,1},{4,6},{5,7},{6,4},{7,5},{8,10},{9,11},{10,... | collective-permute-start | bytes 12296 | tf_op jit(solution)/shard_map/ppermute | solution.py:15
  103.5 3.6 %collective-permute-start.25 = (bf16[64,5,640]{2,0,1:T(8,128)(2,1)S(1)}, bf16[64,5,640]{2,0,1:T(8,128)(2,1)S(1)}, u32[]{:S(2)}, u32[]{:S(2)}) collective-permute-start(bf16[64,5,640]{2,0,1:T(8,128)(2,1)S(1)} %get-tuple-element.16), channel_id=1, source_target_pairs={{0,1},{1,0},{2,3},{3,2},{4,5},{5,4},{6,7},{7,6},{8,9},{9,8},{10,11... | collective-permute-start | bytes 1228808 | tf_op jit(solution)/shard_map/ppermute | solution.py:15
  104.0 3.1 %collective-permute-start.24 = (bf16[64,5,640]{2,0,1:T(8,128)(2,1)S(1)}, bf16[64,5,640]{2,0,1:T(8,128)(2,1)S(1)}, u32[]{:S(2)}, u32[]{:S(2)}) collective-permute-start(bf16[64,5,640]{2,0,1:T(8,128)(2,1)S(1)} %get-tuple-element.15), channel_id=1, source_target_pairs={{0,1},{1,0},{2,3},{3,2},{4,5},{5,4},{6,7},{7,6},{8,9},{9,8},{10,11... | collective-permute-start | bytes 1228808 | tf_op jit(solution)/shard_map/ppermute | solution.py:15
  105.0 48.1 %collective-permute-start.39 = (bf16[32,5,640]{2,0,1:T(8,128)(2,1)}, bf16[32,5,640]{2,0,1:T(8,128)(2,1)}, u32[]{:S(2)}, u32[]{:S(2)}) collective-permute-start(bf16[32,5,640]{2,0,1:T(8,128)(2,1)} %get-tuple-element.18), channel_id=1, source_target_pairs={{0,2},{1,3},{2,0},{3,1},{4,6},{5,7},{6,4},{7,5},{8,10},{9,11},{10,... | collective-permute-start | bytes 614408 | tf_op jit(solution)/shard_map/ppermute | solution.py:15
  106.9 46.2 %collective-permute-start.38 = (bf16[32,5,640]{2,0,1:T(8,128)(2,1)S(1)}, bf16[32,5,640]{2,0,1:T(8,128)(2,1)}, u32[]{:S(2)}, u32[]{:S(2)}) collective-permute-start(bf16[32,5,640]{2,0,1:T(8,128)(2,1)S(1)} %get-tuple-element.17), channel_id=1, source_target_pairs={{0,2},{1,3},{2,0},{3,1},{4,6},{5,7},{6,4},{7,5},{8,10},{9,11},{10,... | collective-permute-start | bytes 614408 | tf_op jit(solution)/shard_map/ppermute | solution.py:15
  109.2 43.9 %collective-permute-start.27 = (bf16[32,5,640]{2,0,1:T(8,128)(2,1)}, bf16[32,5,640]{2,0,1:T(8,128)(2,1)}, u32[]{:S(2)}, u32[]{:S(2)}) collective-permute-start(bf16[32,5,640]{2,0,1:T(8,128)(2,1)} %get-tuple-element.20), channel_id=1, source_target_pairs={{0,2},{1,3},{2,0},{3,1},{4,6},{5,7},{6,4},{7,5},{8,10},{9,11},{10,... | collective-permute-start | bytes 614408 | tf_op jit(solution)/shard_map/ppermute | solution.py:15
  111.2 42.0 %collective-permute-start.26 = (bf16[32,5,640]{2,0,1:T(8,128)(2,1)}, bf16[32,5,640]{2,0,1:T(8,128)(2,1)}, u32[]{:S(2)}, u32[]{:S(2)}) collective-permute-start(bf16[32,5,640]{2,0,1:T(8,128)(2,1)} %get-tuple-element.19), channel_id=1, source_target_pairs={{0,2},{1,3},{2,0},{3,1},{4,6},{5,7},{6,4},{7,5},{8,10},{9,11},{10,... | collective-permute-start | bytes 614408 | tf_op jit(solution)/shard_map/ppermute | solution.py:15
  111.9 5.2 %collective-permute-start.14 = (f32[8,128]{1,0:T(8,128)S(1)}, f32[8,128]{1,0:T(8,128)S(1)}, u32[]{:S(2)}, u32[]{:S(2)}) collective-permute-start(f32[8,128]{1,0:T(8,128)S(1)} %fusion.66), channel_id=1, source_target_pairs={{0,16},{1,17},{2,18},{3,19},{4,20},{5,21},{6,22},{7,23},{8,24},{9,... | collective-permute-start | bytes 12296 | tf_op jit(solution)/shard_map/ppermute | solution.py:15
  117.1 9.6 %collective-permute-start.15 = (f32[8,128]{1,0:T(8,128)S(1)}, f32[8,128]{1,0:T(8,128)S(1)}, u32[]{:S(2)}, u32[]{:S(2)}) collective-permute-start(f32[8,128]{1,0:T(8,128)S(1)} %add.278), channel_id=1, source_target_pairs={{0,64},{1,65},{2,66},{3,67},{4,68},{5,69},{6,70},{7,71},{8,72},{9,... | collective-permute-start | bytes 12296 | tf_op jit(solution)/shard_map/ppermute | solution.py:15
  126.7 4.5 %collective-permute-start.16 = (f32[8,128]{1,0:T(8,128)S(1)}, f32[8,128]{1,0:T(8,128)S(1)}, u32[]{:S(2)}, u32[]{:S(2)}) collective-permute-start(f32[8,128]{1,0:T(8,128)S(1)} %add.279), channel_id=1, source_target_pairs={{0,4},{1,5},{2,6},{3,7},{4,0},{5,1},{6,2},{7,3},{8,12},{9,13},{10,... | collective-permute-start | bytes 12296 | tf_op jit(solution)/shard_map/ppermute | solution.py:15
  131.2 5.1 %collective-permute-start.17 = (f32[8,128]{1,0:T(8,128)S(1)}, f32[8,128]{1,0:T(8,128)S(1)}, u32[]{:S(2)}, u32[]{:S(2)}) collective-permute-start(f32[8,128]{1,0:T(8,128)S(1)} %add.280), channel_id=1, source_target_pairs={{0,32},{1,33},{2,34},{3,35},{4,36},{5,37},{6,38},{7,39},{8,40},{9,... | collective-permute-start | bytes 12296 | tf_op jit(solution)/shard_map/ppermute | solution.py:15
  136.3 7.4 %collective-permute-start.18 = (f32[8,128]{1,0:T(8,128)S(1)}, f32[8,128]{1,0:T(8,128)S(1)}, u32[]{:S(2)}, u32[]{:S(2)}) collective-permute-start(f32[8,128]{1,0:T(8,128)S(1)} %add.281), channel_id=1, source_target_pairs={{0,128},{1,129},{2,130},{3,131},{4,132},{5,133},{6,134},{7,135},{8... | collective-permute-start | bytes 12296 | tf_op jit(solution)/shard_map/ppermute | solution.py:15
  143.7 7.5 %collective-permute-start.19 = (f32[8,128]{1,0:T(8,128)S(1)}, f32[8,128]{1,0:T(8,128)S(1)}, u32[]{:S(2)}, u32[]{:S(2)}) collective-permute-start(f32[8,128]{1,0:T(8,128)S(1)} %add.282), channel_id=1, source_target_pairs={{0,8},{1,9},{2,10},{3,11},{4,12},{5,13},{6,14},{7,15},{8,0},{9,1},... | collective-permute-start | bytes 12296 | tf_op jit(solution)/shard_map/ppermute | solution.py:15
  154.9 4.7 %collective-permute-start.29 = (bf16[16,5,640]{2,0,1:T(8,128)(2,1)S(1)}, bf16[16,5,640]{2,0,1:T(8,128)(2,1)S(1)}, u32[]{:S(2)}, u32[]{:S(2)}) collective-permute-start(bf16[16,5,640]{2,0,1:T(8,128)(2,1)S(1)} %get-tuple-element.24), channel_id=1, source_target_pairs={{0,16},{1,17},{2,18},{3,19},{4,20},{5,21},{6,22},{7,23},{8,24},{9,... | collective-permute-start | bytes 307208 | tf_op jit(solution)/shard_map/ppermute | solution.py:15
  155.0 5.7 %collective-permute-start.28 = (bf16[16,5,640]{2,0,1:T(8,128)(2,1)S(1)}, bf16[16,5,640]{2,0,1:T(8,128)(2,1)S(1)}, u32[]{:S(2)}, u32[]{:S(2)}) collective-permute-start(bf16[16,5,640]{2,0,1:T(8,128)(2,1)S(1)} %get-tuple-element.23), channel_id=1, source_target_pairs={{0,16},{1,17},{2,18},{3,19},{4,20},{5,21},{6,22},{7,23},{8,24},{9,... | collective-permute-start | bytes 307208 | tf_op jit(solution)/shard_map/ppermute | solution.py:15
  157.1 5.9 %collective-permute-start.41 = (bf16[16,5,640]{2,0,1:T(8,128)(2,1)S(1)}, bf16[16,5,640]{2,0,1:T(8,128)(2,1)S(1)}, u32[]{:S(2)}, u32[]{:S(2)}) collective-permute-start(bf16[16,5,640]{2,0,1:T(8,128)(2,1)S(1)} %get-tuple-element.22), channel_id=1, source_target_pairs={{0,16},{1,17},{2,18},{3,19},{4,20},{5,21},{6,22},{7,23},{8,24},{9,... | collective-permute-start | bytes 307208 | tf_op jit(solution)/shard_map/ppermute | solution.py:15
  157.3 5.7 %collective-permute-start.40 = (bf16[16,5,640]{2,0,1:T(8,128)(2,1)S(1)}, bf16[16,5,640]{2,0,1:T(8,128)(2,1)S(1)}, u32[]{:S(2)}, u32[]{:S(2)}) collective-permute-start(bf16[16,5,640]{2,0,1:T(8,128)(2,1)S(1)} %get-tuple-element.21), channel_id=1, source_target_pairs={{0,16},{1,17},{2,18},{3,19},{4,20},{5,21},{6,22},{7,23},{8,24},{9,... | collective-permute-start | bytes 307208 | tf_op jit(solution)/shard_map/ppermute | solution.py:15
  160.8 4.3 %collective-permute-start.31 = (bf16[8,5,640]{2,0,1:T(8,128)(2,1)S(1)}, bf16[8,5,640]{2,0,1:T(8,128)(2,1)S(1)}, u32[]{:S(2)}, u32[]{:S(2)}) collective-permute-start(bf16[8,5,640]{2,0,1:T(8,128)(2,1)S(1)} %get-tuple-element.28), channel_id=1, source_target_pairs={{0,64},{1,65},{2,66},{3,67},{4,68},{5,69},{6,70},{7,71},{8,72},{9,... | collective-permute-start | bytes 153608 | tf_op jit(solution)/shard_map/ppermute | solution.py:15
  162.6 4.1 %collective-permute-start.30 = (bf16[8,5,640]{2,0,1:T(8,128)(2,1)S(1)}, bf16[8,5,640]{2,0,1:T(8,128)(2,1)S(1)}, u32[]{:S(2)}, u32[]{:S(2)}) collective-permute-start(bf16[8,5,640]{2,0,1:T(8,128)(2,1)S(1)} %get-tuple-element.27), channel_id=1, source_target_pairs={{0,64},{1,65},{2,66},{3,67},{4,68},{5,69},{6,70},{7,71},{8,72},{9,... | collective-permute-start | bytes 153608 | tf_op jit(solution)/shard_map/ppermute | solution.py:15
  163.1 4.2 %collective-permute-start.43 = (bf16[8,5,640]{2,0,1:T(8,128)(2,1)S(1)}, bf16[8,5,640]{2,0,1:T(8,128)(2,1)S(1)}, u32[]{:S(2)}, u32[]{:S(2)}) collective-permute-start(bf16[8,5,640]{2,0,1:T(8,128)(2,1)S(1)} %get-tuple-element.26), channel_id=1, source_target_pairs={{0,64},{1,65},{2,66},{3,67},{4,68},{5,69},{6,70},{7,71},{8,72},{9,... | collective-permute-start | bytes 153608 | tf_op jit(solution)/shard_map/ppermute | solution.py:15
  164.8 4.1 %collective-permute-start.42 = (bf16[8,5,640]{2,0,1:T(8,128)(2,1)S(1)}, bf16[8,5,640]{2,0,1:T(8,128)(2,1)S(1)}, u32[]{:S(2)}, u32[]{:S(2)}) collective-permute-start(bf16[8,5,640]{2,0,1:T(8,128)(2,1)S(1)} %get-tuple-element.25), channel_id=1, source_target_pairs={{0,64},{1,65},{2,66},{3,67},{4,68},{5,69},{6,70},{7,71},{8,72},{9,... | collective-permute-start | bytes 153608 | tf_op jit(solution)/shard_map/ppermute | solution.py:15
  166.8 5.1 %collective-permute-start.32 = (bf16[8,5,640]{2,0,1:T(8,128)(2,1)S(1)}, bf16[8,5,640]{2,0,1:T(8,128)(2,1)S(1)}, u32[]{:S(2)}, u32[]{:S(2)}) collective-permute-start(bf16[8,5,640]{2,0,1:T(8,128)(2,1)S(1)} %dynamic-slice_convert_fusion.9), channel_id=1, source_target_pairs={{0,4},{1,5},{2,6},{3,7},{4,0},{5,1},{6,2},{7,3},{8,12},{9,13},{10,... | collective-permute-start | bytes 153608 | tf_op jit(solution)/shard_map/ppermute | solution.py:15
  169.0 5.4 %collective-permute-start.44 = (bf16[8,5,640]{2,0,1:T(8,128)(2,1)S(1)}, bf16[8,5,640]{2,0,1:T(8,128)(2,1)S(1)}, u32[]{:S(2)}, u32[]{:S(2)}) collective-permute-start(bf16[8,5,640]{2,0,1:T(8,128)(2,1)S(1)} %dynamic-slice_convert_fusion.8), channel_id=1, source_target_pairs={{0,4},{1,5},{2,6},{3,7},{4,0},{5,1},{6,2},{7,3},{8,12},{9,13},{10,... | collective-permute-start | bytes 153608 | tf_op jit(solution)/shard_map/ppermute | solution.py:15
  171.9 5.4 %collective-permute-start.33 = (bf16[4,5,640]{2,0,1:T(4,128)(2,1)S(1)}, bf16[4,5,640]{2,0,1:T(4,128)(2,1)S(1)}, u32[]{:S(2)}, u32[]{:S(2)}) collective-permute-start(bf16[4,5,640]{2,0,1:T(4,128)(2,1)S(1)} %dynamic-slice_convert_fusion.11), channel_id=1, source_target_pairs={{0,32},{1,33},{2,34},{3,35},{4,36},{5,37},{6,38},{7,39},{8,40},{9,... | collective-permute-start | bytes 76808 | tf_op jit(solution)/shard_map/ppermute | solution.py:15
  174.5 6.4 %collective-permute-start.45 = (bf16[4,5,640]{2,0,1:T(4,128)(2,1)S(1)}, bf16[4,5,640]{2,0,1:T(4,128)(2,1)S(1)}, u32[]{:S(2)}, u32[]{:S(2)}) collective-permute-start(bf16[4,5,640]{2,0,1:T(4,128)(2,1)S(1)} %dynamic-slice_convert_fusion.10), channel_id=1, source_target_pairs={{0,32},{1,33},{2,34},{3,35},{4,36},{5,37},{6,38},{7,39},{8,40},{9,... | collective-permute-start | bytes 76808 | tf_op jit(solution)/shard_map/ppermute | solution.py:15
  177.4 5.7 %collective-permute-start.34 = (bf16[2,5,640]{2,0,1:T(2,128)(2,1)S(1)}, bf16[2,5,640]{2,0,1:T(2,128)(2,1)S(1)}, u32[]{:S(2)}, u32[]{:S(2)}) collective-permute-start(bf16[2,5,640]{2,0,1:T(2,128)(2,1)S(1)} %dynamic-slice_convert_fusion.13), channel_id=1, source_target_pairs={{0,128},{1,129},{2,130},{3,131},{4,132},{5,133},{6,134},{7,135},{8... | collective-permute-start | bytes 38408 | tf_op jit(solution)/shard_map/ppermute | solution.py:15
  180.9 6.2 %collective-permute-start.46 = (bf16[2,5,640]{2,0,1:T(2,128)(2,1)S(1)}, bf16[2,5,640]{2,0,1:T(2,128)(2,1)S(1)}, u32[]{:S(2)}, u32[]{:S(2)}) collective-permute-start(bf16[2,5,640]{2,0,1:T(2,128)(2,1)S(1)} %dynamic-slice_convert_fusion.12), channel_id=1, source_target_pairs={{0,128},{1,129},{2,130},{3,131},{4,132},{5,133},{6,134},{7,135},{8... | collective-permute-start | bytes 38408 | tf_op jit(solution)/shard_map/ppermute | solution.py:15
  183.2 7.7 %collective-permute-start.35 = (bf16[1,5,640]{2,0,1:T(2,128)(2,1)S(1)}, bf16[1,5,640]{2,0,1:T(2,128)(2,1)S(1)}, u32[]{:S(2)}, u32[]{:S(2)}) collective-permute-start(bf16[1,5,640]{2,0,1:T(2,128)(2,1)S(1)} %dynamic-slice_convert_fusion.15), channel_id=1, source_target_pairs={{0,8},{1,9},{2,10},{3,11},{4,12},{5,13},{6,14},{7,15},{8,0},{9,1},... | collective-permute-start | bytes 19208 | tf_op jit(solution)/shard_map/ppermute | solution.py:15
  187.2 7.7 %collective-permute-start.47 = (bf16[1,5,640]{2,0,1:T(2,128)(2,1)S(1)}, bf16[1,5,640]{2,0,1:T(2,128)(2,1)S(1)}, u32[]{:S(2)}, u32[]{:S(2)}) collective-permute-start(bf16[1,5,640]{2,0,1:T(2,128)(2,1)S(1)} %dynamic-slice_convert_fusion.14), channel_id=1, source_target_pairs={{0,8},{1,9},{2,10},{3,11},{4,12},{5,13},{6,14},{7,15},{8,0},{9,1},... | collective-permute-start | bytes 19208 | tf_op jit(solution)/shard_map/ppermute | solution.py:15
  (9 other events, 136.1 us)

commit v13 on v12

--- a/solution.py
+++ b/solution.py
@@ -65,7 +65,8 @@
         got_parts, got_extra = swap_with((parts, extra), axis, bit)
         got = [jnp.concatenate(g, 0) if pieces > 1 else g[0] for g in got_parts]
         blocks = [k + g.astype(jnp.float32) for k, g in zip(keep, got)]
-        extra = extra + got_extra
+        if extra is not None:
+            extra = extra + got_extra
     return [b[0] for b in blocks], extra
 
 
@@ -134,6 +135,8 @@
     )
     back_pieces = spread(gradient_before_activation, shard_reach)
     backward_tap_pile = jnp.stack(back_pieces[::-1])
+    loss_tile = tree_sum(jnp.broadcast_to(local_loss, (8, 128)), "seq")
+    loss_tile, backward_tap_pile = lax.optimization_barrier((loss_tile, backward_tap_pile))
     grad_neck = jnp.einsum(
         "krc,kbc->rb", backward_tap_pile, conv_weight, preferred_element_type=jnp.float32
     )
@@ -142,9 +145,7 @@
     up_partial = lax.dot_general(
         columns, grad_first, (((0,), (0,)), ((), ())), preferred_element_type=jnp.float32
     )
-    (grad_down, grad_up), loss_tile = tree_scatter(
-        (down_partial, up_partial), jnp.broadcast_to(local_loss, (8, 128)), "seq"
-    )
+    (grad_down, grad_up), _ = tree_scatter((down_partial, up_partial), None, "seq")
     grad_down = grad_down.astype(jnp.bfloat16)
     grad_up = grad_up.astype(jnp.bfloat16)
     loss_total = loss_tile[0, 0]

time: 198 us -> 207 us (1.045)
  waiting for transfers between devices: 55.2 us -> 64.3 us
    ppermute x40, waiting for transfers between devices: 43.9 us -> 53 us  [swap_with(): return lax.ppermute(block, axis, [(i, i ^ bit) for i in range(devices)])]
  transfers between devices with their start and end apart: 48 -> 48, of which waited for: 22 -> 26; matrix products, arithmetic and copies ran while one was open for 13% -> 13% of each run, Pallas kernels for 0% -> 0%
where the time goes in v13:
time: 207 us; the launch traced here: 206 us
  starting transfers between devices  97.2 us (47%)
  waiting for transfers between devices  64.3 us (31%)
  local copies, waits for them, and re-layouts  15.9 us (8%)
  other arithmetic  13.7 us (7%)
  matrix products  9.85 us (5%)
  between operations  4.61 us (2%)
    ppermute x40, starting transfers between devices, swap_with(): return lax.ppermute(block, axis, [(i, i ^ bit) for i in range(devices)])  64.6 us
    ppermute x40, waiting for transfers between devices, swap_with(): return lax.ppermute(block, axis, [(i, i ^ bit) for i in range(devices)])  53 us
    ppermute x8, starting transfers between devices, from_behind(): return lax.ppermute(block, axis, route)  32.6 us
    ppermute x8, waiting for transfers between devices, from_behind(): return lax.ppermute(block, axis, route)  11.3 us
    unnamed x26, local copies, waits for them, and re-layouts  6.22 us
  transfers between devices with their start and end apart: 48, of which 26 were waited for; matrix products, arithmetic and copies ran while one was open for 13% of the time, Pallas kernels for 0%

profile of v13, /device:TPU:32, one launch (start us, length us, event | category | flops | bytes accessed | tf_op | source)
XLA Modules:
  0.0 205.5 jit_solution(12468931287051203524)
XLA Ops:
  6.5 1.9 fusion.53
  9.3 1.9 collective-permute-start.1
  12.1 7.4 %collective-permute-start.8 = (bf16[128,640]{1,0:T(8,128)(2,1)}, bf16[128,640]{1,0:T(8,128)(2,1)S(1)}, u32[]{:S(2)}, u32[]{:S(2)}) collective-permute-start(bf16[128,640]{1,0:T(8,128)(2,1)} %multiply_convert_fusion.1), channel_id=1, source_target_pairs={{0,8},{1,9},{2,10},{3,11},{4,12},{5,13},{6,14},{7,15},{8,16},{9,17... | collective-permute-start | bytes 491528 | tf_op jit(solution)/shard_map/ppermute | solution.py:10
  20.2 1.6 collective-permute-start.2
  21.8 2.1 %collective-permute-done.2 = f32[8,128]{1,0:T(8,128)S(1)} collective-permute-done((f32[8,128]{1,0:T(8,128)S(1)}, f32[8,128]{1,0:T(8,128)S(1)}, u32[]{:S(2)}, u32[]{:S(2)}) %collective-permute-start.2) | collective-permute-done | bytes 4128 | tf_op jit(solution)/shard_map/ppermute | solution.py:15
  23.9 1.6 collective-permute-start.3
  25.4 2.0 collective-permute-done.3
  29.0 3.0 %collective-permute-done.4 = f32[8,128]{1,0:T(8,128)S(1)} collective-permute-done((f32[8,128]{1,0:T(8,128)S(1)}, f32[8,128]{1,0:T(8,128)S(1)}, u32[]{:S(2)}, u32[]{:S(2)}) %collective-permute-start.4) | collective-permute-done | bytes 4128 | tf_op jit(solution)/shard_map/ppermute | solution.py:15
  32.0 3.0 %collective-permute-start.5 = (f32[8,128]{1,0:T(8,128)S(1)}, f32[8,128]{1,0:T(8,128)S(1)}, u32[]{:S(2)}, u32[]{:S(2)}) collective-permute-start(f32[8,128]{1,0:T(8,128)S(1)} %add.261), channel_id=1, source_target_pairs={{0,32},{1,33},{2,34},{3,35},{4,36},{5,37},{6,38},{7,39},{8,40},{9,... | collective-permute-start | bytes 12296 | tf_op jit(solution)/shard_map/ppermute | solution.py:15
  35.0 2.1 %collective-permute-done.5 = f32[8,128]{1,0:T(8,128)S(1)} collective-permute-done((f32[8,128]{1,0:T(8,128)S(1)}, f32[8,128]{1,0:T(8,128)S(1)}, u32[]{:S(2)}, u32[]{:S(2)}) %collective-permute-start.5) | collective-permute-done | bytes 4128 | tf_op jit(solution)/shard_map/ppermute | solution.py:15
  37.1 3.2 %collective-permute-start.6 = (f32[8,128]{1,0:T(8,128)S(1)}, f32[8,128]{1,0:T(8,128)S(1)}, u32[]{:S(2)}, u32[]{:S(2)}) collective-permute-start(f32[8,128]{1,0:T(8,128)S(1)} %add.262), channel_id=1, source_target_pairs={{0,128},{1,129},{2,130},{3,131},{4,132},{5,133},{6,134},{7,135},{8... | collective-permute-start | bytes 12296 | tf_op jit(solution)/shard_map/ppermute | solution.py:15
  40.3 1.9 collective-permute-done.6
  42.6 5.5 %collective-permute-start.9 = (bf16[128,640]{1,0:T(8,128)(2,1)}, bf16[128,640]{1,0:T(8,128)(2,1)}, u32[]{:S(2)}, u32[]{:S(2)}) collective-permute-start(bf16[128,640]{1,0:T(8,128)(2,1)} %multiply_convert_fusion.1), channel_id=1, source_target_pairs={{0,4},{1,5},{2,6},{3,7},{4,8},{5,9},{6,10},{7,11},{8,12},{9,13},{1... | collective-permute-start | bytes 491528 | tf_op jit(solution)/shard_map/ppermute | solution.py:10
  53.6 3.4 %collective-permute-done.10 = bf16[128,640]{1,0:T(8,128)(2,1)S(1)} collective-permute-done((bf16[128,640]{1,0:T(8,128)(2,1)}, bf16[128,640]{1,0:T(8,128)(2,1)S(1)}, u32[]{:S(2)}, u32[]{:S(2)}) %collective-permute-start.10) | collective-permute-done | bytes 163872 | tf_op jit(solution)/shard_map/ppermute | solution.py:10
  57.0 7.9 %collective-permute-done.11 = bf16[128,640]{1,0:T(8,128)(2,1)S(1)} collective-permute-done((bf16[128,640]{1,0:T(8,128)(2,1)}, bf16[128,640]{1,0:T(8,128)(2,1)S(1)}, u32[]{:S(2)}, u32[]{:S(2)}) %collective-permute-start.11) | collective-permute-done | bytes 163872 | tf_op jit(solution)/shard_map/ppermute | solution.py:10
  65.0 3.1 %fusion.54 = (f32[128]{0:T(128)S(1)}, f32[128,640]{1,0:T(8,128)S(1)}) fusion(bf16[5,128,640]{2,1,0:T(8,128)(2,1)S(1)} %bitcast_dynamic-update-slice_fusion.5, bf16[5,640,640]{2,1,0:T(8,128)(2,1)} %param.13), kind=kOutput, calls=%fused_computation.136 | convolution fusion | flops 524369792 | bytes 5243392 | tf_op jit(solution)/shard_map/krc,kcb->rb/dot_general | solution.py:105
  73.6 3.6 %collective-permute-done.13 = f32[8,128]{1,0:T(8,128)S(1)} collective-permute-done((f32[8,128]{1,0:T(8,128)S(1)}, f32[8,128]{1,0:T(8,128)S(1)}, u32[]{:S(2)}, u32[]{:S(2)}) %collective-permute-start.13) | collective-permute-done | bytes 4128 | tf_op jit(solution)/shard_map/ppermute | solution.py:15
  77.9 2.2 %collective-permute-start.14 = (f32[8,128]{1,0:T(8,128)S(1)}, f32[8,128]{1,0:T(8,128)S(1)}, u32[]{:S(2)}, u32[]{:S(2)}) collective-permute-start(f32[8,128]{1,0:T(8,128)S(1)} %fusion.66), channel_id=1, source_target_pairs={{0,16},{1,17},{2,18},{3,19},{4,20},{5,21},{6,22},{7,23},{8,24},{9,... | collective-permute-start | bytes 12296 | tf_op jit(solution)/shard_map/ppermute | solution.py:15
  81.6 3.4 %collective-permute-start.15 = (f32[8,128]{1,0:T(8,128)S(1)}, f32[8,128]{1,0:T(8,128)S(1)}, u32[]{:S(2)}, u32[]{:S(2)}) collective-permute-start(f32[8,128]{1,0:T(8,128)S(1)} %add.278), channel_id=1, source_target_pairs={{0,64},{1,65},{2,66},{3,67},{4,68},{5,69},{6,70},{7,71},{8,72},{9,... | collective-permute-start | bytes 12296 | tf_op jit(solution)/shard_map/ppermute | solution.py:15
  85.0 1.6 collective-permute-done.15
  90.0 6.1 %collective-permute-start.22 = (bf16[128,640]{1,0:T(8,128)(2,1)}, bf16[128,640]{1,0:T(8,128)(2,1)}, u32[]{:S(2)}, u32[]{:S(2)}) collective-permute-start(bf16[128,640]{1,0:T(8,128)(2,1)} %add_convert_fusion.1), channel_id=1, source_target_pairs={{0,4},{1,5},{2,6},{3,7},{4,8},{5,9},{6,10},{7,11},{8,12},{9,13},{1... | collective-permute-start | bytes 491528 | tf_op jit(solution)/shard_map/ppermute | solution.py:10
  96.1 8.5 %collective-permute-start.23 = (bf16[128,640]{1,0:T(8,128)(2,1)}, bf16[128,640]{1,0:T(8,128)(2,1)}, u32[]{:S(2)}, u32[]{:S(2)}) collective-permute-start(bf16[128,640]{1,0:T(8,128)(2,1)} %add_convert_fusion.1), channel_id=1, source_target_pairs={{0,8},{1,9},{2,10},{3,11},{4,12},{5,13},{6,14},{7,15},{8,16},{9,17... | collective-permute-start | bytes 491528 | tf_op jit(solution)/shard_map/ppermute | solution.py:10
  107.3 4.0 %collective-permute-start.17 = (f32[8,128]{1,0:T(8,128)S(1)}, f32[8,128]{1,0:T(8,128)S(1)}, u32[]{:S(2)}, u32[]{:S(2)}) collective-permute-start(f32[8,128]{1,0:T(8,128)S(1)} %add.280), channel_id=1, source_target_pairs={{0,32},{1,33},{2,34},{3,35},{4,36},{5,37},{6,38},{7,39},{8,40},{9,... | collective-permute-start | bytes 12296 | tf_op jit(solution)/shard_map/ppermute | solution.py:15
  112.9 7.7 %collective-permute-start.18 = (f32[8,128]{1,0:T(8,128)S(1)}, f32[8,128]{1,0:T(8,128)S(1)}, u32[]{:S(2)}, u32[]{:S(2)}) collective-permute-start(f32[8,128]{1,0:T(8,128)S(1)} %add.281), channel_id=1, source_target_pairs={{0,128},{1,129},{2,130},{3,131},{4,132},{5,133},{6,134},{7,135},{8... | collective-permute-start | bytes 12296 | tf_op jit(solution)/shard_map/ppermute | solution.py:15
  120.6 1.7 collective-permute-done.18
  123.4 6.5 %collective-permute-done.19 = f32[8,128]{1,0:T(8,128)S(1)} collective-permute-done((f32[8,128]{1,0:T(8,128)S(1)}, f32[8,128]{1,0:T(8,128)S(1)}, u32[]{:S(2)}, u32[]{:S(2)}) %collective-permute-start.19) | collective-permute-done | bytes 4128 | tf_op jit(solution)/shard_map/ppermute | solution.py:15
  134.3 1.5 multiply_reduce_fusion
  138.7 1.8 collective-permute-start.38
  142.9 1.8 collective-permute-start.26
  146.7 4.4 %collective-permute-done.38 = bf16[32,5,640]{2,0,1:T(8,128)(2,1)} collective-permute-done((bf16[32,5,640]{2,0,1:T(8,128)(2,1)S(1)}, bf16[32,5,640]{2,0,1:T(8,128)(2,1)}, u32[]{:S(2)}, u32[]{:S(2)}) %collective-permute-start.38) | collective-permute-done | bytes 204832 | tf_op jit(solution)/shard_map/ppermute | solution.py:15
  151.1 4.4 %collective-permute-done.27 = bf16[32,5,640]{2,0,1:T(8,128)(2,1)} collective-permute-done((bf16[32,5,640]{2,0,1:T(8,128)(2,1)}, bf16[32,5,640]{2,0,1:T(8,128)(2,1)}, u32[]{:S(2)}, u32[]{:S(2)}) %collective-permute-start.27) | collective-permute-done | bytes 204832 | tf_op jit(solution)/shard_map/ppermute | solution.py:15
  155.5 3.5 %collective-permute-done.26 = bf16[32,5,640]{2,0,1:T(8,128)(2,1)} collective-permute-done((bf16[32,5,640]{2,0,1:T(8,128)(2,1)}, bf16[32,5,640]{2,0,1:T(8,128)(2,1)}, u32[]{:S(2)}, u32[]{:S(2)}) %collective-permute-start.26) | collective-permute-done | bytes 204832 | tf_op jit(solution)/shard_map/ppermute | solution.py:15
  159.0 1.7 convert_add_fusion.2
  160.9 2.0 collective-permute-start.28
  163.4 1.7 collective-permute-start.40
  165.1 1.6 collective-permute-done.29
  166.6 2.2 %collective-permute-done.28 = bf16[16,5,640]{2,0,1:T(8,128)(2,1)S(1)} collective-permute-done((bf16[16,5,640]{2,0,1:T(8,128)(2,1)S(1)}, bf16[16,5,640]{2,0,1:T(8,128)(2,1)S(1)}, u32[]{:S(2)}, u32[]{:S(2)}) %collective-permute-start.28) | collective-permute-done | bytes 102432 | tf_op jit(solution)/shard_map/ppermute | solution.py:15
  168.9 1.7 collective-permute-start.31
  171.6 1.7 collective-permute-start.43
  175.8 1.7 collective-permute-done.42
  178.7 1.6 collective-permute-done.32
  180.3 2.6 %collective-permute-start.33 = (bf16[4,5,640]{2,0,1:T(4,128)(2,1)S(1)}, bf16[4,5,640]{2,0,1:T(4,128)(2,1)S(1)}, u32[]{:S(2)}, u32[]{:S(2)}) collective-permute-start(bf16[4,5,640]{2,0,1:T(4,128)(2,1)S(1)} %dynamic-slice_convert_fusion.11), channel_id=1, source_target_pairs={{0,32},{1,33},{2,34},{3,35},{4,36},{5,37},{6,38},{7,39},{8,40},{9,... | collective-permute-start | bytes 76808 | tf_op jit(solution)/shard_map/ppermute | solution.py:15
  183.0 2.1 %collective-permute-start.45 = (bf16[4,5,640]{2,0,1:T(4,128)(2,1)S(1)}, bf16[4,5,640]{2,0,1:T(4,128)(2,1)S(1)}, u32[]{:S(2)}, u32[]{:S(2)}) collective-permute-start(bf16[4,5,640]{2,0,1:T(4,128)(2,1)S(1)} %dynamic-slice_convert_fusion.10), channel_id=1, source_target_pairs={{0,32},{1,33},{2,34},{3,35},{4,36},{5,37},{6,38},{7,39},{8,40},{9,... | collective-permute-start | bytes 76808 | tf_op jit(solution)/shard_map/ppermute | solution.py:15
  185.8 3.1 %collective-permute-start.34 = (bf16[2,5,640]{2,0,1:T(2,128)(2,1)S(1)}, bf16[2,5,640]{2,0,1:T(2,128)(2,1)S(1)}, u32[]{:S(2)}, u32[]{:S(2)}) collective-permute-start(bf16[2,5,640]{2,0,1:T(2,128)(2,1)S(1)} %dynamic-slice_convert_fusion.13), channel_id=1, source_target_pairs={{0,128},{1,129},{2,130},{3,131},{4,132},{5,133},{6,134},{7,135},{8... | collective-permute-start | bytes 38408 | tf_op jit(solution)/shard_map/ppermute | solution.py:15
  188.9 2.3 %collective-permute-start.46 = (bf16[2,5,640]{2,0,1:T(2,128)(2,1)S(1)}, bf16[2,5,640]{2,0,1:T(2,128)(2,1)S(1)}, u32[]{:S(2)}, u32[]{:S(2)}) collective-permute-start(bf16[2,5,640]{2,0,1:T(2,128)(2,1)S(1)} %dynamic-slice_convert_fusion.12), channel_id=1, source_target_pairs={{0,128},{1,129},{2,130},{3,131},{4,132},{5,133},{6,134},{7,135},{8... | collective-permute-start | bytes 38408 | tf_op jit(solution)/shard_map/ppermute | solution.py:15
  191.2 4.8 %collective-permute-start.35 = (bf16[1,5,640]{2,0,1:T(2,128)(2,1)S(1)}, bf16[1,5,640]{2,0,1:T(2,128)(2,1)S(1)}, u32[]{:S(2)}, u32[]{:S(2)}) collective-permute-start(bf16[1,5,640]{2,0,1:T(2,128)(2,1)S(1)} %dynamic-slice_convert_fusion.15), channel_id=1, source_target_pairs={{0,8},{1,9},{2,10},{3,11},{4,12},{5,13},{6,14},{7,15},{8,0},{9,1},... | collective-permute-start | bytes 19208 | tf_op jit(solution)/shard_map/ppermute | solution.py:15
  196.1 2.9 %collective-permute-start.47 = (bf16[1,5,640]{2,0,1:T(2,128)(2,1)S(1)}, bf16[1,5,640]{2,0,1:T(2,128)(2,1)S(1)}, u32[]{:S(2)}, u32[]{:S(2)}) collective-permute-start(bf16[1,5,640]{2,0,1:T(2,128)(2,1)S(1)} %dynamic-slice_convert_fusion.14), channel_id=1, source_target_pairs={{0,8},{1,9},{2,10},{3,11},{4,12},{5,13},{6,14},{7,15},{8,0},{9,1},... | collective-permute-start | bytes 19208 | tf_op jit(solution)/shard_map/ppermute | solution.py:15
  199.6 4.2 %collective-permute-done.47 = bf16[1,5,640]{2,0,1:T(2,128)(2,1)S(1)} collective-permute-done((bf16[1,5,640]{2,0,1:T(2,128)(2,1)S(1)}, bf16[1,5,640]{2,0,1:T(2,128)(2,1)S(1)}, u32[]{:S(2)}, u32[]{:S(2)}) %collective-permute-start.47) | collective-permute-done | bytes 6432 | tf_op jit(solution)/shard_map/ppermute | solution.py:15
  (177 shorter events, 48.8 us)
Async XLA Ops:
  2.7 6.0 %collective-permute-start = (f32[8,128]{1,0:T(8,128)S(1)}, f32[8,128]{1,0:T(8,128)S(1)}, u32[]{:S(2)}, u32[]{:S(2)}) collective-permute-start(f32[8,128]{1,0:T(8,128)S(1)} %broadcast_in_dim.12), channel_id=1, source_target_pairs={{0,1},{1,0},{2,3},{3,2},{4,5},{5,4},{6,7},{7,6},{8,9},{9,8},{10,11... | collective-permute-start | bytes 12296 | tf_op jit(solution)/shard_map/ppermute | solution.py:15
  9.3 10.2 %collective-permute-start.1 = (f32[8,128]{1,0:T(8,128)S(1)}, f32[8,128]{1,0:T(8,128)S(1)}, u32[]{:S(2)}, u32[]{:S(2)}) collective-permute-start(f32[8,128]{1,0:T(8,128)S(1)} %broadcast_add_fusion.1), channel_id=1, source_target_pairs={{0,2},{1,3},{2,0},{3,1},{4,6},{5,7},{6,4},{7,5},{8,10},{9,11},{10,... | collective-permute-start | bytes 12296 | tf_op jit(solution)/shard_map/ppermute | solution.py:15
  12.1 40.3 %collective-permute-start.8 = (bf16[128,640]{1,0:T(8,128)(2,1)}, bf16[128,640]{1,0:T(8,128)(2,1)S(1)}, u32[]{:S(2)}, u32[]{:S(2)}) collective-permute-start(bf16[128,640]{1,0:T(8,128)(2,1)} %multiply_convert_fusion.1), channel_id=1, source_target_pairs={{0,8},{1,9},{2,10},{3,11},{4,12},{5,13},{6,14},{7,15},{8,16},{9,17... | collective-permute-start | bytes 491528 | tf_op jit(solution)/shard_map/ppermute | solution.py:10
  20.2 3.7 %collective-permute-start.2 = (f32[8,128]{1,0:T(8,128)S(1)}, f32[8,128]{1,0:T(8,128)S(1)}, u32[]{:S(2)}, u32[]{:S(2)}) collective-permute-start(f32[8,128]{1,0:T(8,128)S(1)} %fusion.67), channel_id=1, source_target_pairs={{0,16},{1,17},{2,18},{3,19},{4,20},{5,21},{6,22},{7,23},{8,24},{9,... | collective-permute-start | bytes 12296 | tf_op jit(solution)/shard_map/ppermute | solution.py:15
  23.9 3.6 %collective-permute-start.3 = (f32[8,128]{1,0:T(8,128)S(1)}, f32[8,128]{1,0:T(8,128)S(1)}, u32[]{:S(2)}, u32[]{:S(2)}) collective-permute-start(f32[8,128]{1,0:T(8,128)S(1)} %add.259), channel_id=1, source_target_pairs={{0,64},{1,65},{2,66},{3,67},{4,68},{5,69},{6,70},{7,71},{8,72},{9,... | collective-permute-start | bytes 12296 | tf_op jit(solution)/shard_map/ppermute | solution.py:15
  27.5 4.5 %collective-permute-start.4 = (f32[8,128]{1,0:T(8,128)S(1)}, f32[8,128]{1,0:T(8,128)S(1)}, u32[]{:S(2)}, u32[]{:S(2)}) collective-permute-start(f32[8,128]{1,0:T(8,128)S(1)} %add.260), channel_id=1, source_target_pairs={{0,4},{1,5},{2,6},{3,7},{4,0},{5,1},{6,2},{7,3},{8,12},{9,13},{10,... | collective-permute-start | bytes 12296 | tf_op jit(solution)/shard_map/ppermute | solution.py:15
  32.0 5.1 %collective-permute-start.5 = (f32[8,128]{1,0:T(8,128)S(1)}, f32[8,128]{1,0:T(8,128)S(1)}, u32[]{:S(2)}, u32[]{:S(2)}) collective-permute-start(f32[8,128]{1,0:T(8,128)S(1)} %add.261), channel_id=1, source_target_pairs={{0,32},{1,33},{2,34},{3,35},{4,36},{5,37},{6,38},{7,39},{8,40},{9,... | collective-permute-start | bytes 12296 | tf_op jit(solution)/shard_map/ppermute | solution.py:15
  37.1 5.1 %collective-permute-start.6 = (f32[8,128]{1,0:T(8,128)S(1)}, f32[8,128]{1,0:T(8,128)S(1)}, u32[]{:S(2)}, u32[]{:S(2)}) collective-permute-start(f32[8,128]{1,0:T(8,128)S(1)} %add.262), channel_id=1, source_target_pairs={{0,128},{1,129},{2,130},{3,131},{4,132},{5,133},{6,134},{7,135},{8... | collective-permute-start | bytes 12296 | tf_op jit(solution)/shard_map/ppermute | solution.py:15
  42.2 10.1 %collective-permute-start.7 = (f32[8,128]{1,0:T(8,128)S(1)}, f32[8,128]{1,0:T(8,128)S(1)}, u32[]{:S(2)}, u32[]{:S(2)}) collective-permute-start(f32[8,128]{1,0:T(8,128)S(1)} %add.263), channel_id=1, source_target_pairs={{0,8},{1,9},{2,10},{3,11},{4,12},{5,13},{6,14},{7,15},{8,0},{9,1},... | collective-permute-start | bytes 12296 | tf_op jit(solution)/shard_map/ppermute | solution.py:15
  42.6 9.8 %collective-permute-start.9 = (bf16[128,640]{1,0:T(8,128)(2,1)}, bf16[128,640]{1,0:T(8,128)(2,1)}, u32[]{:S(2)}, u32[]{:S(2)}) collective-permute-start(bf16[128,640]{1,0:T(8,128)(2,1)} %multiply_convert_fusion.1), channel_id=1, source_target_pairs={{0,4},{1,5},{2,6},{3,7},{4,8},{5,9},{6,10},{7,11},{8,12},{9,13},{1... | collective-permute-start | bytes 491528 | tf_op jit(solution)/shard_map/ppermute | solution.py:10
  48.1 8.9 %collective-permute-start.10 = (bf16[128,640]{1,0:T(8,128)(2,1)}, bf16[128,640]{1,0:T(8,128)(2,1)S(1)}, u32[]{:S(2)}, u32[]{:S(2)}) collective-permute-start(bf16[128,640]{1,0:T(8,128)(2,1)} %multiply_convert_fusion.1), channel_id=1, source_target_pairs={{4,0},{5,1},{6,2},{7,3},{8,4},{9,5},{10,6},{11,7},{12,8},{13,9},{1... | collective-permute-start | bytes 491528 | tf_op jit(solution)/shard_map/ppermute | solution.py:10
  49.4 15.5 %collective-permute-start.11 = (bf16[128,640]{1,0:T(8,128)(2,1)}, bf16[128,640]{1,0:T(8,128)(2,1)S(1)}, u32[]{:S(2)}, u32[]{:S(2)}) collective-permute-start(bf16[128,640]{1,0:T(8,128)(2,1)} %multiply_convert_fusion.1), channel_id=1, source_target_pairs={{8,0},{9,1},{10,2},{11,3},{12,4},{13,5},{14,6},{15,7},{16,8},{17,9... | collective-permute-start | bytes 491528 | tf_op jit(solution)/shard_map/ppermute | solution.py:10
  70.6 2.3 %collective-permute-start.12 = (f32[8,128]{1,0:T(8,128)S(1)}, f32[8,128]{1,0:T(8,128)S(1)}, u32[]{:S(2)}, u32[]{:S(2)}) collective-permute-start(f32[8,128]{1,0:T(8,128)S(1)} %broadcast_in_dim.13), channel_id=1, source_target_pairs={{0,1},{1,0},{2,3},{3,2},{4,5},{5,4},{6,7},{7,6},{8,9},{9,8},{10,11... | collective-permute-start | bytes 12296 | tf_op jit(solution)/shard_map/ppermute | solution.py:15
  73.5 3.7 %collective-permute-start.13 = (f32[8,128]{1,0:T(8,128)S(1)}, f32[8,128]{1,0:T(8,128)S(1)}, u32[]{:S(2)}, u32[]{:S(2)}) collective-permute-start(f32[8,128]{1,0:T(8,128)S(1)} %broadcast_add_fusion), channel_id=1, source_target_pairs={{0,2},{1,3},{2,0},{3,1},{4,6},{5,7},{6,4},{7,5},{8,10},{9,11},{10,... | collective-permute-start | bytes 12296 | tf_op jit(solution)/shard_map/ppermute | solution.py:15
  77.9 3.7 %collective-permute-start.14 = (f32[8,128]{1,0:T(8,128)S(1)}, f32[8,128]{1,0:T(8,128)S(1)}, u32[]{:S(2)}, u32[]{:S(2)}) collective-permute-start(f32[8,128]{1,0:T(8,128)S(1)} %fusion.66), channel_id=1, source_target_pairs={{0,16},{1,17},{2,18},{3,19},{4,20},{5,21},{6,22},{7,23},{8,24},{9,... | collective-permute-start | bytes 12296 | tf_op jit(solution)/shard_map/ppermute | solution.py:15
  81.6 5.0 %collective-permute-start.15 = (f32[8,128]{1,0:T(8,128)S(1)}, f32[8,128]{1,0:T(8,128)S(1)}, u32[]{:S(2)}, u32[]{:S(2)}) collective-permute-start(f32[8,128]{1,0:T(8,128)S(1)} %add.278), channel_id=1, source_target_pairs={{0,64},{1,65},{2,66},{3,67},{4,68},{5,69},{6,70},{7,71},{8,72},{9,... | collective-permute-start | bytes 12296 | tf_op jit(solution)/shard_map/ppermute | solution.py:15
  86.6 20.6 %collective-permute-start.16 = (f32[8,128]{1,0:T(8,128)S(1)}, f32[8,128]{1,0:T(8,128)S(1)}, u32[]{:S(2)}, u32[]{:S(2)}) collective-permute-start(f32[8,128]{1,0:T(8,128)S(1)} %add.279), channel_id=1, source_target_pairs={{0,4},{1,5},{2,6},{3,7},{4,0},{5,1},{6,2},{7,3},{8,12},{9,13},{10,... | collective-permute-start | bytes 12296 | tf_op jit(solution)/shard_map/ppermute | solution.py:15
  87.4 42.4 %collective-permute-start.20 = (bf16[128,640]{1,0:T(8,128)(2,1)}, bf16[128,640]{1,0:T(8,128)(2,1)}, u32[]{:S(2)}, u32[]{:S(2)}) collective-permute-start(bf16[128,640]{1,0:T(8,128)(2,1)} %add_convert_fusion.1), channel_id=1, source_target_pairs={{8,0},{9,1},{10,2},{11,3},{12,4},{13,5},{14,6},{15,7},{16,8},{17,9... | collective-permute-start | bytes 491528 | tf_op jit(solution)/shard_map/ppermute | solution.py:10
  88.7 42.6 %collective-permute-start.21 = (bf16[128,640]{1,0:T(8,128)(2,1)}, bf16[128,640]{1,0:T(8,128)(2,1)}, u32[]{:S(2)}, u32[]{:S(2)}) collective-permute-start(bf16[128,640]{1,0:T(8,128)(2,1)} %add_convert_fusion.1), channel_id=1, source_target_pairs={{4,0},{5,1},{6,2},{7,3},{8,4},{9,5},{10,6},{11,7},{12,8},{13,9},{1... | collective-permute-start | bytes 491528 | tf_op jit(solution)/shard_map/ppermute | solution.py:10
  90.0 42.4 %collective-permute-start.22 = (bf16[128,640]{1,0:T(8,128)(2,1)}, bf16[128,640]{1,0:T(8,128)(2,1)}, u32[]{:S(2)}, u32[]{:S(2)}) collective-permute-start(bf16[128,640]{1,0:T(8,128)(2,1)} %add_convert_fusion.1), channel_id=1, source_target_pairs={{0,4},{1,5},{2,6},{3,7},{4,8},{5,9},{6,10},{7,11},{8,12},{9,13},{1... | collective-permute-start | bytes 491528 | tf_op jit(solution)/shard_map/ppermute | solution.py:10
  96.1 37.2 %collective-permute-start.23 = (bf16[128,640]{1,0:T(8,128)(2,1)}, bf16[128,640]{1,0:T(8,128)(2,1)}, u32[]{:S(2)}, u32[]{:S(2)}) collective-permute-start(bf16[128,640]{1,0:T(8,128)(2,1)} %add_convert_fusion.1), channel_id=1, source_target_pairs={{0,8},{1,9},{2,10},{3,11},{4,12},{5,13},{6,14},{7,15},{8,16},{9,17... | collective-permute-start | bytes 491528 | tf_op jit(solution)/shard_map/ppermute | solution.py:10
  107.3 5.6 %collective-permute-start.17 = (f32[8,128]{1,0:T(8,128)S(1)}, f32[8,128]{1,0:T(8,128)S(1)}, u32[]{:S(2)}, u32[]{:S(2)}) collective-permute-start(f32[8,128]{1,0:T(8,128)S(1)} %add.280), channel_id=1, source_target_pairs={{0,32},{1,33},{2,34},{3,35},{4,36},{5,37},{6,38},{7,39},{8,40},{9,... | collective-permute-start | bytes 12296 | tf_op jit(solution)/shard_map/ppermute | solution.py:15
  112.9 9.5 %collective-permute-start.18 = (f32[8,128]{1,0:T(8,128)S(1)}, f32[8,128]{1,0:T(8,128)S(1)}, u32[]{:S(2)}, u32[]{:S(2)}) collective-permute-start(f32[8,128]{1,0:T(8,128)S(1)} %add.281), channel_id=1, source_target_pairs={{0,128},{1,129},{2,130},{3,131},{4,132},{5,133},{6,134},{7,135},{8... | collective-permute-start | bytes 12296 | tf_op jit(solution)/shard_map/ppermute | solution.py:15
  122.4 7.5 %collective-permute-start.19 = (f32[8,128]{1,0:T(8,128)S(1)}, f32[8,128]{1,0:T(8,128)S(1)}, u32[]{:S(2)}, u32[]{:S(2)}) collective-permute-start(f32[8,128]{1,0:T(8,128)S(1)} %add.282), channel_id=1, source_target_pairs={{0,8},{1,9},{2,10},{3,11},{4,12},{5,13},{6,14},{7,15},{8,0},{9,1},... | collective-permute-start | bytes 12296 | tf_op jit(solution)/shard_map/ppermute | solution.py:15
  129.9 7.7 %collective-permute-start.37 = (bf16[64,5,640]{2,0,1:T(8,128)(2,1)S(1)}, bf16[64,5,640]{2,0,1:T(8,128)(2,1)S(1)}, u32[]{:S(2)}, u32[]{:S(2)}) collective-permute-start(bf16[64,5,640]{2,0,1:T(8,128)(2,1)S(1)} %get-tuple-element.18), channel_id=1, source_target_pairs={{0,1},{1,0},{2,3},{3,2},{4,5},{5,4},{6,7},{7,6},{8,9},{9,8},{10,11... | collective-permute-start | bytes 1228808 | tf_op jit(solution)/shard_map/ppermute | solution.py:15
  129.9 7.7 %collective-permute-start.36 = (bf16[64,5,640]{2,0,1:T(8,128)(2,1)S(1)}, bf16[64,5,640]{2,0,1:T(8,128)(2,1)S(1)}, u32[]{:S(2)}, u32[]{:S(2)}) collective-permute-start(bf16[64,5,640]{2,0,1:T(8,128)(2,1)S(1)} %get-tuple-element.17), channel_id=1, source_target_pairs={{0,1},{1,0},{2,3},{3,2},{4,5},{5,4},{6,7},{7,6},{8,9},{9,8},{10,11... | collective-permute-start | bytes 1228808 | tf_op jit(solution)/shard_map/ppermute | solution.py:15
  136.9 3.6 %collective-permute-start.25 = (bf16[64,5,640]{2,0,1:T(8,128)(2,1)S(1)}, bf16[64,5,640]{2,0,1:T(8,128)(2,1)S(1)}, u32[]{:S(2)}, u32[]{:S(2)}) collective-permute-start(bf16[64,5,640]{2,0,1:T(8,128)(2,1)S(1)} %get-tuple-element.20), channel_id=1, source_target_pairs={{0,1},{1,0},{2,3},{3,2},{4,5},{5,4},{6,7},{7,6},{8,9},{9,8},{10,11... | collective-permute-start | bytes 1228808 | tf_op jit(solution)/shard_map/ppermute | solution.py:15
  137.1 3.4 %collective-permute-start.24 = (bf16[64,5,640]{2,0,1:T(8,128)(2,1)S(1)}, bf16[64,5,640]{2,0,1:T(8,128)(2,1)S(1)}, u32[]{:S(2)}, u32[]{:S(2)}) collective-permute-start(bf16[64,5,640]{2,0,1:T(8,128)(2,1)S(1)} %get-tuple-element.19), channel_id=1, source_target_pairs={{0,1},{1,0},{2,3},{3,2},{4,5},{5,4},{6,7},{7,6},{8,9},{9,8},{10,11... | collective-permute-start | bytes 1228808 | tf_op jit(solution)/shard_map/ppermute | solution.py:15
  138.5 8.3 %collective-permute-start.39 = (bf16[32,5,640]{2,0,1:T(8,128)(2,1)}, bf16[32,5,640]{2,0,1:T(8,128)(2,1)}, u32[]{:S(2)}, u32[]{:S(2)}) collective-permute-start(bf16[32,5,640]{2,0,1:T(8,128)(2,1)} %get-tuple-element.22), channel_id=1, source_target_pairs={{0,2},{1,3},{2,0},{3,1},{4,6},{5,7},{6,4},{7,5},{8,10},{9,11},{10,... | collective-permute-start | bytes 614408 | tf_op jit(solution)/shard_map/ppermute | solution.py:15
  138.7 12.4 %collective-permute-start.38 = (bf16[32,5,640]{2,0,1:T(8,128)(2,1)S(1)}, bf16[32,5,640]{2,0,1:T(8,128)(2,1)}, u32[]{:S(2)}, u32[]{:S(2)}) collective-permute-start(bf16[32,5,640]{2,0,1:T(8,128)(2,1)S(1)} %get-tuple-element.21), channel_id=1, source_target_pairs={{0,2},{1,3},{2,0},{3,1},{4,6},{5,7},{6,4},{7,5},{8,10},{9,11},{10,... | collective-permute-start | bytes 614408 | tf_op jit(solution)/shard_map/ppermute | solution.py:15
  142.7 12.8 %collective-permute-start.27 = (bf16[32,5,640]{2,0,1:T(8,128)(2,1)}, bf16[32,5,640]{2,0,1:T(8,128)(2,1)}, u32[]{:S(2)}, u32[]{:S(2)}) collective-permute-start(bf16[32,5,640]{2,0,1:T(8,128)(2,1)} %get-tuple-element.24), channel_id=1, source_target_pairs={{0,2},{1,3},{2,0},{3,1},{4,6},{5,7},{6,4},{7,5},{8,10},{9,11},{10,... | collective-permute-start | bytes 614408 | tf_op jit(solution)/shard_map/ppermute | solution.py:15
  142.9 16.1 %collective-permute-start.26 = (bf16[32,5,640]{2,0,1:T(8,128)(2,1)}, bf16[32,5,640]{2,0,1:T(8,128)(2,1)}, u32[]{:S(2)}, u32[]{:S(2)}) collective-permute-start(bf16[32,5,640]{2,0,1:T(8,128)(2,1)} %get-tuple-element.23), channel_id=1, source_target_pairs={{0,2},{1,3},{2,0},{3,1},{4,6},{5,7},{6,4},{7,5},{8,10},{9,11},{10,... | collective-permute-start | bytes 614408 | tf_op jit(solution)/shard_map/ppermute | solution.py:15
  160.8 5.8 %collective-permute-start.29 = (bf16[16,5,640]{2,0,1:T(8,128)(2,1)S(1)}, bf16[16,5,640]{2,0,1:T(8,128)(2,1)S(1)}, u32[]{:S(2)}, u32[]{:S(2)}) collective-permute-start(bf16[16,5,640]{2,0,1:T(8,128)(2,1)S(1)} %get-tuple-element.28), channel_id=1, source_target_pairs={{0,16},{1,17},{2,18},{3,19},{4,20},{5,21},{6,22},{7,23},{8,24},{9,... | collective-permute-start | bytes 307208 | tf_op jit(solution)/shard_map/ppermute | solution.py:15
  160.9 7.9 %collective-permute-start.28 = (bf16[16,5,640]{2,0,1:T(8,128)(2,1)S(1)}, bf16[16,5,640]{2,0,1:T(8,128)(2,1)S(1)}, u32[]{:S(2)}, u32[]{:S(2)}) collective-permute-start(bf16[16,5,640]{2,0,1:T(8,128)(2,1)S(1)} %get-tuple-element.27), channel_id=1, source_target_pairs={{0,16},{1,17},{2,18},{3,19},{4,20},{5,21},{6,22},{7,23},{8,24},{9,... | collective-permute-start | bytes 307208 | tf_op jit(solution)/shard_map/ppermute | solution.py:15
  163.0 8.1 %collective-permute-start.41 = (bf16[16,5,640]{2,0,1:T(8,128)(2,1)S(1)}, bf16[16,5,640]{2,0,1:T(8,128)(2,1)S(1)}, u32[]{:S(2)}, u32[]{:S(2)}) collective-permute-start(bf16[16,5,640]{2,0,1:T(8,128)(2,1)S(1)} %get-tuple-element.26), channel_id=1, source_target_pairs={{0,16},{1,17},{2,18},{3,19},{4,20},{5,21},{6,22},{7,23},{8,24},{9,... | collective-permute-start | bytes 307208 | tf_op jit(solution)/shard_map/ppermute | solution.py:15
  163.4 8.1 %collective-permute-start.40 = (bf16[16,5,640]{2,0,1:T(8,128)(2,1)S(1)}, bf16[16,5,640]{2,0,1:T(8,128)(2,1)S(1)}, u32[]{:S(2)}, u32[]{:S(2)}) collective-permute-start(bf16[16,5,640]{2,0,1:T(8,128)(2,1)S(1)} %get-tuple-element.25), channel_id=1, source_target_pairs={{0,16},{1,17},{2,18},{3,19},{4,20},{5,21},{6,22},{7,23},{8,24},{9,... | collective-permute-start | bytes 307208 | tf_op jit(solution)/shard_map/ppermute | solution.py:15
  168.9 4.8 %collective-permute-start.31 = (bf16[8,5,640]{2,0,1:T(8,128)(2,1)S(1)}, bf16[8,5,640]{2,0,1:T(8,128)(2,1)S(1)}, u32[]{:S(2)}, u32[]{:S(2)}) collective-permute-start(bf16[8,5,640]{2,0,1:T(8,128)(2,1)S(1)} %get-tuple-element.32), channel_id=1, source_target_pairs={{0,64},{1,65},{2,66},{3,67},{4,68},{5,69},{6,70},{7,71},{8,72},{9,... | collective-permute-start | bytes 153608 | tf_op jit(solution)/shard_map/ppermute | solution.py:15
  170.7 4.5 %collective-permute-start.30 = (bf16[8,5,640]{2,0,1:T(8,128)(2,1)S(1)}, bf16[8,5,640]{2,0,1:T(8,128)(2,1)S(1)}, u32[]{:S(2)}, u32[]{:S(2)}) collective-permute-start(bf16[8,5,640]{2,0,1:T(8,128)(2,1)S(1)} %get-tuple-element.31), channel_id=1, source_target_pairs={{0,64},{1,65},{2,66},{3,67},{4,68},{5,69},{6,70},{7,71},{8,72},{9,... | collective-permute-start | bytes 153608 | tf_op jit(solution)/shard_map/ppermute | solution.py:15
  171.6 4.2 %collective-permute-start.43 = (bf16[8,5,640]{2,0,1:T(8,128)(2,1)S(1)}, bf16[8,5,640]{2,0,1:T(8,128)(2,1)S(1)}, u32[]{:S(2)}, u32[]{:S(2)}) collective-permute-start(bf16[8,5,640]{2,0,1:T(8,128)(2,1)S(1)} %get-tuple-element.30), channel_id=1, source_target_pairs={{0,64},{1,65},{2,66},{3,67},{4,68},{5,69},{6,70},{7,71},{8,72},{9,... | collective-permute-start | bytes 153608 | tf_op jit(solution)/shard_map/ppermute | solution.py:15
  173.3 4.1 %collective-permute-start.42 = (bf16[8,5,640]{2,0,1:T(8,128)(2,1)S(1)}, bf16[8,5,640]{2,0,1:T(8,128)(2,1)S(1)}, u32[]{:S(2)}, u32[]{:S(2)}) collective-permute-start(bf16[8,5,640]{2,0,1:T(8,128)(2,1)S(1)} %get-tuple-element.29), channel_id=1, source_target_pairs={{0,64},{1,65},{2,66},{3,67},{4,68},{5,69},{6,70},{7,71},{8,72},{9,... | collective-permute-start | bytes 153608 | tf_op jit(solution)/shard_map/ppermute | solution.py:15
  175.2 5.1 %collective-permute-start.32 = (bf16[8,5,640]{2,0,1:T(8,128)(2,1)S(1)}, bf16[8,5,640]{2,0,1:T(8,128)(2,1)S(1)}, u32[]{:S(2)}, u32[]{:S(2)}) collective-permute-start(bf16[8,5,640]{2,0,1:T(8,128)(2,1)S(1)} %dynamic-slice_convert_fusion.9), channel_id=1, source_target_pairs={{0,4},{1,5},{2,6},{3,7},{4,0},{5,1},{6,2},{7,3},{8,12},{9,13},{10,... | collective-permute-start | bytes 153608 | tf_op jit(solution)/shard_map/ppermute | solution.py:15
  177.5 5.5 %collective-permute-start.44 = (bf16[8,5,640]{2,0,1:T(8,128)(2,1)S(1)}, bf16[8,5,640]{2,0,1:T(8,128)(2,1)S(1)}, u32[]{:S(2)}, u32[]{:S(2)}) collective-permute-start(bf16[8,5,640]{2,0,1:T(8,128)(2,1)S(1)} %dynamic-slice_convert_fusion.8), channel_id=1, source_target_pairs={{0,4},{1,5},{2,6},{3,7},{4,0},{5,1},{6,2},{7,3},{8,12},{9,13},{10,... | collective-permute-start | bytes 153608 | tf_op jit(solution)/shard_map/ppermute | solution.py:15
  180.3 5.4 %collective-permute-start.33 = (bf16[4,5,640]{2,0,1:T(4,128)(2,1)S(1)}, bf16[4,5,640]{2,0,1:T(4,128)(2,1)S(1)}, u32[]{:S(2)}, u32[]{:S(2)}) collective-permute-start(bf16[4,5,640]{2,0,1:T(4,128)(2,1)S(1)} %dynamic-slice_convert_fusion.11), channel_id=1, source_target_pairs={{0,32},{1,33},{2,34},{3,35},{4,36},{5,37},{6,38},{7,39},{8,40},{9,... | collective-permute-start | bytes 76808 | tf_op jit(solution)/shard_map/ppermute | solution.py:15
  183.0 5.9 %collective-permute-start.45 = (bf16[4,5,640]{2,0,1:T(4,128)(2,1)S(1)}, bf16[4,5,640]{2,0,1:T(4,128)(2,1)S(1)}, u32[]{:S(2)}, u32[]{:S(2)}) collective-permute-start(bf16[4,5,640]{2,0,1:T(4,128)(2,1)S(1)} %dynamic-slice_convert_fusion.10), channel_id=1, source_target_pairs={{0,32},{1,33},{2,34},{3,35},{4,36},{5,37},{6,38},{7,39},{8,40},{9,... | collective-permute-start | bytes 76808 | tf_op jit(solution)/shard_map/ppermute | solution.py:15
  185.8 5.4 %collective-permute-start.34 = (bf16[2,5,640]{2,0,1:T(2,128)(2,1)S(1)}, bf16[2,5,640]{2,0,1:T(2,128)(2,1)S(1)}, u32[]{:S(2)}, u32[]{:S(2)}) collective-permute-start(bf16[2,5,640]{2,0,1:T(2,128)(2,1)S(1)} %dynamic-slice_convert_fusion.13), channel_id=1, source_target_pairs={{0,128},{1,129},{2,130},{3,131},{4,132},{5,133},{6,134},{7,135},{8... | collective-permute-start | bytes 38408 | tf_op jit(solution)/shard_map/ppermute | solution.py:15
  188.9 7.1 %collective-permute-start.46 = (bf16[2,5,640]{2,0,1:T(2,128)(2,1)S(1)}, bf16[2,5,640]{2,0,1:T(2,128)(2,1)S(1)}, u32[]{:S(2)}, u32[]{:S(2)}) collective-permute-start(bf16[2,5,640]{2,0,1:T(2,128)(2,1)S(1)} %dynamic-slice_convert_fusion.12), channel_id=1, source_target_pairs={{0,128},{1,129},{2,130},{3,131},{4,132},{5,133},{6,134},{7,135},{8... | collective-permute-start | bytes 38408 | tf_op jit(solution)/shard_map/ppermute | solution.py:15
  191.2 7.7 %collective-permute-start.35 = (bf16[1,5,640]{2,0,1:T(2,128)(2,1)S(1)}, bf16[1,5,640]{2,0,1:T(2,128)(2,1)S(1)}, u32[]{:S(2)}, u32[]{:S(2)}) collective-permute-start(bf16[1,5,640]{2,0,1:T(2,128)(2,1)S(1)} %dynamic-slice_convert_fusion.15), channel_id=1, source_target_pairs={{0,8},{1,9},{2,10},{3,11},{4,12},{5,13},{6,14},{7,15},{8,0},{9,1},... | collective-permute-start | bytes 19208 | tf_op jit(solution)/shard_map/ppermute | solution.py:15
  196.1 7.7 %collective-permute-start.47 = (bf16[1,5,640]{2,0,1:T(2,128)(2,1)S(1)}, bf16[1,5,640]{2,0,1:T(2,128)(2,1)S(1)}, u32[]{:S(2)}, u32[]{:S(2)}) collective-permute-start(bf16[1,5,640]{2,0,1:T(2,128)(2,1)S(1)} %dynamic-slice_convert_fusion.14), channel_id=1, source_target_pairs={{0,8},{1,9},{2,10},{3,11},{4,12},{5,13},{6,14},{7,15},{8,0},{9,1},... | collective-permute-start | bytes 19208 | tf_op jit(solution)/shard_map/ppermute | solution.py:15
  (9 other events, 142.6 us)

commit v14 on v12

--- a/solution.py
+++ b/solution.py
@@ -60,7 +60,7 @@
             lax.dynamic_slice_in_dim(b, (1 - upper) * half, half, 0).astype(jnp.bfloat16)
             for b in blocks
         ]
-        pieces = 2 if half >= 16 else 1
+        pieces = 2 if half >= 32 else 1
         parts = [jnp.split(s, pieces, 0) for s in send]
         got_parts, got_extra = swap_with((parts, extra), axis, bit)
         got = [jnp.concatenate(g, 0) if pieces > 1 else g[0] for g in got_parts]

time: 198 us -> 197 us (level)
    ppermute x40 -> x38, waiting for transfers between devices: 43.9 us -> 44.7 us  [swap_with(): return lax.ppermute(block, axis, [(i, i ^ bit) for i in range(devices)])]
    ppermute x40 -> x38, starting transfers between devices: 64.4 us -> 63.6 us  [swap_with(): return lax.ppermute(block, axis, [(i, i ^ bit) for i in range(devices)])]
  transfers between devices with their start and end apart: 48 -> 46, of which waited for: 22 -> 22; matrix products, arithmetic and copies ran while one was open for 13% -> 13% of each run, Pallas kernels for 0% -> 0%
where the time goes in v14:
time: 197 us
  starting transfers between devices  96.2 us (49%)
  waiting for transfers between devices  56 us (28%)
  local copies, waits for them, and re-layouts  16 us (8%)
  other arithmetic  14.1 us (7%)
  matrix products  9.85 us (5%)
  between operations  4.61 us (2%)
    ppermute x38, starting transfers between devices, swap_with(): return lax.ppermute(block, axis, [(i, i ^ bit) for i in range(devices)])  63.6 us
    ppermute x38, waiting for transfers between devices, swap_with(): return lax.ppermute(block, axis, [(i, i ^ bit) for i in range(devices)])  44.7 us
    ppermute x8, starting transfers between devices, from_behind(): return lax.ppermute(block, axis, route)  32.6 us
    ppermute x8, waiting for transfers between devices, from_behind(): return lax.ppermute(block, axis, route)  11.3 us
    unnamed x26, local copies, waits for them, and re-layouts  6.24 us
  transfers between devices with their start and end apart: 46, of which 22 were waited for; matrix products, arithmetic and copies ran while one was open for 13% of the time, Pallas kernels for 0%

profile of v14, /device:TPU:32, one launch (start us, length us, event | category | flops | bytes accessed | tf_op | source)
XLA Modules:
  0.0 196.8 jit_solution(10518151428041508604)
XLA Ops:
  0.6 1.4 convert_reduce_fusion.1
  5.1 1.4 fusion.9
  6.5 1.9 fusion.51
  9.3 1.9 collective-permute-start.1
  12.1 7.4 %collective-permute-start.8 = (bf16[128,640]{1,0:T(8,128)(2,1)}, bf16[128,640]{1,0:T(8,128)(2,1)S(1)}, u32[]{:S(2)}, u32[]{:S(2)}) collective-permute-start(bf16[128,640]{1,0:T(8,128)(2,1)} %multiply_convert_fusion.1), channel_id=1, source_target_pairs={{0,8},{1,9},{2,10},{3,11},{4,12},{5,13},{6,14},{7,15},{8,16},{9,17... | collective-permute-start | bytes 491528 | tf_op jit(solution)/shard_map/ppermute | solution.py:10
  20.2 1.6 collective-permute-start.2
  21.8 2.1 %collective-permute-done.2 = f32[8,128]{1,0:T(8,128)S(1)} collective-permute-done((f32[8,128]{1,0:T(8,128)S(1)}, f32[8,128]{1,0:T(8,128)S(1)}, u32[]{:S(2)}, u32[]{:S(2)}) %collective-permute-start.2) | collective-permute-done | bytes 4128 | tf_op jit(solution)/shard_map/ppermute | solution.py:15
  23.9 1.6 collective-permute-start.3
  25.4 2.0 %collective-permute-done.3 = f32[8,128]{1,0:T(8,128)S(1)} collective-permute-done((f32[8,128]{1,0:T(8,128)S(1)}, f32[8,128]{1,0:T(8,128)S(1)}, u32[]{:S(2)}, u32[]{:S(2)}) %collective-permute-start.3) | collective-permute-done | bytes 4128 | tf_op jit(solution)/shard_map/ppermute | solution.py:15
  27.5 1.5 collective-permute-start.4
  29.0 3.0 %collective-permute-done.4 = f32[8,128]{1,0:T(8,128)S(1)} collective-permute-done((f32[8,128]{1,0:T(8,128)S(1)}, f32[8,128]{1,0:T(8,128)S(1)}, u32[]{:S(2)}, u32[]{:S(2)}) %collective-permute-start.4) | collective-permute-done | bytes 4128 | tf_op jit(solution)/shard_map/ppermute | solution.py:15
  32.0 3.0 %collective-permute-start.5 = (f32[8,128]{1,0:T(8,128)S(1)}, f32[8,128]{1,0:T(8,128)S(1)}, u32[]{:S(2)}, u32[]{:S(2)}) collective-permute-start(f32[8,128]{1,0:T(8,128)S(1)} %add.261), channel_id=1, source_target_pairs={{0,32},{1,33},{2,34},{3,35},{4,36},{5,37},{6,38},{7,39},{8,40},{9,... | collective-permute-start | bytes 12296 | tf_op jit(solution)/shard_map/ppermute | solution.py:15
  35.0 2.1 %collective-permute-done.5 = f32[8,128]{1,0:T(8,128)S(1)} collective-permute-done((f32[8,128]{1,0:T(8,128)S(1)}, f32[8,128]{1,0:T(8,128)S(1)}, u32[]{:S(2)}, u32[]{:S(2)}) %collective-permute-start.5) | collective-permute-done | bytes 4128 | tf_op jit(solution)/shard_map/ppermute | solution.py:15
  37.1 3.2 %collective-permute-start.6 = (f32[8,128]{1,0:T(8,128)S(1)}, f32[8,128]{1,0:T(8,128)S(1)}, u32[]{:S(2)}, u32[]{:S(2)}) collective-permute-start(f32[8,128]{1,0:T(8,128)S(1)} %add.262), channel_id=1, source_target_pairs={{0,128},{1,129},{2,130},{3,131},{4,132},{5,133},{6,134},{7,135},{8... | collective-permute-start | bytes 12296 | tf_op jit(solution)/shard_map/ppermute | solution.py:15
  40.3 1.9 collective-permute-done.6
  42.6 5.5 %collective-permute-start.9 = (bf16[128,640]{1,0:T(8,128)(2,1)}, bf16[128,640]{1,0:T(8,128)(2,1)}, u32[]{:S(2)}, u32[]{:S(2)}) collective-permute-start(bf16[128,640]{1,0:T(8,128)(2,1)} %multiply_convert_fusion.1), channel_id=1, source_target_pairs={{0,4},{1,5},{2,6},{3,7},{4,8},{5,9},{6,10},{7,11},{8,12},{9,13},{1... | collective-permute-start | bytes 491528 | tf_op jit(solution)/shard_map/ppermute | solution.py:10
  53.6 3.4 %collective-permute-done.10 = bf16[128,640]{1,0:T(8,128)(2,1)S(1)} collective-permute-done((bf16[128,640]{1,0:T(8,128)(2,1)}, bf16[128,640]{1,0:T(8,128)(2,1)S(1)}, u32[]{:S(2)}, u32[]{:S(2)}) %collective-permute-start.10) | collective-permute-done | bytes 163872 | tf_op jit(solution)/shard_map/ppermute | solution.py:10
  57.0 7.9 %collective-permute-done.11 = bf16[128,640]{1,0:T(8,128)(2,1)S(1)} collective-permute-done((bf16[128,640]{1,0:T(8,128)(2,1)}, bf16[128,640]{1,0:T(8,128)(2,1)S(1)}, u32[]{:S(2)}, u32[]{:S(2)}) %collective-permute-start.11) | collective-permute-done | bytes 163872 | tf_op jit(solution)/shard_map/ppermute | solution.py:10
  65.0 3.1 %fusion.52 = (f32[128]{0:T(128)S(1)}, f32[128,640]{1,0:T(8,128)S(1)}) fusion(bf16[5,128,640]{2,1,0:T(8,128)(2,1)S(1)} %bitcast_dynamic-update-slice_fusion.5, bf16[5,640,640]{2,1,0:T(8,128)(2,1)} %param.13), kind=kOutput, calls=%fused_computation.134 | convolution fusion | flops 524369792 | bytes 5243392 | tf_op jit(solution)/shard_map/krc,kcb->rb/dot_general | solution.py:104
  74.8 1.3 collective-permute-start.21
  76.1 6.1 %collective-permute-start.22 = (bf16[128,640]{1,0:T(8,128)(2,1)}, bf16[128,640]{1,0:T(8,128)(2,1)}, u32[]{:S(2)}, u32[]{:S(2)}) collective-permute-start(bf16[128,640]{1,0:T(8,128)(2,1)} %add_convert_fusion.1), channel_id=1, source_target_pairs={{0,4},{1,5},{2,6},{3,7},{4,8},{5,9},{6,10},{7,11},{8,12},{9,13},{1... | collective-permute-start | bytes 491528 | tf_op jit(solution)/shard_map/ppermute | solution.py:10
  82.3 8.5 %collective-permute-start.23 = (bf16[128,640]{1,0:T(8,128)(2,1)}, bf16[128,640]{1,0:T(8,128)(2,1)}, u32[]{:S(2)}, u32[]{:S(2)}) collective-permute-start(bf16[128,640]{1,0:T(8,128)(2,1)} %add_convert_fusion.1), channel_id=1, source_target_pairs={{0,8},{1,9},{2,10},{3,11},{4,12},{5,13},{6,14},{7,15},{8,16},{9,17... | collective-permute-start | bytes 491528 | tf_op jit(solution)/shard_map/ppermute | solution.py:10
  100.8 1.5 multiply_reduce_fusion
  105.0 1.9 collective-permute-start.38
  109.3 1.9 collective-permute-start.27
  112.0 3.6 %collective-permute-start.14 = (f32[8,128]{1,0:T(8,128)S(1)}, f32[8,128]{1,0:T(8,128)S(1)}, u32[]{:S(2)}, u32[]{:S(2)}) collective-permute-start(f32[8,128]{1,0:T(8,128)S(1)} %fusion.64), channel_id=1, source_target_pairs={{0,16},{1,17},{2,18},{3,19},{4,20},{5,21},{6,22},{7,23},{8,24},{9,... | collective-permute-start | bytes 12296 | tf_op jit(solution)/shard_map/ppermute | solution.py:15
  115.6 1.6 collective-permute-done.14
  117.2 8.0 %collective-permute-start.15 = (f32[8,128]{1,0:T(8,128)S(1)}, f32[8,128]{1,0:T(8,128)S(1)}, u32[]{:S(2)}, u32[]{:S(2)}) collective-permute-start(f32[8,128]{1,0:T(8,128)S(1)} %add.278), channel_id=1, source_target_pairs={{0,64},{1,65},{2,66},{3,67},{4,68},{5,69},{6,70},{7,71},{8,72},{9,... | collective-permute-start | bytes 12296 | tf_op jit(solution)/shard_map/ppermute | solution.py:15
  125.1 1.6 collective-permute-done.15
  126.9 4.3 %collective-permute-done.16 = f32[8,128]{1,0:T(8,128)S(1)} collective-permute-done((f32[8,128]{1,0:T(8,128)S(1)}, f32[8,128]{1,0:T(8,128)S(1)}, u32[]{:S(2)}, u32[]{:S(2)}) %collective-permute-start.16) | collective-permute-done | bytes 4128 | tf_op jit(solution)/shard_map/ppermute | solution.py:15
  131.6 4.8 %collective-permute-done.17 = f32[8,128]{1,0:T(8,128)S(1)} collective-permute-done((f32[8,128]{1,0:T(8,128)S(1)}, f32[8,128]{1,0:T(8,128)S(1)}, u32[]{:S(2)}, u32[]{:S(2)}) %collective-permute-start.17) | collective-permute-done | bytes 4128 | tf_op jit(solution)/shard_map/ppermute | solution.py:15
  136.3 5.8 %collective-permute-start.18 = (f32[8,128]{1,0:T(8,128)S(1)}, f32[8,128]{1,0:T(8,128)S(1)}, u32[]{:S(2)}, u32[]{:S(2)}) collective-permute-start(f32[8,128]{1,0:T(8,128)S(1)} %add.281), channel_id=1, source_target_pairs={{0,128},{1,129},{2,130},{3,131},{4,132},{5,133},{6,134},{7,135},{8... | collective-permute-start | bytes 12296 | tf_op jit(solution)/shard_map/ppermute | solution.py:15
  142.2 1.6 collective-permute-done.18
  144.1 7.1 %collective-permute-done.19 = f32[8,128]{1,0:T(8,128)S(1)} collective-permute-done((f32[8,128]{1,0:T(8,128)S(1)}, f32[8,128]{1,0:T(8,128)S(1)}, u32[]{:S(2)}, u32[]{:S(2)}) %collective-permute-start.19) | collective-permute-done | bytes 4128 | tf_op jit(solution)/shard_map/ppermute | solution.py:15
  153.2 1.7 convert_add_fusion.2
  155.0 2.0 %collective-permute-start.28 = (bf16[16,5,640]{2,0,1:T(8,128)(2,1)S(1)}, bf16[16,5,640]{2,0,1:T(8,128)(2,1)S(1)}, u32[]{:S(2)}, u32[]{:S(2)}) collective-permute-start(bf16[16,5,640]{2,0,1:T(8,128)(2,1)S(1)} %get-tuple-element.23), channel_id=1, source_target_pairs={{0,16},{1,17},{2,18},{3,19},{4,20},{5,21},{6,22},{7,23},{8,24},{9,... | collective-permute-start | bytes 307208 | tf_op jit(solution)/shard_map/ppermute | solution.py:15
  157.3 1.9 collective-permute-start.39
  160.9 1.8 collective-permute-start.30
  163.0 1.8 collective-permute-start.41
  165.8 2.0 %collective-permute-done.41 = bf16[16,5,640]{2,0,1:T(8,128)(2,1)S(1)} collective-permute-done((bf16[16,5,640]{2,0,1:T(8,128)(2,1)S(1)}, bf16[16,5,640]{2,0,1:T(8,128)(2,1)S(1)}, u32[]{:S(2)}, u32[]{:S(2)}) %collective-permute-start.41) | collective-permute-done | bytes 102432 | tf_op jit(solution)/shard_map/ppermute | solution.py:15
  168.8 1.9 collective-permute-done.31
  170.8 2.6 %collective-permute-start.32 = (bf16[4,5,640]{2,0,1:T(4,128)(2,1)S(1)}, bf16[4,5,640]{2,0,1:T(4,128)(2,1)S(1)}, u32[]{:S(2)}, u32[]{:S(2)}) collective-permute-start(bf16[4,5,640]{2,0,1:T(4,128)(2,1)S(1)} %dynamic-slice_convert_fusion.11), channel_id=1, source_target_pairs={{0,32},{1,33},{2,34},{3,35},{4,36},{5,37},{6,38},{7,39},{8,40},{9,... | collective-permute-start | bytes 76808 | tf_op jit(solution)/shard_map/ppermute | solution.py:15
  173.4 2.1 %collective-permute-start.43 = (bf16[4,5,640]{2,0,1:T(4,128)(2,1)S(1)}, bf16[4,5,640]{2,0,1:T(4,128)(2,1)S(1)}, u32[]{:S(2)}, u32[]{:S(2)}) collective-permute-start(bf16[4,5,640]{2,0,1:T(4,128)(2,1)S(1)} %dynamic-slice_convert_fusion.10), channel_id=1, source_target_pairs={{0,32},{1,33},{2,34},{3,35},{4,36},{5,37},{6,38},{7,39},{8,40},{9,... | collective-permute-start | bytes 76808 | tf_op jit(solution)/shard_map/ppermute | solution.py:15
  176.3 3.7 %collective-permute-start.33 = (bf16[2,5,640]{2,0,1:T(2,128)(2,1)S(1)}, bf16[2,5,640]{2,0,1:T(2,128)(2,1)S(1)}, u32[]{:S(2)}, u32[]{:S(2)}) collective-permute-start(bf16[2,5,640]{2,0,1:T(2,128)(2,1)S(1)} %dynamic-slice_convert_fusion.13), channel_id=1, source_target_pairs={{0,128},{1,129},{2,130},{3,131},{4,132},{5,133},{6,134},{7,135},{8... | collective-permute-start | bytes 38408 | tf_op jit(solution)/shard_map/ppermute | solution.py:15
  180.0 2.1 %collective-permute-start.44 = (bf16[2,5,640]{2,0,1:T(2,128)(2,1)S(1)}, bf16[2,5,640]{2,0,1:T(2,128)(2,1)S(1)}, u32[]{:S(2)}, u32[]{:S(2)}) collective-permute-start(bf16[2,5,640]{2,0,1:T(2,128)(2,1)S(1)} %dynamic-slice_convert_fusion.12), channel_id=1, source_target_pairs={{0,128},{1,129},{2,130},{3,131},{4,132},{5,133},{6,134},{7,135},{8... | collective-permute-start | bytes 38408 | tf_op jit(solution)/shard_map/ppermute | solution.py:15
  182.1 5.0 %collective-permute-start.34 = (bf16[1,5,640]{2,0,1:T(2,128)(2,1)S(1)}, bf16[1,5,640]{2,0,1:T(2,128)(2,1)S(1)}, u32[]{:S(2)}, u32[]{:S(2)}) collective-permute-start(bf16[1,5,640]{2,0,1:T(2,128)(2,1)S(1)} %dynamic-slice_convert_fusion.15), channel_id=1, source_target_pairs={{0,8},{1,9},{2,10},{3,11},{4,12},{5,13},{6,14},{7,15},{8,0},{9,1},... | collective-permute-start | bytes 19208 | tf_op jit(solution)/shard_map/ppermute | solution.py:15
  187.2 2.0 %collective-permute-start.45 = (bf16[1,5,640]{2,0,1:T(2,128)(2,1)S(1)}, bf16[1,5,640]{2,0,1:T(2,128)(2,1)S(1)}, u32[]{:S(2)}, u32[]{:S(2)}) collective-permute-start(bf16[1,5,640]{2,0,1:T(2,128)(2,1)S(1)} %dynamic-slice_convert_fusion.14), channel_id=1, source_target_pairs={{0,8},{1,9},{2,10},{3,11},{4,12},{5,13},{6,14},{7,15},{8,0},{9,1},... | collective-permute-start | bytes 19208 | tf_op jit(solution)/shard_map/ppermute | solution.py:15
  190.5 4.5 %collective-permute-done.45 = bf16[1,5,640]{2,0,1:T(2,128)(2,1)S(1)} collective-permute-done((bf16[1,5,640]{2,0,1:T(2,128)(2,1)S(1)}, bf16[1,5,640]{2,0,1:T(2,128)(2,1)S(1)}, u32[]{:S(2)}, u32[]{:S(2)}) %collective-permute-start.45) | collective-permute-done | bytes 6432 | tf_op jit(solution)/shard_map/ppermute | solution.py:15
  (171 shorter events, 41.4 us)
Async XLA Ops:
  0.6 68.2 %copy-start = (bf16[1280,640]{1,0:T(8,128)(2,1)S(1)}, bf16[1280,640]{1,0:T(8,128)(2,1)}, u32[]{:S(2)}) copy-start(bf16[1280,640]{1,0:T(8,128)(2,1)} %param.14) | copy-start | bytes 4915204
  2.7 6.0 %collective-permute-start = (f32[8,128]{1,0:T(8,128)S(1)}, f32[8,128]{1,0:T(8,128)S(1)}, u32[]{:S(2)}, u32[]{:S(2)}) collective-permute-start(f32[8,128]{1,0:T(8,128)S(1)} %broadcast_in_dim.12), channel_id=1, source_target_pairs={{0,1},{1,0},{2,3},{3,2},{4,5},{5,4},{6,7},{7,6},{8,9},{9,8},{10,11... | collective-permute-start | bytes 12296 | tf_op jit(solution)/shard_map/ppermute | solution.py:15
  6.5 44.2 %copy-start.7 = (s32[128]{0:T(128)S(1)}, s32[128]{0:T(128)}, u32[]{:S(2)}) copy-start(s32[128]{0:T(128)} %param.9) | copy-start | bytes 1540
  9.3 10.2 %collective-permute-start.1 = (f32[8,128]{1,0:T(8,128)S(1)}, f32[8,128]{1,0:T(8,128)S(1)}, u32[]{:S(2)}, u32[]{:S(2)}) collective-permute-start(f32[8,128]{1,0:T(8,128)S(1)} %broadcast_add_fusion.1), channel_id=1, source_target_pairs={{0,2},{1,3},{2,0},{3,1},{4,6},{5,7},{6,4},{7,5},{8,10},{9,11},{10,... | collective-permute-start | bytes 12296 | tf_op jit(solution)/shard_map/ppermute | solution.py:15
  12.1 40.3 %collective-permute-start.8 = (bf16[128,640]{1,0:T(8,128)(2,1)}, bf16[128,640]{1,0:T(8,128)(2,1)S(1)}, u32[]{:S(2)}, u32[]{:S(2)}) collective-permute-start(bf16[128,640]{1,0:T(8,128)(2,1)} %multiply_convert_fusion.1), channel_id=1, source_target_pairs={{0,8},{1,9},{2,10},{3,11},{4,12},{5,13},{6,14},{7,15},{8,16},{9,17... | collective-permute-start | bytes 491528 | tf_op jit(solution)/shard_map/ppermute | solution.py:10
  20.2 3.7 %collective-permute-start.2 = (f32[8,128]{1,0:T(8,128)S(1)}, f32[8,128]{1,0:T(8,128)S(1)}, u32[]{:S(2)}, u32[]{:S(2)}) collective-permute-start(f32[8,128]{1,0:T(8,128)S(1)} %fusion.65), channel_id=1, source_target_pairs={{0,16},{1,17},{2,18},{3,19},{4,20},{5,21},{6,22},{7,23},{8,24},{9,... | collective-permute-start | bytes 12296 | tf_op jit(solution)/shard_map/ppermute | solution.py:15
  23.9 3.6 %collective-permute-start.3 = (f32[8,128]{1,0:T(8,128)S(1)}, f32[8,128]{1,0:T(8,128)S(1)}, u32[]{:S(2)}, u32[]{:S(2)}) collective-permute-start(f32[8,128]{1,0:T(8,128)S(1)} %add.259), channel_id=1, source_target_pairs={{0,64},{1,65},{2,66},{3,67},{4,68},{5,69},{6,70},{7,71},{8,72},{9,... | collective-permute-start | bytes 12296 | tf_op jit(solution)/shard_map/ppermute | solution.py:15
  27.5 4.5 %collective-permute-start.4 = (f32[8,128]{1,0:T(8,128)S(1)}, f32[8,128]{1,0:T(8,128)S(1)}, u32[]{:S(2)}, u32[]{:S(2)}) collective-permute-start(f32[8,128]{1,0:T(8,128)S(1)} %add.260), channel_id=1, source_target_pairs={{0,4},{1,5},{2,6},{3,7},{4,0},{5,1},{6,2},{7,3},{8,12},{9,13},{10,... | collective-permute-start | bytes 12296 | tf_op jit(solution)/shard_map/ppermute | solution.py:15
  32.0 5.1 %collective-permute-start.5 = (f32[8,128]{1,0:T(8,128)S(1)}, f32[8,128]{1,0:T(8,128)S(1)}, u32[]{:S(2)}, u32[]{:S(2)}) collective-permute-start(f32[8,128]{1,0:T(8,128)S(1)} %add.261), channel_id=1, source_target_pairs={{0,32},{1,33},{2,34},{3,35},{4,36},{5,37},{6,38},{7,39},{8,40},{9,... | collective-permute-start | bytes 12296 | tf_op jit(solution)/shard_map/ppermute | solution.py:15
  37.1 5.1 %collective-permute-start.6 = (f32[8,128]{1,0:T(8,128)S(1)}, f32[8,128]{1,0:T(8,128)S(1)}, u32[]{:S(2)}, u32[]{:S(2)}) collective-permute-start(f32[8,128]{1,0:T(8,128)S(1)} %add.262), channel_id=1, source_target_pairs={{0,128},{1,129},{2,130},{3,131},{4,132},{5,133},{6,134},{7,135},{8... | collective-permute-start | bytes 12296 | tf_op jit(solution)/shard_map/ppermute | solution.py:15
  42.2 10.2 %collective-permute-start.7 = (f32[8,128]{1,0:T(8,128)S(1)}, f32[8,128]{1,0:T(8,128)S(1)}, u32[]{:S(2)}, u32[]{:S(2)}) collective-permute-start(f32[8,128]{1,0:T(8,128)S(1)} %add.263), channel_id=1, source_target_pairs={{0,8},{1,9},{2,10},{3,11},{4,12},{5,13},{6,14},{7,15},{8,0},{9,1},... | collective-permute-start | bytes 12296 | tf_op jit(solution)/shard_map/ppermute | solution.py:15
  42.6 9.8 %collective-permute-start.9 = (bf16[128,640]{1,0:T(8,128)(2,1)}, bf16[128,640]{1,0:T(8,128)(2,1)}, u32[]{:S(2)}, u32[]{:S(2)}) collective-permute-start(bf16[128,640]{1,0:T(8,128)(2,1)} %multiply_convert_fusion.1), channel_id=1, source_target_pairs={{0,4},{1,5},{2,6},{3,7},{4,8},{5,9},{6,10},{7,11},{8,12},{9,13},{1... | collective-permute-start | bytes 491528 | tf_op jit(solution)/shard_map/ppermute | solution.py:10
  48.1 8.9 %collective-permute-start.10 = (bf16[128,640]{1,0:T(8,128)(2,1)}, bf16[128,640]{1,0:T(8,128)(2,1)S(1)}, u32[]{:S(2)}, u32[]{:S(2)}) collective-permute-start(bf16[128,640]{1,0:T(8,128)(2,1)} %multiply_convert_fusion.1), channel_id=1, source_target_pairs={{4,0},{5,1},{6,2},{7,3},{8,4},{9,5},{10,6},{11,7},{12,8},{13,9},{1... | collective-permute-start | bytes 491528 | tf_op jit(solution)/shard_map/ppermute | solution.py:10
  49.4 15.5 %collective-permute-start.11 = (bf16[128,640]{1,0:T(8,128)(2,1)}, bf16[128,640]{1,0:T(8,128)(2,1)S(1)}, u32[]{:S(2)}, u32[]{:S(2)}) collective-permute-start(bf16[128,640]{1,0:T(8,128)(2,1)} %multiply_convert_fusion.1), channel_id=1, source_target_pairs={{8,0},{9,1},{10,2},{11,3},{12,4},{13,5},{14,6},{15,7},{16,8},{17,9... | collective-permute-start | bytes 491528 | tf_op jit(solution)/shard_map/ppermute | solution.py:10
  73.5 23.1 %collective-permute-start.20 = (bf16[128,640]{1,0:T(8,128)(2,1)}, bf16[128,640]{1,0:T(8,128)(2,1)}, u32[]{:S(2)}, u32[]{:S(2)}) collective-permute-start(bf16[128,640]{1,0:T(8,128)(2,1)} %add_convert_fusion.1), channel_id=1, source_target_pairs={{8,0},{9,1},{10,2},{11,3},{12,4},{13,5},{14,6},{15,7},{16,8},{17,9... | collective-permute-start | bytes 491528 | tf_op jit(solution)/shard_map/ppermute | solution.py:10
  74.8 22.9 %collective-permute-start.21 = (bf16[128,640]{1,0:T(8,128)(2,1)}, bf16[128,640]{1,0:T(8,128)(2,1)}, u32[]{:S(2)}, u32[]{:S(2)}) collective-permute-start(bf16[128,640]{1,0:T(8,128)(2,1)} %add_convert_fusion.1), channel_id=1, source_target_pairs={{4,0},{5,1},{6,2},{7,3},{8,4},{9,5},{10,6},{11,7},{12,8},{13,9},{1... | collective-permute-start | bytes 491528 | tf_op jit(solution)/shard_map/ppermute | solution.py:10
  76.1 22.8 %collective-permute-start.22 = (bf16[128,640]{1,0:T(8,128)(2,1)}, bf16[128,640]{1,0:T(8,128)(2,1)}, u32[]{:S(2)}, u32[]{:S(2)}) collective-permute-start(bf16[128,640]{1,0:T(8,128)(2,1)} %add_convert_fusion.1), channel_id=1, source_target_pairs={{0,4},{1,5},{2,6},{3,7},{4,8},{5,9},{6,10},{7,11},{8,12},{9,13},{1... | collective-permute-start | bytes 491528 | tf_op jit(solution)/shard_map/ppermute | solution.py:10
  82.3 17.6 %collective-permute-start.23 = (bf16[128,640]{1,0:T(8,128)(2,1)}, bf16[128,640]{1,0:T(8,128)(2,1)}, u32[]{:S(2)}, u32[]{:S(2)}) collective-permute-start(bf16[128,640]{1,0:T(8,128)(2,1)} %add_convert_fusion.1), channel_id=1, source_target_pairs={{0,8},{1,9},{2,10},{3,11},{4,12},{5,13},{6,14},{7,15},{8,16},{9,17... | collective-permute-start | bytes 491528 | tf_op jit(solution)/shard_map/ppermute | solution.py:10
  91.4 3.6 %collective-permute-start.12 = (f32[8,128]{1,0:T(8,128)S(1)}, f32[8,128]{1,0:T(8,128)S(1)}, u32[]{:S(2)}, u32[]{:S(2)}) collective-permute-start(f32[8,128]{1,0:T(8,128)S(1)} %broadcast_in_dim.13), channel_id=1, source_target_pairs={{0,1},{1,0},{2,3},{3,2},{4,5},{5,4},{6,7},{7,6},{8,9},{9,8},{10,11... | collective-permute-start | bytes 12296 | tf_op jit(solution)/shard_map/ppermute | solution.py:15
  95.0 9.1 %collective-permute-start.36 = (bf16[64,5,640]{2,0,1:T(8,128)(2,1)S(1)}, bf16[64,5,640]{2,0,1:T(8,128)(2,1)S(1)}, u32[]{:S(2)}, u32[]{:S(2)}) collective-permute-start(bf16[64,5,640]{2,0,1:T(8,128)(2,1)S(1)} %get-tuple-element.14), channel_id=1, source_target_pairs={{0,1},{1,0},{2,3},{3,2},{4,5},{5,4},{6,7},{7,6},{8,9},{9,8},{10,11... | collective-permute-start | bytes 1228808 | tf_op jit(solution)/shard_map/ppermute | solution.py:15
  96.7 7.4 %collective-permute-start.35 = (bf16[64,5,640]{2,0,1:T(8,128)(2,1)S(1)}, bf16[64,5,640]{2,0,1:T(8,128)(2,1)S(1)}, u32[]{:S(2)}, u32[]{:S(2)}) collective-permute-start(bf16[64,5,640]{2,0,1:T(8,128)(2,1)S(1)} %get-tuple-element.13), channel_id=1, source_target_pairs={{0,1},{1,0},{2,3},{3,2},{4,5},{5,4},{6,7},{7,6},{8,9},{9,8},{10,11... | collective-permute-start | bytes 1228808 | tf_op jit(solution)/shard_map/ppermute | solution.py:15
  97.7 13.6 %collective-permute-start.13 = (f32[8,128]{1,0:T(8,128)S(1)}, f32[8,128]{1,0:T(8,128)S(1)}, u32[]{:S(2)}, u32[]{:S(2)}) collective-permute-start(f32[8,128]{1,0:T(8,128)S(1)} %broadcast_add_fusion), channel_id=1, source_target_pairs={{0,2},{1,3},{2,0},{3,1},{4,6},{5,7},{6,4},{7,5},{8,10},{9,11},{10,... | collective-permute-start | bytes 12296 | tf_op jit(solution)/shard_map/ppermute | solution.py:15
  103.5 3.6 %collective-permute-start.25 = (bf16[64,5,640]{2,0,1:T(8,128)(2,1)S(1)}, bf16[64,5,640]{2,0,1:T(8,128)(2,1)S(1)}, u32[]{:S(2)}, u32[]{:S(2)}) collective-permute-start(bf16[64,5,640]{2,0,1:T(8,128)(2,1)S(1)} %get-tuple-element.16), channel_id=1, source_target_pairs={{0,1},{1,0},{2,3},{3,2},{4,5},{5,4},{6,7},{7,6},{8,9},{9,8},{10,11... | collective-permute-start | bytes 1228808 | tf_op jit(solution)/shard_map/ppermute | solution.py:15
  104.0 3.1 %collective-permute-start.24 = (bf16[64,5,640]{2,0,1:T(8,128)(2,1)S(1)}, bf16[64,5,640]{2,0,1:T(8,128)(2,1)S(1)}, u32[]{:S(2)}, u32[]{:S(2)}) collective-permute-start(bf16[64,5,640]{2,0,1:T(8,128)(2,1)S(1)} %get-tuple-element.15), channel_id=1, source_target_pairs={{0,1},{1,0},{2,3},{3,2},{4,5},{5,4},{6,7},{7,6},{8,9},{9,8},{10,11... | collective-permute-start | bytes 1228808 | tf_op jit(solution)/shard_map/ppermute | solution.py:15
  105.0 48.1 %collective-permute-start.38 = (bf16[32,5,640]{2,0,1:T(8,128)(2,1)}, bf16[32,5,640]{2,0,1:T(8,128)(2,1)}, u32[]{:S(2)}, u32[]{:S(2)}) collective-permute-start(bf16[32,5,640]{2,0,1:T(8,128)(2,1)} %get-tuple-element.18), channel_id=1, source_target_pairs={{0,2},{1,3},{2,0},{3,1},{4,6},{5,7},{6,4},{7,5},{8,10},{9,11},{10,... | collective-permute-start | bytes 614408 | tf_op jit(solution)/shard_map/ppermute | solution.py:15
  107.0 46.2 %collective-permute-start.37 = (bf16[32,5,640]{2,0,1:T(8,128)(2,1)S(1)}, bf16[32,5,640]{2,0,1:T(8,128)(2,1)}, u32[]{:S(2)}, u32[]{:S(2)}) collective-permute-start(bf16[32,5,640]{2,0,1:T(8,128)(2,1)S(1)} %get-tuple-element.17), channel_id=1, source_target_pairs={{0,2},{1,3},{2,0},{3,1},{4,6},{5,7},{6,4},{7,5},{8,10},{9,11},{10,... | collective-permute-start | bytes 614408 | tf_op jit(solution)/shard_map/ppermute | solution.py:15
  109.3 43.9 %collective-permute-start.27 = (bf16[32,5,640]{2,0,1:T(8,128)(2,1)}, bf16[32,5,640]{2,0,1:T(8,128)(2,1)}, u32[]{:S(2)}, u32[]{:S(2)}) collective-permute-start(bf16[32,5,640]{2,0,1:T(8,128)(2,1)} %get-tuple-element.20), channel_id=1, source_target_pairs={{0,2},{1,3},{2,0},{3,1},{4,6},{5,7},{6,4},{7,5},{8,10},{9,11},{10,... | collective-permute-start | bytes 614408 | tf_op jit(solution)/shard_map/ppermute | solution.py:15
  111.2 41.9 %collective-permute-start.26 = (bf16[32,5,640]{2,0,1:T(8,128)(2,1)}, bf16[32,5,640]{2,0,1:T(8,128)(2,1)}, u32[]{:S(2)}, u32[]{:S(2)}) collective-permute-start(bf16[32,5,640]{2,0,1:T(8,128)(2,1)} %get-tuple-element.19), channel_id=1, source_target_pairs={{0,2},{1,3},{2,0},{3,1},{4,6},{5,7},{6,4},{7,5},{8,10},{9,11},{10,... | collective-permute-start | bytes 614408 | tf_op jit(solution)/shard_map/ppermute | solution.py:15
  112.0 5.2 %collective-permute-start.14 = (f32[8,128]{1,0:T(8,128)S(1)}, f32[8,128]{1,0:T(8,128)S(1)}, u32[]{:S(2)}, u32[]{:S(2)}) collective-permute-start(f32[8,128]{1,0:T(8,128)S(1)} %fusion.64), channel_id=1, source_target_pairs={{0,16},{1,17},{2,18},{3,19},{4,20},{5,21},{6,22},{7,23},{8,24},{9,... | collective-permute-start | bytes 12296 | tf_op jit(solution)/shard_map/ppermute | solution.py:15
  117.2 9.6 %collective-permute-start.15 = (f32[8,128]{1,0:T(8,128)S(1)}, f32[8,128]{1,0:T(8,128)S(1)}, u32[]{:S(2)}, u32[]{:S(2)}) collective-permute-start(f32[8,128]{1,0:T(8,128)S(1)} %add.278), channel_id=1, source_target_pairs={{0,64},{1,65},{2,66},{3,67},{4,68},{5,69},{6,70},{7,71},{8,72},{9,... | collective-permute-start | bytes 12296 | tf_op jit(solution)/shard_map/ppermute | solution.py:15
  126.7 4.5 %collective-permute-start.16 = (f32[8,128]{1,0:T(8,128)S(1)}, f32[8,128]{1,0:T(8,128)S(1)}, u32[]{:S(2)}, u32[]{:S(2)}) collective-permute-start(f32[8,128]{1,0:T(8,128)S(1)} %add.279), channel_id=1, source_target_pairs={{0,4},{1,5},{2,6},{3,7},{4,0},{5,1},{6,2},{7,3},{8,12},{9,13},{10,... | collective-permute-start | bytes 12296 | tf_op jit(solution)/shard_map/ppermute | solution.py:15
  131.2 5.1 %collective-permute-start.17 = (f32[8,128]{1,0:T(8,128)S(1)}, f32[8,128]{1,0:T(8,128)S(1)}, u32[]{:S(2)}, u32[]{:S(2)}) collective-permute-start(f32[8,128]{1,0:T(8,128)S(1)} %add.280), channel_id=1, source_target_pairs={{0,32},{1,33},{2,34},{3,35},{4,36},{5,37},{6,38},{7,39},{8,40},{9,... | collective-permute-start | bytes 12296 | tf_op jit(solution)/shard_map/ppermute | solution.py:15
  136.3 7.4 %collective-permute-start.18 = (f32[8,128]{1,0:T(8,128)S(1)}, f32[8,128]{1,0:T(8,128)S(1)}, u32[]{:S(2)}, u32[]{:S(2)}) collective-permute-start(f32[8,128]{1,0:T(8,128)S(1)} %add.281), channel_id=1, source_target_pairs={{0,128},{1,129},{2,130},{3,131},{4,132},{5,133},{6,134},{7,135},{8... | collective-permute-start | bytes 12296 | tf_op jit(solution)/shard_map/ppermute | solution.py:15
  143.8 7.5 %collective-permute-start.19 = (f32[8,128]{1,0:T(8,128)S(1)}, f32[8,128]{1,0:T(8,128)S(1)}, u32[]{:S(2)}, u32[]{:S(2)}) collective-permute-start(f32[8,128]{1,0:T(8,128)S(1)} %add.282), channel_id=1, source_target_pairs={{0,8},{1,9},{2,10},{3,11},{4,12},{5,13},{6,14},{7,15},{8,0},{9,1},... | collective-permute-start | bytes 12296 | tf_op jit(solution)/shard_map/ppermute | solution.py:15
  154.9 4.7 %collective-permute-start.29 = (bf16[16,5,640]{2,0,1:T(8,128)(2,1)S(1)}, bf16[16,5,640]{2,0,1:T(8,128)(2,1)S(1)}, u32[]{:S(2)}, u32[]{:S(2)}) collective-permute-start(bf16[16,5,640]{2,0,1:T(8,128)(2,1)S(1)} %get-tuple-element.24), channel_id=1, source_target_pairs={{0,16},{1,17},{2,18},{3,19},{4,20},{5,21},{6,22},{7,23},{8,24},{9,... | collective-permute-start | bytes 307208 | tf_op jit(solution)/shard_map/ppermute | solution.py:15
  155.0 5.7 %collective-permute-start.28 = (bf16[16,5,640]{2,0,1:T(8,128)(2,1)S(1)}, bf16[16,5,640]{2,0,1:T(8,128)(2,1)S(1)}, u32[]{:S(2)}, u32[]{:S(2)}) collective-permute-start(bf16[16,5,640]{2,0,1:T(8,128)(2,1)S(1)} %get-tuple-element.23), channel_id=1, source_target_pairs={{0,16},{1,17},{2,18},{3,19},{4,20},{5,21},{6,22},{7,23},{8,24},{9,... | collective-permute-start | bytes 307208 | tf_op jit(solution)/shard_map/ppermute | solution.py:15
  157.1 5.5 %collective-permute-start.40 = (bf16[16,5,640]{2,0,1:T(8,128)(2,1)S(1)}, bf16[16,5,640]{2,0,1:T(8,128)(2,1)S(1)}, u32[]{:S(2)}, u32[]{:S(2)}) collective-permute-start(bf16[16,5,640]{2,0,1:T(8,128)(2,1)S(1)} %get-tuple-element.22), channel_id=1, source_target_pairs={{0,16},{1,17},{2,18},{3,19},{4,20},{5,21},{6,22},{7,23},{8,24},{9,... | collective-permute-start | bytes 307208 | tf_op jit(solution)/shard_map/ppermute | solution.py:15
  157.3 5.7 %collective-permute-start.39 = (bf16[16,5,640]{2,0,1:T(8,128)(2,1)S(1)}, bf16[16,5,640]{2,0,1:T(8,128)(2,1)S(1)}, u32[]{:S(2)}, u32[]{:S(2)}) collective-permute-start(bf16[16,5,640]{2,0,1:T(8,128)(2,1)S(1)} %get-tuple-element.21), channel_id=1, source_target_pairs={{0,16},{1,17},{2,18},{3,19},{4,20},{5,21},{6,22},{7,23},{8,24},{9,... | collective-permute-start | bytes 307208 | tf_op jit(solution)/shard_map/ppermute | solution.py:15
  160.9 4.7 %collective-permute-start.30 = (bf16[16,5,640]{2,0,1:T(8,128)(2,1)S(1)}, bf16[16,5,640]{2,0,1:T(8,128)(2,1)S(1)}, u32[]{:S(2)}, u32[]{:S(2)}) collective-permute-start(bf16[16,5,640]{2,0,1:T(8,128)(2,1)S(1)} %dynamic-slice_convert_fusion.7), channel_id=1, source_target_pairs={{0,64},{1,65},{2,66},{3,67},{4,68},{5,69},{6,70},{7,71},{8,72},{9,... | collective-permute-start | bytes 307208 | tf_op jit(solution)/shard_map/ppermute | solution.py:15
  163.0 4.7 %collective-permute-start.41 = (bf16[16,5,640]{2,0,1:T(8,128)(2,1)S(1)}, bf16[16,5,640]{2,0,1:T(8,128)(2,1)S(1)}, u32[]{:S(2)}, u32[]{:S(2)}) collective-permute-start(bf16[16,5,640]{2,0,1:T(8,128)(2,1)S(1)} %dynamic-slice_convert_fusion.6), channel_id=1, source_target_pairs={{0,64},{1,65},{2,66},{3,67},{4,68},{5,69},{6,70},{7,71},{8,72},{9,... | collective-permute-start | bytes 307208 | tf_op jit(solution)/shard_map/ppermute | solution.py:15
  165.7 5.1 %collective-permute-start.31 = (bf16[8,5,640]{2,0,1:T(8,128)(2,1)S(1)}, bf16[8,5,640]{2,0,1:T(8,128)(2,1)S(1)}, u32[]{:S(2)}, u32[]{:S(2)}) collective-permute-start(bf16[8,5,640]{2,0,1:T(8,128)(2,1)S(1)} %dynamic-slice_convert_fusion.9), channel_id=1, source_target_pairs={{0,4},{1,5},{2,6},{3,7},{4,0},{5,1},{6,2},{7,3},{8,12},{9,13},{10,... | collective-permute-start | bytes 153608 | tf_op jit(solution)/shard_map/ppermute | solution.py:15
  167.8 5.5 %collective-permute-start.42 = (bf16[8,5,640]{2,0,1:T(8,128)(2,1)S(1)}, bf16[8,5,640]{2,0,1:T(8,128)(2,1)S(1)}, u32[]{:S(2)}, u32[]{:S(2)}) collective-permute-start(bf16[8,5,640]{2,0,1:T(8,128)(2,1)S(1)} %dynamic-slice_convert_fusion.8), channel_id=1, source_target_pairs={{0,4},{1,5},{2,6},{3,7},{4,0},{5,1},{6,2},{7,3},{8,12},{9,13},{10,... | collective-permute-start | bytes 153608 | tf_op jit(solution)/shard_map/ppermute | solution.py:15
  170.8 5.4 %collective-permute-start.32 = (bf16[4,5,640]{2,0,1:T(4,128)(2,1)S(1)}, bf16[4,5,640]{2,0,1:T(4,128)(2,1)S(1)}, u32[]{:S(2)}, u32[]{:S(2)}) collective-permute-start(bf16[4,5,640]{2,0,1:T(4,128)(2,1)S(1)} %dynamic-slice_convert_fusion.11), channel_id=1, source_target_pairs={{0,32},{1,33},{2,34},{3,35},{4,36},{5,37},{6,38},{7,39},{8,40},{9,... | collective-permute-start | bytes 76808 | tf_op jit(solution)/shard_map/ppermute | solution.py:15
  173.4 6.5 %collective-permute-start.43 = (bf16[4,5,640]{2,0,1:T(4,128)(2,1)S(1)}, bf16[4,5,640]{2,0,1:T(4,128)(2,1)S(1)}, u32[]{:S(2)}, u32[]{:S(2)}) collective-permute-start(bf16[4,5,640]{2,0,1:T(4,128)(2,1)S(1)} %dynamic-slice_convert_fusion.10), channel_id=1, source_target_pairs={{0,32},{1,33},{2,34},{3,35},{4,36},{5,37},{6,38},{7,39},{8,40},{9,... | collective-permute-start | bytes 76808 | tf_op jit(solution)/shard_map/ppermute | solution.py:15
  176.3 5.8 %collective-permute-start.33 = (bf16[2,5,640]{2,0,1:T(2,128)(2,1)S(1)}, bf16[2,5,640]{2,0,1:T(2,128)(2,1)S(1)}, u32[]{:S(2)}, u32[]{:S(2)}) collective-permute-start(bf16[2,5,640]{2,0,1:T(2,128)(2,1)S(1)} %dynamic-slice_convert_fusion.13), channel_id=1, source_target_pairs={{0,128},{1,129},{2,130},{3,131},{4,132},{5,133},{6,134},{7,135},{8... | collective-permute-start | bytes 38408 | tf_op jit(solution)/shard_map/ppermute | solution.py:15
  180.0 7.2 %collective-permute-start.44 = (bf16[2,5,640]{2,0,1:T(2,128)(2,1)S(1)}, bf16[2,5,640]{2,0,1:T(2,128)(2,1)S(1)}, u32[]{:S(2)}, u32[]{:S(2)}) collective-permute-start(bf16[2,5,640]{2,0,1:T(2,128)(2,1)S(1)} %dynamic-slice_convert_fusion.12), channel_id=1, source_target_pairs={{0,128},{1,129},{2,130},{3,131},{4,132},{5,133},{6,134},{7,135},{8... | collective-permute-start | bytes 38408 | tf_op jit(solution)/shard_map/ppermute | solution.py:15
  182.1 7.7 %collective-permute-start.34 = (bf16[1,5,640]{2,0,1:T(2,128)(2,1)S(1)}, bf16[1,5,640]{2,0,1:T(2,128)(2,1)S(1)}, u32[]{:S(2)}, u32[]{:S(2)}) collective-permute-start(bf16[1,5,640]{2,0,1:T(2,128)(2,1)S(1)} %dynamic-slice_convert_fusion.15), channel_id=1, source_target_pairs={{0,8},{1,9},{2,10},{3,11},{4,12},{5,13},{6,14},{7,15},{8,0},{9,1},... | collective-permute-start | bytes 19208 | tf_op jit(solution)/shard_map/ppermute | solution.py:15
  187.2 7.8 %collective-permute-start.45 = (bf16[1,5,640]{2,0,1:T(2,128)(2,1)S(1)}, bf16[1,5,640]{2,0,1:T(2,128)(2,1)S(1)}, u32[]{:S(2)}, u32[]{:S(2)}) collective-permute-start(bf16[1,5,640]{2,0,1:T(2,128)(2,1)S(1)} %dynamic-slice_convert_fusion.14), channel_id=1, source_target_pairs={{0,8},{1,9},{2,10},{3,11},{4,12},{5,13},{6,14},{7,15},{8,0},{9,1},... | collective-permute-start | bytes 19208 | tf_op jit(solution)/shard_map/ppermute | solution.py:15
  (7 other events, 23.7 us)

commit v15 on v14

--- a/solution.py
+++ b/solution.py
@@ -60,7 +60,7 @@
             lax.dynamic_slice_in_dim(b, (1 - upper) * half, half, 0).astype(jnp.bfloat16)
             for b in blocks
         ]
-        pieces = 2 if half >= 32 else 1
+        pieces = 2 if half >= 64 else 1
         parts = [jnp.split(s, pieces, 0) for s in send]
         got_parts, got_extra = swap_with((parts, extra), axis, bit)
         got = [jnp.concatenate(g, 0) if pieces > 1 else g[0] for g in got_parts]

time: 197 us -> 200 us (1.015)
  starting transfers between devices: 96.2 us -> 107 us
  waiting for transfers between devices: 56 us -> 51.5 us
  local copies, waits for them, and re-layouts: 16 us -> 13.2 us
    ppermute x38 -> x36, starting transfers between devices: 63.6 us -> 75.9 us  [swap_with(): return lax.ppermute(block, axis, [(i, i ^ bit) for i in range(devices)])]
    ppermute x8, waiting for transfers between devices: 11.3 us -> 0.02 us  [from_behind(): return lax.ppermute(block, axis, route)]
    ppermute x38 -> x36, waiting for transfers between devices: 44.7 us -> 51.5 us  [swap_with(): return lax.ppermute(block, axis, [(i, i ^ bit) for i in range(devices)])]
    unnamed x26 -> x24, local copies, waits for them, and re-layouts: 6.24 us -> 5.04 us
  transfers between devices with their start and end apart: 46 -> 44, of which waited for: 22 -> 23; matrix products, arithmetic and copies ran while one was open for 13% -> 13% of each run, Pallas kernels for 0% -> 0%
where the time goes in v15:
time: 200 us; the launch traced here: 198 us
  starting transfers between devices  107 us (54%)
  waiting for transfers between devices  51.5 us (26%)
  local copies, waits for them, and re-layouts  13.2 us (7%)
  other arithmetic  12.2 us (6%)
  matrix products  9.84 us (5%)
  between operations  4.56 us (2%)
    ppermute x36, starting transfers between devices, swap_with(): return lax.ppermute(block, axis, [(i, i ^ bit) for i in range(devices)])  75.9 us
    ppermute x36, waiting for transfers between devices, swap_with(): return lax.ppermute(block, axis, [(i, i ^ bit) for i in range(devices)])  51.5 us
    ppermute x8, starting transfers between devices, from_behind(): return lax.ppermute(block, axis, route)  31.1 us
    unnamed x24, local copies, waits for them, and re-layouts  5.04 us
  transfers between devices with their start and end apart: 44, of which 23 were waited for; matrix products, arithmetic and copies ran while one was open for 13% of the time, Pallas kernels for 0%

profile of v15, /device:TPU:32, one launch (start us, length us, event | category | flops | bytes accessed | tf_op | source)
XLA Modules:
  0.0 198.4 jit_solution(9608201831661704984)
XLA Ops:
  5.1 1.4 fusion.9
  6.5 1.9 fusion.49
  9.3 1.9 collective-permute-start.1
  12.1 7.4 %collective-permute-start.8 = (bf16[128,640]{1,0:T(8,128)(2,1)}, bf16[128,640]{1,0:T(8,128)(2,1)S(1)}, u32[]{:S(2)}, u32[]{:S(2)}) collective-permute-start(bf16[128,640]{1,0:T(8,128)(2,1)} %multiply_convert_fusion.1), channel_id=1, source_target_pairs={{0,8},{1,9},{2,10},{3,11},{4,12},{5,13},{6,14},{7,15},{8,16},{9,17... | collective-permute-start | bytes 491528 | tf_op jit(solution)/shard_map/ppermute | solution.py:10
  20.2 1.6 collective-permute-start.2
  21.8 2.1 %collective-permute-done.2 = f32[8,128]{1,0:T(8,128)S(1)} collective-permute-done((f32[8,128]{1,0:T(8,128)S(1)}, f32[8,128]{1,0:T(8,128)S(1)}, u32[]{:S(2)}, u32[]{:S(2)}) %collective-permute-start.2) | collective-permute-done | bytes 4128 | tf_op jit(solution)/shard_map/ppermute | solution.py:15
  23.9 1.6 collective-permute-start.3
  25.5 2.0 %collective-permute-done.3 = f32[8,128]{1,0:T(8,128)S(1)} collective-permute-done((f32[8,128]{1,0:T(8,128)S(1)}, f32[8,128]{1,0:T(8,128)S(1)}, u32[]{:S(2)}, u32[]{:S(2)}) %collective-permute-start.3) | collective-permute-done | bytes 4128 | tf_op jit(solution)/shard_map/ppermute | solution.py:15
  27.5 1.5 collective-permute-start.4
  29.0 4.0 %collective-permute-start.9 = (bf16[128,640]{1,0:T(8,128)(2,1)}, bf16[128,640]{1,0:T(8,128)(2,1)}, u32[]{:S(2)}, u32[]{:S(2)}) collective-permute-start(bf16[128,640]{1,0:T(8,128)(2,1)} %multiply_convert_fusion.1), channel_id=1, source_target_pairs={{0,4},{1,5},{2,6},{3,7},{4,8},{5,9},{6,10},{7,11},{8,12},{9,13},{1... | collective-permute-start | bytes 491528 | tf_op jit(solution)/shard_map/ppermute | solution.py:10
  35.8 7.8 %collective-permute-start.5 = (f32[8,128]{1,0:T(8,128)S(1)}, f32[8,128]{1,0:T(8,128)S(1)}, u32[]{:S(2)}, u32[]{:S(2)}) collective-permute-start(f32[8,128]{1,0:T(8,128)S(1)} %add.261), channel_id=1, source_target_pairs={{0,32},{1,33},{2,34},{3,35},{4,36},{5,37},{6,38},{7,39},{8,40},{9,... | collective-permute-start | bytes 12296 | tf_op jit(solution)/shard_map/ppermute | solution.py:15
  43.6 1.6 collective-permute-done.5
  45.2 5.8 %collective-permute-start.6 = (f32[8,128]{1,0:T(8,128)S(1)}, f32[8,128]{1,0:T(8,128)S(1)}, u32[]{:S(2)}, u32[]{:S(2)}) collective-permute-start(f32[8,128]{1,0:T(8,128)S(1)} %add.262), channel_id=1, source_target_pairs={{0,128},{1,129},{2,130},{3,131},{4,132},{5,133},{6,134},{7,135},{8... | collective-permute-start | bytes 12296 | tf_op jit(solution)/shard_map/ppermute | solution.py:15
  51.0 1.6 collective-permute-done.6
  52.6 5.4 %collective-permute-start.7 = (f32[8,128]{1,0:T(8,128)S(1)}, f32[8,128]{1,0:T(8,128)S(1)}, u32[]{:S(2)}, u32[]{:S(2)}) collective-permute-start(f32[8,128]{1,0:T(8,128)S(1)} %add.263), channel_id=1, source_target_pairs={{0,8},{1,9},{2,10},{3,11},{4,12},{5,13},{6,14},{7,15},{8,0},{9,1},... | collective-permute-start | bytes 12296 | tf_op jit(solution)/shard_map/ppermute | solution.py:15
  61.5 3.1 %fusion.50 = (f32[128]{0:T(128)S(1)}, f32[128,640]{1,0:T(8,128)S(1)}) fusion(bf16[5,128,640]{2,1,0:T(8,128)(2,1)S(1)} %bitcast_dynamic-update-slice_fusion.5, bf16[5,640,640]{2,1,0:T(8,128)(2,1)} %param.13), kind=kOutput, calls=%fused_computation.132 | convolution fusion | flops 524369792 | bytes 5243392 | tf_op jit(solution)/shard_map/krc,kcb->rb/dot_general | solution.py:104
  70.0 2.0 %collective-permute-start.13 = (f32[8,128]{1,0:T(8,128)S(1)}, f32[8,128]{1,0:T(8,128)S(1)}, u32[]{:S(2)}, u32[]{:S(2)}) collective-permute-start(f32[8,128]{1,0:T(8,128)S(1)} %broadcast_add_fusion), channel_id=1, source_target_pairs={{0,2},{1,3},{2,0},{3,1},{4,6},{5,7},{6,4},{7,5},{8,10},{9,11},{10,... | collective-permute-start | bytes 12296 | tf_op jit(solution)/shard_map/ppermute | solution.py:15
  72.0 1.7 collective-permute-done.13
  74.9 3.1 %collective-permute-done.14 = f32[8,128]{1,0:T(8,128)S(1)} collective-permute-done((f32[8,128]{1,0:T(8,128)S(1)}, f32[8,128]{1,0:T(8,128)S(1)}, u32[]{:S(2)}, u32[]{:S(2)}) %collective-permute-start.14) | collective-permute-done | bytes 4128 | tf_op jit(solution)/shard_map/ppermute | solution.py:15
  78.0 1.9 collective-permute-start.15
  80.0 1.7 collective-permute-done.15
  81.6 1.8 collective-permute-start.16
  86.8 6.1 %collective-permute-start.22 = (bf16[128,640]{1,0:T(8,128)(2,1)}, bf16[128,640]{1,0:T(8,128)(2,1)}, u32[]{:S(2)}, u32[]{:S(2)}) collective-permute-start(bf16[128,640]{1,0:T(8,128)(2,1)} %add_convert_fusion.1), channel_id=1, source_target_pairs={{0,4},{1,5},{2,6},{3,7},{4,8},{5,9},{6,10},{7,11},{8,12},{9,13},{1... | collective-permute-start | bytes 491528 | tf_op jit(solution)/shard_map/ppermute | solution.py:10
  93.0 8.4 %collective-permute-start.23 = (bf16[128,640]{1,0:T(8,128)(2,1)}, bf16[128,640]{1,0:T(8,128)(2,1)}, u32[]{:S(2)}, u32[]{:S(2)}) collective-permute-start(bf16[128,640]{1,0:T(8,128)(2,1)} %add_convert_fusion.1), channel_id=1, source_target_pairs={{0,8},{1,9},{2,10},{3,11},{4,12},{5,13},{6,14},{7,15},{8,16},{9,17... | collective-permute-start | bytes 491528 | tf_op jit(solution)/shard_map/ppermute | solution.py:10
  104.1 2.2 %collective-permute-start.17 = (f32[8,128]{1,0:T(8,128)S(1)}, f32[8,128]{1,0:T(8,128)S(1)}, u32[]{:S(2)}, u32[]{:S(2)}) collective-permute-start(f32[8,128]{1,0:T(8,128)S(1)} %add.280), channel_id=1, source_target_pairs={{0,32},{1,33},{2,34},{3,35},{4,36},{5,37},{6,38},{7,39},{8,40},{9,... | collective-permute-start | bytes 12296 | tf_op jit(solution)/shard_map/ppermute | solution.py:15
  107.0 2.6 %collective-permute-done.17 = f32[8,128]{1,0:T(8,128)S(1)} collective-permute-done((f32[8,128]{1,0:T(8,128)S(1)}, f32[8,128]{1,0:T(8,128)S(1)}, u32[]{:S(2)}, u32[]{:S(2)}) %collective-permute-start.17) | collective-permute-done | bytes 4128 | tf_op jit(solution)/shard_map/ppermute | solution.py:15
  109.7 4.5 %collective-permute-start.18 = (f32[8,128]{1,0:T(8,128)S(1)}, f32[8,128]{1,0:T(8,128)S(1)}, u32[]{:S(2)}, u32[]{:S(2)}) collective-permute-start(f32[8,128]{1,0:T(8,128)S(1)} %add.281), channel_id=1, source_target_pairs={{0,128},{1,129},{2,130},{3,131},{4,132},{5,133},{6,134},{7,135},{8... | collective-permute-start | bytes 12296 | tf_op jit(solution)/shard_map/ppermute | solution.py:15
  114.3 1.5 collective-permute-done.18
  115.8 2.4 %collective-permute-start.19 = (f32[8,128]{1,0:T(8,128)S(1)}, f32[8,128]{1,0:T(8,128)S(1)}, u32[]{:S(2)}, u32[]{:S(2)}) collective-permute-start(f32[8,128]{1,0:T(8,128)S(1)} %add.282), channel_id=1, source_target_pairs={{0,8},{1,9},{2,10},{3,11},{4,12},{5,13},{6,14},{7,15},{8,0},{9,1},... | collective-permute-start | bytes 12296 | tf_op jit(solution)/shard_map/ppermute | solution.py:15
  118.3 5.0 %collective-permute-done.19 = f32[8,128]{1,0:T(8,128)S(1)} collective-permute-done((f32[8,128]{1,0:T(8,128)S(1)}, f32[8,128]{1,0:T(8,128)S(1)}, u32[]{:S(2)}, u32[]{:S(2)}) %collective-permute-start.19) | collective-permute-done | bytes 4128 | tf_op jit(solution)/shard_map/ppermute | solution.py:15
  129.7 1.5 multiply_reduce_fusion
  135.5 5.7 %collective-permute-done.37 = bf16[32,5,640]{2,0,1:T(8,128)(2,1)S(1)} collective-permute-done((bf16[32,5,640]{2,0,1:T(8,128)(2,1)S(1)}, bf16[32,5,640]{2,0,1:T(8,128)(2,1)S(1)}, u32[]{:S(2)}, u32[]{:S(2)}) %collective-permute-start.37) | collective-permute-done | bytes 204832 | tf_op jit(solution)/shard_map/ppermute | solution.py:15
  141.2 3.5 %collective-permute-done.36 = bf16[32,5,640]{2,0,1:T(8,128)(2,1)S(1)} collective-permute-done((bf16[32,5,640]{2,0,1:T(8,128)(2,1)S(1)}, bf16[32,5,640]{2,0,1:T(8,128)(2,1)S(1)}, u32[]{:S(2)}, u32[]{:S(2)}) %collective-permute-start.36) | collective-permute-done | bytes 204832 | tf_op jit(solution)/shard_map/ppermute | solution.py:15
  147.7 3.4 %collective-permute-done.38 = bf16[32,5,640]{2,0,1:T(8,128)(2,1)S(1)} collective-permute-done((bf16[32,5,640]{2,0,1:T(8,128)(2,1)S(1)}, bf16[32,5,640]{2,0,1:T(8,128)(2,1)S(1)}, u32[]{:S(2)}, u32[]{:S(2)}) %collective-permute-start.38) | collective-permute-done | bytes 204832 | tf_op jit(solution)/shard_map/ppermute | solution.py:15
  151.2 1.7 collective-permute-start.39
  153.6 2.4 %collective-permute-done.26 = bf16[32,5,640]{2,0,1:T(8,128)(2,1)S(1)} collective-permute-done((bf16[32,5,640]{2,0,1:T(8,128)(2,1)S(1)}, bf16[32,5,640]{2,0,1:T(8,128)(2,1)S(1)}, u32[]{:S(2)}, u32[]{:S(2)}) %collective-permute-start.26) | collective-permute-done | bytes 204832 | tf_op jit(solution)/shard_map/ppermute | solution.py:15
  156.3 2.5 %collective-permute-start.40 = (bf16[8,5,640]{2,0,1:T(8,128)(2,1)S(1)}, bf16[8,5,640]{2,0,1:T(8,128)(2,1)S(1)}, u32[]{:S(2)}, u32[]{:S(2)}) collective-permute-start(bf16[8,5,640]{2,0,1:T(8,128)(2,1)S(1)} %dynamic-slice_convert_fusion.8), channel_id=1, source_target_pairs={{0,4},{1,5},{2,6},{3,7},{4,0},{5,1},{6,2},{7,3},{8,12},{9,13},{10,... | collective-permute-start | bytes 153608 | tf_op jit(solution)/shard_map/ppermute | solution.py:15
  158.8 1.4 collective-permute-start.28
  161.5 2.5 %collective-permute-start.41 = (bf16[4,5,640]{2,0,1:T(4,128)(2,1)S(1)}, bf16[4,5,640]{2,0,1:T(4,128)(2,1)S(1)}, u32[]{:S(2)}, u32[]{:S(2)}) collective-permute-start(bf16[4,5,640]{2,0,1:T(4,128)(2,1)S(1)} %dynamic-slice_convert_fusion.10), channel_id=1, source_target_pairs={{0,32},{1,33},{2,34},{3,35},{4,36},{5,37},{6,38},{7,39},{8,40},{9,... | collective-permute-start | bytes 76808 | tf_op jit(solution)/shard_map/ppermute | solution.py:15
  167.0 2.5 %collective-permute-done.29 = bf16[16,5,640]{2,0,1:T(8,128)(2,1)S(1)} collective-permute-done((bf16[16,5,640]{2,0,1:T(8,128)(2,1)S(1)}, bf16[16,5,640]{2,0,1:T(8,128)(2,1)S(1)}, u32[]{:S(2)}, u32[]{:S(2)}) %collective-permute-start.29) | collective-permute-done | bytes 102432 | tf_op jit(solution)/shard_map/ppermute | solution.py:15
  169.5 2.3 %collective-permute-start.30 = (bf16[8,5,640]{2,0,1:T(8,128)(2,1)S(1)}, bf16[8,5,640]{2,0,1:T(8,128)(2,1)S(1)}, u32[]{:S(2)}, u32[]{:S(2)}) collective-permute-start(bf16[8,5,640]{2,0,1:T(8,128)(2,1)S(1)} %dynamic-slice_convert_fusion.9), channel_id=1, source_target_pairs={{0,4},{1,5},{2,6},{3,7},{4,0},{5,1},{6,2},{7,3},{8,12},{9,13},{10,... | collective-permute-start | bytes 153608 | tf_op jit(solution)/shard_map/ppermute | solution.py:15
  171.9 3.4 %collective-permute-start.42 = (bf16[2,5,640]{2,0,1:T(2,128)(2,1)S(1)}, bf16[2,5,640]{2,0,1:T(2,128)(2,1)S(1)}, u32[]{:S(2)}, u32[]{:S(2)}) collective-permute-start(bf16[2,5,640]{2,0,1:T(2,128)(2,1)S(1)} %dynamic-slice_convert_fusion.12), channel_id=1, source_target_pairs={{0,128},{1,129},{2,130},{3,131},{4,132},{5,133},{6,134},{7,135},{8... | collective-permute-start | bytes 38408 | tf_op jit(solution)/shard_map/ppermute | solution.py:15
  175.3 2.6 %collective-permute-start.31 = (bf16[4,5,640]{2,0,1:T(4,128)(2,1)S(1)}, bf16[4,5,640]{2,0,1:T(4,128)(2,1)S(1)}, u32[]{:S(2)}, u32[]{:S(2)}) collective-permute-start(bf16[4,5,640]{2,0,1:T(4,128)(2,1)S(1)} %dynamic-slice_convert_fusion.11), channel_id=1, source_target_pairs={{0,32},{1,33},{2,34},{3,35},{4,36},{5,37},{6,38},{7,39},{8,40},{9,... | collective-permute-start | bytes 76808 | tf_op jit(solution)/shard_map/ppermute | solution.py:15
  177.9 2.8 %collective-permute-done.31 = bf16[4,5,640]{2,0,1:T(4,128)(2,1)S(1)} collective-permute-done((bf16[4,5,640]{2,0,1:T(4,128)(2,1)S(1)}, bf16[4,5,640]{2,0,1:T(4,128)(2,1)S(1)}, u32[]{:S(2)}, u32[]{:S(2)}) %collective-permute-start.31) | collective-permute-done | bytes 25632 | tf_op jit(solution)/shard_map/ppermute | solution.py:15
  180.8 2.4 %collective-permute-start.32 = (bf16[2,5,640]{2,0,1:T(2,128)(2,1)S(1)}, bf16[2,5,640]{2,0,1:T(2,128)(2,1)S(1)}, u32[]{:S(2)}, u32[]{:S(2)}) collective-permute-start(bf16[2,5,640]{2,0,1:T(2,128)(2,1)S(1)} %dynamic-slice_convert_fusion.13), channel_id=1, source_target_pairs={{0,128},{1,129},{2,130},{3,131},{4,132},{5,133},{6,134},{7,135},{8... | collective-permute-start | bytes 38408 | tf_op jit(solution)/shard_map/ppermute | solution.py:15
  183.2 5.7 %collective-permute-start.43 = (bf16[1,5,640]{2,0,1:T(2,128)(2,1)S(1)}, bf16[1,5,640]{2,0,1:T(2,128)(2,1)S(1)}, u32[]{:S(2)}, u32[]{:S(2)}) collective-permute-start(bf16[1,5,640]{2,0,1:T(2,128)(2,1)S(1)} %dynamic-slice_convert_fusion.14), channel_id=1, source_target_pairs={{0,8},{1,9},{2,10},{3,11},{4,12},{5,13},{6,14},{7,15},{8,0},{9,1},... | collective-permute-start | bytes 19208 | tf_op jit(solution)/shard_map/ppermute | solution.py:15
  189.0 3.2 %collective-permute-start.33 = (bf16[1,5,640]{2,0,1:T(2,128)(2,1)S(1)}, bf16[1,5,640]{2,0,1:T(2,128)(2,1)S(1)}, u32[]{:S(2)}, u32[]{:S(2)}) collective-permute-start(bf16[1,5,640]{2,0,1:T(2,128)(2,1)S(1)} %dynamic-slice_convert_fusion.15), channel_id=1, source_target_pairs={{0,8},{1,9},{2,10},{3,11},{4,12},{5,13},{6,14},{7,15},{8,0},{9,1},... | collective-permute-start | bytes 19208 | tf_op jit(solution)/shard_map/ppermute | solution.py:15
  192.8 3.9 %collective-permute-done.33 = bf16[1,5,640]{2,0,1:T(2,128)(2,1)S(1)} collective-permute-done((bf16[1,5,640]{2,0,1:T(2,128)(2,1)S(1)}, bf16[1,5,640]{2,0,1:T(2,128)(2,1)S(1)}, u32[]{:S(2)}, u32[]{:S(2)}) %collective-permute-start.33) | collective-permute-done | bytes 6432 | tf_op jit(solution)/shard_map/ppermute | solution.py:15
  (164 shorter events, 44.5 us)
Async XLA Ops:
  0.6 64.2 %copy-start = (bf16[1280,640]{1,0:T(8,128)(2,1)S(1)}, bf16[1280,640]{1,0:T(8,128)(2,1)}, u32[]{:S(2)}) copy-start(bf16[1280,640]{1,0:T(8,128)(2,1)} %param.14) | copy-start | bytes 4915204
  2.7 6.0 %collective-permute-start = (f32[8,128]{1,0:T(8,128)S(1)}, f32[8,128]{1,0:T(8,128)S(1)}, u32[]{:S(2)}, u32[]{:S(2)}) collective-permute-start(f32[8,128]{1,0:T(8,128)S(1)} %broadcast_in_dim.12), channel_id=1, source_target_pairs={{0,1},{1,0},{2,3},{3,2},{4,5},{5,4},{6,7},{7,6},{8,9},{9,8},{10,11... | collective-permute-start | bytes 12296 | tf_op jit(solution)/shard_map/ppermute | solution.py:15
  6.5 29.3 %copy-start.6 = (s32[128]{0:T(128)S(1)}, s32[128]{0:T(128)}, u32[]{:S(2)}) copy-start(s32[128]{0:T(128)} %param.9) | copy-start | bytes 1540
  9.3 10.2 %collective-permute-start.1 = (f32[8,128]{1,0:T(8,128)S(1)}, f32[8,128]{1,0:T(8,128)S(1)}, u32[]{:S(2)}, u32[]{:S(2)}) collective-permute-start(f32[8,128]{1,0:T(8,128)S(1)} %broadcast_add_fusion.1), channel_id=1, source_target_pairs={{0,2},{1,3},{2,0},{3,1},{4,6},{5,7},{6,4},{7,5},{8,10},{9,11},{10,... | collective-permute-start | bytes 12296 | tf_op jit(solution)/shard_map/ppermute | solution.py:15
  12.1 48.0 %collective-permute-start.8 = (bf16[128,640]{1,0:T(8,128)(2,1)}, bf16[128,640]{1,0:T(8,128)(2,1)S(1)}, u32[]{:S(2)}, u32[]{:S(2)}) collective-permute-start(bf16[128,640]{1,0:T(8,128)(2,1)} %multiply_convert_fusion.1), channel_id=1, source_target_pairs={{0,8},{1,9},{2,10},{3,11},{4,12},{5,13},{6,14},{7,15},{8,16},{9,17... | collective-permute-start | bytes 491528 | tf_op jit(solution)/shard_map/ppermute | solution.py:10
  20.2 3.7 %collective-permute-start.2 = (f32[8,128]{1,0:T(8,128)S(1)}, f32[8,128]{1,0:T(8,128)S(1)}, u32[]{:S(2)}, u32[]{:S(2)}) collective-permute-start(f32[8,128]{1,0:T(8,128)S(1)} %fusion.63), channel_id=1, source_target_pairs={{0,16},{1,17},{2,18},{3,19},{4,20},{5,21},{6,22},{7,23},{8,24},{9,... | collective-permute-start | bytes 12296 | tf_op jit(solution)/shard_map/ppermute | solution.py:15
  23.9 3.6 %collective-permute-start.3 = (f32[8,128]{1,0:T(8,128)S(1)}, f32[8,128]{1,0:T(8,128)S(1)}, u32[]{:S(2)}, u32[]{:S(2)}) collective-permute-start(f32[8,128]{1,0:T(8,128)S(1)} %add.259), channel_id=1, source_target_pairs={{0,64},{1,65},{2,66},{3,67},{4,68},{5,69},{6,70},{7,71},{8,72},{9,... | collective-permute-start | bytes 12296 | tf_op jit(solution)/shard_map/ppermute | solution.py:15
  27.5 8.3 %collective-permute-start.4 = (f32[8,128]{1,0:T(8,128)S(1)}, f32[8,128]{1,0:T(8,128)S(1)}, u32[]{:S(2)}, u32[]{:S(2)}) collective-permute-start(f32[8,128]{1,0:T(8,128)S(1)} %add.260), channel_id=1, source_target_pairs={{0,4},{1,5},{2,6},{3,7},{4,0},{5,1},{6,2},{7,3},{8,12},{9,13},{10,... | collective-permute-start | bytes 12296 | tf_op jit(solution)/shard_map/ppermute | solution.py:15
  29.0 31.2 %collective-permute-start.9 = (bf16[128,640]{1,0:T(8,128)(2,1)}, bf16[128,640]{1,0:T(8,128)(2,1)}, u32[]{:S(2)}, u32[]{:S(2)}) collective-permute-start(bf16[128,640]{1,0:T(8,128)(2,1)} %multiply_convert_fusion.1), channel_id=1, source_target_pairs={{0,4},{1,5},{2,6},{3,7},{4,8},{5,9},{6,10},{7,11},{8,12},{9,13},{1... | collective-permute-start | bytes 491528 | tf_op jit(solution)/shard_map/ppermute | solution.py:10
  33.0 28.4 %collective-permute-start.10 = (bf16[128,640]{1,0:T(8,128)(2,1)}, bf16[128,640]{1,0:T(8,128)(2,1)S(1)}, u32[]{:S(2)}, u32[]{:S(2)}) collective-permute-start(bf16[128,640]{1,0:T(8,128)(2,1)} %multiply_convert_fusion.1), channel_id=1, source_target_pairs={{4,0},{5,1},{6,2},{7,3},{8,4},{9,5},{10,6},{11,7},{12,8},{13,9},{1... | collective-permute-start | bytes 491528 | tf_op jit(solution)/shard_map/ppermute | solution.py:10
  34.3 27.1 %collective-permute-start.11 = (bf16[128,640]{1,0:T(8,128)(2,1)}, bf16[128,640]{1,0:T(8,128)(2,1)S(1)}, u32[]{:S(2)}, u32[]{:S(2)}) collective-permute-start(bf16[128,640]{1,0:T(8,128)(2,1)} %multiply_convert_fusion.1), channel_id=1, source_target_pairs={{8,0},{9,1},{10,2},{11,3},{12,4},{13,5},{14,6},{15,7},{16,8},{17,9... | collective-permute-start | bytes 491528 | tf_op jit(solution)/shard_map/ppermute | solution.py:10
  35.8 9.4 %collective-permute-start.5 = (f32[8,128]{1,0:T(8,128)S(1)}, f32[8,128]{1,0:T(8,128)S(1)}, u32[]{:S(2)}, u32[]{:S(2)}) collective-permute-start(f32[8,128]{1,0:T(8,128)S(1)} %add.261), channel_id=1, source_target_pairs={{0,32},{1,33},{2,34},{3,35},{4,36},{5,37},{6,38},{7,39},{8,40},{9,... | collective-permute-start | bytes 12296 | tf_op jit(solution)/shard_map/ppermute | solution.py:15
  45.2 7.4 %collective-permute-start.6 = (f32[8,128]{1,0:T(8,128)S(1)}, f32[8,128]{1,0:T(8,128)S(1)}, u32[]{:S(2)}, u32[]{:S(2)}) collective-permute-start(f32[8,128]{1,0:T(8,128)S(1)} %add.262), channel_id=1, source_target_pairs={{0,128},{1,129},{2,130},{3,131},{4,132},{5,133},{6,134},{7,135},{8... | collective-permute-start | bytes 12296 | tf_op jit(solution)/shard_map/ppermute | solution.py:15
  52.6 7.5 %collective-permute-start.7 = (f32[8,128]{1,0:T(8,128)S(1)}, f32[8,128]{1,0:T(8,128)S(1)}, u32[]{:S(2)}, u32[]{:S(2)}) collective-permute-start(f32[8,128]{1,0:T(8,128)S(1)} %add.263), channel_id=1, source_target_pairs={{0,8},{1,9},{2,10},{3,11},{4,12},{5,13},{6,14},{7,15},{8,0},{9,1},... | collective-permute-start | bytes 12296 | tf_op jit(solution)/shard_map/ppermute | solution.py:15
  64.6 3.7 %copy-start.4 = (bf16[128,1280]{1,0:T(8,128)(2,1)S(1)}, bf16[128,1280]{1,0:T(8,128)(2,1)}, u32[]{:S(2)}) copy-start(bf16[128,1280]{1,0:T(8,128)(2,1)} %param.11) | copy-start | bytes 983044
  67.0 2.3 %collective-permute-start.12 = (f32[8,128]{1,0:T(8,128)S(1)}, f32[8,128]{1,0:T(8,128)S(1)}, u32[]{:S(2)}, u32[]{:S(2)}) collective-permute-start(f32[8,128]{1,0:T(8,128)S(1)} %broadcast_in_dim.13), channel_id=1, source_target_pairs={{0,1},{1,0},{2,3},{3,2},{4,5},{5,4},{6,7},{7,6},{8,9},{9,8},{10,11... | collective-permute-start | bytes 12296 | tf_op jit(solution)/shard_map/ppermute | solution.py:15
  70.0 3.7 %collective-permute-start.13 = (f32[8,128]{1,0:T(8,128)S(1)}, f32[8,128]{1,0:T(8,128)S(1)}, u32[]{:S(2)}, u32[]{:S(2)}) collective-permute-start(f32[8,128]{1,0:T(8,128)S(1)} %broadcast_add_fusion), channel_id=1, source_target_pairs={{0,2},{1,3},{2,0},{3,1},{4,6},{5,7},{6,4},{7,5},{8,10},{9,11},{10,... | collective-permute-start | bytes 12296 | tf_op jit(solution)/shard_map/ppermute | solution.py:15
  74.3 3.7 %collective-permute-start.14 = (f32[8,128]{1,0:T(8,128)S(1)}, f32[8,128]{1,0:T(8,128)S(1)}, u32[]{:S(2)}, u32[]{:S(2)}) collective-permute-start(f32[8,128]{1,0:T(8,128)S(1)} %fusion.62), channel_id=1, source_target_pairs={{0,16},{1,17},{2,18},{3,19},{4,20},{5,21},{6,22},{7,23},{8,24},{9,... | collective-permute-start | bytes 12296 | tf_op jit(solution)/shard_map/ppermute | solution.py:15
  78.0 3.6 %collective-permute-start.15 = (f32[8,128]{1,0:T(8,128)S(1)}, f32[8,128]{1,0:T(8,128)S(1)}, u32[]{:S(2)}, u32[]{:S(2)}) collective-permute-start(f32[8,128]{1,0:T(8,128)S(1)} %add.278), channel_id=1, source_target_pairs={{0,64},{1,65},{2,66},{3,67},{4,68},{5,69},{6,70},{7,71},{8,72},{9,... | collective-permute-start | bytes 12296 | tf_op jit(solution)/shard_map/ppermute | solution.py:15
  81.6 22.4 %collective-permute-start.16 = (f32[8,128]{1,0:T(8,128)S(1)}, f32[8,128]{1,0:T(8,128)S(1)}, u32[]{:S(2)}, u32[]{:S(2)}) collective-permute-start(f32[8,128]{1,0:T(8,128)S(1)} %add.279), channel_id=1, source_target_pairs={{0,4},{1,5},{2,6},{3,7},{4,0},{5,1},{6,2},{7,3},{8,12},{9,13},{10,... | collective-permute-start | bytes 12296 | tf_op jit(solution)/shard_map/ppermute | solution.py:15
  84.2 40.9 %collective-permute-start.20 = (bf16[128,640]{1,0:T(8,128)(2,1)}, bf16[128,640]{1,0:T(8,128)(2,1)}, u32[]{:S(2)}, u32[]{:S(2)}) collective-permute-start(bf16[128,640]{1,0:T(8,128)(2,1)} %add_convert_fusion.1), channel_id=1, source_target_pairs={{8,0},{9,1},{10,2},{11,3},{12,4},{13,5},{14,6},{15,7},{16,8},{17,9... | collective-permute-start | bytes 491528 | tf_op jit(solution)/shard_map/ppermute | solution.py:10
  85.5 41.1 %collective-permute-start.21 = (bf16[128,640]{1,0:T(8,128)(2,1)}, bf16[128,640]{1,0:T(8,128)(2,1)}, u32[]{:S(2)}, u32[]{:S(2)}) collective-permute-start(bf16[128,640]{1,0:T(8,128)(2,1)} %add_convert_fusion.1), channel_id=1, source_target_pairs={{4,0},{5,1},{6,2},{7,3},{8,4},{9,5},{10,6},{11,7},{12,8},{13,9},{1... | collective-permute-start | bytes 491528 | tf_op jit(solution)/shard_map/ppermute | solution.py:10
  86.8 40.9 %collective-permute-start.22 = (bf16[128,640]{1,0:T(8,128)(2,1)}, bf16[128,640]{1,0:T(8,128)(2,1)}, u32[]{:S(2)}, u32[]{:S(2)}) collective-permute-start(bf16[128,640]{1,0:T(8,128)(2,1)} %add_convert_fusion.1), channel_id=1, source_target_pairs={{0,4},{1,5},{2,6},{3,7},{4,8},{5,9},{6,10},{7,11},{8,12},{9,13},{1... | collective-permute-start | bytes 491528 | tf_op jit(solution)/shard_map/ppermute | solution.py:10
  93.0 35.7 %collective-permute-start.23 = (bf16[128,640]{1,0:T(8,128)(2,1)}, bf16[128,640]{1,0:T(8,128)(2,1)}, u32[]{:S(2)}, u32[]{:S(2)}) collective-permute-start(bf16[128,640]{1,0:T(8,128)(2,1)} %add_convert_fusion.1), channel_id=1, source_target_pairs={{0,8},{1,9},{2,10},{3,11},{4,12},{5,13},{6,14},{7,15},{8,16},{9,17... | collective-permute-start | bytes 491528 | tf_op jit(solution)/shard_map/ppermute | solution.py:10
  104.1 5.6 %collective-permute-start.17 = (f32[8,128]{1,0:T(8,128)S(1)}, f32[8,128]{1,0:T(8,128)S(1)}, u32[]{:S(2)}, u32[]{:S(2)}) collective-permute-start(f32[8,128]{1,0:T(8,128)S(1)} %add.280), channel_id=1, source_target_pairs={{0,32},{1,33},{2,34},{3,35},{4,36},{5,37},{6,38},{7,39},{8,40},{9,... | collective-permute-start | bytes 12296 | tf_op jit(solution)/shard_map/ppermute | solution.py:15
  109.7 6.1 %collective-permute-start.18 = (f32[8,128]{1,0:T(8,128)S(1)}, f32[8,128]{1,0:T(8,128)S(1)}, u32[]{:S(2)}, u32[]{:S(2)}) collective-permute-start(f32[8,128]{1,0:T(8,128)S(1)} %add.281), channel_id=1, source_target_pairs={{0,128},{1,129},{2,130},{3,131},{4,132},{5,133},{6,134},{7,135},{8... | collective-permute-start | bytes 12296 | tf_op jit(solution)/shard_map/ppermute | solution.py:15
  114.2 15.5 %copy-start.1 = (bf16[5,640,640]{2,1,0:T(8,128)(2,1)S(1)}, bf16[5,640,640]{2,1,0:T(8,128)(2,1)}, u32[]{:S(2)}) copy-start(bf16[5,640,640]{2,1,0:T(8,128)(2,1)} %param.13) | copy-start | bytes 12288004
  115.8 7.5 %collective-permute-start.19 = (f32[8,128]{1,0:T(8,128)S(1)}, f32[8,128]{1,0:T(8,128)S(1)}, u32[]{:S(2)}, u32[]{:S(2)}) collective-permute-start(f32[8,128]{1,0:T(8,128)S(1)} %add.282), channel_id=1, source_target_pairs={{0,8},{1,9},{2,10},{3,11},{4,12},{5,13},{6,14},{7,15},{8,0},{9,1},... | collective-permute-start | bytes 12296 | tf_op jit(solution)/shard_map/ppermute | solution.py:15
  123.3 9.6 %collective-permute-start.35 = (bf16[64,5,640]{2,0,1:T(8,128)(2,1)S(1)}, bf16[64,5,640]{2,0,1:T(8,128)(2,1)S(1)}, u32[]{:S(2)}, u32[]{:S(2)}) collective-permute-start(bf16[64,5,640]{2,0,1:T(8,128)(2,1)S(1)} %get-tuple-element.14), channel_id=1, source_target_pairs={{0,1},{1,0},{2,3},{3,2},{4,5},{5,4},{6,7},{7,6},{8,9},{9,8},{10,11... | collective-permute-start | bytes 1228808 | tf_op jit(solution)/shard_map/ppermute | solution.py:15
  125.2 7.8 %collective-permute-start.34 = (bf16[64,5,640]{2,0,1:T(8,128)(2,1)S(1)}, bf16[64,5,640]{2,0,1:T(8,128)(2,1)S(1)}, u32[]{:S(2)}, u32[]{:S(2)}) collective-permute-start(bf16[64,5,640]{2,0,1:T(8,128)(2,1)S(1)} %get-tuple-element.13), channel_id=1, source_target_pairs={{0,1},{1,0},{2,3},{3,2},{4,5},{5,4},{6,7},{7,6},{8,9},{9,8},{10,11... | collective-permute-start | bytes 1228808 | tf_op jit(solution)/shard_map/ppermute | solution.py:15
  132.3 3.0 %collective-permute-start.25 = (bf16[64,5,640]{2,0,1:T(8,128)(2,1)S(1)}, bf16[64,5,640]{2,0,1:T(8,128)(2,1)S(1)}, u32[]{:S(2)}, u32[]{:S(2)}) collective-permute-start(bf16[64,5,640]{2,0,1:T(8,128)(2,1)S(1)} %get-tuple-element.16), channel_id=1, source_target_pairs={{0,1},{1,0},{2,3},{3,2},{4,5},{5,4},{6,7},{7,6},{8,9},{9,8},{10,11... | collective-permute-start | bytes 1228808 | tf_op jit(solution)/shard_map/ppermute | solution.py:15
  132.4 2.9 %collective-permute-start.24 = (bf16[64,5,640]{2,0,1:T(8,128)(2,1)S(1)}, bf16[64,5,640]{2,0,1:T(8,128)(2,1)S(1)}, u32[]{:S(2)}, u32[]{:S(2)}) collective-permute-start(bf16[64,5,640]{2,0,1:T(8,128)(2,1)S(1)} %get-tuple-element.15), channel_id=1, source_target_pairs={{0,1},{1,0},{2,3},{3,2},{4,5},{5,4},{6,7},{7,6},{8,9},{9,8},{10,11... | collective-permute-start | bytes 1228808 | tf_op jit(solution)/shard_map/ppermute | solution.py:15
  133.2 8.0 %collective-permute-start.37 = (bf16[32,5,640]{2,0,1:T(8,128)(2,1)S(1)}, bf16[32,5,640]{2,0,1:T(8,128)(2,1)S(1)}, u32[]{:S(2)}, u32[]{:S(2)}) collective-permute-start(bf16[32,5,640]{2,0,1:T(8,128)(2,1)S(1)} %get-tuple-element.18), channel_id=1, source_target_pairs={{0,2},{1,3},{2,0},{3,1},{4,6},{5,7},{6,4},{7,5},{8,10},{9,11},{10,... | collective-permute-start | bytes 614408 | tf_op jit(solution)/shard_map/ppermute | solution.py:15
  134.1 10.6 %collective-permute-start.36 = (bf16[32,5,640]{2,0,1:T(8,128)(2,1)S(1)}, bf16[32,5,640]{2,0,1:T(8,128)(2,1)S(1)}, u32[]{:S(2)}, u32[]{:S(2)}) collective-permute-start(bf16[32,5,640]{2,0,1:T(8,128)(2,1)S(1)} %get-tuple-element.17), channel_id=1, source_target_pairs={{0,2},{1,3},{2,0},{3,1},{4,6},{5,7},{6,4},{7,5},{8,10},{9,11},{10,... | collective-permute-start | bytes 614408 | tf_op jit(solution)/shard_map/ppermute | solution.py:15
  144.8 6.3 %collective-permute-start.38 = (bf16[32,5,640]{2,0,1:T(8,128)(2,1)S(1)}, bf16[32,5,640]{2,0,1:T(8,128)(2,1)S(1)}, u32[]{:S(2)}, u32[]{:S(2)}) collective-permute-start(bf16[32,5,640]{2,0,1:T(8,128)(2,1)S(1)} %dynamic-slice_convert_fusion.4), channel_id=1, source_target_pairs={{0,16},{1,17},{2,18},{3,19},{4,20},{5,21},{6,22},{7,23},{8,24},{9,... | collective-permute-start | bytes 614408 | tf_op jit(solution)/shard_map/ppermute | solution.py:15
  145.6 8.0 %collective-permute-start.27 = (bf16[32,5,640]{2,0,1:T(8,128)(2,1)S(1)}, bf16[32,5,640]{2,0,1:T(8,128)(2,1)S(1)}, u32[]{:S(2)}, u32[]{:S(2)}) collective-permute-start(bf16[32,5,640]{2,0,1:T(8,128)(2,1)S(1)} %get-tuple-element.20), channel_id=1, source_target_pairs={{0,2},{1,3},{2,0},{3,1},{4,6},{5,7},{6,4},{7,5},{8,10},{9,11},{10,... | collective-permute-start | bytes 614408 | tf_op jit(solution)/shard_map/ppermute | solution.py:15
  146.7 9.3 %collective-permute-start.26 = (bf16[32,5,640]{2,0,1:T(8,128)(2,1)S(1)}, bf16[32,5,640]{2,0,1:T(8,128)(2,1)S(1)}, u32[]{:S(2)}, u32[]{:S(2)}) collective-permute-start(bf16[32,5,640]{2,0,1:T(8,128)(2,1)S(1)} %get-tuple-element.19), channel_id=1, source_target_pairs={{0,2},{1,3},{2,0},{3,1},{4,6},{5,7},{6,4},{7,5},{8,10},{9,11},{10,... | collective-permute-start | bytes 614408 | tf_op jit(solution)/shard_map/ppermute | solution.py:15
  151.2 5.0 %collective-permute-start.39 = (bf16[16,5,640]{2,0,1:T(8,128)(2,1)S(1)}, bf16[16,5,640]{2,0,1:T(8,128)(2,1)S(1)}, u32[]{:S(2)}, u32[]{:S(2)}) collective-permute-start(bf16[16,5,640]{2,0,1:T(8,128)(2,1)S(1)} %dynamic-slice_convert_fusion.6), channel_id=1, source_target_pairs={{0,64},{1,65},{2,66},{3,67},{4,68},{5,69},{6,70},{7,71},{8,72},{9,... | collective-permute-start | bytes 307208 | tf_op jit(solution)/shard_map/ppermute | solution.py:15
  156.3 5.2 %collective-permute-start.40 = (bf16[8,5,640]{2,0,1:T(8,128)(2,1)S(1)}, bf16[8,5,640]{2,0,1:T(8,128)(2,1)S(1)}, u32[]{:S(2)}, u32[]{:S(2)}) collective-permute-start(bf16[8,5,640]{2,0,1:T(8,128)(2,1)S(1)} %dynamic-slice_convert_fusion.8), channel_id=1, source_target_pairs={{0,4},{1,5},{2,6},{3,7},{4,0},{5,1},{6,2},{7,3},{8,12},{9,13},{10,... | collective-permute-start | bytes 153608 | tf_op jit(solution)/shard_map/ppermute | solution.py:15
  158.8 5.8 %collective-permute-start.28 = (bf16[32,5,640]{2,0,1:T(8,128)(2,1)S(1)}, bf16[32,5,640]{2,0,1:T(8,128)(2,1)S(1)}, u32[]{:S(2)}, u32[]{:S(2)}) collective-permute-start(bf16[32,5,640]{2,0,1:T(8,128)(2,1)S(1)} %dynamic-slice_convert_fusion.5), channel_id=1, source_target_pairs={{0,16},{1,17},{2,18},{3,19},{4,20},{5,21},{6,22},{7,23},{8,24},{9,... | collective-permute-start | bytes 614408 | tf_op jit(solution)/shard_map/ppermute | solution.py:15
  161.5 5.4 %collective-permute-start.41 = (bf16[4,5,640]{2,0,1:T(4,128)(2,1)S(1)}, bf16[4,5,640]{2,0,1:T(4,128)(2,1)S(1)}, u32[]{:S(2)}, u32[]{:S(2)}) collective-permute-start(bf16[4,5,640]{2,0,1:T(4,128)(2,1)S(1)} %dynamic-slice_convert_fusion.10), channel_id=1, source_target_pairs={{0,32},{1,33},{2,34},{3,35},{4,36},{5,37},{6,38},{7,39},{8,40},{9,... | collective-permute-start | bytes 76808 | tf_op jit(solution)/shard_map/ppermute | solution.py:15
  164.7 4.7 %collective-permute-start.29 = (bf16[16,5,640]{2,0,1:T(8,128)(2,1)S(1)}, bf16[16,5,640]{2,0,1:T(8,128)(2,1)S(1)}, u32[]{:S(2)}, u32[]{:S(2)}) collective-permute-start(bf16[16,5,640]{2,0,1:T(8,128)(2,1)S(1)} %dynamic-slice_convert_fusion.7), channel_id=1, source_target_pairs={{0,64},{1,65},{2,66},{3,67},{4,68},{5,69},{6,70},{7,71},{8,72},{9,... | collective-permute-start | bytes 307208 | tf_op jit(solution)/shard_map/ppermute | solution.py:15
  169.5 5.8 %collective-permute-start.30 = (bf16[8,5,640]{2,0,1:T(8,128)(2,1)S(1)}, bf16[8,5,640]{2,0,1:T(8,128)(2,1)S(1)}, u32[]{:S(2)}, u32[]{:S(2)}) collective-permute-start(bf16[8,5,640]{2,0,1:T(8,128)(2,1)S(1)} %dynamic-slice_convert_fusion.9), channel_id=1, source_target_pairs={{0,4},{1,5},{2,6},{3,7},{4,0},{5,1},{6,2},{7,3},{8,12},{9,13},{10,... | collective-permute-start | bytes 153608 | tf_op jit(solution)/shard_map/ppermute | solution.py:15
  171.9 6.0 %collective-permute-start.42 = (bf16[2,5,640]{2,0,1:T(2,128)(2,1)S(1)}, bf16[2,5,640]{2,0,1:T(2,128)(2,1)S(1)}, u32[]{:S(2)}, u32[]{:S(2)}) collective-permute-start(bf16[2,5,640]{2,0,1:T(2,128)(2,1)S(1)} %dynamic-slice_convert_fusion.12), channel_id=1, source_target_pairs={{0,128},{1,129},{2,130},{3,131},{4,132},{5,133},{6,134},{7,135},{8... | collective-permute-start | bytes 38408 | tf_op jit(solution)/shard_map/ppermute | solution.py:15
  175.3 5.4 %collective-permute-start.31 = (bf16[4,5,640]{2,0,1:T(4,128)(2,1)S(1)}, bf16[4,5,640]{2,0,1:T(4,128)(2,1)S(1)}, u32[]{:S(2)}, u32[]{:S(2)}) collective-permute-start(bf16[4,5,640]{2,0,1:T(4,128)(2,1)S(1)} %dynamic-slice_convert_fusion.11), channel_id=1, source_target_pairs={{0,32},{1,33},{2,34},{3,35},{4,36},{5,37},{6,38},{7,39},{8,40},{9,... | collective-permute-start | bytes 76808 | tf_op jit(solution)/shard_map/ppermute | solution.py:15
  180.8 8.1 %collective-permute-start.32 = (bf16[2,5,640]{2,0,1:T(2,128)(2,1)S(1)}, bf16[2,5,640]{2,0,1:T(2,128)(2,1)S(1)}, u32[]{:S(2)}, u32[]{:S(2)}) collective-permute-start(bf16[2,5,640]{2,0,1:T(2,128)(2,1)S(1)} %dynamic-slice_convert_fusion.13), channel_id=1, source_target_pairs={{0,128},{1,129},{2,130},{3,131},{4,132},{5,133},{6,134},{7,135},{8... | collective-permute-start | bytes 38408 | tf_op jit(solution)/shard_map/ppermute | solution.py:15
  183.2 9.0 %collective-permute-start.43 = (bf16[1,5,640]{2,0,1:T(2,128)(2,1)S(1)}, bf16[1,5,640]{2,0,1:T(2,128)(2,1)S(1)}, u32[]{:S(2)}, u32[]{:S(2)}) collective-permute-start(bf16[1,5,640]{2,0,1:T(2,128)(2,1)S(1)} %dynamic-slice_convert_fusion.14), channel_id=1, source_target_pairs={{0,8},{1,9},{2,10},{3,11},{4,12},{5,13},{6,14},{7,15},{8,0},{9,1},... | collective-permute-start | bytes 19208 | tf_op jit(solution)/shard_map/ppermute | solution.py:15
  189.0 7.7 %collective-permute-start.33 = (bf16[1,5,640]{2,0,1:T(2,128)(2,1)S(1)}, bf16[1,5,640]{2,0,1:T(2,128)(2,1)S(1)}, u32[]{:S(2)}, u32[]{:S(2)}) collective-permute-start(bf16[1,5,640]{2,0,1:T(2,128)(2,1)S(1)} %dynamic-slice_convert_fusion.15), channel_id=1, source_target_pairs={{0,8},{1,9},{2,10},{3,11},{4,12},{5,13},{6,14},{7,15},{8,0},{9,1},... | collective-permute-start | bytes 19208 | tf_op jit(solution)/shard_map/ppermute | solution.py:15
  (4 other events, 12.0 us)
